TPU v7x, 1024 devices: a whole 4x8x16 slice. The times are simulated.
1024 devices in a mesh: seq: 32 (over y, x_hi, core), tp: 32 (over z, x_lo).
Axes of the slice: x: 4 (x_hi: 2, x_lo: 2; x = x_hi * 2 + x_lo), y: 8, z: 16, core: 2. Of those that a mesh axis runs over, the one named last changes fastest.
Arguments:
- tokens: bfloat16 [4096, 8192], P('seq', 'tp'), may hold values from -6 to 6
- w_gate: bfloat16 [8192, 8192], P(None, 'tp'), may hold values from -0.125 to 0.125
- w_conv_in: bfloat16 [8192, 8192], P(None, 'tp'), may hold values from -0.125 to 0.125
- conv_weight: float32 [4, 8192], P(None, 'tp'), may hold values from -3 to 3
- conv_bias: float32 [8192], P('tp'), may hold values from -3 to 3
- score_head: bfloat16 [10, 8192], P(None, 'tp'), may hold values from -6 to 6
- targets: int32 [4096], P('seq'), may hold values from 0 to 9
- loss_mask: int32 [4096], P('seq'), may hold values 0 or 1
Outputs:
- gated: bfloat16 [4096, 8192], P('seq', 'tp')
- d_tokens: bfloat16 [4096, 8192], P('seq', 'tp')
All inputs are finite; a program needn't handle non-finite values. No bound on the sum of `loss_mask` on one device may be relied on, other than what follows from the above.
Results may differ from a plain program's by a relative error of at most 0.03.
Values may be sent and summed in bfloat16 or wider, within the bound.
No kernel may reach another device: no remote copies, remote signals or barrier semaphores. Data moves between devices by JAX's collectives and lax.ppermute only.
A program may use at most 32 MiB of HBM per device.

v0:
```python
import jax
import jax.numpy as jnp
from jax import lax
from jax.sharding import PartitionSpec as P


def passed_along(block, axis, distance):
    devices = range(lax.axis_size(axis))
    route = [(i - distance, i) for i in devices if i - distance in devices]
    return lax.ppermute(block, axis, route)


def silu_slope(value):
    sig = jax.nn.sigmoid(value)
    return sig * (1.0 + value * (1.0 - sig))


def conv_back(weights, padded, count):
    taps = weights.shape[0]
    return sum(
        (weights[k][None, :] * padded[taps - 1 - k : taps - 1 - k + count] for k in range(taps))
    )


def on_device(tokens, w_gate, w_conv_in, conv_weight, conv_bias, score_head, targets, loss_mask):
    rows = tokens.shape[0]
    chans = w_gate.shape[1]
    taps = conv_weight.shape[0]
    piece = lax.all_gather(tokens, "tp", axis=1, tiled=True)
    gate_acc = jnp.dot(piece, w_gate, preferred_element_type=jnp.float32)
    xin_acc = jnp.dot(piece, w_conv_in, preferred_element_type=jnp.float32)
    gate16 = lax.optimization_barrier(gate_acc.astype(jnp.bfloat16))
    zgate = gate16.astype(jnp.float32)
    xin16 = lax.optimization_barrier(xin_acc.astype(jnp.bfloat16))
    before = passed_along(xin16[rows - (taps - 1) :], "seq", 1)
    padded = jnp.concatenate([before, xin16], axis=0).astype(jnp.float32)
    conv_out = conv_bias[None, :] + sum(
        (conv_weight[k][None, :] * padded[k : k + rows] for k in range(taps))
    )
    active = jax.nn.silu(conv_out)
    sgate = jax.nn.silu(zgate)
    gated = (active * sgate).astype(jnp.bfloat16)
    scores = score_head.shape[0]
    onehot = (targets[:, None] == jnp.arange(scores, dtype=jnp.int32)[None, :]).astype(jnp.bfloat16)
    picked = jnp.dot(onehot, score_head, preferred_element_type=jnp.float32)
    dgated = loss_mask.astype(jnp.float32)[:, None] * picked
    dgate16 = (dgated * active * silu_slope(zgate)).astype(jnp.bfloat16)
    dconv = dgated * sgate * silu_slope(conv_out)
    edge_zeros = jnp.zeros((taps - 1, chans), jnp.float32)
    local = conv_back(conv_weight, jnp.concatenate([dconv, edge_zeros], axis=0), rows)
    front = conv_back(
        conv_weight, jnp.concatenate([edge_zeros, dconv[: taps - 1]], axis=0), taps - 1
    )
    arrived = passed_along(front, "seq", -1)
    dxin = jnp.concatenate(
        [local[: rows - (taps - 1)], local[rows - (taps - 1) :] + arrived], axis=0
    )
    dxin16 = dxin.astype(jnp.bfloat16)
    spec = (((1,), (1,)), ((), ()))
    terms = lax.dot_general(dgate16, w_gate, spec, preferred_element_type=jnp.float32)
    terms = terms + lax.dot_general(dxin16, w_conv_in, spec, preferred_element_type=jnp.float32)
    d_tokens = lax.psum_scatter(terms.astype(jnp.bfloat16), "tp", scatter_dimension=1, tiled=True)
    return (gated, d_tokens)


def solution(mesh):
    placed = (
        P("seq", "tp"),
        P(None, "tp"),
        P(None, "tp"),
        P(None, "tp"),
        P("tp"),
        P(None, "tp"),
        P("seq"),
        P("seq"),
    )
    return jax.shard_map(
        on_device,
        mesh=mesh,
        in_specs=placed,
        out_specs=(P("seq", "tp"), P("seq", "tp")),
        check_vma=False,
    )
```

profile of v0, /device:TPU:56, one launch (start us, length us, event | category | flops | bytes accessed | tf_op | source)
XLA Modules:
  0.0 324.5 jit_solution(15891775615607382127)
XLA Ops:
  7.2 0.0 copy-start
  7.2 0.0 all-gather.2.cloned.1.call-start
  7.2 0.7 all-gather.2.cloned.1.call-update
  7.9 0.0 reduce-scatter.2.cloned.1.call-start
  8.0 0.7 convert_element_type.31
  8.6 0.8 fusion.31
  9.5 148.1 %all-gather.2.cloned.1.call-done = bf16[128,8192]{1,0:T(8,128)(2,1)} async-done(((bf16[128,256]{1,0:T(8,128)(2,1)}), bf16[128,8192]{1,0:T(8,128)(2,1)}) %all-gather.2.cloned.1.call-update) | async-done | bytes 2097168 | tf_op jit(solution)/shard_map/all_gather | solution.py:29
  157.5 0.0 copy-start.1
  157.5 0.0 copy-start.3
  157.5 3.7 %convolution_convert_fusion.1 = bf16[128,256]{1,0:T(8,128)(2,1)S(1)} fusion(bf16[128,8192]{1,0:T(8,128)(2,1)} %all-gather.2.cloned.1.call-done, bf16[8192,256]{1,0:T(8,128)(2,1)} %param.10), kind=kOutput, calls=%fused_computation.4 | convolution fusion | flops 536903680 | bytes 6356992 | tf_op jit(solution)/shard_map/dot_general | solution.py:31
  161.2 0.0 copy-start.4
  161.2 0.0 copy-start.5
  161.3 2.1 collective-permute-start
  163.3 0.0 copy-done.1
  163.3 0.0 copy-done.3
  163.4 0.8 convolution_convert_fusion
  164.1 4.6 %collective-permute-done = bf16[3,256]{1,0:T(4,128)(2,1)S(1)} collective-permute-done((bf16[3,256]{1,0:T(4,128)(2,1)S(1)}, bf16[3,256]{1,0:T(4,128)(2,1)S(1)}, u32[]{:S(2)}, u32[]{:S(2)}) %collective-permute-start) | collective-permute-done | bytes 1568 | tf_op jit(solution)/shard_map/ppermute | solution.py:10
  168.7 0.0 copy-done
  168.7 0.0 copy-done.4
  168.8 0.0 copy-done.5
  168.8 0.3 multiply_multiply_fusion
  169.0 1.9 collective-permute-start.1
  171.0 0.0 copy-start.2
  171.0 1.4 fusion.14
  172.4 0.1 multiply_add_fusion
  172.5 0.0 collective-permute-done.1
  172.5 0.6 copy-done.2
  173.2 2.8 fusion
  176.0 0.0 reduce-scatter.2.cloned.1.call-update
  176.0 0.7 multiply_convert_fusion
  176.7 140.9 %reduce-scatter.2.cloned.1.call-done = bf16[128,256]{1,0:T(8,128)(2,1)} async-done(((bf16[128,8192]{1,0:T(8,128)(2,1)}), bf16[128,256]{1,0:T(8,128)(2,1)}) %reduce-scatter.2.cloned.1.call-update) | async-done | bytes 65552 | tf_op jit(solution)/shard_map/reduce_scatter | solution.py:62
  (7 shorter events, 0.1 us)
Async XLA Ops:
  7.2 161.6 %copy-start = (bf16[10,256]{1,0:T(8,128)(2,1)S(1)}, bf16[10,256]{1,0:T(8,128)(2,1)}, u32[]{:S(2)}) copy-start(bf16[10,256]{1,0:T(8,128)(2,1)} %param.13) | copy-start | bytes 15364
  7.2 150.4 %all-gather.2.cloned.1.call-start = ((), (), s32[]{:S(2)}) async-start(), calls=%async_computation.1 | async-start | bytes 2162688 | tf_op jit(solution)/shard_map/all_gather | solution.py:29
  7.9 309.8 %reduce-scatter.2.cloned.1.call-start = ((), (), s32[]{:S(2)}) async-start(), calls=%async_computation.2 | async-start | bytes 2162688 | tf_op jit(solution)/shard_map/reduce_scatter | solution.py:62
  157.5 5.8 %copy-start.1 = (bf16[8192,256]{1,0:T(8,128)(2,1)S(1)}, bf16[8192,256]{1,0:T(8,128)(2,1)}, u32[]{:S(2)}) copy-start(bf16[8192,256]{1,0:T(8,128)(2,1)} %param.9) | copy-start | bytes 12582916
  157.5 5.8 %copy-start.3 = (bf16[128,8192]{1,0:T(8,128)(2,1)S(1)}, bf16[128,8192]{1,0:T(8,128)(2,1)}, u32[]{:S(2)}) copy-start(bf16[128,8192]{1,0:T(8,128)(2,1)} %all-gather.2.cloned.1.call-done) | copy-start | bytes 6291460
  161.2 7.5 %copy-start.4 = (f32[256]{0:T(256)S(1)}, f32[256]{0:T(256)}, u32[]{:S(2)}) copy-start(f32[256]{0:T(256)} %param.12) | copy-start | bytes 3076
  161.2 7.5 %copy-start.5 = (s32[128]{0:T(128)S(1)}, s32[128]{0:T(128)}, u32[]{:S(2)}) copy-start(s32[128]{0:T(128)} %param.14) | copy-start | bytes 1540
  161.3 7.4 %collective-permute-start = (bf16[3,256]{1,0:T(4,128)(2,1)S(1)}, bf16[3,256]{1,0:T(4,128)(2,1)S(1)}, u32[]{:S(2)}, u32[]{:S(2)}) collective-permute-start(bf16[3,256]{1,0:T(4,128)(2,1)S(1)} %slice.77), channel_id=1, source_target_pairs={{0,32},{32,64},{64,96},{96,128},{128,160},{160,192},{192,224},{224... | collective-permute-start | bytes 4616 | tf_op jit(solution)/shard_map/ppermute | solution.py:10
  169.0 3.5 %collective-permute-start.1 = (f32[3,256]{1,0:T(4,128)S(1)}, f32[3,256]{1,0:T(4,128)S(1)}, u32[]{:S(2)}, u32[]{:S(2)}) collective-permute-start(f32[3,256]{1,0:T(4,128)S(1)} %fusion.25), channel_id=1, source_target_pairs={{32,0},{64,32},{96,64},{128,96},{160,128},{192,160},{224,192},{256... | collective-permute-start | bytes 9224 | tf_op jit(solution)/shard_map/ppermute | solution.py:10
  171.0 2.2 copy-start.2
Sparse Core Ops, SparseCore 0:
  10.6 146.8 all-gather.1
  176.1 141.4 reduce-scatter.1
where the time goes:
time: 325 us
  waiting for transfers between devices  294 us (90%)
  between operations  14.2 us (4%)
  matrix products  8.95 us (3%)
  starting transfers between devices  4.05 us (1%)
    all_gather x1, waiting for transfers between devices, on_device(): piece = lax.all_gather(tokens, 'tp', axis=1, tiled=True)  148 us
    reduce_scatter x1, waiting for transfers between devices, on_device(): lax.psum_scatter(terms.astype(jnp.bfloat16), 'tp', scatter_dimension=1, t...  141 us
  transfers between devices with their start and end apart: 4, of which 3 were waited for; matrix products, arithmetic and copies ran while one was open for 1% of the time, Pallas kernels for 0%

commit v1 on v0

--- a/solution.py
+++ b/solution.py
@@ -1,7 +1,68 @@
 import jax
 import jax.numpy as jnp
 from jax import lax
+from jax.sharding import Mesh
 from jax.sharding import PartitionSpec as P
+
+TP = ("tz", "tx")
+
+
+def shifted(block, axis, distance):
+    size = lax.axis_size(axis)
+    return lax.ppermute(block, axis, [(i, (i + distance) % size) for i in range(size)])
+
+
+def halves_in_order(mine, other):
+    first = lax.axis_index("tx") == 0
+    return jnp.where(first, jnp.concatenate([mine, other], 1), jnp.concatenate([other, mine], 1))
+
+
+def gather_features(tokens):
+    rows = tokens.shape[0]
+    pair = halves_in_order(tokens, shifted(tokens, "tx", 1))
+    count = lax.axis_size("tz")
+    blocks = [pair] * count
+    ahead = pair
+    behind = pair
+    for step in range(1, count // 2 + 1):
+        ahead = shifted(ahead, "tz", 1)
+        blocks[-step % count] = ahead
+        if step < count - step:
+            behind = shifted(behind, "tz", -1)
+            blocks[step] = behind
+    stacked = jnp.stack(blocks, 0)
+    doubled = jnp.concatenate([stacked, stacked], 0)
+    start = (count - lax.axis_index("tz")) % count
+    ordered = lax.dynamic_slice_in_dim(doubled, start, count, 0)
+    return ordered.transpose(1, 0, 2).reshape(rows, -1)
+
+
+def scatter_features(terms16):
+    rows = terms16.shape[0]
+    count = lax.axis_size("tz")
+    width = terms16.shape[1] // count
+    per_dest = terms16.reshape(rows, count, width).transpose(1, 0, 2)
+    doubled = jnp.concatenate([per_dest, per_dest], 0)
+    own = lax.dynamic_slice_in_dim(doubled, lax.axis_index("tz"), count, 0).astype(jnp.float32)
+    right = count - 1 - count // 2
+    left = count // 2
+    total = own[0]
+    if right > 0:
+        acc = own[right]
+        for step in range(1, right):
+            acc = shifted(acc.astype(jnp.bfloat16), "tz", 1).astype(jnp.float32) + own[right - step]
+        total = total + shifted(acc.astype(jnp.bfloat16), "tz", 1).astype(jnp.float32)
+    if left > 0:
+        acc = own[left]
+        for step in range(1, left):
+            acc = shifted(acc.astype(jnp.bfloat16), "tz", -1).astype(jnp.float32) + own[left + step]
+        total = total + shifted(acc.astype(jnp.bfloat16), "tz", -1).astype(jnp.float32)
+    half = width // 2
+    first = lax.axis_index("tx") == 0
+    mine = jnp.where(first, total[:, :half], total[:, half:])
+    other = jnp.where(first, total[:, half:], total[:, :half])
+    arrived = shifted(other.astype(jnp.bfloat16), "tx", 1).astype(jnp.float32)
+    return (mine + arrived).astype(jnp.bfloat16)
 
 
 def passed_along(block, axis, distance):
@@ -26,7 +87,7 @@
     rows = tokens.shape[0]
     chans = w_gate.shape[1]
     taps = conv_weight.shape[0]
-    piece = lax.all_gather(tokens, "tp", axis=1, tiled=True)
+    piece = gather_features(tokens)
     gate_acc = jnp.dot(piece, w_gate, preferred_element_type=jnp.float32)
     xin_acc = jnp.dot(piece, w_conv_in, preferred_element_type=jnp.float32)
     gate16 = lax.optimization_barrier(gate_acc.astype(jnp.bfloat16))
@@ -59,18 +120,20 @@
     spec = (((1,), (1,)), ((), ()))
     terms = lax.dot_general(dgate16, w_gate, spec, preferred_element_type=jnp.float32)
     terms = terms + lax.dot_general(dxin16, w_conv_in, spec, preferred_element_type=jnp.float32)
-    d_tokens = lax.psum_scatter(terms.astype(jnp.bfloat16), "tp", scatter_dimension=1, tiled=True)
+    d_tokens = scatter_features(terms.astype(jnp.bfloat16))
     return (gated, d_tokens)
 
 
 def solution(mesh):
+    seq, tp = mesh.shape["seq"], mesh.shape["tp"]
+    mesh = Mesh(mesh.devices.reshape(seq, tp // 2, 2), ("seq", "tz", "tx"))
     placed = (
-        P("seq", "tp"),
-        P(None, "tp"),
-        P(None, "tp"),
-        P(None, "tp"),
-        P("tp"),
-        P(None, "tp"),
+        P("seq", TP),
+        P(None, TP),
+        P(None, TP),
+        P(None, TP),
+        P(TP),
+        P(None, TP),
         P("seq"),
         P("seq"),
     )
@@ -78,6 +141,6 @@
         on_device,
         mesh=mesh,
         in_specs=placed,
-        out_specs=(P("seq", "tp"), P("seq", "tp")),
+        out_specs=(P("seq", TP), P("seq", TP)),
         check_vma=False,
     )

time: 325 us -> 194 us (0.60)
  waiting for transfers between devices: 294 us -> 46.9 us
  starting transfers between devices: 4.05 us -> 131 us
  between operations: 14.2 us -> 1.43 us
  matrix products: 8.95 us -> 5.22 us
    all_gather x1 -> x0, waiting for transfers between devices: 148 us -> none  [on_device(): piece = lax.all_gather(tokens, 'tp', axis=1, tiled=True)]
    reduce_scatter x1 -> x0, waiting for transfers between devices: 141 us -> none  [on_device(): lax.psum_scatter(terms.astype(jnp.bfloat16), 'tp', scatter_dimension=1, t...]
    ppermute x0 -> x32, starting transfers between devices: none -> 127 us  [shifted(): lax.ppermute(block, axis, [(i, (i + distance) % size) for i in range(size)])]
    ppermute x0 -> x32, waiting for transfers between devices: none -> 42.5 us  [shifted(): lax.ppermute(block, axis, [(i, (i + distance) % size) for i in range(size)])]
  transfers between devices with their start and end apart: 4 -> 34, of which waited for: 3 -> 28; matrix products, arithmetic and copies ran while one was open for 1% -> 3% of each run, Pallas kernels for 0% -> 0%
where the time goes in v1:
time: 194 us; the launch traced here: 192 us
  starting transfers between devices  131 us (68%)
  waiting for transfers between devices  46.9 us (24%)
  matrix products  5.22 us (3%)
  local copies, waits for them, and re-layouts  4.34 us (2%)
  other arithmetic  3.66 us (2%)
    ppermute x32, starting transfers between devices, shifted(): lax.ppermute(block, axis, [(i, (i + distance) % size) for i in range(size)])  127 us
    ppermute x32, waiting for transfers between devices, shifted(): lax.ppermute(block, axis, [(i, (i + distance) % size) for i in range(size)])  42.5 us
    ppermute x2, waiting for transfers between devices, passed_along(): return lax.ppermute(block, axis, route)  4.32 us
  transfers between devices with their start and end apart: 34, of which 28 were waited for; matrix products, arithmetic and copies ran while one was open for 3% of the time, Pallas kernels for 0%

profile of v1, /device:TPU:56, one launch (start us, length us, event | category | flops | bytes accessed | tf_op | source)
XLA Modules:
  0.0 192.2 jit_solution(518911114622505145)
XLA Ops:
  0.6 1.0 copy.11
  1.6 3.4 %collective-permute-start = (bf16[128,256]{0,1:T(8,128)(2,1)S(1)}, bf16[128,256]{0,1:T(8,128)(2,1)S(1)}, u32[]{:S(2)}, u32[]{:S(2)}) collective-permute-start(bf16[128,256]{0,1:T(8,128)(2,1)S(1)} %copy.11), channel_id=1, source_target_pairs={{0,1},{1,0},{2,3},{3,2},{4,5},{5,4},{6,7},{7,6},{8,9},{9,8},{10,11... | collective-permute-start | bytes 196616 | tf_op jit(solution)/shard_map/ppermute | solution.py:12
  5.0 0.8 fusion.62
  5.9 1.9 collective-permute-done
  7.8 18.2 %collective-permute-start.1 = (bf16[128,512]{0,1:T(8,128)(2,1)S(1)}, bf16[128,512]{0,1:T(8,128)(2,1)S(1)}, u32[]{:S(2)}, u32[]{:S(2)}) collective-permute-start(bf16[128,512]{0,1:T(8,128)(2,1)S(1)} %maximum_select_fusion.1), channel_id=1, source_target_pairs={{0,30},{2,0},{4,2},{6,4},{8,6},{10,8},{12,10},{14,12},{16,14},{18,... | collective-permute-start | bytes 393224 | tf_op jit(solution)/shard_map/ppermute | solution.py:12
  26.0 1.9 collective-permute-start.8
  28.7 5.4 %collective-permute-start.2 = (bf16[128,512]{0,1:T(8,128)(2,1)S(1)}, bf16[128,512]{0,1:T(8,128)(2,1)S(1)}, u32[]{:S(2)}, u32[]{:S(2)}) collective-permute-start(bf16[128,512]{0,1:T(8,128)(2,1)S(1)} %collective-permute-done.1), channel_id=1, source_target_pairs={{0,30},{2,0},{4,2},{6,4},{8,6},{10,8},{12,10},{14,12},{16,14},{18,... | collective-permute-start | bytes 393224 | tf_op jit(solution)/shard_map/ppermute | solution.py:12
  34.1 1.9 collective-permute-start.9
  36.6 5.6 %collective-permute-start.3 = (bf16[128,512]{0,1:T(8,128)(2,1)S(1)}, bf16[128,512]{0,1:T(8,128)(2,1)S(1)}, u32[]{:S(2)}, u32[]{:S(2)}) collective-permute-start(bf16[128,512]{0,1:T(8,128)(2,1)S(1)} %collective-permute-done.2), channel_id=1, source_target_pairs={{0,30},{2,0},{4,2},{6,4},{8,6},{10,8},{12,10},{14,12},{16,14},{18,... | collective-permute-start | bytes 393224 | tf_op jit(solution)/shard_map/ppermute | solution.py:12
  42.2 1.9 collective-permute-start.10
  44.7 5.6 %collective-permute-start.4 = (bf16[128,512]{0,1:T(8,128)(2,1)S(1)}, bf16[128,512]{0,1:T(8,128)(2,1)S(1)}, u32[]{:S(2)}, u32[]{:S(2)}) collective-permute-start(bf16[128,512]{0,1:T(8,128)(2,1)S(1)} %collective-permute-done.3), channel_id=1, source_target_pairs={{0,30},{2,0},{4,2},{6,4},{8,6},{10,8},{12,10},{14,12},{16,14},{18,... | collective-permute-start | bytes 393224 | tf_op jit(solution)/shard_map/ppermute | solution.py:12
  50.2 1.9 collective-permute-start.11
  52.7 5.6 %collective-permute-start.5 = (bf16[128,512]{0,1:T(8,128)(2,1)S(1)}, bf16[128,512]{0,1:T(8,128)(2,1)S(1)}, u32[]{:S(2)}, u32[]{:S(2)}) collective-permute-start(bf16[128,512]{0,1:T(8,128)(2,1)S(1)} %collective-permute-done.4), channel_id=1, source_target_pairs={{0,30},{2,0},{4,2},{6,4},{8,6},{10,8},{12,10},{14,12},{16,14},{18,... | collective-permute-start | bytes 393224 | tf_op jit(solution)/shard_map/ppermute | solution.py:12
  58.4 1.9 collective-permute-start.12
  60.4 1.5 collective-permute-done.5
  61.9 5.6 %collective-permute-start.6 = (bf16[128,512]{0,1:T(8,128)(2,1)S(1)}, bf16[128,512]{0,1:T(8,128)(2,1)S(1)}, u32[]{:S(2)}, u32[]{:S(2)}) collective-permute-start(bf16[128,512]{0,1:T(8,128)(2,1)S(1)} %collective-permute-done.5), channel_id=1, source_target_pairs={{0,30},{2,0},{4,2},{6,4},{8,6},{10,8},{12,10},{14,12},{16,14},{18,... | collective-permute-start | bytes 393224 | tf_op jit(solution)/shard_map/ppermute | solution.py:12
  67.8 1.9 collective-permute-start.13
  69.7 0.7 collective-permute-done.6
  70.5 5.6 %collective-permute-start.7 = (bf16[128,512]{0,1:T(8,128)(2,1)S(1)}, bf16[128,512]{0,1:T(8,128)(2,1)S(1)}, u32[]{:S(2)}, u32[]{:S(2)}) collective-permute-start(bf16[128,512]{0,1:T(8,128)(2,1)S(1)} %collective-permute-done.6), channel_id=1, source_target_pairs={{0,30},{2,0},{4,2},{6,4},{8,6},{10,8},{12,10},{14,12},{16,14},{18,... | collective-permute-start | bytes 393224 | tf_op jit(solution)/shard_map/ppermute | solution.py:12
  76.4 1.9 collective-permute-start.14
  78.3 6.1 %collective-permute-done.14 = bf16[128,512]{0,1:T(8,128)(2,1)S(1)} collective-permute-done((bf16[128,512]{0,1:T(8,128)(2,1)S(1)}, bf16[128,512]{0,1:T(8,128)(2,1)S(1)}, u32[]{:S(2)}, u32[]{:S(2)}) %collective-permute-start.14) | collective-permute-done | bytes 131104 | tf_op jit(solution)/shard_map/ppermute | solution.py:12
  84.5 1.9 collective-permute-start.15
  86.4 6.1 %collective-permute-done.15 = bf16[128,512]{0,1:T(8,128)(2,1)S(1)} collective-permute-done((bf16[128,512]{0,1:T(8,128)(2,1)S(1)}, bf16[128,512]{0,1:T(8,128)(2,1)S(1)}, u32[]{:S(2)}, u32[]{:S(2)}) %collective-permute-start.15) | collective-permute-done | bytes 131104 | tf_op jit(solution)/shard_map/ppermute | solution.py:12
  93.4 1.5 copy-done.2
  94.9 1.0 convolution_convert_fusion.1
  96.0 1.9 collective-permute-start.16
  97.9 1.0 convolution_convert_fusion
  98.9 4.3 %collective-permute-done.16 = bf16[3,256]{1,0:T(4,128)(2,1)S(1)} collective-permute-done((bf16[3,256]{1,0:T(4,128)(2,1)S(1)}, bf16[3,256]{1,0:T(4,128)(2,1)S(1)}, u32[]{:S(2)}, u32[]{:S(2)}) %collective-permute-start.16) | collective-permute-done | bytes 1568 | tf_op jit(solution)/shard_map/ppermute | solution.py:71
  103.6 1.9 collective-permute-start.17
  105.5 1.4 fusion.43
  107.1 1.5 fusion
  108.8 0.9 fusion.59
  109.7 1.9 collective-permute-start.25
  111.7 3.9 %collective-permute-start.18 = (bf16[128,512]{1,0:T(8,128)(2,1)S(1)}, bf16[128,512]{1,0:T(8,128)(2,1)S(1)}, u32[]{:S(2)}, u32[]{:S(2)}) collective-permute-start(bf16[128,512]{1,0:T(8,128)(2,1)S(1)} %get-tuple-element.18), channel_id=1, source_target_pairs={{0,2},{2,4},{4,6},{6,8},{8,10},{10,12},{12,14},{14,16},{16,18},{18... | collective-permute-start | bytes 393224 | tf_op jit(solution)/shard_map/ppermute | solution.py:12
  115.6 1.4 collective-permute-done.25
  117.0 2.8 %collective-permute-start.26 = (bf16[128,512]{1,0:T(8,128)(2,1)S(1)}, bf16[128,512]{1,0:T(8,128)(2,1)S(1)}, u32[]{:S(2)}, u32[]{:S(2)}) collective-permute-start(bf16[128,512]{1,0:T(8,128)(2,1)S(1)} %fusion.15), channel_id=1, source_target_pairs={{0,30},{2,0},{4,2},{6,4},{8,6},{10,8},{12,10},{14,12},{16,14},{18,... | collective-permute-start | bytes 393224 | tf_op jit(solution)/shard_map/ppermute | solution.py:12
  120.2 5.0 %collective-permute-done.26 = bf16[128,512]{1,0:T(8,128)(2,1)S(1)} collective-permute-done((bf16[128,512]{1,0:T(8,128)(2,1)S(1)}, bf16[128,512]{1,0:T(8,128)(2,1)S(1)}, u32[]{:S(2)}, u32[]{:S(2)}) %collective-permute-start.26) | collective-permute-done | bytes 131104 | tf_op jit(solution)/shard_map/ppermute | solution.py:12
  125.2 1.9 collective-permute-start.19
  127.2 5.1 %collective-permute-start.27 = (bf16[128,512]{1,0:T(8,128)(2,1)S(1)}, bf16[128,512]{1,0:T(8,128)(2,1)S(1)}, u32[]{:S(2)}, u32[]{:S(2)}) collective-permute-start(bf16[128,512]{1,0:T(8,128)(2,1)S(1)} %get-tuple-element.17), channel_id=1, source_target_pairs={{0,30},{2,0},{4,2},{6,4},{8,6},{10,8},{12,10},{14,12},{16,14},{18,... | collective-permute-start | bytes 393224 | tf_op jit(solution)/shard_map/ppermute | solution.py:12
  132.3 1.4 collective-permute-done.19
  133.7 1.2 collective-permute-done.27
  134.9 1.9 collective-permute-start.20
  136.9 5.6 %collective-permute-start.28 = (bf16[128,512]{1,0:T(8,128)(2,1)S(1)}, bf16[128,512]{1,0:T(8,128)(2,1)S(1)}, u32[]{:S(2)}, u32[]{:S(2)}) collective-permute-start(bf16[128,512]{1,0:T(8,128)(2,1)S(1)} %get-tuple-element.15), channel_id=1, source_target_pairs={{0,30},{2,0},{4,2},{6,4},{8,6},{10,8},{12,10},{14,12},{16,14},{18,... | collective-permute-start | bytes 393224 | tf_op jit(solution)/shard_map/ppermute | solution.py:12
  142.5 1.0 collective-permute-done.20
  143.5 1.5 collective-permute-done.28
  145.1 1.9 collective-permute-start.21
  147.0 5.6 %collective-permute-start.29 = (bf16[128,512]{1,0:T(8,128)(2,1)S(1)}, bf16[128,512]{1,0:T(8,128)(2,1)S(1)}, u32[]{:S(2)}, u32[]{:S(2)}) collective-permute-start(bf16[128,512]{1,0:T(8,128)(2,1)S(1)} %get-tuple-element.13), channel_id=1, source_target_pairs={{0,30},{2,0},{4,2},{6,4},{8,6},{10,8},{12,10},{14,12},{16,14},{18,... | collective-permute-start | bytes 393224 | tf_op jit(solution)/shard_map/ppermute | solution.py:12
  152.6 1.0 collective-permute-done.21
  153.6 1.5 collective-permute-done.29
  155.1 1.9 collective-permute-start.22
  157.1 5.6 %collective-permute-start.30 = (bf16[128,512]{1,0:T(8,128)(2,1)S(1)}, bf16[128,512]{1,0:T(8,128)(2,1)S(1)}, u32[]{:S(2)}, u32[]{:S(2)}) collective-permute-start(bf16[128,512]{1,0:T(8,128)(2,1)S(1)} %get-tuple-element.11), channel_id=1, source_target_pairs={{0,30},{2,0},{4,2},{6,4},{8,6},{10,8},{12,10},{14,12},{16,14},{18,... | collective-permute-start | bytes 393224 | tf_op jit(solution)/shard_map/ppermute | solution.py:12
  162.6 1.0 collective-permute-done.22
  163.6 1.5 collective-permute-done.30
  165.2 1.9 collective-permute-start.23
  167.1 5.6 %collective-permute-start.31 = (bf16[128,512]{1,0:T(8,128)(2,1)S(1)}, bf16[128,512]{1,0:T(8,128)(2,1)S(1)}, u32[]{:S(2)}, u32[]{:S(2)}) collective-permute-start(bf16[128,512]{1,0:T(8,128)(2,1)S(1)} %get-tuple-element.9), channel_id=1, source_target_pairs={{0,30},{2,0},{4,2},{6,4},{8,6},{10,8},{12,10},{14,12},{16,14},{18,... | collective-permute-start | bytes 393224 | tf_op jit(solution)/shard_map/ppermute | solution.py:12
  172.7 1.0 collective-permute-done.23
  173.7 1.5 collective-permute-done.31
  175.3 1.9 collective-permute-start.24
  177.2 5.6 %collective-permute-start.32 = (bf16[128,512]{1,0:T(8,128)(2,1)S(1)}, bf16[128,512]{1,0:T(8,128)(2,1)S(1)}, u32[]{:S(2)}, u32[]{:S(2)}) collective-permute-start(bf16[128,512]{1,0:T(8,128)(2,1)S(1)} %get-tuple-element.7), channel_id=1, source_target_pairs={{0,30},{2,0},{4,2},{6,4},{8,6},{10,8},{12,10},{14,12},{16,14},{18,... | collective-permute-start | bytes 393224 | tf_op jit(solution)/shard_map/ppermute | solution.py:12
  182.8 1.0 collective-permute-done.24
  183.8 1.5 collective-permute-done.32
  185.4 3.5 %collective-permute-start.33 = (bf16[128,256]{1,0:T(8,128)(2,1)S(1)}, bf16[128,256]{1,0:T(8,128)(2,1)S(1)}, u32[]{:S(2)}, u32[]{:S(2)}) collective-permute-start(bf16[128,256]{1,0:T(8,128)(2,1)S(1)} %select_convert_fusion), channel_id=1, source_target_pairs={{0,1},{1,0},{2,3},{3,2},{4,5},{5,4},{6,7},{7,6},{8,9},{9,8},{10,11... | collective-permute-start | bytes 196616 | tf_op jit(solution)/shard_map/ppermute | solution.py:12
  188.9 0.7 multiply_convert_fusion
  189.6 1.9 %collective-permute-done.33 = bf16[128,256]{1,0:T(8,128)(2,1)S(1)} collective-permute-done((bf16[128,256]{1,0:T(8,128)(2,1)S(1)}, bf16[128,256]{1,0:T(8,128)(2,1)S(1)}, u32[]{:S(2)}, u32[]{:S(2)}) %collective-permute-start.33) | collective-permute-done | bytes 65568 | tf_op jit(solution)/shard_map/ppermute | solution.py:12
  (78 shorter events, 6.1 us)
Async XLA Ops:
  0.6 102.7 %copy-start = (bf16[10,256]{1,0:T(8,128)(2,1)S(1)}, bf16[10,256]{1,0:T(8,128)(2,1)}, u32[]{:S(2)}) copy-start(bf16[10,256]{1,0:T(8,128)(2,1)} %param.13) | copy-start | bytes 15364
  1.6 6.2 %collective-permute-start = (bf16[128,256]{0,1:T(8,128)(2,1)S(1)}, bf16[128,256]{0,1:T(8,128)(2,1)S(1)}, u32[]{:S(2)}, u32[]{:S(2)}) collective-permute-start(bf16[128,256]{0,1:T(8,128)(2,1)S(1)} %copy.11), channel_id=1, source_target_pairs={{0,1},{1,0},{2,3},{3,2},{4,5},{5,4},{6,7},{7,6},{8,9},{9,8},{10,11... | collective-permute-start | bytes 196616 | tf_op jit(solution)/shard_map/ppermute | solution.py:12
  7.8 20.9 %collective-permute-start.1 = (bf16[128,512]{0,1:T(8,128)(2,1)S(1)}, bf16[128,512]{0,1:T(8,128)(2,1)S(1)}, u32[]{:S(2)}, u32[]{:S(2)}) collective-permute-start(bf16[128,512]{0,1:T(8,128)(2,1)S(1)} %maximum_select_fusion.1), channel_id=1, source_target_pairs={{0,30},{2,0},{4,2},{6,4},{8,6},{10,8},{12,10},{14,12},{16,14},{18,... | collective-permute-start | bytes 393224 | tf_op jit(solution)/shard_map/ppermute | solution.py:12
  26.0 8.1 %collective-permute-start.8 = (bf16[128,512]{0,1:T(8,128)(2,1)S(1)}, bf16[128,512]{0,1:T(8,128)(2,1)S(1)}, u32[]{:S(2)}, u32[]{:S(2)}) collective-permute-start(bf16[128,512]{0,1:T(8,128)(2,1)S(1)} %maximum_select_fusion.1), channel_id=1, source_target_pairs={{0,2},{2,4},{4,6},{6,8},{8,10},{10,12},{12,14},{14,16},{16,18},{18... | collective-permute-start | bytes 393224 | tf_op jit(solution)/shard_map/ppermute | solution.py:12
  28.7 7.9 %collective-permute-start.2 = (bf16[128,512]{0,1:T(8,128)(2,1)S(1)}, bf16[128,512]{0,1:T(8,128)(2,1)S(1)}, u32[]{:S(2)}, u32[]{:S(2)}) collective-permute-start(bf16[128,512]{0,1:T(8,128)(2,1)S(1)} %collective-permute-done.1), channel_id=1, source_target_pairs={{0,30},{2,0},{4,2},{6,4},{8,6},{10,8},{12,10},{14,12},{16,14},{18,... | collective-permute-start | bytes 393224 | tf_op jit(solution)/shard_map/ppermute | solution.py:12
  34.1 8.1 %collective-permute-start.9 = (bf16[128,512]{0,1:T(8,128)(2,1)S(1)}, bf16[128,512]{0,1:T(8,128)(2,1)S(1)}, u32[]{:S(2)}, u32[]{:S(2)}) collective-permute-start(bf16[128,512]{0,1:T(8,128)(2,1)S(1)} %collective-permute-done.8), channel_id=1, source_target_pairs={{0,2},{2,4},{4,6},{6,8},{8,10},{10,12},{12,14},{14,16},{16,18},{18... | collective-permute-start | bytes 393224 | tf_op jit(solution)/shard_map/ppermute | solution.py:12
  36.6 8.1 %collective-permute-start.3 = (bf16[128,512]{0,1:T(8,128)(2,1)S(1)}, bf16[128,512]{0,1:T(8,128)(2,1)S(1)}, u32[]{:S(2)}, u32[]{:S(2)}) collective-permute-start(bf16[128,512]{0,1:T(8,128)(2,1)S(1)} %collective-permute-done.2), channel_id=1, source_target_pairs={{0,30},{2,0},{4,2},{6,4},{8,6},{10,8},{12,10},{14,12},{16,14},{18,... | collective-permute-start | bytes 393224 | tf_op jit(solution)/shard_map/ppermute | solution.py:12
  42.2 8.1 %collective-permute-start.10 = (bf16[128,512]{0,1:T(8,128)(2,1)S(1)}, bf16[128,512]{0,1:T(8,128)(2,1)S(1)}, u32[]{:S(2)}, u32[]{:S(2)}) collective-permute-start(bf16[128,512]{0,1:T(8,128)(2,1)S(1)} %collective-permute-done.9), channel_id=1, source_target_pairs={{0,2},{2,4},{4,6},{6,8},{8,10},{10,12},{12,14},{14,16},{16,18},{18... | collective-permute-start | bytes 393224 | tf_op jit(solution)/shard_map/ppermute | solution.py:12
  44.7 8.1 %collective-permute-start.4 = (bf16[128,512]{0,1:T(8,128)(2,1)S(1)}, bf16[128,512]{0,1:T(8,128)(2,1)S(1)}, u32[]{:S(2)}, u32[]{:S(2)}) collective-permute-start(bf16[128,512]{0,1:T(8,128)(2,1)S(1)} %collective-permute-done.3), channel_id=1, source_target_pairs={{0,30},{2,0},{4,2},{6,4},{8,6},{10,8},{12,10},{14,12},{16,14},{18,... | collective-permute-start | bytes 393224 | tf_op jit(solution)/shard_map/ppermute | solution.py:12
  50.2 8.2 %collective-permute-start.11 = (bf16[128,512]{0,1:T(8,128)(2,1)S(1)}, bf16[128,512]{0,1:T(8,128)(2,1)S(1)}, u32[]{:S(2)}, u32[]{:S(2)}) collective-permute-start(bf16[128,512]{0,1:T(8,128)(2,1)S(1)} %collective-permute-done.10), channel_id=1, source_target_pairs={{0,2},{2,4},{4,6},{6,8},{8,10},{10,12},{12,14},{14,16},{16,18},{18... | collective-permute-start | bytes 393224 | tf_op jit(solution)/shard_map/ppermute | solution.py:12
  52.7 9.2 %collective-permute-start.5 = (bf16[128,512]{0,1:T(8,128)(2,1)S(1)}, bf16[128,512]{0,1:T(8,128)(2,1)S(1)}, u32[]{:S(2)}, u32[]{:S(2)}) collective-permute-start(bf16[128,512]{0,1:T(8,128)(2,1)S(1)} %collective-permute-done.4), channel_id=1, source_target_pairs={{0,30},{2,0},{4,2},{6,4},{8,6},{10,8},{12,10},{14,12},{16,14},{18,... | collective-permute-start | bytes 393224 | tf_op jit(solution)/shard_map/ppermute | solution.py:12
  58.4 9.3 %collective-permute-start.12 = (bf16[128,512]{0,1:T(8,128)(2,1)S(1)}, bf16[128,512]{0,1:T(8,128)(2,1)S(1)}, u32[]{:S(2)}, u32[]{:S(2)}) collective-permute-start(bf16[128,512]{0,1:T(8,128)(2,1)S(1)} %collective-permute-done.11), channel_id=1, source_target_pairs={{0,2},{2,4},{4,6},{6,8},{8,10},{10,12},{12,14},{14,16},{16,18},{18... | collective-permute-start | bytes 393224 | tf_op jit(solution)/shard_map/ppermute | solution.py:12
  61.9 8.6 %collective-permute-start.6 = (bf16[128,512]{0,1:T(8,128)(2,1)S(1)}, bf16[128,512]{0,1:T(8,128)(2,1)S(1)}, u32[]{:S(2)}, u32[]{:S(2)}) collective-permute-start(bf16[128,512]{0,1:T(8,128)(2,1)S(1)} %collective-permute-done.5), channel_id=1, source_target_pairs={{0,30},{2,0},{4,2},{6,4},{8,6},{10,8},{12,10},{14,12},{16,14},{18,... | collective-permute-start | bytes 393224 | tf_op jit(solution)/shard_map/ppermute | solution.py:12
  67.8 8.6 %collective-permute-start.13 = (bf16[128,512]{0,1:T(8,128)(2,1)S(1)}, bf16[128,512]{0,1:T(8,128)(2,1)S(1)}, u32[]{:S(2)}, u32[]{:S(2)}) collective-permute-start(bf16[128,512]{0,1:T(8,128)(2,1)S(1)} %collective-permute-done.12), channel_id=1, source_target_pairs={{0,2},{2,4},{4,6},{6,8},{8,10},{10,12},{12,14},{14,16},{16,18},{18... | collective-permute-start | bytes 393224 | tf_op jit(solution)/shard_map/ppermute | solution.py:12
  70.5 15.9 %collective-permute-start.7 = (bf16[128,512]{0,1:T(8,128)(2,1)S(1)}, bf16[128,512]{0,1:T(8,128)(2,1)S(1)}, u32[]{:S(2)}, u32[]{:S(2)}) collective-permute-start(bf16[128,512]{0,1:T(8,128)(2,1)S(1)} %collective-permute-done.6), channel_id=1, source_target_pairs={{0,30},{2,0},{4,2},{6,4},{8,6},{10,8},{12,10},{14,12},{16,14},{18,... | collective-permute-start | bytes 393224 | tf_op jit(solution)/shard_map/ppermute | solution.py:12
  76.4 8.1 %collective-permute-start.14 = (bf16[128,512]{0,1:T(8,128)(2,1)S(1)}, bf16[128,512]{0,1:T(8,128)(2,1)S(1)}, u32[]{:S(2)}, u32[]{:S(2)}) collective-permute-start(bf16[128,512]{0,1:T(8,128)(2,1)S(1)} %collective-permute-done.13), channel_id=1, source_target_pairs={{0,2},{2,4},{4,6},{6,8},{8,10},{10,12},{12,14},{14,16},{16,18},{18... | collective-permute-start | bytes 393224 | tf_op jit(solution)/shard_map/ppermute | solution.py:12
  84.5 8.1 %collective-permute-start.15 = (bf16[128,512]{0,1:T(8,128)(2,1)S(1)}, bf16[128,512]{0,1:T(8,128)(2,1)S(1)}, u32[]{:S(2)}, u32[]{:S(2)}) collective-permute-start(bf16[128,512]{0,1:T(8,128)(2,1)S(1)} %collective-permute-done.14), channel_id=1, source_target_pairs={{0,2},{2,4},{4,6},{6,8},{8,10},{10,12},{12,14},{14,16},{16,18},{18... | collective-permute-start | bytes 393224 | tf_op jit(solution)/shard_map/ppermute | solution.py:12
  92.7 2.2 %copy-start.2 = (bf16[8192,256]{1,0:T(8,128)(2,1)S(1)}, bf16[8192,256]{1,0:T(8,128)(2,1)}, u32[]{:S(2)}) copy-start(bf16[8192,256]{1,0:T(8,128)(2,1)} %param.10) | copy-start | bytes 12582916
  93.4 4.5 %copy-start.1 = (bf16[8192,256]{1,0:T(8,128)(2,1)S(1)}, bf16[8192,256]{1,0:T(8,128)(2,1)}, u32[]{:S(2)}) copy-start(bf16[8192,256]{1,0:T(8,128)(2,1)} %param.9) | copy-start | bytes 12582916
  95.9 7.4 %copy-start.3 = (f32[256]{0:T(256)S(1)}, f32[256]{0:T(256)}, u32[]{:S(2)}) copy-start(f32[256]{0:T(256)} %param.12) | copy-start | bytes 3076
  95.9 7.4 %copy-start.4 = (s32[128]{0:T(128)S(1)}, s32[128]{0:T(128)}, u32[]{:S(2)}) copy-start(s32[128]{0:T(128)} %param.14) | copy-start | bytes 1540
  96.0 7.3 %collective-permute-start.16 = (bf16[3,256]{1,0:T(4,128)(2,1)S(1)}, bf16[3,256]{1,0:T(4,128)(2,1)S(1)}, u32[]{:S(2)}, u32[]{:S(2)}) collective-permute-start(bf16[3,256]{1,0:T(4,128)(2,1)S(1)} %slice.153), channel_id=1, source_target_pairs={{0,32},{32,64},{64,96},{96,128},{128,160},{160,192},{192,224},{224... | collective-permute-start | bytes 4616 | tf_op jit(solution)/shard_map/ppermute | solution.py:71
  103.6 3.5 %collective-permute-start.17 = (f32[3,256]{1,0:T(4,128)S(1)}, f32[3,256]{1,0:T(4,128)S(1)}, u32[]{:S(2)}, u32[]{:S(2)}) collective-permute-start(f32[3,256]{1,0:T(4,128)S(1)} %fusion.54), channel_id=1, source_target_pairs={{32,0},{64,32},{96,64},{128,96},{160,128},{192,160},{224,192},{256... | collective-permute-start | bytes 9224 | tf_op jit(solution)/shard_map/ppermute | solution.py:71
  109.7 7.3 %collective-permute-start.25 = (bf16[128,512]{1,0:T(8,128)(2,1)S(1)}, bf16[128,512]{1,0:T(8,128)(2,1)S(1)}, u32[]{:S(2)}, u32[]{:S(2)}) collective-permute-start(bf16[128,512]{1,0:T(8,128)(2,1)S(1)} %get-tuple-element.19), channel_id=1, source_target_pairs={{0,30},{2,0},{4,2},{6,4},{8,6},{10,8},{12,10},{14,12},{16,14},{18,... | collective-permute-start | bytes 393224 | tf_op jit(solution)/shard_map/ppermute | solution.py:12
  111.7 8.5 %collective-permute-start.18 = (bf16[128,512]{1,0:T(8,128)(2,1)S(1)}, bf16[128,512]{1,0:T(8,128)(2,1)S(1)}, u32[]{:S(2)}, u32[]{:S(2)}) collective-permute-start(bf16[128,512]{1,0:T(8,128)(2,1)S(1)} %get-tuple-element.18), channel_id=1, source_target_pairs={{0,2},{2,4},{4,6},{6,8},{8,10},{10,12},{12,14},{14,16},{16,18},{18... | collective-permute-start | bytes 393224 | tf_op jit(solution)/shard_map/ppermute | solution.py:12
  117.0 8.1 %collective-permute-start.26 = (bf16[128,512]{1,0:T(8,128)(2,1)S(1)}, bf16[128,512]{1,0:T(8,128)(2,1)S(1)}, u32[]{:S(2)}, u32[]{:S(2)}) collective-permute-start(bf16[128,512]{1,0:T(8,128)(2,1)S(1)} %fusion.15), channel_id=1, source_target_pairs={{0,30},{2,0},{4,2},{6,4},{8,6},{10,8},{12,10},{14,12},{16,14},{18,... | collective-permute-start | bytes 393224 | tf_op jit(solution)/shard_map/ppermute | solution.py:12
  125.2 8.5 %collective-permute-start.19 = (bf16[128,512]{1,0:T(8,128)(2,1)S(1)}, bf16[128,512]{1,0:T(8,128)(2,1)S(1)}, u32[]{:S(2)}, u32[]{:S(2)}) collective-permute-start(bf16[128,512]{1,0:T(8,128)(2,1)S(1)} %get-tuple-element.16), channel_id=1, source_target_pairs={{0,2},{2,4},{4,6},{6,8},{8,10},{10,12},{12,14},{14,16},{16,18},{18... | collective-permute-start | bytes 393224 | tf_op jit(solution)/shard_map/ppermute | solution.py:12
  127.2 7.7 %collective-permute-start.27 = (bf16[128,512]{1,0:T(8,128)(2,1)S(1)}, bf16[128,512]{1,0:T(8,128)(2,1)S(1)}, u32[]{:S(2)}, u32[]{:S(2)}) collective-permute-start(bf16[128,512]{1,0:T(8,128)(2,1)S(1)} %get-tuple-element.17), channel_id=1, source_target_pairs={{0,30},{2,0},{4,2},{6,4},{8,6},{10,8},{12,10},{14,12},{16,14},{18,... | collective-permute-start | bytes 393224 | tf_op jit(solution)/shard_map/ppermute | solution.py:12
  134.9 8.5 %collective-permute-start.20 = (bf16[128,512]{1,0:T(8,128)(2,1)S(1)}, bf16[128,512]{1,0:T(8,128)(2,1)S(1)}, u32[]{:S(2)}, u32[]{:S(2)}) collective-permute-start(bf16[128,512]{1,0:T(8,128)(2,1)S(1)} %get-tuple-element.14), channel_id=1, source_target_pairs={{0,2},{2,4},{4,6},{6,8},{8,10},{10,12},{12,14},{14,16},{16,18},{18... | collective-permute-start | bytes 393224 | tf_op jit(solution)/shard_map/ppermute | solution.py:12
  136.9 8.1 %collective-permute-start.28 = (bf16[128,512]{1,0:T(8,128)(2,1)S(1)}, bf16[128,512]{1,0:T(8,128)(2,1)S(1)}, u32[]{:S(2)}, u32[]{:S(2)}) collective-permute-start(bf16[128,512]{1,0:T(8,128)(2,1)S(1)} %get-tuple-element.15), channel_id=1, source_target_pairs={{0,30},{2,0},{4,2},{6,4},{8,6},{10,8},{12,10},{14,12},{16,14},{18,... | collective-permute-start | bytes 393224 | tf_op jit(solution)/shard_map/ppermute | solution.py:12
  145.1 8.5 %collective-permute-start.21 = (bf16[128,512]{1,0:T(8,128)(2,1)S(1)}, bf16[128,512]{1,0:T(8,128)(2,1)S(1)}, u32[]{:S(2)}, u32[]{:S(2)}) collective-permute-start(bf16[128,512]{1,0:T(8,128)(2,1)S(1)} %get-tuple-element.12), channel_id=1, source_target_pairs={{0,2},{2,4},{4,6},{6,8},{8,10},{10,12},{12,14},{14,16},{16,18},{18... | collective-permute-start | bytes 393224 | tf_op jit(solution)/shard_map/ppermute | solution.py:12
  147.0 8.1 %collective-permute-start.29 = (bf16[128,512]{1,0:T(8,128)(2,1)S(1)}, bf16[128,512]{1,0:T(8,128)(2,1)S(1)}, u32[]{:S(2)}, u32[]{:S(2)}) collective-permute-start(bf16[128,512]{1,0:T(8,128)(2,1)S(1)} %get-tuple-element.13), channel_id=1, source_target_pairs={{0,30},{2,0},{4,2},{6,4},{8,6},{10,8},{12,10},{14,12},{16,14},{18,... | collective-permute-start | bytes 393224 | tf_op jit(solution)/shard_map/ppermute | solution.py:12
  155.1 8.5 %collective-permute-start.22 = (bf16[128,512]{1,0:T(8,128)(2,1)S(1)}, bf16[128,512]{1,0:T(8,128)(2,1)S(1)}, u32[]{:S(2)}, u32[]{:S(2)}) collective-permute-start(bf16[128,512]{1,0:T(8,128)(2,1)S(1)} %get-tuple-element.10), channel_id=1, source_target_pairs={{0,2},{2,4},{4,6},{6,8},{8,10},{10,12},{12,14},{14,16},{16,18},{18... | collective-permute-start | bytes 393224 | tf_op jit(solution)/shard_map/ppermute | solution.py:12
  157.1 8.1 %collective-permute-start.30 = (bf16[128,512]{1,0:T(8,128)(2,1)S(1)}, bf16[128,512]{1,0:T(8,128)(2,1)S(1)}, u32[]{:S(2)}, u32[]{:S(2)}) collective-permute-start(bf16[128,512]{1,0:T(8,128)(2,1)S(1)} %get-tuple-element.11), channel_id=1, source_target_pairs={{0,30},{2,0},{4,2},{6,4},{8,6},{10,8},{12,10},{14,12},{16,14},{18,... | collective-permute-start | bytes 393224 | tf_op jit(solution)/shard_map/ppermute | solution.py:12
  165.2 8.5 %collective-permute-start.23 = (bf16[128,512]{1,0:T(8,128)(2,1)S(1)}, bf16[128,512]{1,0:T(8,128)(2,1)S(1)}, u32[]{:S(2)}, u32[]{:S(2)}) collective-permute-start(bf16[128,512]{1,0:T(8,128)(2,1)S(1)} %get-tuple-element.8), channel_id=1, source_target_pairs={{0,2},{2,4},{4,6},{6,8},{8,10},{10,12},{12,14},{14,16},{16,18},{18... | collective-permute-start | bytes 393224 | tf_op jit(solution)/shard_map/ppermute | solution.py:12
  167.1 8.1 %collective-permute-start.31 = (bf16[128,512]{1,0:T(8,128)(2,1)S(1)}, bf16[128,512]{1,0:T(8,128)(2,1)S(1)}, u32[]{:S(2)}, u32[]{:S(2)}) collective-permute-start(bf16[128,512]{1,0:T(8,128)(2,1)S(1)} %get-tuple-element.9), channel_id=1, source_target_pairs={{0,30},{2,0},{4,2},{6,4},{8,6},{10,8},{12,10},{14,12},{16,14},{18,... | collective-permute-start | bytes 393224 | tf_op jit(solution)/shard_map/ppermute | solution.py:12
  175.3 8.5 %collective-permute-start.24 = (bf16[128,512]{1,0:T(8,128)(2,1)S(1)}, bf16[128,512]{1,0:T(8,128)(2,1)S(1)}, u32[]{:S(2)}, u32[]{:S(2)}) collective-permute-start(bf16[128,512]{1,0:T(8,128)(2,1)S(1)} %get-tuple-element.6), channel_id=1, source_target_pairs={{0,2},{2,4},{4,6},{6,8},{8,10},{10,12},{12,14},{14,16},{16,18},{18... | collective-permute-start | bytes 393224 | tf_op jit(solution)/shard_map/ppermute | solution.py:12
  177.2 8.1 %collective-permute-start.32 = (bf16[128,512]{1,0:T(8,128)(2,1)S(1)}, bf16[128,512]{1,0:T(8,128)(2,1)S(1)}, u32[]{:S(2)}, u32[]{:S(2)}) collective-permute-start(bf16[128,512]{1,0:T(8,128)(2,1)S(1)} %get-tuple-element.7), channel_id=1, source_target_pairs={{0,30},{2,0},{4,2},{6,4},{8,6},{10,8},{12,10},{14,12},{16,14},{18,... | collective-permute-start | bytes 393224 | tf_op jit(solution)/shard_map/ppermute | solution.py:12
  185.4 6.2 %collective-permute-start.33 = (bf16[128,256]{1,0:T(8,128)(2,1)S(1)}, bf16[128,256]{1,0:T(8,128)(2,1)S(1)}, u32[]{:S(2)}, u32[]{:S(2)}) collective-permute-start(bf16[128,256]{1,0:T(8,128)(2,1)S(1)} %select_convert_fusion), channel_id=1, source_target_pairs={{0,1},{1,0},{2,3},{3,2},{4,5},{5,4},{6,7},{7,6},{8,9},{9,8},{10,11... | collective-permute-start | bytes 196616 | tf_op jit(solution)/shard_map/ppermute | solution.py:12

commit v2 on v1

--- a/solution.py
+++ b/solution.py
@@ -44,25 +44,50 @@
     per_dest = terms16.reshape(rows, count, width).transpose(1, 0, 2)
     doubled = jnp.concatenate([per_dest, per_dest], 0)
     own = lax.dynamic_slice_in_dim(doubled, lax.axis_index("tz"), count, 0).astype(jnp.float32)
+    total = ring_reduce(own) if count != 16 else stride_two_reduce(own)
+    half = width // 2
+    first = lax.axis_index("tx") == 0
+    mine = jnp.where(first, total[:, :half], total[:, half:])
+    other = jnp.where(first, total[:, half:], total[:, :half])
+    arrived = shifted(other.astype(jnp.bfloat16), "tx", 1).astype(jnp.float32)
+    return (mine + arrived).astype(jnp.bfloat16)
+
+
+def hop(acc, distance):
+    return shifted(acc.astype(jnp.bfloat16), "tz", distance).astype(jnp.float32)
+
+
+def ring_reduce(own):
+    count = own.shape[0]
     right = count - 1 - count // 2
     left = count // 2
     total = own[0]
     if right > 0:
         acc = own[right]
         for step in range(1, right):
-            acc = shifted(acc.astype(jnp.bfloat16), "tz", 1).astype(jnp.float32) + own[right - step]
-        total = total + shifted(acc.astype(jnp.bfloat16), "tz", 1).astype(jnp.float32)
+            acc = hop(acc, 1) + own[right - step]
+        total = total + hop(acc, 1)
     if left > 0:
         acc = own[left]
         for step in range(1, left):
-            acc = shifted(acc.astype(jnp.bfloat16), "tz", -1).astype(jnp.float32) + own[left + step]
-        total = total + shifted(acc.astype(jnp.bfloat16), "tz", -1).astype(jnp.float32)
-    half = width // 2
-    first = lax.axis_index("tx") == 0
-    mine = jnp.where(first, total[:, :half], total[:, half:])
-    other = jnp.where(first, total[:, half:], total[:, :half])
-    arrived = shifted(other.astype(jnp.bfloat16), "tx", 1).astype(jnp.float32)
-    return (mine + arrived).astype(jnp.bfloat16)
+            acc = hop(acc, -1) + own[left + step]
+        total = total + hop(acc, -1)
+    return total
+
+
+def stride_two_reduce(own):
+    ahead = jnp.stack([own[7], own[8]])
+    behind = jnp.stack([own[9], own[10]])
+    total = own[0]
+    for step in range(1, 4):
+        ahead = hop(ahead, 2) + jnp.stack([own[7 - 2 * step], own[8 - 2 * step]])
+        got = hop(behind, -2)
+        if step < 3:
+            behind = got + jnp.stack([own[9 + 2 * step], own[10 + 2 * step]])
+        else:
+            total = total + got[1]
+            behind_odd = got[0] + own[15]
+    return total + hop(ahead[0], 1) + hop(ahead[1], 2) + hop(behind_odd, -1)
 
 
 def passed_along(block, axis, distance):

time: 194 us -> 194 us (level)
  waiting for transfers between devices: 46.9 us -> 72.4 us
  starting transfers between devices: 131 us -> 106 us
    ppermute x32 -> x26, waiting for transfers between devices: 42.5 us -> 68.1 us  [shifted(): lax.ppermute(block, axis, [(i, (i + distance) % size) for i in range(size)])]
    ppermute x32 -> x26, starting transfers between devices: 127 us -> 102 us  [shifted(): lax.ppermute(block, axis, [(i, (i + distance) % size) for i in range(size)])]
  transfers between devices with their start and end apart: 34 -> 28, of which waited for: 28 -> 19; matrix products, arithmetic and copies ran while one was open for 3% -> 3% of each run, Pallas kernels for 0% -> 0%
where the time goes in v2:
time: 194 us; the launch traced here: 193 us
  starting transfers between devices  106 us (55%)
  waiting for transfers between devices  72.4 us (37%)
  matrix products  5.22 us (3%)
  local copies, waits for them, and re-layouts  4.38 us (2%)
  other arithmetic  3.74 us (2%)
    ppermute x26, starting transfers between devices, shifted(): lax.ppermute(block, axis, [(i, (i + distance) % size) for i in range(size)])  102 us
    ppermute x26, waiting for transfers between devices, shifted(): lax.ppermute(block, axis, [(i, (i + distance) % size) for i in range(size)])  68.1 us
    ppermute x2, waiting for transfers between devices, passed_along(): return lax.ppermute(block, axis, route)  4.32 us
  transfers between devices with their start and end apart: 28, of which 19 were waited for; matrix products, arithmetic and copies ran while one was open for 3% of the time, Pallas kernels for 0%

profile of v2, /device:TPU:56, one launch (start us, length us, event | category | flops | bytes accessed | tf_op | source)
XLA Modules:
  0.0 192.7 jit_solution(6990160410722301738)
XLA Ops:
  0.6 1.0 copy.11
  1.6 3.4 %collective-permute-start = (bf16[128,256]{0,1:T(8,128)(2,1)S(1)}, bf16[128,256]{0,1:T(8,128)(2,1)S(1)}, u32[]{:S(2)}, u32[]{:S(2)}) collective-permute-start(bf16[128,256]{0,1:T(8,128)(2,1)S(1)} %copy.11), channel_id=1, source_target_pairs={{0,1},{1,0},{2,3},{3,2},{4,5},{5,4},{6,7},{7,6},{8,9},{9,8},{10,11... | collective-permute-start | bytes 196616 | tf_op jit(solution)/shard_map/ppermute | solution.py:12
  5.0 0.8 fusion.46
  5.9 1.9 collective-permute-done
  7.8 18.2 %collective-permute-start.1 = (bf16[128,512]{0,1:T(8,128)(2,1)S(1)}, bf16[128,512]{0,1:T(8,128)(2,1)S(1)}, u32[]{:S(2)}, u32[]{:S(2)}) collective-permute-start(bf16[128,512]{0,1:T(8,128)(2,1)S(1)} %maximum_select_fusion.1), channel_id=1, source_target_pairs={{0,30},{2,0},{4,2},{6,4},{8,6},{10,8},{12,10},{14,12},{16,14},{18,... | collective-permute-start | bytes 393224 | tf_op jit(solution)/shard_map/ppermute | solution.py:12
  26.0 1.9 collective-permute-start.8
  28.0 0.7 convert_element_type.98
  28.7 5.4 %collective-permute-start.2 = (bf16[128,512]{0,1:T(8,128)(2,1)S(1)}, bf16[128,512]{0,1:T(8,128)(2,1)S(1)}, u32[]{:S(2)}, u32[]{:S(2)}) collective-permute-start(bf16[128,512]{0,1:T(8,128)(2,1)S(1)} %collective-permute-done.1), channel_id=1, source_target_pairs={{0,30},{2,0},{4,2},{6,4},{8,6},{10,8},{12,10},{14,12},{16,14},{18,... | collective-permute-start | bytes 393224 | tf_op jit(solution)/shard_map/ppermute | solution.py:12
  34.1 1.9 collective-permute-start.9
  36.1 0.5 collective-permute-done.2
  36.6 5.6 %collective-permute-start.3 = (bf16[128,512]{0,1:T(8,128)(2,1)S(1)}, bf16[128,512]{0,1:T(8,128)(2,1)S(1)}, u32[]{:S(2)}, u32[]{:S(2)}) collective-permute-start(bf16[128,512]{0,1:T(8,128)(2,1)S(1)} %collective-permute-done.2), channel_id=1, source_target_pairs={{0,30},{2,0},{4,2},{6,4},{8,6},{10,8},{12,10},{14,12},{16,14},{18,... | collective-permute-start | bytes 393224 | tf_op jit(solution)/shard_map/ppermute | solution.py:12
  42.2 1.9 collective-permute-start.10
  44.1 0.5 collective-permute-done.3
  44.7 5.6 %collective-permute-start.4 = (bf16[128,512]{0,1:T(8,128)(2,1)S(1)}, bf16[128,512]{0,1:T(8,128)(2,1)S(1)}, u32[]{:S(2)}, u32[]{:S(2)}) collective-permute-start(bf16[128,512]{0,1:T(8,128)(2,1)S(1)} %collective-permute-done.3), channel_id=1, source_target_pairs={{0,30},{2,0},{4,2},{6,4},{8,6},{10,8},{12,10},{14,12},{16,14},{18,... | collective-permute-start | bytes 393224 | tf_op jit(solution)/shard_map/ppermute | solution.py:12
  50.2 1.9 collective-permute-start.11
  52.2 0.5 collective-permute-done.4
  52.7 5.6 %collective-permute-start.5 = (bf16[128,512]{0,1:T(8,128)(2,1)S(1)}, bf16[128,512]{0,1:T(8,128)(2,1)S(1)}, u32[]{:S(2)}, u32[]{:S(2)}) collective-permute-start(bf16[128,512]{0,1:T(8,128)(2,1)S(1)} %collective-permute-done.4), channel_id=1, source_target_pairs={{0,30},{2,0},{4,2},{6,4},{8,6},{10,8},{12,10},{14,12},{16,14},{18,... | collective-permute-start | bytes 393224 | tf_op jit(solution)/shard_map/ppermute | solution.py:12
  58.3 0.2 collective-permute-done.11
  58.4 1.9 collective-permute-start.12
  60.4 1.5 collective-permute-done.5
  61.9 5.6 %collective-permute-start.6 = (bf16[128,512]{0,1:T(8,128)(2,1)S(1)}, bf16[128,512]{0,1:T(8,128)(2,1)S(1)}, u32[]{:S(2)}, u32[]{:S(2)}) collective-permute-start(bf16[128,512]{0,1:T(8,128)(2,1)S(1)} %collective-permute-done.5), channel_id=1, source_target_pairs={{0,30},{2,0},{4,2},{6,4},{8,6},{10,8},{12,10},{14,12},{16,14},{18,... | collective-permute-start | bytes 393224 | tf_op jit(solution)/shard_map/ppermute | solution.py:12
  67.5 0.3 collective-permute-done.12
  67.8 1.9 collective-permute-start.13
  69.7 0.7 collective-permute-done.6
  70.5 5.6 %collective-permute-start.7 = (bf16[128,512]{0,1:T(8,128)(2,1)S(1)}, bf16[128,512]{0,1:T(8,128)(2,1)S(1)}, u32[]{:S(2)}, u32[]{:S(2)}) collective-permute-start(bf16[128,512]{0,1:T(8,128)(2,1)S(1)} %collective-permute-done.6), channel_id=1, source_target_pairs={{0,30},{2,0},{4,2},{6,4},{8,6},{10,8},{12,10},{14,12},{16,14},{18,... | collective-permute-start | bytes 393224 | tf_op jit(solution)/shard_map/ppermute | solution.py:12
  76.1 0.3 collective-permute-done.13
  76.4 1.9 collective-permute-start.14
  78.3 6.1 %collective-permute-done.14 = bf16[128,512]{0,1:T(8,128)(2,1)S(1)} collective-permute-done((bf16[128,512]{0,1:T(8,128)(2,1)S(1)}, bf16[128,512]{0,1:T(8,128)(2,1)S(1)}, u32[]{:S(2)}, u32[]{:S(2)}) %collective-permute-start.14) | collective-permute-done | bytes 131104 | tf_op jit(solution)/shard_map/ppermute | solution.py:12
  84.5 1.9 collective-permute-start.15
  86.4 6.1 %collective-permute-done.15 = bf16[128,512]{0,1:T(8,128)(2,1)S(1)} collective-permute-done((bf16[128,512]{0,1:T(8,128)(2,1)S(1)}, bf16[128,512]{0,1:T(8,128)(2,1)S(1)}, u32[]{:S(2)}, u32[]{:S(2)}) %collective-permute-start.15) | collective-permute-done | bytes 131104 | tf_op jit(solution)/shard_map/ppermute | solution.py:12
  93.2 0.2 constant_dynamic-slice_fusion
  93.4 1.5 copy-done.2
  94.9 1.0 convolution_convert_fusion.1
  96.0 1.9 collective-permute-start.16
  97.9 1.0 convolution_convert_fusion
  98.9 4.3 %collective-permute-done.16 = bf16[3,256]{1,0:T(4,128)(2,1)S(1)} collective-permute-done((bf16[3,256]{1,0:T(4,128)(2,1)S(1)}, bf16[3,256]{1,0:T(4,128)(2,1)S(1)}, u32[]{:S(2)}, u32[]{:S(2)}) %collective-permute-start.16) | collective-permute-done | bytes 1568 | tf_op jit(solution)/shard_map/ppermute | solution.py:96
  103.3 0.3 multiply_multiply_fusion
  103.6 1.9 collective-permute-start.17
  105.5 1.4 fusion.26
  107.1 1.5 fusion
  108.6 0.2 copy.18
  108.8 0.9 fusion.42
  109.8 1.9 collective-permute-start.21
  111.7 6.0 %collective-permute-start.18 = (bf16[2,128,512]{2,1,0:T(8,128)(2,1)S(1)}, bf16[2,128,512]{2,1,0:T(8,128)(2,1)S(1)}, u32[]{:S(2)}, u32[]{:S(2)}) collective-permute-start(bf16[2,128,512]{2,1,0:T(8,128)(2,1)S(1)} %get-tuple-element.11), channel_id=1, source_target_pairs={{0,28},{2,30},{4,0},{6,2},{8,4},{10,6},{12,8},{14,10},{16,12},{18,... | collective-permute-start | bytes 786440 | tf_op jit(solution)/shard_map/ppermute | solution.py:12
  117.7 9.4 %collective-permute-done.21 = bf16[2,128,512]{2,1,0:T(8,128)(2,1)S(1)} collective-permute-done((bf16[2,128,512]{2,1,0:T(8,128)(2,1)S(1)}, bf16[2,128,512]{2,1,0:T(8,128)(2,1)S(1)}, u32[]{:S(2)}, u32[]{:S(2)}) %collective-permute-start.21) | collective-permute-done | bytes 262176 | tf_op jit(solution)/shard_map/ppermute | solution.py:12
  127.2 1.9 collective-permute-start.22
  129.1 14.6 %collective-permute-done.22 = bf16[2,128,512]{2,1,0:T(8,128)(2,1)S(1)} collective-permute-done((bf16[2,128,512]{2,1,0:T(8,128)(2,1)S(1)}, bf16[2,128,512]{2,1,0:T(8,128)(2,1)S(1)}, u32[]{:S(2)}, u32[]{:S(2)}) %collective-permute-start.22) | collective-permute-done | bytes 262176 | tf_op jit(solution)/shard_map/ppermute | solution.py:12
  143.8 0.2 fusion.3
  144.0 1.9 collective-permute-start.19
  145.9 4.8 %collective-permute-start.23 = (bf16[2,128,512]{2,1,0:T(8,128)(2,1)S(1)}, bf16[2,128,512]{2,1,0:T(8,128)(2,1)S(1)}, u32[]{:S(2)}, u32[]{:S(2)}) collective-permute-start(bf16[2,128,512]{2,1,0:T(8,128)(2,1)S(1)} %get-tuple-element.8), channel_id=1, source_target_pairs={{0,4},{2,6},{4,8},{6,10},{8,12},{10,14},{12,16},{14,18},{16,20},{1... | collective-permute-start | bytes 786440 | tf_op jit(solution)/shard_map/ppermute | solution.py:12
  150.7 4.4 %collective-permute-done.19 = bf16[2,128,512]{2,1,0:T(8,128)(2,1)S(1)} collective-permute-done((bf16[2,128,512]{2,1,0:T(8,128)(2,1)S(1)}, bf16[2,128,512]{2,1,0:T(8,128)(2,1)S(1)}, u32[]{:S(2)}, u32[]{:S(2)}) %collective-permute-start.19) | collective-permute-done | bytes 262176 | tf_op jit(solution)/shard_map/ppermute | solution.py:12
  155.1 8.6 %collective-permute-done.23 = bf16[2,128,512]{2,1,0:T(8,128)(2,1)S(1)} collective-permute-done((bf16[2,128,512]{2,1,0:T(8,128)(2,1)S(1)}, bf16[2,128,512]{2,1,0:T(8,128)(2,1)S(1)}, u32[]{:S(2)}, u32[]{:S(2)}) %collective-permute-start.23) | collective-permute-done | bytes 262176 | tf_op jit(solution)/shard_map/ppermute | solution.py:12
  163.6 0.2 fusion.2
  163.8 1.9 collective-permute-start.20
  165.8 2.5 %collective-permute-start.24 = (bf16[128,512]{1,0:T(8,128)(2,1)S(1)}, bf16[128,512]{1,0:T(8,128)(2,1)S(1)}, u32[]{:S(2)}, u32[]{:S(2)}) collective-permute-start(bf16[128,512]{1,0:T(8,128)(2,1)S(1)} %get-tuple-element.12), channel_id=1, source_target_pairs={{0,2},{2,4},{4,6},{6,8},{8,10},{10,12},{12,14},{14,16},{16,18},{18... | collective-permute-start | bytes 393224 | tf_op jit(solution)/shard_map/ppermute | solution.py:12
  168.3 4.2 %collective-permute-start.25 = (bf16[128,512]{1,0:T(8,128)(2,1)S(1)}, bf16[128,512]{1,0:T(8,128)(2,1)S(1)}, u32[]{:S(2)}, u32[]{:S(2)}) collective-permute-start(bf16[128,512]{1,0:T(8,128)(2,1)S(1)} %get-tuple-element.13), channel_id=1, source_target_pairs={{0,4},{2,6},{4,8},{6,10},{8,12},{10,14},{12,16},{14,18},{16,20},{1... | collective-permute-start | bytes 393224 | tf_op jit(solution)/shard_map/ppermute | solution.py:12
  172.5 5.9 %collective-permute-done.20 = bf16[2,128,512]{2,1,0:T(8,128)(2,1)S(1)} collective-permute-done((bf16[2,128,512]{2,1,0:T(8,128)(2,1)S(1)}, bf16[2,128,512]{2,1,0:T(8,128)(2,1)S(1)}, u32[]{:S(2)}, u32[]{:S(2)}) %collective-permute-start.20) | collective-permute-done | bytes 262176 | tf_op jit(solution)/shard_map/ppermute | solution.py:12
  178.5 4.1 %collective-permute-start.26 = (bf16[128,512]{1,0:T(8,128)(2,1)S(1)}, bf16[128,512]{1,0:T(8,128)(2,1)S(1)}, u32[]{:S(2)}, u32[]{:S(2)}) collective-permute-start(bf16[128,512]{1,0:T(8,128)(2,1)S(1)} %fusion.19), channel_id=1, source_target_pairs={{0,30},{2,0},{4,2},{6,4},{8,6},{10,8},{12,10},{14,12},{16,14},{18,... | collective-permute-start | bytes 393224 | tf_op jit(solution)/shard_map/ppermute | solution.py:12
  182.6 3.2 %collective-permute-done.26 = bf16[128,512]{1,0:T(8,128)(2,1)S(1)} collective-permute-done((bf16[128,512]{1,0:T(8,128)(2,1)S(1)}, bf16[128,512]{1,0:T(8,128)(2,1)S(1)}, u32[]{:S(2)}, u32[]{:S(2)}) %collective-permute-start.26) | collective-permute-done | bytes 131104 | tf_op jit(solution)/shard_map/ppermute | solution.py:12
  185.8 0.1 fusion.11
  185.9 2.3 %collective-permute-start.27 = (bf16[128,256]{1,0:T(8,128)(2,1)S(1)}, bf16[128,256]{1,0:T(8,128)(2,1)S(1)}, u32[]{:S(2)}, u32[]{:S(2)}) collective-permute-start(bf16[128,256]{1,0:T(8,128)(2,1)S(1)} %select_convert_fusion), channel_id=1, source_target_pairs={{0,1},{1,0},{2,3},{3,2},{4,5},{5,4},{6,7},{7,6},{8,9},{9,8},{10,11... | collective-permute-start | bytes 196616 | tf_op jit(solution)/shard_map/ppermute | solution.py:12
  188.2 0.7 multiply_convert_fusion
  188.9 3.2 %collective-permute-done.27 = bf16[128,256]{1,0:T(8,128)(2,1)S(1)} collective-permute-done((bf16[128,256]{1,0:T(8,128)(2,1)S(1)}, bf16[128,256]{1,0:T(8,128)(2,1)S(1)}, u32[]{:S(2)}, u32[]{:S(2)}) %collective-permute-start.27) | collective-permute-done | bytes 65568 | tf_op jit(solution)/shard_map/ppermute | solution.py:12
  192.1 0.7 add_convert_fusion
  (65 shorter events, 1.2 us)
Async XLA Ops:
  0.6 102.7 %copy-start = (bf16[10,256]{1,0:T(8,128)(2,1)S(1)}, bf16[10,256]{1,0:T(8,128)(2,1)}, u32[]{:S(2)}) copy-start(bf16[10,256]{1,0:T(8,128)(2,1)} %param.13) | copy-start | bytes 15364
  1.6 6.2 %collective-permute-start = (bf16[128,256]{0,1:T(8,128)(2,1)S(1)}, bf16[128,256]{0,1:T(8,128)(2,1)S(1)}, u32[]{:S(2)}, u32[]{:S(2)}) collective-permute-start(bf16[128,256]{0,1:T(8,128)(2,1)S(1)} %copy.11), channel_id=1, source_target_pairs={{0,1},{1,0},{2,3},{3,2},{4,5},{5,4},{6,7},{7,6},{8,9},{9,8},{10,11... | collective-permute-start | bytes 196616 | tf_op jit(solution)/shard_map/ppermute | solution.py:12
  7.8 20.9 %collective-permute-start.1 = (bf16[128,512]{0,1:T(8,128)(2,1)S(1)}, bf16[128,512]{0,1:T(8,128)(2,1)S(1)}, u32[]{:S(2)}, u32[]{:S(2)}) collective-permute-start(bf16[128,512]{0,1:T(8,128)(2,1)S(1)} %maximum_select_fusion.1), channel_id=1, source_target_pairs={{0,30},{2,0},{4,2},{6,4},{8,6},{10,8},{12,10},{14,12},{16,14},{18,... | collective-permute-start | bytes 393224 | tf_op jit(solution)/shard_map/ppermute | solution.py:12
  26.0 8.1 %collective-permute-start.8 = (bf16[128,512]{0,1:T(8,128)(2,1)S(1)}, bf16[128,512]{0,1:T(8,128)(2,1)S(1)}, u32[]{:S(2)}, u32[]{:S(2)}) collective-permute-start(bf16[128,512]{0,1:T(8,128)(2,1)S(1)} %maximum_select_fusion.1), channel_id=1, source_target_pairs={{0,2},{2,4},{4,6},{6,8},{8,10},{10,12},{12,14},{14,16},{16,18},{18... | collective-permute-start | bytes 393224 | tf_op jit(solution)/shard_map/ppermute | solution.py:12
  28.7 7.9 %collective-permute-start.2 = (bf16[128,512]{0,1:T(8,128)(2,1)S(1)}, bf16[128,512]{0,1:T(8,128)(2,1)S(1)}, u32[]{:S(2)}, u32[]{:S(2)}) collective-permute-start(bf16[128,512]{0,1:T(8,128)(2,1)S(1)} %collective-permute-done.1), channel_id=1, source_target_pairs={{0,30},{2,0},{4,2},{6,4},{8,6},{10,8},{12,10},{14,12},{16,14},{18,... | collective-permute-start | bytes 393224 | tf_op jit(solution)/shard_map/ppermute | solution.py:12
  34.1 8.1 %collective-permute-start.9 = (bf16[128,512]{0,1:T(8,128)(2,1)S(1)}, bf16[128,512]{0,1:T(8,128)(2,1)S(1)}, u32[]{:S(2)}, u32[]{:S(2)}) collective-permute-start(bf16[128,512]{0,1:T(8,128)(2,1)S(1)} %collective-permute-done.8), channel_id=1, source_target_pairs={{0,2},{2,4},{4,6},{6,8},{8,10},{10,12},{12,14},{14,16},{16,18},{18... | collective-permute-start | bytes 393224 | tf_op jit(solution)/shard_map/ppermute | solution.py:12
  36.6 8.1 %collective-permute-start.3 = (bf16[128,512]{0,1:T(8,128)(2,1)S(1)}, bf16[128,512]{0,1:T(8,128)(2,1)S(1)}, u32[]{:S(2)}, u32[]{:S(2)}) collective-permute-start(bf16[128,512]{0,1:T(8,128)(2,1)S(1)} %collective-permute-done.2), channel_id=1, source_target_pairs={{0,30},{2,0},{4,2},{6,4},{8,6},{10,8},{12,10},{14,12},{16,14},{18,... | collective-permute-start | bytes 393224 | tf_op jit(solution)/shard_map/ppermute | solution.py:12
  42.2 8.1 %collective-permute-start.10 = (bf16[128,512]{0,1:T(8,128)(2,1)S(1)}, bf16[128,512]{0,1:T(8,128)(2,1)S(1)}, u32[]{:S(2)}, u32[]{:S(2)}) collective-permute-start(bf16[128,512]{0,1:T(8,128)(2,1)S(1)} %collective-permute-done.9), channel_id=1, source_target_pairs={{0,2},{2,4},{4,6},{6,8},{8,10},{10,12},{12,14},{14,16},{16,18},{18... | collective-permute-start | bytes 393224 | tf_op jit(solution)/shard_map/ppermute | solution.py:12
  44.7 8.1 %collective-permute-start.4 = (bf16[128,512]{0,1:T(8,128)(2,1)S(1)}, bf16[128,512]{0,1:T(8,128)(2,1)S(1)}, u32[]{:S(2)}, u32[]{:S(2)}) collective-permute-start(bf16[128,512]{0,1:T(8,128)(2,1)S(1)} %collective-permute-done.3), channel_id=1, source_target_pairs={{0,30},{2,0},{4,2},{6,4},{8,6},{10,8},{12,10},{14,12},{16,14},{18,... | collective-permute-start | bytes 393224 | tf_op jit(solution)/shard_map/ppermute | solution.py:12
  50.2 8.2 %collective-permute-start.11 = (bf16[128,512]{0,1:T(8,128)(2,1)S(1)}, bf16[128,512]{0,1:T(8,128)(2,1)S(1)}, u32[]{:S(2)}, u32[]{:S(2)}) collective-permute-start(bf16[128,512]{0,1:T(8,128)(2,1)S(1)} %collective-permute-done.10), channel_id=1, source_target_pairs={{0,2},{2,4},{4,6},{6,8},{8,10},{10,12},{12,14},{14,16},{16,18},{18... | collective-permute-start | bytes 393224 | tf_op jit(solution)/shard_map/ppermute | solution.py:12
  52.7 9.2 %collective-permute-start.5 = (bf16[128,512]{0,1:T(8,128)(2,1)S(1)}, bf16[128,512]{0,1:T(8,128)(2,1)S(1)}, u32[]{:S(2)}, u32[]{:S(2)}) collective-permute-start(bf16[128,512]{0,1:T(8,128)(2,1)S(1)} %collective-permute-done.4), channel_id=1, source_target_pairs={{0,30},{2,0},{4,2},{6,4},{8,6},{10,8},{12,10},{14,12},{16,14},{18,... | collective-permute-start | bytes 393224 | tf_op jit(solution)/shard_map/ppermute | solution.py:12
  58.4 9.3 %collective-permute-start.12 = (bf16[128,512]{0,1:T(8,128)(2,1)S(1)}, bf16[128,512]{0,1:T(8,128)(2,1)S(1)}, u32[]{:S(2)}, u32[]{:S(2)}) collective-permute-start(bf16[128,512]{0,1:T(8,128)(2,1)S(1)} %collective-permute-done.11), channel_id=1, source_target_pairs={{0,2},{2,4},{4,6},{6,8},{8,10},{10,12},{12,14},{14,16},{16,18},{18... | collective-permute-start | bytes 393224 | tf_op jit(solution)/shard_map/ppermute | solution.py:12
  61.9 8.6 %collective-permute-start.6 = (bf16[128,512]{0,1:T(8,128)(2,1)S(1)}, bf16[128,512]{0,1:T(8,128)(2,1)S(1)}, u32[]{:S(2)}, u32[]{:S(2)}) collective-permute-start(bf16[128,512]{0,1:T(8,128)(2,1)S(1)} %collective-permute-done.5), channel_id=1, source_target_pairs={{0,30},{2,0},{4,2},{6,4},{8,6},{10,8},{12,10},{14,12},{16,14},{18,... | collective-permute-start | bytes 393224 | tf_op jit(solution)/shard_map/ppermute | solution.py:12
  67.8 8.6 %collective-permute-start.13 = (bf16[128,512]{0,1:T(8,128)(2,1)S(1)}, bf16[128,512]{0,1:T(8,128)(2,1)S(1)}, u32[]{:S(2)}, u32[]{:S(2)}) collective-permute-start(bf16[128,512]{0,1:T(8,128)(2,1)S(1)} %collective-permute-done.12), channel_id=1, source_target_pairs={{0,2},{2,4},{4,6},{6,8},{8,10},{10,12},{12,14},{14,16},{16,18},{18... | collective-permute-start | bytes 393224 | tf_op jit(solution)/shard_map/ppermute | solution.py:12
  70.5 15.9 %collective-permute-start.7 = (bf16[128,512]{0,1:T(8,128)(2,1)S(1)}, bf16[128,512]{0,1:T(8,128)(2,1)S(1)}, u32[]{:S(2)}, u32[]{:S(2)}) collective-permute-start(bf16[128,512]{0,1:T(8,128)(2,1)S(1)} %collective-permute-done.6), channel_id=1, source_target_pairs={{0,30},{2,0},{4,2},{6,4},{8,6},{10,8},{12,10},{14,12},{16,14},{18,... | collective-permute-start | bytes 393224 | tf_op jit(solution)/shard_map/ppermute | solution.py:12
  76.4 8.1 %collective-permute-start.14 = (bf16[128,512]{0,1:T(8,128)(2,1)S(1)}, bf16[128,512]{0,1:T(8,128)(2,1)S(1)}, u32[]{:S(2)}, u32[]{:S(2)}) collective-permute-start(bf16[128,512]{0,1:T(8,128)(2,1)S(1)} %collective-permute-done.13), channel_id=1, source_target_pairs={{0,2},{2,4},{4,6},{6,8},{8,10},{10,12},{12,14},{14,16},{16,18},{18... | collective-permute-start | bytes 393224 | tf_op jit(solution)/shard_map/ppermute | solution.py:12
  84.5 8.1 %collective-permute-start.15 = (bf16[128,512]{0,1:T(8,128)(2,1)S(1)}, bf16[128,512]{0,1:T(8,128)(2,1)S(1)}, u32[]{:S(2)}, u32[]{:S(2)}) collective-permute-start(bf16[128,512]{0,1:T(8,128)(2,1)S(1)} %collective-permute-done.14), channel_id=1, source_target_pairs={{0,2},{2,4},{4,6},{6,8},{8,10},{10,12},{12,14},{14,16},{16,18},{18... | collective-permute-start | bytes 393224 | tf_op jit(solution)/shard_map/ppermute | solution.py:12
  92.7 2.2 %copy-start.2 = (bf16[8192,256]{1,0:T(8,128)(2,1)S(1)}, bf16[8192,256]{1,0:T(8,128)(2,1)}, u32[]{:S(2)}) copy-start(bf16[8192,256]{1,0:T(8,128)(2,1)} %param.10) | copy-start | bytes 12582916
  93.4 4.5 %copy-start.1 = (bf16[8192,256]{1,0:T(8,128)(2,1)S(1)}, bf16[8192,256]{1,0:T(8,128)(2,1)}, u32[]{:S(2)}) copy-start(bf16[8192,256]{1,0:T(8,128)(2,1)} %param.9) | copy-start | bytes 12582916
  95.9 7.4 %copy-start.3 = (f32[256]{0:T(256)S(1)}, f32[256]{0:T(256)}, u32[]{:S(2)}) copy-start(f32[256]{0:T(256)} %param.12) | copy-start | bytes 3076
  95.9 7.4 %copy-start.4 = (s32[128]{0:T(128)S(1)}, s32[128]{0:T(128)}, u32[]{:S(2)}) copy-start(s32[128]{0:T(128)} %param.14) | copy-start | bytes 1540
  96.0 7.3 %collective-permute-start.16 = (bf16[3,256]{1,0:T(4,128)(2,1)S(1)}, bf16[3,256]{1,0:T(4,128)(2,1)S(1)}, u32[]{:S(2)}, u32[]{:S(2)}) collective-permute-start(bf16[3,256]{1,0:T(4,128)(2,1)S(1)} %slice.136), channel_id=1, source_target_pairs={{0,32},{32,64},{64,96},{96,128},{128,160},{160,192},{192,224},{224... | collective-permute-start | bytes 4616 | tf_op jit(solution)/shard_map/ppermute | solution.py:96
  103.6 3.5 %collective-permute-start.17 = (f32[3,256]{1,0:T(4,128)S(1)}, f32[3,256]{1,0:T(4,128)S(1)}, u32[]{:S(2)}, u32[]{:S(2)}) collective-permute-start(f32[3,256]{1,0:T(4,128)S(1)} %fusion.37), channel_id=1, source_target_pairs={{32,0},{64,32},{96,64},{128,96},{160,128},{192,160},{224,192},{256... | collective-permute-start | bytes 9224 | tf_op jit(solution)/shard_map/ppermute | solution.py:96
  109.8 17.4 %collective-permute-start.21 = (bf16[2,128,512]{2,1,0:T(8,128)(2,1)S(1)}, bf16[2,128,512]{2,1,0:T(8,128)(2,1)S(1)}, u32[]{:S(2)}, u32[]{:S(2)}) collective-permute-start(bf16[2,128,512]{2,1,0:T(8,128)(2,1)S(1)} %get-tuple-element.10), channel_id=1, source_target_pairs={{0,4},{2,6},{4,8},{6,10},{8,12},{10,14},{12,16},{14,18},{16,20},{1... | collective-permute-start | bytes 786440 | tf_op jit(solution)/shard_map/ppermute | solution.py:12
  111.7 17.4 %collective-permute-start.18 = (bf16[2,128,512]{2,1,0:T(8,128)(2,1)S(1)}, bf16[2,128,512]{2,1,0:T(8,128)(2,1)S(1)}, u32[]{:S(2)}, u32[]{:S(2)}) collective-permute-start(bf16[2,128,512]{2,1,0:T(8,128)(2,1)S(1)} %get-tuple-element.11), channel_id=1, source_target_pairs={{0,28},{2,30},{4,0},{6,2},{8,4},{10,6},{12,8},{14,10},{16,12},{18,... | collective-permute-start | bytes 786440 | tf_op jit(solution)/shard_map/ppermute | solution.py:12
  127.2 16.6 %collective-permute-start.22 = (bf16[2,128,512]{2,1,0:T(8,128)(2,1)S(1)}, bf16[2,128,512]{2,1,0:T(8,128)(2,1)S(1)}, u32[]{:S(2)}, u32[]{:S(2)}) collective-permute-start(bf16[2,128,512]{2,1,0:T(8,128)(2,1)S(1)} %fusion.4), channel_id=1, source_target_pairs={{0,4},{2,6},{4,8},{6,10},{8,12},{10,14},{12,16},{14,18},{16,20},{1... | collective-permute-start | bytes 786440 | tf_op jit(solution)/shard_map/ppermute | solution.py:12
  144.0 11.1 %collective-permute-start.19 = (bf16[2,128,512]{2,1,0:T(8,128)(2,1)S(1)}, bf16[2,128,512]{2,1,0:T(8,128)(2,1)S(1)}, u32[]{:S(2)}, u32[]{:S(2)}) collective-permute-start(bf16[2,128,512]{2,1,0:T(8,128)(2,1)S(1)} %get-tuple-element.9), channel_id=1, source_target_pairs={{0,28},{2,30},{4,0},{6,2},{8,4},{10,6},{12,8},{14,10},{16,12},{18,... | collective-permute-start | bytes 786440 | tf_op jit(solution)/shard_map/ppermute | solution.py:12
  145.9 17.8 %collective-permute-start.23 = (bf16[2,128,512]{2,1,0:T(8,128)(2,1)S(1)}, bf16[2,128,512]{2,1,0:T(8,128)(2,1)S(1)}, u32[]{:S(2)}, u32[]{:S(2)}) collective-permute-start(bf16[2,128,512]{2,1,0:T(8,128)(2,1)S(1)} %get-tuple-element.8), channel_id=1, source_target_pairs={{0,4},{2,6},{4,8},{6,10},{8,12},{10,14},{12,16},{14,18},{16,20},{1... | collective-permute-start | bytes 786440 | tf_op jit(solution)/shard_map/ppermute | solution.py:12
  163.8 14.6 %collective-permute-start.20 = (bf16[2,128,512]{2,1,0:T(8,128)(2,1)S(1)}, bf16[2,128,512]{2,1,0:T(8,128)(2,1)S(1)}, u32[]{:S(2)}, u32[]{:S(2)}) collective-permute-start(bf16[2,128,512]{2,1,0:T(8,128)(2,1)S(1)} %get-tuple-element.7), channel_id=1, source_target_pairs={{0,28},{2,30},{4,0},{6,2},{8,4},{10,6},{12,8},{14,10},{16,12},{18,... | collective-permute-start | bytes 786440 | tf_op jit(solution)/shard_map/ppermute | solution.py:12
  165.8 16.8 %collective-permute-start.24 = (bf16[128,512]{1,0:T(8,128)(2,1)S(1)}, bf16[128,512]{1,0:T(8,128)(2,1)S(1)}, u32[]{:S(2)}, u32[]{:S(2)}) collective-permute-start(bf16[128,512]{1,0:T(8,128)(2,1)S(1)} %get-tuple-element.12), channel_id=1, source_target_pairs={{0,2},{2,4},{4,6},{6,8},{8,10},{10,12},{12,14},{14,16},{16,18},{18... | collective-permute-start | bytes 393224 | tf_op jit(solution)/shard_map/ppermute | solution.py:12
  168.3 14.3 %collective-permute-start.25 = (bf16[128,512]{1,0:T(8,128)(2,1)S(1)}, bf16[128,512]{1,0:T(8,128)(2,1)S(1)}, u32[]{:S(2)}, u32[]{:S(2)}) collective-permute-start(bf16[128,512]{1,0:T(8,128)(2,1)S(1)} %get-tuple-element.13), channel_id=1, source_target_pairs={{0,4},{2,6},{4,8},{6,10},{8,12},{10,14},{12,16},{14,18},{16,20},{1... | collective-permute-start | bytes 393224 | tf_op jit(solution)/shard_map/ppermute | solution.py:12
  178.5 7.3 %collective-permute-start.26 = (bf16[128,512]{1,0:T(8,128)(2,1)S(1)}, bf16[128,512]{1,0:T(8,128)(2,1)S(1)}, u32[]{:S(2)}, u32[]{:S(2)}) collective-permute-start(bf16[128,512]{1,0:T(8,128)(2,1)S(1)} %fusion.19), channel_id=1, source_target_pairs={{0,30},{2,0},{4,2},{6,4},{8,6},{10,8},{12,10},{14,12},{16,14},{18,... | collective-permute-start | bytes 393224 | tf_op jit(solution)/shard_map/ppermute | solution.py:12
  185.9 6.2 %collective-permute-start.27 = (bf16[128,256]{1,0:T(8,128)(2,1)S(1)}, bf16[128,256]{1,0:T(8,128)(2,1)S(1)}, u32[]{:S(2)}, u32[]{:S(2)}) collective-permute-start(bf16[128,256]{1,0:T(8,128)(2,1)S(1)} %select_convert_fusion), channel_id=1, source_target_pairs={{0,1},{1,0},{2,3},{3,2},{4,5},{5,4},{6,7},{7,6},{8,9},{9,8},{10,11... | collective-permute-start | bytes 196616 | tf_op jit(solution)/shard_map/ppermute | solution.py:12

commit v3 on v1

--- a/solution.py
+++ b/solution.py
@@ -17,52 +17,60 @@
     return jnp.where(first, jnp.concatenate([mine, other], 1), jnp.concatenate([other, mine], 1))
 
 
-def gather_features(tokens):
-    rows = tokens.shape[0]
+def gathered_blocks(tokens):
     pair = halves_in_order(tokens, shifted(tokens, "tx", 1))
     count = lax.axis_size("tz")
-    blocks = [pair] * count
+    here = lax.axis_index("tz")
+    found = [(pair, here)]
     ahead = pair
     behind = pair
     for step in range(1, count // 2 + 1):
         ahead = shifted(ahead, "tz", 1)
-        blocks[-step % count] = ahead
+        found.append((ahead, (here - step) % count))
         if step < count - step:
             behind = shifted(behind, "tz", -1)
-            blocks[step] = behind
-    stacked = jnp.stack(blocks, 0)
-    doubled = jnp.concatenate([stacked, stacked], 0)
-    start = (count - lax.axis_index("tz")) % count
-    ordered = lax.dynamic_slice_in_dim(doubled, start, count, 0)
-    return ordered.transpose(1, 0, 2).reshape(rows, -1)
+            found.append((behind, (here + step) % count))
+    return found
 
 
-def scatter_features(terms16):
-    rows = terms16.shape[0]
+def project(found, weights):
+    width = found[0][0].shape[1]
+    total = None
+    for block, place in found:
+        rows = lax.dynamic_slice_in_dim(weights, place * width, width, 0)
+        part = jnp.dot(block, rows, preferred_element_type=jnp.float32)
+        total = part if total is None else total + part
+    return total
+
+
+def scatter_features(make_block):
     count = lax.axis_size("tz")
-    width = terms16.shape[1] // count
-    per_dest = terms16.reshape(rows, count, width).transpose(1, 0, 2)
-    doubled = jnp.concatenate([per_dest, per_dest], 0)
-    own = lax.dynamic_slice_in_dim(doubled, lax.axis_index("tz"), count, 0).astype(jnp.float32)
+    here = lax.axis_index("tz")
+    own = lambda offset: make_block((here + offset) % count).astype(jnp.float32)
     right = count - 1 - count // 2
     left = count // 2
-    total = own[0]
+    total = None
     if right > 0:
-        acc = own[right]
+        acc = own(right)
         for step in range(1, right):
-            acc = shifted(acc.astype(jnp.bfloat16), "tz", 1).astype(jnp.float32) + own[right - step]
-        total = total + shifted(acc.astype(jnp.bfloat16), "tz", 1).astype(jnp.float32)
+            acc = hop(acc, 1) + own(right - step)
+        total = hop(acc, 1)
     if left > 0:
-        acc = own[left]
+        acc = own(left)
         for step in range(1, left):
-            acc = shifted(acc.astype(jnp.bfloat16), "tz", -1).astype(jnp.float32) + own[left + step]
-        total = total + shifted(acc.astype(jnp.bfloat16), "tz", -1).astype(jnp.float32)
-    half = width // 2
+            acc = hop(acc, -1) + own(left + step)
+        total = hop(acc, -1) if total is None else total + hop(acc, -1)
+    total = own(0) if total is None else total + own(0)
+    half = total.shape[1] // 2
     first = lax.axis_index("tx") == 0
     mine = jnp.where(first, total[:, :half], total[:, half:])
     other = jnp.where(first, total[:, half:], total[:, :half])
     arrived = shifted(other.astype(jnp.bfloat16), "tx", 1).astype(jnp.float32)
     return (mine + arrived).astype(jnp.bfloat16)
+
+
+def hop(acc, distance):
+    return shifted(acc.astype(jnp.bfloat16), "tz", distance).astype(jnp.float32)
 
 
 def passed_along(block, axis, distance):
@@ -87,9 +95,9 @@
     rows = tokens.shape[0]
     chans = w_gate.shape[1]
     taps = conv_weight.shape[0]
-    piece = gather_features(tokens)
-    gate_acc = jnp.dot(piece, w_gate, preferred_element_type=jnp.float32)
-    xin_acc = jnp.dot(piece, w_conv_in, preferred_element_type=jnp.float32)
+    found = gathered_blocks(tokens)
+    gate_acc = project(found, w_gate)
+    xin_acc = project(found, w_conv_in)
     gate16 = lax.optimization_barrier(gate_acc.astype(jnp.bfloat16))
     zgate = gate16.astype(jnp.float32)
     xin16 = lax.optimization_barrier(xin_acc.astype(jnp.bfloat16))
@@ -118,9 +126,16 @@
     )
     dxin16 = dxin.astype(jnp.bfloat16)
     spec = (((1,), (1,)), ((), ()))
-    terms = lax.dot_general(dgate16, w_gate, spec, preferred_element_type=jnp.float32)
-    terms = terms + lax.dot_general(dxin16, w_conv_in, spec, preferred_element_type=jnp.float32)
-    d_tokens = scatter_features(terms.astype(jnp.bfloat16))
+    width = 2 * tokens.shape[1]
+
+    def block_terms(place):
+        gate_rows = lax.dynamic_slice_in_dim(w_gate, place * width, width, 0)
+        conv_rows = lax.dynamic_slice_in_dim(w_conv_in, place * width, width, 0)
+        part = lax.dot_general(dgate16, gate_rows, spec, preferred_element_type=jnp.float32)
+        part = part + lax.dot_general(dxin16, conv_rows, spec, preferred_element_type=jnp.float32)
+        return part.astype(jnp.bfloat16)
+
+    d_tokens = scatter_features(block_terms)
     return (gated, d_tokens)
 
 

time: 194 us -> 192 us (0.990)
  matrix products: 5.22 us -> 23.2 us
  waiting for transfers between devices: 46.9 us -> 33.7 us
  starting transfers between devices: 131 us -> 126 us
  local copies, waits for them, and re-layouts: 4.34 us -> 0.89 us
    dot_general x4 -> x64, matrix products: 4.97 us -> 23 us  [the longest x32 15.8 us: project(): part = jnp.dot(block, rows, preferred_element_type=jnp.float32)]
    ppermute x32, waiting for transfers between devices: 42.5 us -> 28.5 us  [shifted(): lax.ppermute(block, axis, [(i, (i + distance) % size) for i in range(size)])]
    ppermute x32, starting transfers between devices: 127 us -> 122 us  [shifted(): lax.ppermute(block, axis, [(i, (i + distance) % size) for i in range(size)])]
    unnamed x40 -> x10, local copies, waits for them, and re-layouts: 3.05 us -> 0.03 us
  transfers between devices with their start and end apart: 34 -> 34, of which waited for: 28 -> 16; matrix products, arithmetic and copies ran while one was open for 3% -> 10% of each run, Pallas kernels for 0% -> 0%
where the time goes in v3:
time: 192 us; the launch traced here: 189 us
  starting transfers between devices  126 us (66%)
  waiting for transfers between devices  33.7 us (18%)
  matrix products  23.2 us (12%)
  other arithmetic  3.09 us (2%)
    ppermute x32, starting transfers between devices, shifted(): lax.ppermute(block, axis, [(i, (i + distance) % size) for i in range(size)])  122 us
    ppermute x32, waiting for transfers between devices, shifted(): lax.ppermute(block, axis, [(i, (i + distance) % size) for i in range(size)])  28.5 us
    dot_general x32, matrix products, project(): part = jnp.dot(block, rows, preferred_element_type=jnp.float32)  15.8 us
    ppermute x2, waiting for transfers between devices, passed_along(): return lax.ppermute(block, axis, route)  5.18 us
    ppermute x2, starting transfers between devices, passed_along(): return lax.ppermute(block, axis, route)  3.84 us
  transfers between devices with their start and end apart: 34, of which 16 were waited for; matrix products, arithmetic and copies ran while one was open for 10% of the time, Pallas kernels for 0%

profile of v3, /device:TPU:56, one launch (start us, length us, event | category | flops | bytes accessed | tf_op | source)
XLA Modules:
  0.0 188.5 jit_solution(12153947962656478264)
XLA Ops:
  0.6 3.4 %collective-permute-start = (bf16[128,256]{1,0:T(8,128)(2,1)}, bf16[128,256]{1,0:T(8,128)(2,1)S(1)}, u32[]{:S(2)}, u32[]{:S(2)}) collective-permute-start(bf16[128,256]{1,0:T(8,128)(2,1)} %param.8), channel_id=1, source_target_pairs={{0,1},{1,0},{2,3},{3,2},{4,5},{5,4},{6,7},{7,6},{8,9},{9,8},{10,11... | collective-permute-start | bytes 196616 | tf_op jit(solution)/shard_map/ppermute | solution.py:12
  4.1 0.8 fusion.255
  5.0 0.7 convert_element_type.215
  5.6 1.4 collective-permute-done
  7.0 1.0 maximum_select_fusion
  8.0 18.2 %collective-permute-start.2 = (bf16[128,512]{1,0:T(8,128)(2,1)S(1)}, bf16[128,512]{1,0:T(8,128)(2,1)S(1)}, u32[]{:S(2)}, u32[]{:S(2)}) collective-permute-start(bf16[128,512]{1,0:T(8,128)(2,1)S(1)} %maximum_select_fusion), channel_id=1, source_target_pairs={{0,30},{2,0},{4,2},{6,4},{8,6},{10,8},{12,10},{14,12},{16,14},{18,... | collective-permute-start | bytes 393224 | tf_op jit(solution)/shard_map/ppermute | solution.py:12
  26.2 1.9 %collective-permute-start.1 = (bf16[128,512]{1,0:T(8,128)(2,1)S(1)}, bf16[128,512]{1,0:T(8,128)(2,1)S(1)}, u32[]{:S(2)}, u32[]{:S(2)}) collective-permute-start(bf16[128,512]{1,0:T(8,128)(2,1)S(1)} %maximum_select_fusion), channel_id=1, source_target_pairs={{0,2},{2,4},{4,6},{6,8},{8,10},{10,12},{12,14},{14,16},{16,18},{18... | collective-permute-start | bytes 393224 | tf_op jit(solution)/shard_map/ppermute | solution.py:12
  28.1 0.6 collective-permute-done.2
  28.7 1.1 fusion.119
  29.9 4.4 %collective-permute-done.1 = bf16[128,512]{1,0:T(8,128)(2,1)S(1)} collective-permute-done((bf16[128,512]{1,0:T(8,128)(2,1)S(1)}, bf16[128,512]{1,0:T(8,128)(2,1)S(1)}, u32[]{:S(2)}, u32[]{:S(2)}) %collective-permute-start.1) | collective-permute-done | bytes 131104 | tf_op jit(solution)/shard_map/ppermute | solution.py:12
  34.3 1.1 fusion.80
  35.4 1.1 fusion.36
  36.6 1.9 %collective-permute-start.4 = (bf16[128,512]{1,0:T(8,128)(2,1)S(1)}, bf16[128,512]{1,0:T(8,128)(2,1)S(1)}, u32[]{:S(2)}, u32[]{:S(2)}) collective-permute-start(bf16[128,512]{1,0:T(8,128)(2,1)S(1)} %collective-permute-done.2), channel_id=1, source_target_pairs={{0,30},{2,0},{4,2},{6,4},{8,6},{10,8},{12,10},{14,12},{16,14},{18,... | collective-permute-start | bytes 393224 | tf_op jit(solution)/shard_map/ppermute | solution.py:12
  38.5 3.9 %collective-permute-start.3 = (bf16[128,512]{1,0:T(8,128)(2,1)S(1)}, bf16[128,512]{1,0:T(8,128)(2,1)S(1)}, u32[]{:S(2)}, u32[]{:S(2)}) collective-permute-start(bf16[128,512]{1,0:T(8,128)(2,1)S(1)} %collective-permute-done.1), channel_id=1, source_target_pairs={{0,2},{2,4},{4,6},{6,8},{8,10},{10,12},{12,14},{14,16},{16,18},{18... | collective-permute-start | bytes 393224 | tf_op jit(solution)/shard_map/ppermute | solution.py:12
  42.4 1.1 fusion.150
  43.6 1.1 fusion.90
  44.7 1.1 fusion.43
  45.9 3.1 %collective-permute-start.6 = (bf16[128,512]{1,0:T(8,128)(2,1)S(1)}, bf16[128,512]{1,0:T(8,128)(2,1)S(1)}, u32[]{:S(2)}, u32[]{:S(2)}) collective-permute-start(bf16[128,512]{1,0:T(8,128)(2,1)S(1)} %collective-permute-done.4), channel_id=1, source_target_pairs={{0,30},{2,0},{4,2},{6,4},{8,6},{10,8},{12,10},{14,12},{16,14},{18,... | collective-permute-start | bytes 393224 | tf_op jit(solution)/shard_map/ppermute | solution.py:12
  49.1 1.1 fusion.115
  50.4 2.7 %collective-permute-start.5 = (bf16[128,512]{1,0:T(8,128)(2,1)S(1)}, bf16[128,512]{1,0:T(8,128)(2,1)S(1)}, u32[]{:S(2)}, u32[]{:S(2)}) collective-permute-start(bf16[128,512]{1,0:T(8,128)(2,1)S(1)} %collective-permute-done.3), channel_id=1, source_target_pairs={{0,2},{2,4},{4,6},{6,8},{8,10},{10,12},{12,14},{14,16},{16,18},{18... | collective-permute-start | bytes 393224 | tf_op jit(solution)/shard_map/ppermute | solution.py:12
  53.1 1.1 fusion.35
  54.5 4.3 %collective-permute-start.8 = (bf16[128,512]{1,0:T(8,128)(2,1)S(1)}, bf16[128,512]{1,0:T(8,128)(2,1)S(1)}, u32[]{:S(2)}, u32[]{:S(2)}) collective-permute-start(bf16[128,512]{1,0:T(8,128)(2,1)S(1)} %collective-permute-done.6), channel_id=1, source_target_pairs={{0,30},{2,0},{4,2},{6,4},{8,6},{10,8},{12,10},{14,12},{16,14},{18,... | collective-permute-start | bytes 393224 | tf_op jit(solution)/shard_map/ppermute | solution.py:12
  58.9 1.1 fusion.111
  60.2 1.9 %collective-permute-start.7 = (bf16[128,512]{1,0:T(8,128)(2,1)S(1)}, bf16[128,512]{1,0:T(8,128)(2,1)S(1)}, u32[]{:S(2)}, u32[]{:S(2)}) collective-permute-start(bf16[128,512]{1,0:T(8,128)(2,1)S(1)} %collective-permute-done.5), channel_id=1, source_target_pairs={{0,2},{2,4},{4,6},{6,8},{8,10},{10,12},{12,14},{14,16},{16,18},{18... | collective-permute-start | bytes 393224 | tf_op jit(solution)/shard_map/ppermute | solution.py:12
  62.2 1.1 fusion.34
  63.5 5.1 %collective-permute-start.10 = (bf16[128,512]{1,0:T(8,128)(2,1)S(1)}, bf16[128,512]{1,0:T(8,128)(2,1)S(1)}, u32[]{:S(2)}, u32[]{:S(2)}) collective-permute-start(bf16[128,512]{1,0:T(8,128)(2,1)S(1)} %collective-permute-done.8), channel_id=1, source_target_pairs={{0,30},{2,0},{4,2},{6,4},{8,6},{10,8},{12,10},{14,12},{16,14},{18,... | collective-permute-start | bytes 393224 | tf_op jit(solution)/shard_map/ppermute | solution.py:12
  69.1 1.9 %collective-permute-start.9 = (bf16[128,512]{1,0:T(8,128)(2,1)S(1)}, bf16[128,512]{1,0:T(8,128)(2,1)S(1)}, u32[]{:S(2)}, u32[]{:S(2)}) collective-permute-start(bf16[128,512]{1,0:T(8,128)(2,1)S(1)} %collective-permute-done.7), channel_id=1, source_target_pairs={{0,2},{2,4},{4,6},{6,8},{8,10},{10,12},{12,14},{14,16},{16,18},{18... | collective-permute-start | bytes 393224 | tf_op jit(solution)/shard_map/ppermute | solution.py:12
  71.5 5.3 %collective-permute-start.12 = (bf16[128,512]{1,0:T(8,128)(2,1)S(1)}, bf16[128,512]{1,0:T(8,128)(2,1)S(1)}, u32[]{:S(2)}, u32[]{:S(2)}) collective-permute-start(bf16[128,512]{1,0:T(8,128)(2,1)S(1)} %collective-permute-done.10), channel_id=1, source_target_pairs={{0,30},{2,0},{4,2},{6,4},{8,6},{10,8},{12,10},{14,12},{16,14},{18,... | collective-permute-start | bytes 393224 | tf_op jit(solution)/shard_map/ppermute | solution.py:12
  77.2 1.9 %collective-permute-start.11 = (bf16[128,512]{1,0:T(8,128)(2,1)S(1)}, bf16[128,512]{1,0:T(8,128)(2,1)S(1)}, u32[]{:S(2)}, u32[]{:S(2)}) collective-permute-start(bf16[128,512]{1,0:T(8,128)(2,1)S(1)} %collective-permute-done.9), channel_id=1, source_target_pairs={{0,2},{2,4},{4,6},{6,8},{8,10},{10,12},{12,14},{14,16},{16,18},{18... | collective-permute-start | bytes 393224 | tf_op jit(solution)/shard_map/ppermute | solution.py:12
  79.5 5.3 %collective-permute-start.14 = (bf16[128,512]{1,0:T(8,128)(2,1)S(1)}, bf16[128,512]{1,0:T(8,128)(2,1)S(1)}, u32[]{:S(2)}, u32[]{:S(2)}) collective-permute-start(bf16[128,512]{1,0:T(8,128)(2,1)S(1)} %collective-permute-done.12), channel_id=1, source_target_pairs={{0,30},{2,0},{4,2},{6,4},{8,6},{10,8},{12,10},{14,12},{16,14},{18,... | collective-permute-start | bytes 393224 | tf_op jit(solution)/shard_map/ppermute | solution.py:12
  85.3 1.9 %collective-permute-start.13 = (bf16[128,512]{1,0:T(8,128)(2,1)S(1)}, bf16[128,512]{1,0:T(8,128)(2,1)S(1)}, u32[]{:S(2)}, u32[]{:S(2)}) collective-permute-start(bf16[128,512]{1,0:T(8,128)(2,1)S(1)} %collective-permute-done.11), channel_id=1, source_target_pairs={{0,2},{2,4},{4,6},{6,8},{8,10},{10,12},{12,14},{14,16},{16,18},{18... | collective-permute-start | bytes 393224 | tf_op jit(solution)/shard_map/ppermute | solution.py:12
  88.0 6.4 %collective-permute-done.13 = bf16[128,512]{1,0:T(8,128)(2,1)S(1)} collective-permute-done((bf16[128,512]{1,0:T(8,128)(2,1)S(1)}, bf16[128,512]{1,0:T(8,128)(2,1)S(1)}, u32[]{:S(2)}, u32[]{:S(2)}) %collective-permute-start.13) | collective-permute-done | bytes 131104 | tf_op jit(solution)/shard_map/ppermute | solution.py:12
  94.4 1.9 %collective-permute-start.15 = (bf16[128,512]{1,0:T(8,128)(2,1)S(1)}, bf16[128,512]{1,0:T(8,128)(2,1)S(1)}, u32[]{:S(2)}, u32[]{:S(2)}) collective-permute-start(bf16[128,512]{1,0:T(8,128)(2,1)S(1)} %collective-permute-done.13), channel_id=1, source_target_pairs={{0,2},{2,4},{4,6},{6,8},{8,10},{10,12},{12,14},{14,16},{16,18},{18... | collective-permute-start | bytes 393224 | tf_op jit(solution)/shard_map/ppermute | solution.py:12
  96.7 5.7 %collective-permute-done.15 = bf16[128,512]{1,0:T(8,128)(2,1)S(1)} collective-permute-done((bf16[128,512]{1,0:T(8,128)(2,1)S(1)}, bf16[128,512]{1,0:T(8,128)(2,1)S(1)}, u32[]{:S(2)}, u32[]{:S(2)}) %collective-permute-start.15) | collective-permute-done | bytes 131104 | tf_op jit(solution)/shard_map/ppermute | solution.py:12
  102.7 1.9 %collective-permute-start.16 = (bf16[3,256]{1,0:T(4,128)(2,1)S(1)}, bf16[3,256]{1,0:T(4,128)(2,1)S(1)}, u32[]{:S(2)}, u32[]{:S(2)}) collective-permute-start(bf16[3,256]{1,0:T(4,128)(2,1)S(1)} %slice.87), channel_id=1, source_target_pairs={{0,32},{32,64},{64,96},{96,128},{128,160},{160,192},{192,224},{224... | collective-permute-start | bytes 4616 | tf_op jit(solution)/shard_map/ppermute | solution.py:79
  104.8 5.2 %collective-permute-done.16 = bf16[3,256]{1,0:T(4,128)(2,1)S(1)} collective-permute-done((bf16[3,256]{1,0:T(4,128)(2,1)S(1)}, bf16[3,256]{1,0:T(4,128)(2,1)S(1)}, u32[]{:S(2)}, u32[]{:S(2)}) %collective-permute-start.16) | collective-permute-done | bytes 1568 | tf_op jit(solution)/shard_map/ppermute | solution.py:79
  110.3 0.8 fusion.160
  112.9 1.9 %collective-permute-start.17 = (f32[3,256]{1,0:T(4,128)S(1)}, f32[3,256]{1,0:T(4,128)S(1)}, u32[]{:S(2)}, u32[]{:S(2)}) collective-permute-start(f32[3,256]{1,0:T(4,128)S(1)} %fusion.251), channel_id=1, source_target_pairs={{32,0},{64,32},{96,64},{128,96},{160,128},{192,160},{224,192},{256... | collective-permute-start | bytes 9224 | tf_op jit(solution)/shard_map/ppermute | solution.py:79
  116.8 1.9 %collective-permute-start.25 = (bf16[128,512]{1,0:T(8,128)(2,1)S(1)}, bf16[128,512]{1,0:T(8,128)(2,1)S(1)}, u32[]{:S(2)}, u32[]{:S(2)}) collective-permute-start(bf16[128,512]{1,0:T(8,128)(2,1)S(1)} %fusion.13), channel_id=1, source_target_pairs={{0,30},{2,0},{4,2},{6,4},{8,6},{10,8},{12,10},{14,12},{16,14},{18,... | collective-permute-start | bytes 393224 | tf_op jit(solution)/shard_map/ppermute | solution.py:12
  119.0 3.9 %collective-permute-start.18 = (bf16[128,512]{1,0:T(8,128)(2,1)S(1)}, bf16[128,512]{1,0:T(8,128)(2,1)S(1)}, u32[]{:S(2)}, u32[]{:S(2)}) collective-permute-start(bf16[128,512]{1,0:T(8,128)(2,1)S(1)} %fusion), channel_id=1, source_target_pairs={{0,2},{2,4},{4,6},{6,8},{8,10},{10,12},{12,14},{14,16},{16,18},{18... | collective-permute-start | bytes 393224 | tf_op jit(solution)/shard_map/ppermute | solution.py:12
  122.9 1.4 collective-permute-done.25
  124.5 2.8 %collective-permute-start.26 = (bf16[128,512]{1,0:T(8,128)(2,1)S(1)}, bf16[128,512]{1,0:T(8,128)(2,1)S(1)}, u32[]{:S(2)}, u32[]{:S(2)}) collective-permute-start(bf16[128,512]{1,0:T(8,128)(2,1)S(1)} %add_convert_fusion.6), channel_id=1, source_target_pairs={{0,30},{2,0},{4,2},{6,4},{8,6},{10,8},{12,10},{14,12},{16,14},{18,... | collective-permute-start | bytes 393224 | tf_op jit(solution)/shard_map/ppermute | solution.py:12
  127.3 0.3 collective-permute-done.18
  127.9 3.0 %collective-permute-start.19 = (bf16[128,512]{1,0:T(8,128)(2,1)S(1)}, bf16[128,512]{1,0:T(8,128)(2,1)S(1)}, u32[]{:S(2)}, u32[]{:S(2)}) collective-permute-start(bf16[128,512]{1,0:T(8,128)(2,1)S(1)} %add_convert_fusion.12), channel_id=1, source_target_pairs={{0,2},{2,4},{4,6},{6,8},{8,10},{10,12},{12,14},{14,16},{16,18},{18... | collective-permute-start | bytes 393224 | tf_op jit(solution)/shard_map/ppermute | solution.py:12
  130.9 1.5 collective-permute-done.26
  132.6 4.3 %collective-permute-start.27 = (bf16[128,512]{1,0:T(8,128)(2,1)S(1)}, bf16[128,512]{1,0:T(8,128)(2,1)S(1)}, u32[]{:S(2)}, u32[]{:S(2)}) collective-permute-start(bf16[128,512]{1,0:T(8,128)(2,1)S(1)} %add_convert_fusion.5), channel_id=1, source_target_pairs={{0,30},{2,0},{4,2},{6,4},{8,6},{10,8},{12,10},{14,12},{16,14},{18,... | collective-permute-start | bytes 393224 | tf_op jit(solution)/shard_map/ppermute | solution.py:12
  137.2 1.9 %collective-permute-start.20 = (bf16[128,512]{1,0:T(8,128)(2,1)S(1)}, bf16[128,512]{1,0:T(8,128)(2,1)S(1)}, u32[]{:S(2)}, u32[]{:S(2)}) collective-permute-start(bf16[128,512]{1,0:T(8,128)(2,1)S(1)} %add_convert_fusion.11), channel_id=1, source_target_pairs={{0,2},{2,4},{4,6},{6,8},{8,10},{10,12},{12,14},{14,16},{16,18},{18... | collective-permute-start | bytes 393224 | tf_op jit(solution)/shard_map/ppermute | solution.py:12
  139.2 0.8 collective-permute-done.27
  140.2 5.6 %collective-permute-start.28 = (bf16[128,512]{1,0:T(8,128)(2,1)S(1)}, bf16[128,512]{1,0:T(8,128)(2,1)S(1)}, u32[]{:S(2)}, u32[]{:S(2)}) collective-permute-start(bf16[128,512]{1,0:T(8,128)(2,1)S(1)} %add_convert_fusion.4), channel_id=1, source_target_pairs={{0,30},{2,0},{4,2},{6,4},{8,6},{10,8},{12,10},{14,12},{16,14},{18,... | collective-permute-start | bytes 393224 | tf_op jit(solution)/shard_map/ppermute | solution.py:12
  146.0 1.9 %collective-permute-start.21 = (bf16[128,512]{1,0:T(8,128)(2,1)S(1)}, bf16[128,512]{1,0:T(8,128)(2,1)S(1)}, u32[]{:S(2)}, u32[]{:S(2)}) collective-permute-start(bf16[128,512]{1,0:T(8,128)(2,1)S(1)} %add_convert_fusion.10), channel_id=1, source_target_pairs={{0,2},{2,4},{4,6},{6,8},{8,10},{10,12},{12,14},{14,16},{16,18},{18... | collective-permute-start | bytes 393224 | tf_op jit(solution)/shard_map/ppermute | solution.py:12
  147.9 0.3 collective-permute-done.28
  148.5 5.6 %collective-permute-start.29 = (bf16[128,512]{1,0:T(8,128)(2,1)S(1)}, bf16[128,512]{1,0:T(8,128)(2,1)S(1)}, u32[]{:S(2)}, u32[]{:S(2)}) collective-permute-start(bf16[128,512]{1,0:T(8,128)(2,1)S(1)} %add_convert_fusion.3), channel_id=1, source_target_pairs={{0,30},{2,0},{4,2},{6,4},{8,6},{10,8},{12,10},{14,12},{16,14},{18,... | collective-permute-start | bytes 393224 | tf_op jit(solution)/shard_map/ppermute | solution.py:12
  154.3 1.9 %collective-permute-start.22 = (bf16[128,512]{1,0:T(8,128)(2,1)S(1)}, bf16[128,512]{1,0:T(8,128)(2,1)S(1)}, u32[]{:S(2)}, u32[]{:S(2)}) collective-permute-start(bf16[128,512]{1,0:T(8,128)(2,1)S(1)} %add_convert_fusion.9), channel_id=1, source_target_pairs={{0,2},{2,4},{4,6},{6,8},{8,10},{10,12},{12,14},{14,16},{16,18},{18... | collective-permute-start | bytes 393224 | tf_op jit(solution)/shard_map/ppermute | solution.py:12
  156.2 0.3 collective-permute-done.29
  156.8 5.6 %collective-permute-start.30 = (bf16[128,512]{1,0:T(8,128)(2,1)S(1)}, bf16[128,512]{1,0:T(8,128)(2,1)S(1)}, u32[]{:S(2)}, u32[]{:S(2)}) collective-permute-start(bf16[128,512]{1,0:T(8,128)(2,1)S(1)} %add_convert_fusion.2), channel_id=1, source_target_pairs={{0,30},{2,0},{4,2},{6,4},{8,6},{10,8},{12,10},{14,12},{16,14},{18,... | collective-permute-start | bytes 393224 | tf_op jit(solution)/shard_map/ppermute | solution.py:12
  162.6 1.9 %collective-permute-start.23 = (bf16[128,512]{1,0:T(8,128)(2,1)S(1)}, bf16[128,512]{1,0:T(8,128)(2,1)S(1)}, u32[]{:S(2)}, u32[]{:S(2)}) collective-permute-start(bf16[128,512]{1,0:T(8,128)(2,1)S(1)} %add_convert_fusion.8), channel_id=1, source_target_pairs={{0,2},{2,4},{4,6},{6,8},{8,10},{10,12},{12,14},{14,16},{16,18},{18... | collective-permute-start | bytes 393224 | tf_op jit(solution)/shard_map/ppermute | solution.py:12
  164.6 0.3 collective-permute-done.30
  165.1 5.6 %collective-permute-start.31 = (bf16[128,512]{1,0:T(8,128)(2,1)S(1)}, bf16[128,512]{1,0:T(8,128)(2,1)S(1)}, u32[]{:S(2)}, u32[]{:S(2)}) collective-permute-start(bf16[128,512]{1,0:T(8,128)(2,1)S(1)} %add_convert_fusion.1), channel_id=1, source_target_pairs={{0,30},{2,0},{4,2},{6,4},{8,6},{10,8},{12,10},{14,12},{16,14},{18,... | collective-permute-start | bytes 393224 | tf_op jit(solution)/shard_map/ppermute | solution.py:12
  170.9 1.9 %collective-permute-start.24 = (bf16[128,512]{1,0:T(8,128)(2,1)S(1)}, bf16[128,512]{1,0:T(8,128)(2,1)S(1)}, u32[]{:S(2)}, u32[]{:S(2)}) collective-permute-start(bf16[128,512]{1,0:T(8,128)(2,1)S(1)} %add_convert_fusion.7), channel_id=1, source_target_pairs={{0,2},{2,4},{4,6},{6,8},{8,10},{10,12},{12,14},{14,16},{16,18},{18... | collective-permute-start | bytes 393224 | tf_op jit(solution)/shard_map/ppermute | solution.py:12
  173.4 5.6 %collective-permute-start.32 = (bf16[128,512]{1,0:T(8,128)(2,1)S(1)}, bf16[128,512]{1,0:T(8,128)(2,1)S(1)}, u32[]{:S(2)}, u32[]{:S(2)}) collective-permute-start(bf16[128,512]{1,0:T(8,128)(2,1)S(1)} %add_convert_fusion), channel_id=1, source_target_pairs={{0,30},{2,0},{4,2},{6,4},{8,6},{10,8},{12,10},{14,12},{16,14},{18,... | collective-permute-start | bytes 393224 | tf_op jit(solution)/shard_map/ppermute | solution.py:12
  179.2 2.3 %collective-permute-done.32 = bf16[128,512]{1,0:T(8,128)(2,1)S(1)} collective-permute-done((bf16[128,512]{1,0:T(8,128)(2,1)S(1)}, bf16[128,512]{1,0:T(8,128)(2,1)S(1)}, u32[]{:S(2)}, u32[]{:S(2)}) %collective-permute-start.32) | collective-permute-done | bytes 131104 | tf_op jit(solution)/shard_map/ppermute | solution.py:12
  181.7 3.8 %collective-permute-start.33 = (bf16[128,256]{1,0:T(8,128)(2,1)S(1)}, bf16[128,256]{1,0:T(8,128)(2,1)S(1)}, u32[]{:S(2)}, u32[]{:S(2)}) collective-permute-start(bf16[128,256]{1,0:T(8,128)(2,1)S(1)} %select_convert_fusion), channel_id=1, source_target_pairs={{0,1},{1,0},{2,3},{3,2},{4,5},{5,4},{6,7},{7,6},{8,9},{9,8},{10,11... | collective-permute-start | bytes 196616 | tf_op jit(solution)/shard_map/ppermute | solution.py:12
  185.5 2.4 %collective-permute-done.33 = bf16[128,256]{1,0:T(8,128)(2,1)S(1)} collective-permute-done((bf16[128,256]{1,0:T(8,128)(2,1)S(1)}, bf16[128,256]{1,0:T(8,128)(2,1)S(1)}, u32[]{:S(2)}, u32[]{:S(2)}) %collective-permute-start.33) | collective-permute-done | bytes 65568 | tf_op jit(solution)/shard_map/ppermute | solution.py:12
  187.9 0.7 add_convert_fusion.13
  (92 shorter events, 12.4 us)
Async XLA Ops:
  0.6 109.4 %copy-start = (bf16[10,256]{1,0:T(8,128)(2,1)S(1)}, bf16[10,256]{1,0:T(8,128)(2,1)}, u32[]{:S(2)}) copy-start(bf16[10,256]{1,0:T(8,128)(2,1)} %param.13) | copy-start | bytes 15364
  0.6 6.4 %collective-permute-start = (bf16[128,256]{1,0:T(8,128)(2,1)}, bf16[128,256]{1,0:T(8,128)(2,1)S(1)}, u32[]{:S(2)}, u32[]{:S(2)}) collective-permute-start(bf16[128,256]{1,0:T(8,128)(2,1)} %param.8), channel_id=1, source_target_pairs={{0,1},{1,0},{2,3},{3,2},{4,5},{5,4},{6,7},{7,6},{8,9},{9,8},{10,11... | collective-permute-start | bytes 196616 | tf_op jit(solution)/shard_map/ppermute | solution.py:12
  5.6 44.6 %copy-start.1 = (bf16[8192,256]{1,0:T(8,128)(2,1)S(1)}, bf16[8192,256]{1,0:T(8,128)(2,1)}, u32[]{:S(2)}) copy-start(bf16[8192,256]{1,0:T(8,128)(2,1)} %param.10) | copy-start | bytes 12582916
  8.0 20.7 %collective-permute-start.2 = (bf16[128,512]{1,0:T(8,128)(2,1)S(1)}, bf16[128,512]{1,0:T(8,128)(2,1)S(1)}, u32[]{:S(2)}, u32[]{:S(2)}) collective-permute-start(bf16[128,512]{1,0:T(8,128)(2,1)S(1)} %maximum_select_fusion), channel_id=1, source_target_pairs={{0,30},{2,0},{4,2},{6,4},{8,6},{10,8},{12,10},{14,12},{16,14},{18,... | collective-permute-start | bytes 393224 | tf_op jit(solution)/shard_map/ppermute | solution.py:12
  26.2 8.1 %collective-permute-start.1 = (bf16[128,512]{1,0:T(8,128)(2,1)S(1)}, bf16[128,512]{1,0:T(8,128)(2,1)S(1)}, u32[]{:S(2)}, u32[]{:S(2)}) collective-permute-start(bf16[128,512]{1,0:T(8,128)(2,1)S(1)} %maximum_select_fusion), channel_id=1, source_target_pairs={{0,2},{2,4},{4,6},{6,8},{8,10},{10,12},{12,14},{14,16},{16,18},{18... | collective-permute-start | bytes 393224 | tf_op jit(solution)/shard_map/ppermute | solution.py:12
  29.8 38.8 %copy-start.2 = (bf16[8192,256]{1,0:T(8,128)(2,1)S(1)}, bf16[8192,256]{1,0:T(8,128)(2,1)}, u32[]{:S(2)}) copy-start(bf16[8192,256]{1,0:T(8,128)(2,1)} %param.9) | copy-start | bytes 12582916
  36.6 9.3 %collective-permute-start.4 = (bf16[128,512]{1,0:T(8,128)(2,1)S(1)}, bf16[128,512]{1,0:T(8,128)(2,1)S(1)}, u32[]{:S(2)}, u32[]{:S(2)}) collective-permute-start(bf16[128,512]{1,0:T(8,128)(2,1)S(1)} %collective-permute-done.2), channel_id=1, source_target_pairs={{0,30},{2,0},{4,2},{6,4},{8,6},{10,8},{12,10},{14,12},{16,14},{18,... | collective-permute-start | bytes 393224 | tf_op jit(solution)/shard_map/ppermute | solution.py:12
  38.5 11.9 %collective-permute-start.3 = (bf16[128,512]{1,0:T(8,128)(2,1)S(1)}, bf16[128,512]{1,0:T(8,128)(2,1)S(1)}, u32[]{:S(2)}, u32[]{:S(2)}) collective-permute-start(bf16[128,512]{1,0:T(8,128)(2,1)S(1)} %collective-permute-done.1), channel_id=1, source_target_pairs={{0,2},{2,4},{4,6},{6,8},{8,10},{10,12},{12,14},{14,16},{16,18},{18... | collective-permute-start | bytes 393224 | tf_op jit(solution)/shard_map/ppermute | solution.py:12
  45.9 8.6 %collective-permute-start.6 = (bf16[128,512]{1,0:T(8,128)(2,1)S(1)}, bf16[128,512]{1,0:T(8,128)(2,1)S(1)}, u32[]{:S(2)}, u32[]{:S(2)}) collective-permute-start(bf16[128,512]{1,0:T(8,128)(2,1)S(1)} %collective-permute-done.4), channel_id=1, source_target_pairs={{0,30},{2,0},{4,2},{6,4},{8,6},{10,8},{12,10},{14,12},{16,14},{18,... | collective-permute-start | bytes 393224 | tf_op jit(solution)/shard_map/ppermute | solution.py:12
  50.4 9.8 %collective-permute-start.5 = (bf16[128,512]{1,0:T(8,128)(2,1)S(1)}, bf16[128,512]{1,0:T(8,128)(2,1)S(1)}, u32[]{:S(2)}, u32[]{:S(2)}) collective-permute-start(bf16[128,512]{1,0:T(8,128)(2,1)S(1)} %collective-permute-done.3), channel_id=1, source_target_pairs={{0,2},{2,4},{4,6},{6,8},{8,10},{10,12},{12,14},{14,16},{16,18},{18... | collective-permute-start | bytes 393224 | tf_op jit(solution)/shard_map/ppermute | solution.py:12
  54.5 9.0 %collective-permute-start.8 = (bf16[128,512]{1,0:T(8,128)(2,1)S(1)}, bf16[128,512]{1,0:T(8,128)(2,1)S(1)}, u32[]{:S(2)}, u32[]{:S(2)}) collective-permute-start(bf16[128,512]{1,0:T(8,128)(2,1)S(1)} %collective-permute-done.6), channel_id=1, source_target_pairs={{0,30},{2,0},{4,2},{6,4},{8,6},{10,8},{12,10},{14,12},{16,14},{18,... | collective-permute-start | bytes 393224 | tf_op jit(solution)/shard_map/ppermute | solution.py:12
  60.2 8.9 %collective-permute-start.7 = (bf16[128,512]{1,0:T(8,128)(2,1)S(1)}, bf16[128,512]{1,0:T(8,128)(2,1)S(1)}, u32[]{:S(2)}, u32[]{:S(2)}) collective-permute-start(bf16[128,512]{1,0:T(8,128)(2,1)S(1)} %collective-permute-done.5), channel_id=1, source_target_pairs={{0,2},{2,4},{4,6},{6,8},{8,10},{10,12},{12,14},{14,16},{16,18},{18... | collective-permute-start | bytes 393224 | tf_op jit(solution)/shard_map/ppermute | solution.py:12
  63.5 7.9 %collective-permute-start.10 = (bf16[128,512]{1,0:T(8,128)(2,1)S(1)}, bf16[128,512]{1,0:T(8,128)(2,1)S(1)}, u32[]{:S(2)}, u32[]{:S(2)}) collective-permute-start(bf16[128,512]{1,0:T(8,128)(2,1)S(1)} %collective-permute-done.8), channel_id=1, source_target_pairs={{0,30},{2,0},{4,2},{6,4},{8,6},{10,8},{12,10},{14,12},{16,14},{18,... | collective-permute-start | bytes 393224 | tf_op jit(solution)/shard_map/ppermute | solution.py:12
  69.1 8.1 %collective-permute-start.9 = (bf16[128,512]{1,0:T(8,128)(2,1)S(1)}, bf16[128,512]{1,0:T(8,128)(2,1)S(1)}, u32[]{:S(2)}, u32[]{:S(2)}) collective-permute-start(bf16[128,512]{1,0:T(8,128)(2,1)S(1)} %collective-permute-done.7), channel_id=1, source_target_pairs={{0,2},{2,4},{4,6},{6,8},{8,10},{10,12},{12,14},{14,16},{16,18},{18... | collective-permute-start | bytes 393224 | tf_op jit(solution)/shard_map/ppermute | solution.py:12
  71.5 8.1 %collective-permute-start.12 = (bf16[128,512]{1,0:T(8,128)(2,1)S(1)}, bf16[128,512]{1,0:T(8,128)(2,1)S(1)}, u32[]{:S(2)}, u32[]{:S(2)}) collective-permute-start(bf16[128,512]{1,0:T(8,128)(2,1)S(1)} %collective-permute-done.10), channel_id=1, source_target_pairs={{0,30},{2,0},{4,2},{6,4},{8,6},{10,8},{12,10},{14,12},{16,14},{18,... | collective-permute-start | bytes 393224 | tf_op jit(solution)/shard_map/ppermute | solution.py:12
  77.1 32.9 %copy-start.3 = (f32[256]{0:T(256)S(1)}, f32[256]{0:T(256)}, u32[]{:S(2)}) copy-start(f32[256]{0:T(256)} %param.12) | copy-start | bytes 3076
  77.2 32.9 %copy-start.4 = (s32[128]{0:T(128)S(1)}, s32[128]{0:T(128)}, u32[]{:S(2)}) copy-start(s32[128]{0:T(128)} %param.14) | copy-start | bytes 1540
  77.2 8.1 %collective-permute-start.11 = (bf16[128,512]{1,0:T(8,128)(2,1)S(1)}, bf16[128,512]{1,0:T(8,128)(2,1)S(1)}, u32[]{:S(2)}, u32[]{:S(2)}) collective-permute-start(bf16[128,512]{1,0:T(8,128)(2,1)S(1)} %collective-permute-done.9), channel_id=1, source_target_pairs={{0,2},{2,4},{4,6},{6,8},{8,10},{10,12},{12,14},{14,16},{16,18},{18... | collective-permute-start | bytes 393224 | tf_op jit(solution)/shard_map/ppermute | solution.py:12
  79.5 8.1 %collective-permute-start.14 = (bf16[128,512]{1,0:T(8,128)(2,1)S(1)}, bf16[128,512]{1,0:T(8,128)(2,1)S(1)}, u32[]{:S(2)}, u32[]{:S(2)}) collective-permute-start(bf16[128,512]{1,0:T(8,128)(2,1)S(1)} %collective-permute-done.12), channel_id=1, source_target_pairs={{0,30},{2,0},{4,2},{6,4},{8,6},{10,8},{12,10},{14,12},{16,14},{18,... | collective-permute-start | bytes 393224 | tf_op jit(solution)/shard_map/ppermute | solution.py:12
  85.3 9.1 %collective-permute-start.13 = (bf16[128,512]{1,0:T(8,128)(2,1)S(1)}, bf16[128,512]{1,0:T(8,128)(2,1)S(1)}, u32[]{:S(2)}, u32[]{:S(2)}) collective-permute-start(bf16[128,512]{1,0:T(8,128)(2,1)S(1)} %collective-permute-done.11), channel_id=1, source_target_pairs={{0,2},{2,4},{4,6},{6,8},{8,10},{10,12},{12,14},{14,16},{16,18},{18... | collective-permute-start | bytes 393224 | tf_op jit(solution)/shard_map/ppermute | solution.py:12
  94.4 8.1 %collective-permute-start.15 = (bf16[128,512]{1,0:T(8,128)(2,1)S(1)}, bf16[128,512]{1,0:T(8,128)(2,1)S(1)}, u32[]{:S(2)}, u32[]{:S(2)}) collective-permute-start(bf16[128,512]{1,0:T(8,128)(2,1)S(1)} %collective-permute-done.13), channel_id=1, source_target_pairs={{0,2},{2,4},{4,6},{6,8},{8,10},{10,12},{12,14},{14,16},{16,18},{18... | collective-permute-start | bytes 393224 | tf_op jit(solution)/shard_map/ppermute | solution.py:12
  102.7 7.3 %collective-permute-start.16 = (bf16[3,256]{1,0:T(4,128)(2,1)S(1)}, bf16[3,256]{1,0:T(4,128)(2,1)S(1)}, u32[]{:S(2)}, u32[]{:S(2)}) collective-permute-start(bf16[3,256]{1,0:T(4,128)(2,1)S(1)} %slice.87), channel_id=1, source_target_pairs={{0,32},{32,64},{64,96},{96,128},{128,160},{160,192},{192,224},{224... | collective-permute-start | bytes 4616 | tf_op jit(solution)/shard_map/ppermute | solution.py:79
  112.9 3.6 %collective-permute-start.17 = (f32[3,256]{1,0:T(4,128)S(1)}, f32[3,256]{1,0:T(4,128)S(1)}, u32[]{:S(2)}, u32[]{:S(2)}) collective-permute-start(f32[3,256]{1,0:T(4,128)S(1)} %fusion.251), channel_id=1, source_target_pairs={{32,0},{64,32},{96,64},{128,96},{160,128},{192,160},{224,192},{256... | collective-permute-start | bytes 9224 | tf_op jit(solution)/shard_map/ppermute | solution.py:79
  116.8 7.5 %collective-permute-start.25 = (bf16[128,512]{1,0:T(8,128)(2,1)S(1)}, bf16[128,512]{1,0:T(8,128)(2,1)S(1)}, u32[]{:S(2)}, u32[]{:S(2)}) collective-permute-start(bf16[128,512]{1,0:T(8,128)(2,1)S(1)} %fusion.13), channel_id=1, source_target_pairs={{0,30},{2,0},{4,2},{6,4},{8,6},{10,8},{12,10},{14,12},{16,14},{18,... | collective-permute-start | bytes 393224 | tf_op jit(solution)/shard_map/ppermute | solution.py:12
  119.0 8.7 %collective-permute-start.18 = (bf16[128,512]{1,0:T(8,128)(2,1)S(1)}, bf16[128,512]{1,0:T(8,128)(2,1)S(1)}, u32[]{:S(2)}, u32[]{:S(2)}) collective-permute-start(bf16[128,512]{1,0:T(8,128)(2,1)S(1)} %fusion), channel_id=1, source_target_pairs={{0,2},{2,4},{4,6},{6,8},{8,10},{10,12},{12,14},{14,16},{16,18},{18... | collective-permute-start | bytes 393224 | tf_op jit(solution)/shard_map/ppermute | solution.py:12
  124.5 7.9 %collective-permute-start.26 = (bf16[128,512]{1,0:T(8,128)(2,1)S(1)}, bf16[128,512]{1,0:T(8,128)(2,1)S(1)}, u32[]{:S(2)}, u32[]{:S(2)}) collective-permute-start(bf16[128,512]{1,0:T(8,128)(2,1)S(1)} %add_convert_fusion.6), channel_id=1, source_target_pairs={{0,30},{2,0},{4,2},{6,4},{8,6},{10,8},{12,10},{14,12},{16,14},{18,... | collective-permute-start | bytes 393224 | tf_op jit(solution)/shard_map/ppermute | solution.py:12
  127.9 9.1 %collective-permute-start.19 = (bf16[128,512]{1,0:T(8,128)(2,1)S(1)}, bf16[128,512]{1,0:T(8,128)(2,1)S(1)}, u32[]{:S(2)}, u32[]{:S(2)}) collective-permute-start(bf16[128,512]{1,0:T(8,128)(2,1)S(1)} %add_convert_fusion.12), channel_id=1, source_target_pairs={{0,2},{2,4},{4,6},{6,8},{8,10},{10,12},{12,14},{14,16},{16,18},{18... | collective-permute-start | bytes 393224 | tf_op jit(solution)/shard_map/ppermute | solution.py:12
  132.6 7.3 %collective-permute-start.27 = (bf16[128,512]{1,0:T(8,128)(2,1)S(1)}, bf16[128,512]{1,0:T(8,128)(2,1)S(1)}, u32[]{:S(2)}, u32[]{:S(2)}) collective-permute-start(bf16[128,512]{1,0:T(8,128)(2,1)S(1)} %add_convert_fusion.5), channel_id=1, source_target_pairs={{0,30},{2,0},{4,2},{6,4},{8,6},{10,8},{12,10},{14,12},{16,14},{18,... | collective-permute-start | bytes 393224 | tf_op jit(solution)/shard_map/ppermute | solution.py:12
  137.2 8.5 %collective-permute-start.20 = (bf16[128,512]{1,0:T(8,128)(2,1)S(1)}, bf16[128,512]{1,0:T(8,128)(2,1)S(1)}, u32[]{:S(2)}, u32[]{:S(2)}) collective-permute-start(bf16[128,512]{1,0:T(8,128)(2,1)S(1)} %add_convert_fusion.11), channel_id=1, source_target_pairs={{0,2},{2,4},{4,6},{6,8},{8,10},{10,12},{12,14},{14,16},{16,18},{18... | collective-permute-start | bytes 393224 | tf_op jit(solution)/shard_map/ppermute | solution.py:12
  140.2 8.1 %collective-permute-start.28 = (bf16[128,512]{1,0:T(8,128)(2,1)S(1)}, bf16[128,512]{1,0:T(8,128)(2,1)S(1)}, u32[]{:S(2)}, u32[]{:S(2)}) collective-permute-start(bf16[128,512]{1,0:T(8,128)(2,1)S(1)} %add_convert_fusion.4), channel_id=1, source_target_pairs={{0,30},{2,0},{4,2},{6,4},{8,6},{10,8},{12,10},{14,12},{16,14},{18,... | collective-permute-start | bytes 393224 | tf_op jit(solution)/shard_map/ppermute | solution.py:12
  146.0 8.1 %collective-permute-start.21 = (bf16[128,512]{1,0:T(8,128)(2,1)S(1)}, bf16[128,512]{1,0:T(8,128)(2,1)S(1)}, u32[]{:S(2)}, u32[]{:S(2)}) collective-permute-start(bf16[128,512]{1,0:T(8,128)(2,1)S(1)} %add_convert_fusion.10), channel_id=1, source_target_pairs={{0,2},{2,4},{4,6},{6,8},{8,10},{10,12},{12,14},{14,16},{16,18},{18... | collective-permute-start | bytes 393224 | tf_op jit(solution)/shard_map/ppermute | solution.py:12
  148.5 8.1 %collective-permute-start.29 = (bf16[128,512]{1,0:T(8,128)(2,1)S(1)}, bf16[128,512]{1,0:T(8,128)(2,1)S(1)}, u32[]{:S(2)}, u32[]{:S(2)}) collective-permute-start(bf16[128,512]{1,0:T(8,128)(2,1)S(1)} %add_convert_fusion.3), channel_id=1, source_target_pairs={{0,30},{2,0},{4,2},{6,4},{8,6},{10,8},{12,10},{14,12},{16,14},{18,... | collective-permute-start | bytes 393224 | tf_op jit(solution)/shard_map/ppermute | solution.py:12
  154.3 8.1 %collective-permute-start.22 = (bf16[128,512]{1,0:T(8,128)(2,1)S(1)}, bf16[128,512]{1,0:T(8,128)(2,1)S(1)}, u32[]{:S(2)}, u32[]{:S(2)}) collective-permute-start(bf16[128,512]{1,0:T(8,128)(2,1)S(1)} %add_convert_fusion.9), channel_id=1, source_target_pairs={{0,2},{2,4},{4,6},{6,8},{8,10},{10,12},{12,14},{14,16},{16,18},{18... | collective-permute-start | bytes 393224 | tf_op jit(solution)/shard_map/ppermute | solution.py:12
  156.8 8.1 %collective-permute-start.30 = (bf16[128,512]{1,0:T(8,128)(2,1)S(1)}, bf16[128,512]{1,0:T(8,128)(2,1)S(1)}, u32[]{:S(2)}, u32[]{:S(2)}) collective-permute-start(bf16[128,512]{1,0:T(8,128)(2,1)S(1)} %add_convert_fusion.2), channel_id=1, source_target_pairs={{0,30},{2,0},{4,2},{6,4},{8,6},{10,8},{12,10},{14,12},{16,14},{18,... | collective-permute-start | bytes 393224 | tf_op jit(solution)/shard_map/ppermute | solution.py:12
  162.6 8.1 %collective-permute-start.23 = (bf16[128,512]{1,0:T(8,128)(2,1)S(1)}, bf16[128,512]{1,0:T(8,128)(2,1)S(1)}, u32[]{:S(2)}, u32[]{:S(2)}) collective-permute-start(bf16[128,512]{1,0:T(8,128)(2,1)S(1)} %add_convert_fusion.8), channel_id=1, source_target_pairs={{0,2},{2,4},{4,6},{6,8},{8,10},{10,12},{12,14},{14,16},{16,18},{18... | collective-permute-start | bytes 393224 | tf_op jit(solution)/shard_map/ppermute | solution.py:12
  165.1 8.1 %collective-permute-start.31 = (bf16[128,512]{1,0:T(8,128)(2,1)S(1)}, bf16[128,512]{1,0:T(8,128)(2,1)S(1)}, u32[]{:S(2)}, u32[]{:S(2)}) collective-permute-start(bf16[128,512]{1,0:T(8,128)(2,1)S(1)} %add_convert_fusion.1), channel_id=1, source_target_pairs={{0,30},{2,0},{4,2},{6,4},{8,6},{10,8},{12,10},{14,12},{16,14},{18,... | collective-permute-start | bytes 393224 | tf_op jit(solution)/shard_map/ppermute | solution.py:12
  170.9 8.3 %collective-permute-start.24 = (bf16[128,512]{1,0:T(8,128)(2,1)S(1)}, bf16[128,512]{1,0:T(8,128)(2,1)S(1)}, u32[]{:S(2)}, u32[]{:S(2)}) collective-permute-start(bf16[128,512]{1,0:T(8,128)(2,1)S(1)} %add_convert_fusion.7), channel_id=1, source_target_pairs={{0,2},{2,4},{4,6},{6,8},{8,10},{10,12},{12,14},{14,16},{16,18},{18... | collective-permute-start | bytes 393224 | tf_op jit(solution)/shard_map/ppermute | solution.py:12
  173.4 8.1 %collective-permute-start.32 = (bf16[128,512]{1,0:T(8,128)(2,1)S(1)}, bf16[128,512]{1,0:T(8,128)(2,1)S(1)}, u32[]{:S(2)}, u32[]{:S(2)}) collective-permute-start(bf16[128,512]{1,0:T(8,128)(2,1)S(1)} %add_convert_fusion), channel_id=1, source_target_pairs={{0,30},{2,0},{4,2},{6,4},{8,6},{10,8},{12,10},{14,12},{16,14},{18,... | collective-permute-start | bytes 393224 | tf_op jit(solution)/shard_map/ppermute | solution.py:12
  181.7 6.2 %collective-permute-start.33 = (bf16[128,256]{1,0:T(8,128)(2,1)S(1)}, bf16[128,256]{1,0:T(8,128)(2,1)S(1)}, u32[]{:S(2)}, u32[]{:S(2)}) collective-permute-start(bf16[128,256]{1,0:T(8,128)(2,1)S(1)} %select_convert_fusion), channel_id=1, source_target_pairs={{0,1},{1,0},{2,3},{3,2},{4,5},{5,4},{6,7},{7,6},{8,9},{9,8},{10,11... | collective-permute-start | bytes 196616 | tf_op jit(solution)/shard_map/ppermute | solution.py:12

commit v4 on v3

--- a/solution.py
+++ b/solution.py
@@ -121,19 +121,21 @@
         conv_weight, jnp.concatenate([edge_zeros, dconv[: taps - 1]], axis=0), taps - 1
     )
     arrived = passed_along(front, "seq", -1)
-    dxin = jnp.concatenate(
-        [local[: rows - (taps - 1)], local[rows - (taps - 1) :] + arrived], axis=0
-    )
-    dxin16 = dxin.astype(jnp.bfloat16)
+    cut = rows - (taps - 1)
+    top16 = local[:cut].astype(jnp.bfloat16)
+    tail16 = (local[cut:] + arrived).astype(jnp.bfloat16)
     spec = (((1,), (1,)), ((), ()))
     width = 2 * tokens.shape[1]
 
     def block_terms(place):
         gate_rows = lax.dynamic_slice_in_dim(w_gate, place * width, width, 0)
         conv_rows = lax.dynamic_slice_in_dim(w_conv_in, place * width, width, 0)
-        part = lax.dot_general(dgate16, gate_rows, spec, preferred_element_type=jnp.float32)
-        part = part + lax.dot_general(dxin16, conv_rows, spec, preferred_element_type=jnp.float32)
-        return part.astype(jnp.bfloat16)
+        parts = []
+        for gate_part, conv_part in ((dgate16[:cut], top16), (dgate16[cut:], tail16)):
+            part = lax.dot_general(gate_part, gate_rows, spec, preferred_element_type=jnp.float32)
+            part = part + lax.dot_general(conv_part, conv_rows, spec, preferred_element_type=jnp.float32)
+            parts.append(part.astype(jnp.bfloat16))
+        return jnp.concatenate(parts, 0)
 
     d_tokens = scatter_features(block_terms)
     return (gated, d_tokens)

time: 192 us -> 201 us (1.047)
  matrix products: 23.2 us -> 29.2 us
  waiting for transfers between devices: 33.7 us -> 37.6 us
    dot_general x32 -> x64, matrix products: 7.22 us -> 13.2 us  [the longest x32 6.66 us: block_terms(): lax.dot_general(conv_part, conv_rows, spec, preferred_element_type=jnp.fl...]
    ppermute x32, waiting for transfers between devices: 28.5 us -> 32.4 us  [shifted(): lax.ppermute(block, axis, [(i, (i + distance) % size) for i in range(size)])]
  transfers between devices with their start and end apart: 34 -> 34, of which waited for: 16 -> 18; matrix products, arithmetic and copies ran while one was open for 10% -> 10% of each run, Pallas kernels for 0% -> 0%
where the time goes in v4:
time: 201 us; the launch traced here: 198 us
  starting transfers between devices  124 us (62%)
  waiting for transfers between devices  37.6 us (19%)
  matrix products  29.2 us (15%)
  other arithmetic  4.32 us (2%)
    ppermute x32, starting transfers between devices, shifted(): lax.ppermute(block, axis, [(i, (i + distance) % size) for i in range(size)])  121 us
    ppermute x32, waiting for transfers between devices, shifted(): lax.ppermute(block, axis, [(i, (i + distance) % size) for i in range(size)])  32.4 us
    dot_general x32, matrix products, project(): part = jnp.dot(block, rows, preferred_element_type=jnp.float32)  15.8 us
    dot_general x32, matrix products, block_terms(): lax.dot_general(conv_part, conv_rows, spec, preferred_element_type=jnp.fl...  6.66 us
    dot_general x32, matrix products, block_terms(): lax.dot_general(gate_part, gate_rows, spec, preferred_element_type=jnp.fl...  6.54 us
    ppermute x2, waiting for transfers between devices, passed_along(): return lax.ppermute(block, axis, route)  5.18 us
  transfers between devices with their start and end apart: 34, of which 18 were waited for; matrix products, arithmetic and copies ran while one was open for 10% of the time, Pallas kernels for 0%

profile of v4, /device:TPU:56, one launch (start us, length us, event | category | flops | bytes accessed | tf_op | source)
XLA Modules:
  0.0 198.2 jit_solution(18164524818094931135)
XLA Ops:
  0.6 3.4 %collective-permute-start = (bf16[128,256]{1,0:T(8,128)(2,1)}, bf16[128,256]{1,0:T(8,128)(2,1)S(1)}, u32[]{:S(2)}, u32[]{:S(2)}) collective-permute-start(bf16[128,256]{1,0:T(8,128)(2,1)} %param.8), channel_id=1, source_target_pairs={{0,1},{1,0},{2,3},{3,2},{4,5},{5,4},{6,7},{7,6},{8,9},{9,8},{10,11... | collective-permute-start | bytes 196616 | tf_op jit(solution)/shard_map/ppermute | solution.py:12
  4.1 0.8 fusion.341
  5.0 0.7 convert_element_type.266
  5.6 1.4 collective-permute-done
  7.0 1.5 maximum_select_fusion
  8.6 18.2 %collective-permute-start.2 = (bf16[128,512]{1,0:T(8,128)(2,1)S(1)}, bf16[128,512]{1,0:T(8,128)(2,1)S(1)}, u32[]{:S(2)}, u32[]{:S(2)}) collective-permute-start(bf16[128,512]{1,0:T(8,128)(2,1)S(1)} %maximum_select_fusion), channel_id=1, source_target_pairs={{0,30},{2,0},{4,2},{6,4},{8,6},{10,8},{12,10},{14,12},{16,14},{18,... | collective-permute-start | bytes 393224 | tf_op jit(solution)/shard_map/ppermute | solution.py:12
  26.8 1.9 collective-permute-start.1
  28.7 0.6 collective-permute-done.2
  29.3 1.1 fusion.162
  30.4 4.4 %collective-permute-done.1 = bf16[128,512]{1,0:T(8,128)(2,1)S(1)} collective-permute-done((bf16[128,512]{1,0:T(8,128)(2,1)S(1)}, bf16[128,512]{1,0:T(8,128)(2,1)S(1)}, u32[]{:S(2)}, u32[]{:S(2)}) %collective-permute-start.1) | collective-permute-done | bytes 131104 | tf_op jit(solution)/shard_map/ppermute | solution.py:12
  34.9 1.1 fusion.55
  36.0 1.1 fusion.22
  37.2 1.9 collective-permute-start.4
  39.1 1.1 fusion.190
  40.3 1.1 fusion.65
  41.4 3.9 %collective-permute-start.3 = (bf16[128,512]{1,0:T(8,128)(2,1)S(1)}, bf16[128,512]{1,0:T(8,128)(2,1)S(1)}, u32[]{:S(2)}, u32[]{:S(2)}) collective-permute-start(bf16[128,512]{1,0:T(8,128)(2,1)S(1)} %collective-permute-done.1), channel_id=1, source_target_pairs={{0,2},{2,4},{4,6},{6,8},{8,10},{10,12},{12,14},{14,16},{16,18},{18... | collective-permute-start | bytes 393224 | tf_op jit(solution)/shard_map/ppermute | solution.py:12
  45.3 1.1 fusion.29
  46.5 3.1 %collective-permute-start.6 = (bf16[128,512]{1,0:T(8,128)(2,1)S(1)}, bf16[128,512]{1,0:T(8,128)(2,1)S(1)}, u32[]{:S(2)}, u32[]{:S(2)}) collective-permute-start(bf16[128,512]{1,0:T(8,128)(2,1)S(1)} %collective-permute-done.4), channel_id=1, source_target_pairs={{0,30},{2,0},{4,2},{6,4},{8,6},{10,8},{12,10},{14,12},{16,14},{18,... | collective-permute-start | bytes 393224 | tf_op jit(solution)/shard_map/ppermute | solution.py:12
  49.6 1.1 fusion.156
  50.8 1.1 fusion.186
  52.0 2.7 %collective-permute-start.5 = (bf16[128,512]{1,0:T(8,128)(2,1)S(1)}, bf16[128,512]{1,0:T(8,128)(2,1)S(1)}, u32[]{:S(2)}, u32[]{:S(2)}) collective-permute-start(bf16[128,512]{1,0:T(8,128)(2,1)S(1)} %collective-permute-done.3), channel_id=1, source_target_pairs={{0,2},{2,4},{4,6},{6,8},{8,10},{10,12},{12,14},{14,16},{16,18},{18... | collective-permute-start | bytes 393224 | tf_op jit(solution)/shard_map/ppermute | solution.py:12
  54.9 1.1 fusion.28
  56.1 4.3 %collective-permute-start.8 = (bf16[128,512]{1,0:T(8,128)(2,1)S(1)}, bf16[128,512]{1,0:T(8,128)(2,1)S(1)}, u32[]{:S(2)}, u32[]{:S(2)}) collective-permute-start(bf16[128,512]{1,0:T(8,128)(2,1)S(1)} %collective-permute-done.6), channel_id=1, source_target_pairs={{0,30},{2,0},{4,2},{6,4},{8,6},{10,8},{12,10},{14,12},{16,14},{18,... | collective-permute-start | bytes 393224 | tf_op jit(solution)/shard_map/ppermute | solution.py:12
  60.6 1.1 fusion.182
  61.8 1.9 collective-permute-start.7
  64.1 5.1 %collective-permute-start.10 = (bf16[128,512]{1,0:T(8,128)(2,1)S(1)}, bf16[128,512]{1,0:T(8,128)(2,1)S(1)}, u32[]{:S(2)}, u32[]{:S(2)}) collective-permute-start(bf16[128,512]{1,0:T(8,128)(2,1)S(1)} %collective-permute-done.8), channel_id=1, source_target_pairs={{0,30},{2,0},{4,2},{6,4},{8,6},{10,8},{12,10},{14,12},{16,14},{18,... | collective-permute-start | bytes 393224 | tf_op jit(solution)/shard_map/ppermute | solution.py:12
  69.8 1.9 collective-permute-start.9
  72.2 5.1 %collective-permute-start.12 = (bf16[128,512]{1,0:T(8,128)(2,1)S(1)}, bf16[128,512]{1,0:T(8,128)(2,1)S(1)}, u32[]{:S(2)}, u32[]{:S(2)}) collective-permute-start(bf16[128,512]{1,0:T(8,128)(2,1)S(1)} %collective-permute-done.10), channel_id=1, source_target_pairs={{0,30},{2,0},{4,2},{6,4},{8,6},{10,8},{12,10},{14,12},{16,14},{18,... | collective-permute-start | bytes 393224 | tf_op jit(solution)/shard_map/ppermute | solution.py:12
  77.9 1.9 collective-permute-start.11
  80.2 5.1 %collective-permute-start.14 = (bf16[128,512]{1,0:T(8,128)(2,1)S(1)}, bf16[128,512]{1,0:T(8,128)(2,1)S(1)}, u32[]{:S(2)}, u32[]{:S(2)}) collective-permute-start(bf16[128,512]{1,0:T(8,128)(2,1)S(1)} %collective-permute-done.12), channel_id=1, source_target_pairs={{0,30},{2,0},{4,2},{6,4},{8,6},{10,8},{12,10},{14,12},{16,14},{18,... | collective-permute-start | bytes 393224 | tf_op jit(solution)/shard_map/ppermute | solution.py:12
  85.8 0.5 collective-permute-done.11
  86.4 1.9 collective-permute-start.13
  89.1 6.6 %collective-permute-done.13 = bf16[128,512]{1,0:T(8,128)(2,1)S(1)} collective-permute-done((bf16[128,512]{1,0:T(8,128)(2,1)S(1)}, bf16[128,512]{1,0:T(8,128)(2,1)S(1)}, u32[]{:S(2)}, u32[]{:S(2)}) %collective-permute-start.13) | collective-permute-done | bytes 131104 | tf_op jit(solution)/shard_map/ppermute | solution.py:12
  95.7 1.9 collective-permute-start.15
  98.0 5.7 %collective-permute-done.15 = bf16[128,512]{1,0:T(8,128)(2,1)S(1)} collective-permute-done((bf16[128,512]{1,0:T(8,128)(2,1)S(1)}, bf16[128,512]{1,0:T(8,128)(2,1)S(1)}, u32[]{:S(2)}, u32[]{:S(2)}) %collective-permute-start.15) | collective-permute-done | bytes 131104 | tf_op jit(solution)/shard_map/ppermute | solution.py:12
  104.0 1.9 collective-permute-start.16
  106.1 5.2 %collective-permute-done.16 = bf16[3,256]{1,0:T(4,128)(2,1)S(1)} collective-permute-done((bf16[3,256]{1,0:T(4,128)(2,1)S(1)}, bf16[3,256]{1,0:T(4,128)(2,1)S(1)}, u32[]{:S(2)}, u32[]{:S(2)}) %collective-permute-start.16) | collective-permute-done | bytes 1568 | tf_op jit(solution)/shard_map/ppermute | solution.py:79
  111.7 0.7 fusion.198
  118.9 1.9 collective-permute-start.17
  127.5 1.9 collective-permute-start.25
  129.5 3.9 %collective-permute-start.18 = (bf16[128,512]{1,0:T(8,128)(2,1)S(1)}, bf16[128,512]{1,0:T(8,128)(2,1)S(1)}, u32[]{:S(2)}, u32[]{:S(2)}) collective-permute-start(bf16[128,512]{1,0:T(8,128)(2,1)S(1)} %pad_maximum_fusion), channel_id=1, source_target_pairs={{0,2},{2,4},{4,6},{6,8},{8,10},{10,12},{12,14},{14,16},{16,18},{18... | collective-permute-start | bytes 393224 | tf_op jit(solution)/shard_map/ppermute | solution.py:12
  133.6 1.7 collective-permute-done.25
  135.4 3.4 %collective-permute-start.26 = (bf16[128,512]{1,0:T(8,128)(2,1)S(1)}, bf16[128,512]{1,0:T(8,128)(2,1)S(1)}, u32[]{:S(2)}, u32[]{:S(2)}) collective-permute-start(bf16[128,512]{1,0:T(8,128)(2,1)S(1)} %add_convert_fusion.6), channel_id=1, source_target_pairs={{0,30},{2,0},{4,2},{6,4},{8,6},{10,8},{12,10},{14,12},{16,14},{18,... | collective-permute-start | bytes 393224 | tf_op jit(solution)/shard_map/ppermute | solution.py:12
  138.8 2.4 %collective-permute-start.19 = (bf16[128,512]{1,0:T(8,128)(2,1)S(1)}, bf16[128,512]{1,0:T(8,128)(2,1)S(1)}, u32[]{:S(2)}, u32[]{:S(2)}) collective-permute-start(bf16[128,512]{1,0:T(8,128)(2,1)S(1)} %add_convert_fusion.12), channel_id=1, source_target_pairs={{0,2},{2,4},{4,6},{6,8},{8,10},{10,12},{12,14},{14,16},{16,18},{18... | collective-permute-start | bytes 393224 | tf_op jit(solution)/shard_map/ppermute | solution.py:12
  141.3 1.1 collective-permute-done.26
  142.4 4.8 %collective-permute-start.27 = (bf16[128,512]{1,0:T(8,128)(2,1)S(1)}, bf16[128,512]{1,0:T(8,128)(2,1)S(1)}, u32[]{:S(2)}, u32[]{:S(2)}) collective-permute-start(bf16[128,512]{1,0:T(8,128)(2,1)S(1)} %add_convert_fusion.5), channel_id=1, source_target_pairs={{0,30},{2,0},{4,2},{6,4},{8,6},{10,8},{12,10},{14,12},{16,14},{18,... | collective-permute-start | bytes 393224 | tf_op jit(solution)/shard_map/ppermute | solution.py:12
  147.3 1.9 collective-permute-start.20
  149.2 0.5 collective-permute-done.27
  149.8 5.6 %collective-permute-start.28 = (bf16[128,512]{1,0:T(8,128)(2,1)S(1)}, bf16[128,512]{1,0:T(8,128)(2,1)S(1)}, u32[]{:S(2)}, u32[]{:S(2)}) collective-permute-start(bf16[128,512]{1,0:T(8,128)(2,1)S(1)} %add_convert_fusion.4), channel_id=1, source_target_pairs={{0,30},{2,0},{4,2},{6,4},{8,6},{10,8},{12,10},{14,12},{16,14},{18,... | collective-permute-start | bytes 393224 | tf_op jit(solution)/shard_map/ppermute | solution.py:12
  155.4 1.9 collective-permute-start.21
  157.3 0.5 collective-permute-done.28
  157.9 5.6 %collective-permute-start.29 = (bf16[128,512]{1,0:T(8,128)(2,1)S(1)}, bf16[128,512]{1,0:T(8,128)(2,1)S(1)}, u32[]{:S(2)}, u32[]{:S(2)}) collective-permute-start(bf16[128,512]{1,0:T(8,128)(2,1)S(1)} %add_convert_fusion.3), channel_id=1, source_target_pairs={{0,30},{2,0},{4,2},{6,4},{8,6},{10,8},{12,10},{14,12},{16,14},{18,... | collective-permute-start | bytes 393224 | tf_op jit(solution)/shard_map/ppermute | solution.py:12
  163.5 1.9 collective-permute-start.22
  166.0 5.6 %collective-permute-start.30 = (bf16[128,512]{1,0:T(8,128)(2,1)S(1)}, bf16[128,512]{1,0:T(8,128)(2,1)S(1)}, u32[]{:S(2)}, u32[]{:S(2)}) collective-permute-start(bf16[128,512]{1,0:T(8,128)(2,1)S(1)} %add_convert_fusion.2), channel_id=1, source_target_pairs={{0,30},{2,0},{4,2},{6,4},{8,6},{10,8},{12,10},{14,12},{16,14},{18,... | collective-permute-start | bytes 393224 | tf_op jit(solution)/shard_map/ppermute | solution.py:12
  171.6 1.9 collective-permute-start.23
  173.6 0.5 collective-permute-done.30
  174.1 5.6 %collective-permute-start.31 = (bf16[128,512]{1,0:T(8,128)(2,1)S(1)}, bf16[128,512]{1,0:T(8,128)(2,1)S(1)}, u32[]{:S(2)}, u32[]{:S(2)}) collective-permute-start(bf16[128,512]{1,0:T(8,128)(2,1)S(1)} %add_convert_fusion.1), channel_id=1, source_target_pairs={{0,30},{2,0},{4,2},{6,4},{8,6},{10,8},{12,10},{14,12},{16,14},{18,... | collective-permute-start | bytes 393224 | tf_op jit(solution)/shard_map/ppermute | solution.py:12
  179.8 1.9 collective-permute-start.24
  181.7 1.5 collective-permute-done.31
  183.2 5.6 %collective-permute-start.32 = (bf16[128,512]{1,0:T(8,128)(2,1)S(1)}, bf16[128,512]{1,0:T(8,128)(2,1)S(1)}, u32[]{:S(2)}, u32[]{:S(2)}) collective-permute-start(bf16[128,512]{1,0:T(8,128)(2,1)S(1)} %add_convert_fusion), channel_id=1, source_target_pairs={{0,30},{2,0},{4,2},{6,4},{8,6},{10,8},{12,10},{14,12},{16,14},{18,... | collective-permute-start | bytes 393224 | tf_op jit(solution)/shard_map/ppermute | solution.py:12
  189.0 2.3 %collective-permute-done.32 = bf16[128,512]{1,0:T(8,128)(2,1)S(1)} collective-permute-done((bf16[128,512]{1,0:T(8,128)(2,1)S(1)}, bf16[128,512]{1,0:T(8,128)(2,1)S(1)}, u32[]{:S(2)}, u32[]{:S(2)}) %collective-permute-start.32) | collective-permute-done | bytes 131104 | tf_op jit(solution)/shard_map/ppermute | solution.py:12
  191.4 2.1 %collective-permute-start.33 = (bf16[128,256]{1,0:T(8,128)(2,1)S(1)}, bf16[128,256]{1,0:T(8,128)(2,1)S(1)}, u32[]{:S(2)}, u32[]{:S(2)}) collective-permute-start(bf16[128,256]{1,0:T(8,128)(2,1)S(1)} %select_convert_fusion), channel_id=1, source_target_pairs={{0,1},{1,0},{2,3},{3,2},{4,5},{5,4},{6,7},{7,6},{8,9},{9,8},{10,11... | collective-permute-start | bytes 196616 | tf_op jit(solution)/shard_map/ppermute | solution.py:12
  193.6 4.0 %collective-permute-done.33 = bf16[128,256]{1,0:T(8,128)(2,1)S(1)} collective-permute-done((bf16[128,256]{1,0:T(8,128)(2,1)S(1)}, bf16[128,256]{1,0:T(8,128)(2,1)S(1)}, u32[]{:S(2)}, u32[]{:S(2)}) %collective-permute-start.33) | collective-permute-done | bytes 65568 | tf_op jit(solution)/shard_map/ppermute | solution.py:12
  197.6 0.7 add_convert_fusion.13
  (140 shorter events, 19.5 us)
Async XLA Ops:
  0.6 110.7 %copy-start = (bf16[10,256]{1,0:T(8,128)(2,1)S(1)}, bf16[10,256]{1,0:T(8,128)(2,1)}, u32[]{:S(2)}) copy-start(bf16[10,256]{1,0:T(8,128)(2,1)} %param.13) | copy-start | bytes 15364
  0.6 6.4 %collective-permute-start = (bf16[128,256]{1,0:T(8,128)(2,1)}, bf16[128,256]{1,0:T(8,128)(2,1)S(1)}, u32[]{:S(2)}, u32[]{:S(2)}) collective-permute-start(bf16[128,256]{1,0:T(8,128)(2,1)} %param.8), channel_id=1, source_target_pairs={{0,1},{1,0},{2,3},{3,2},{4,5},{5,4},{6,7},{7,6},{8,9},{9,8},{10,11... | collective-permute-start | bytes 196616 | tf_op jit(solution)/shard_map/ppermute | solution.py:12
  5.6 49.1 %copy-start.1 = (bf16[8192,256]{1,0:T(8,128)(2,1)S(1)}, bf16[8192,256]{1,0:T(8,128)(2,1)}, u32[]{:S(2)}) copy-start(bf16[8192,256]{1,0:T(8,128)(2,1)} %param.9) | copy-start | bytes 12582916
  5.6 58.3 %copy-start.2 = (bf16[8192,256]{1,0:T(8,128)(2,1)S(1)}, bf16[8192,256]{1,0:T(8,128)(2,1)}, u32[]{:S(2)}) copy-start(bf16[8192,256]{1,0:T(8,128)(2,1)} %param.10) | copy-start | bytes 12582916
  8.6 20.7 %collective-permute-start.2 = (bf16[128,512]{1,0:T(8,128)(2,1)S(1)}, bf16[128,512]{1,0:T(8,128)(2,1)S(1)}, u32[]{:S(2)}, u32[]{:S(2)}) collective-permute-start(bf16[128,512]{1,0:T(8,128)(2,1)S(1)} %maximum_select_fusion), channel_id=1, source_target_pairs={{0,30},{2,0},{4,2},{6,4},{8,6},{10,8},{12,10},{14,12},{16,14},{18,... | collective-permute-start | bytes 393224 | tf_op jit(solution)/shard_map/ppermute | solution.py:12
  26.8 8.1 %collective-permute-start.1 = (bf16[128,512]{1,0:T(8,128)(2,1)S(1)}, bf16[128,512]{1,0:T(8,128)(2,1)S(1)}, u32[]{:S(2)}, u32[]{:S(2)}) collective-permute-start(bf16[128,512]{1,0:T(8,128)(2,1)S(1)} %maximum_select_fusion), channel_id=1, source_target_pairs={{0,2},{2,4},{4,6},{6,8},{8,10},{10,12},{12,14},{14,16},{16,18},{18... | collective-permute-start | bytes 393224 | tf_op jit(solution)/shard_map/ppermute | solution.py:12
  37.2 9.3 %collective-permute-start.4 = (bf16[128,512]{1,0:T(8,128)(2,1)S(1)}, bf16[128,512]{1,0:T(8,128)(2,1)S(1)}, u32[]{:S(2)}, u32[]{:S(2)}) collective-permute-start(bf16[128,512]{1,0:T(8,128)(2,1)S(1)} %collective-permute-done.2), channel_id=1, source_target_pairs={{0,30},{2,0},{4,2},{6,4},{8,6},{10,8},{12,10},{14,12},{16,14},{18,... | collective-permute-start | bytes 393224 | tf_op jit(solution)/shard_map/ppermute | solution.py:12
  41.4 10.5 %collective-permute-start.3 = (bf16[128,512]{1,0:T(8,128)(2,1)S(1)}, bf16[128,512]{1,0:T(8,128)(2,1)S(1)}, u32[]{:S(2)}, u32[]{:S(2)}) collective-permute-start(bf16[128,512]{1,0:T(8,128)(2,1)S(1)} %collective-permute-done.1), channel_id=1, source_target_pairs={{0,2},{2,4},{4,6},{6,8},{8,10},{10,12},{12,14},{14,16},{16,18},{18... | collective-permute-start | bytes 393224 | tf_op jit(solution)/shard_map/ppermute | solution.py:12
  46.5 9.5 %collective-permute-start.6 = (bf16[128,512]{1,0:T(8,128)(2,1)S(1)}, bf16[128,512]{1,0:T(8,128)(2,1)S(1)}, u32[]{:S(2)}, u32[]{:S(2)}) collective-permute-start(bf16[128,512]{1,0:T(8,128)(2,1)S(1)} %collective-permute-done.4), channel_id=1, source_target_pairs={{0,30},{2,0},{4,2},{6,4},{8,6},{10,8},{12,10},{14,12},{16,14},{18,... | collective-permute-start | bytes 393224 | tf_op jit(solution)/shard_map/ppermute | solution.py:12
  52.0 9.8 %collective-permute-start.5 = (bf16[128,512]{1,0:T(8,128)(2,1)S(1)}, bf16[128,512]{1,0:T(8,128)(2,1)S(1)}, u32[]{:S(2)}, u32[]{:S(2)}) collective-permute-start(bf16[128,512]{1,0:T(8,128)(2,1)S(1)} %collective-permute-done.3), channel_id=1, source_target_pairs={{0,2},{2,4},{4,6},{6,8},{8,10},{10,12},{12,14},{14,16},{16,18},{18... | collective-permute-start | bytes 393224 | tf_op jit(solution)/shard_map/ppermute | solution.py:12
  56.1 8.1 %collective-permute-start.8 = (bf16[128,512]{1,0:T(8,128)(2,1)S(1)}, bf16[128,512]{1,0:T(8,128)(2,1)S(1)}, u32[]{:S(2)}, u32[]{:S(2)}) collective-permute-start(bf16[128,512]{1,0:T(8,128)(2,1)S(1)} %collective-permute-done.6), channel_id=1, source_target_pairs={{0,30},{2,0},{4,2},{6,4},{8,6},{10,8},{12,10},{14,12},{16,14},{18,... | collective-permute-start | bytes 393224 | tf_op jit(solution)/shard_map/ppermute | solution.py:12
  61.8 8.1 %collective-permute-start.7 = (bf16[128,512]{1,0:T(8,128)(2,1)S(1)}, bf16[128,512]{1,0:T(8,128)(2,1)S(1)}, u32[]{:S(2)}, u32[]{:S(2)}) collective-permute-start(bf16[128,512]{1,0:T(8,128)(2,1)S(1)} %collective-permute-done.5), channel_id=1, source_target_pairs={{0,2},{2,4},{4,6},{6,8},{8,10},{10,12},{12,14},{14,16},{16,18},{18... | collective-permute-start | bytes 393224 | tf_op jit(solution)/shard_map/ppermute | solution.py:12
  64.1 8.0 %collective-permute-start.10 = (bf16[128,512]{1,0:T(8,128)(2,1)S(1)}, bf16[128,512]{1,0:T(8,128)(2,1)S(1)}, u32[]{:S(2)}, u32[]{:S(2)}) collective-permute-start(bf16[128,512]{1,0:T(8,128)(2,1)S(1)} %collective-permute-done.8), channel_id=1, source_target_pairs={{0,30},{2,0},{4,2},{6,4},{8,6},{10,8},{12,10},{14,12},{16,14},{18,... | collective-permute-start | bytes 393224 | tf_op jit(solution)/shard_map/ppermute | solution.py:12
  69.8 8.1 %collective-permute-start.9 = (bf16[128,512]{1,0:T(8,128)(2,1)S(1)}, bf16[128,512]{1,0:T(8,128)(2,1)S(1)}, u32[]{:S(2)}, u32[]{:S(2)}) collective-permute-start(bf16[128,512]{1,0:T(8,128)(2,1)S(1)} %collective-permute-done.7), channel_id=1, source_target_pairs={{0,2},{2,4},{4,6},{6,8},{8,10},{10,12},{12,14},{14,16},{16,18},{18... | collective-permute-start | bytes 393224 | tf_op jit(solution)/shard_map/ppermute | solution.py:12
  72.2 8.1 %collective-permute-start.12 = (bf16[128,512]{1,0:T(8,128)(2,1)S(1)}, bf16[128,512]{1,0:T(8,128)(2,1)S(1)}, u32[]{:S(2)}, u32[]{:S(2)}) collective-permute-start(bf16[128,512]{1,0:T(8,128)(2,1)S(1)} %collective-permute-done.10), channel_id=1, source_target_pairs={{0,30},{2,0},{4,2},{6,4},{8,6},{10,8},{12,10},{14,12},{16,14},{18,... | collective-permute-start | bytes 393224 | tf_op jit(solution)/shard_map/ppermute | solution.py:12
  77.7 33.6 %copy-start.3 = (f32[256]{0:T(256)S(1)}, f32[256]{0:T(256)}, u32[]{:S(2)}) copy-start(f32[256]{0:T(256)} %param.12) | copy-start | bytes 3076
  77.8 33.6 %copy-start.4 = (s32[128]{0:T(128)S(1)}, s32[128]{0:T(128)}, u32[]{:S(2)}) copy-start(s32[128]{0:T(128)} %param.14) | copy-start | bytes 1540
  77.9 8.4 %collective-permute-start.11 = (bf16[128,512]{1,0:T(8,128)(2,1)S(1)}, bf16[128,512]{1,0:T(8,128)(2,1)S(1)}, u32[]{:S(2)}, u32[]{:S(2)}) collective-permute-start(bf16[128,512]{1,0:T(8,128)(2,1)S(1)} %collective-permute-done.9), channel_id=1, source_target_pairs={{0,2},{2,4},{4,6},{6,8},{8,10},{10,12},{12,14},{14,16},{16,18},{18... | collective-permute-start | bytes 393224 | tf_op jit(solution)/shard_map/ppermute | solution.py:12
  80.2 8.4 %collective-permute-start.14 = (bf16[128,512]{1,0:T(8,128)(2,1)S(1)}, bf16[128,512]{1,0:T(8,128)(2,1)S(1)}, u32[]{:S(2)}, u32[]{:S(2)}) collective-permute-start(bf16[128,512]{1,0:T(8,128)(2,1)S(1)} %collective-permute-done.12), channel_id=1, source_target_pairs={{0,30},{2,0},{4,2},{6,4},{8,6},{10,8},{12,10},{14,12},{16,14},{18,... | collective-permute-start | bytes 393224 | tf_op jit(solution)/shard_map/ppermute | solution.py:12
  86.4 9.3 %collective-permute-start.13 = (bf16[128,512]{1,0:T(8,128)(2,1)S(1)}, bf16[128,512]{1,0:T(8,128)(2,1)S(1)}, u32[]{:S(2)}, u32[]{:S(2)}) collective-permute-start(bf16[128,512]{1,0:T(8,128)(2,1)S(1)} %collective-permute-done.11), channel_id=1, source_target_pairs={{0,2},{2,4},{4,6},{6,8},{8,10},{10,12},{12,14},{14,16},{16,18},{18... | collective-permute-start | bytes 393224 | tf_op jit(solution)/shard_map/ppermute | solution.py:12
  95.7 8.1 %collective-permute-start.15 = (bf16[128,512]{1,0:T(8,128)(2,1)S(1)}, bf16[128,512]{1,0:T(8,128)(2,1)S(1)}, u32[]{:S(2)}, u32[]{:S(2)}) collective-permute-start(bf16[128,512]{1,0:T(8,128)(2,1)S(1)} %collective-permute-done.13), channel_id=1, source_target_pairs={{0,2},{2,4},{4,6},{6,8},{8,10},{10,12},{12,14},{14,16},{16,18},{18... | collective-permute-start | bytes 393224 | tf_op jit(solution)/shard_map/ppermute | solution.py:12
  104.0 7.3 %collective-permute-start.16 = (bf16[3,256]{1,0:T(4,128)(2,1)S(1)}, bf16[3,256]{1,0:T(4,128)(2,1)S(1)}, u32[]{:S(2)}, u32[]{:S(2)}) collective-permute-start(bf16[3,256]{1,0:T(4,128)(2,1)S(1)} %slice.125), channel_id=1, source_target_pairs={{0,32},{32,64},{64,96},{96,128},{128,160},{160,192},{192,224},{224... | collective-permute-start | bytes 4616 | tf_op jit(solution)/shard_map/ppermute | solution.py:79
  118.9 5.9 %collective-permute-start.17 = (f32[3,256]{1,0:T(4,128)S(1)}, f32[3,256]{1,0:T(4,128)S(1)}, u32[]{:S(2)}, u32[]{:S(2)}) collective-permute-start(f32[3,256]{1,0:T(4,128)S(1)} %fusion.305), channel_id=1, source_target_pairs={{32,0},{64,32},{96,64},{128,96},{160,128},{192,160},{224,192},{256... | collective-permute-start | bytes 9224 | tf_op jit(solution)/shard_map/ppermute | solution.py:79
  127.5 7.8 %collective-permute-start.25 = (bf16[128,512]{1,0:T(8,128)(2,1)S(1)}, bf16[128,512]{1,0:T(8,128)(2,1)S(1)}, u32[]{:S(2)}, u32[]{:S(2)}) collective-permute-start(bf16[128,512]{1,0:T(8,128)(2,1)S(1)} %pad_maximum_fusion.1), channel_id=1, source_target_pairs={{0,30},{2,0},{4,2},{6,4},{8,6},{10,8},{12,10},{14,12},{16,14},{18,... | collective-permute-start | bytes 393224 | tf_op jit(solution)/shard_map/ppermute | solution.py:12
  129.5 9.3 %collective-permute-start.18 = (bf16[128,512]{1,0:T(8,128)(2,1)S(1)}, bf16[128,512]{1,0:T(8,128)(2,1)S(1)}, u32[]{:S(2)}, u32[]{:S(2)}) collective-permute-start(bf16[128,512]{1,0:T(8,128)(2,1)S(1)} %pad_maximum_fusion), channel_id=1, source_target_pairs={{0,2},{2,4},{4,6},{6,8},{8,10},{10,12},{12,14},{14,16},{16,18},{18... | collective-permute-start | bytes 393224 | tf_op jit(solution)/shard_map/ppermute | solution.py:12
  135.4 7.0 %collective-permute-start.26 = (bf16[128,512]{1,0:T(8,128)(2,1)S(1)}, bf16[128,512]{1,0:T(8,128)(2,1)S(1)}, u32[]{:S(2)}, u32[]{:S(2)}) collective-permute-start(bf16[128,512]{1,0:T(8,128)(2,1)S(1)} %add_convert_fusion.6), channel_id=1, source_target_pairs={{0,30},{2,0},{4,2},{6,4},{8,6},{10,8},{12,10},{14,12},{16,14},{18,... | collective-permute-start | bytes 393224 | tf_op jit(solution)/shard_map/ppermute | solution.py:12
  138.8 8.4 %collective-permute-start.19 = (bf16[128,512]{1,0:T(8,128)(2,1)S(1)}, bf16[128,512]{1,0:T(8,128)(2,1)S(1)}, u32[]{:S(2)}, u32[]{:S(2)}) collective-permute-start(bf16[128,512]{1,0:T(8,128)(2,1)S(1)} %add_convert_fusion.12), channel_id=1, source_target_pairs={{0,2},{2,4},{4,6},{6,8},{8,10},{10,12},{12,14},{14,16},{16,18},{18... | collective-permute-start | bytes 393224 | tf_op jit(solution)/shard_map/ppermute | solution.py:12
  142.4 7.3 %collective-permute-start.27 = (bf16[128,512]{1,0:T(8,128)(2,1)S(1)}, bf16[128,512]{1,0:T(8,128)(2,1)S(1)}, u32[]{:S(2)}, u32[]{:S(2)}) collective-permute-start(bf16[128,512]{1,0:T(8,128)(2,1)S(1)} %add_convert_fusion.5), channel_id=1, source_target_pairs={{0,30},{2,0},{4,2},{6,4},{8,6},{10,8},{12,10},{14,12},{16,14},{18,... | collective-permute-start | bytes 393224 | tf_op jit(solution)/shard_map/ppermute | solution.py:12
  147.3 8.1 %collective-permute-start.20 = (bf16[128,512]{1,0:T(8,128)(2,1)S(1)}, bf16[128,512]{1,0:T(8,128)(2,1)S(1)}, u32[]{:S(2)}, u32[]{:S(2)}) collective-permute-start(bf16[128,512]{1,0:T(8,128)(2,1)S(1)} %add_convert_fusion.11), channel_id=1, source_target_pairs={{0,2},{2,4},{4,6},{6,8},{8,10},{10,12},{12,14},{14,16},{16,18},{18... | collective-permute-start | bytes 393224 | tf_op jit(solution)/shard_map/ppermute | solution.py:12
  149.8 8.1 %collective-permute-start.28 = (bf16[128,512]{1,0:T(8,128)(2,1)S(1)}, bf16[128,512]{1,0:T(8,128)(2,1)S(1)}, u32[]{:S(2)}, u32[]{:S(2)}) collective-permute-start(bf16[128,512]{1,0:T(8,128)(2,1)S(1)} %add_convert_fusion.4), channel_id=1, source_target_pairs={{0,30},{2,0},{4,2},{6,4},{8,6},{10,8},{12,10},{14,12},{16,14},{18,... | collective-permute-start | bytes 393224 | tf_op jit(solution)/shard_map/ppermute | solution.py:12
  155.4 8.1 %collective-permute-start.21 = (bf16[128,512]{1,0:T(8,128)(2,1)S(1)}, bf16[128,512]{1,0:T(8,128)(2,1)S(1)}, u32[]{:S(2)}, u32[]{:S(2)}) collective-permute-start(bf16[128,512]{1,0:T(8,128)(2,1)S(1)} %add_convert_fusion.10), channel_id=1, source_target_pairs={{0,2},{2,4},{4,6},{6,8},{8,10},{10,12},{12,14},{14,16},{16,18},{18... | collective-permute-start | bytes 393224 | tf_op jit(solution)/shard_map/ppermute | solution.py:12
  157.9 8.1 %collective-permute-start.29 = (bf16[128,512]{1,0:T(8,128)(2,1)S(1)}, bf16[128,512]{1,0:T(8,128)(2,1)S(1)}, u32[]{:S(2)}, u32[]{:S(2)}) collective-permute-start(bf16[128,512]{1,0:T(8,128)(2,1)S(1)} %add_convert_fusion.3), channel_id=1, source_target_pairs={{0,30},{2,0},{4,2},{6,4},{8,6},{10,8},{12,10},{14,12},{16,14},{18,... | collective-permute-start | bytes 393224 | tf_op jit(solution)/shard_map/ppermute | solution.py:12
  163.5 8.1 %collective-permute-start.22 = (bf16[128,512]{1,0:T(8,128)(2,1)S(1)}, bf16[128,512]{1,0:T(8,128)(2,1)S(1)}, u32[]{:S(2)}, u32[]{:S(2)}) collective-permute-start(bf16[128,512]{1,0:T(8,128)(2,1)S(1)} %add_convert_fusion.9), channel_id=1, source_target_pairs={{0,2},{2,4},{4,6},{6,8},{8,10},{10,12},{12,14},{14,16},{16,18},{18... | collective-permute-start | bytes 393224 | tf_op jit(solution)/shard_map/ppermute | solution.py:12
  166.0 8.1 %collective-permute-start.30 = (bf16[128,512]{1,0:T(8,128)(2,1)S(1)}, bf16[128,512]{1,0:T(8,128)(2,1)S(1)}, u32[]{:S(2)}, u32[]{:S(2)}) collective-permute-start(bf16[128,512]{1,0:T(8,128)(2,1)S(1)} %add_convert_fusion.2), channel_id=1, source_target_pairs={{0,30},{2,0},{4,2},{6,4},{8,6},{10,8},{12,10},{14,12},{16,14},{18,... | collective-permute-start | bytes 393224 | tf_op jit(solution)/shard_map/ppermute | solution.py:12
  171.6 8.1 %collective-permute-start.23 = (bf16[128,512]{1,0:T(8,128)(2,1)S(1)}, bf16[128,512]{1,0:T(8,128)(2,1)S(1)}, u32[]{:S(2)}, u32[]{:S(2)}) collective-permute-start(bf16[128,512]{1,0:T(8,128)(2,1)S(1)} %add_convert_fusion.8), channel_id=1, source_target_pairs={{0,2},{2,4},{4,6},{6,8},{8,10},{10,12},{12,14},{14,16},{16,18},{18... | collective-permute-start | bytes 393224 | tf_op jit(solution)/shard_map/ppermute | solution.py:12
  174.1 9.1 %collective-permute-start.31 = (bf16[128,512]{1,0:T(8,128)(2,1)S(1)}, bf16[128,512]{1,0:T(8,128)(2,1)S(1)}, u32[]{:S(2)}, u32[]{:S(2)}) collective-permute-start(bf16[128,512]{1,0:T(8,128)(2,1)S(1)} %add_convert_fusion.1), channel_id=1, source_target_pairs={{0,30},{2,0},{4,2},{6,4},{8,6},{10,8},{12,10},{14,12},{16,14},{18,... | collective-permute-start | bytes 393224 | tf_op jit(solution)/shard_map/ppermute | solution.py:12
  179.8 9.2 %collective-permute-start.24 = (bf16[128,512]{1,0:T(8,128)(2,1)S(1)}, bf16[128,512]{1,0:T(8,128)(2,1)S(1)}, u32[]{:S(2)}, u32[]{:S(2)}) collective-permute-start(bf16[128,512]{1,0:T(8,128)(2,1)S(1)} %add_convert_fusion.7), channel_id=1, source_target_pairs={{0,2},{2,4},{4,6},{6,8},{8,10},{10,12},{12,14},{14,16},{16,18},{18... | collective-permute-start | bytes 393224 | tf_op jit(solution)/shard_map/ppermute | solution.py:12
  183.2 8.1 %collective-permute-start.32 = (bf16[128,512]{1,0:T(8,128)(2,1)S(1)}, bf16[128,512]{1,0:T(8,128)(2,1)S(1)}, u32[]{:S(2)}, u32[]{:S(2)}) collective-permute-start(bf16[128,512]{1,0:T(8,128)(2,1)S(1)} %add_convert_fusion), channel_id=1, source_target_pairs={{0,30},{2,0},{4,2},{6,4},{8,6},{10,8},{12,10},{14,12},{16,14},{18,... | collective-permute-start | bytes 393224 | tf_op jit(solution)/shard_map/ppermute | solution.py:12
  191.4 6.2 %collective-permute-start.33 = (bf16[128,256]{1,0:T(8,128)(2,1)S(1)}, bf16[128,256]{1,0:T(8,128)(2,1)S(1)}, u32[]{:S(2)}, u32[]{:S(2)}) collective-permute-start(bf16[128,256]{1,0:T(8,128)(2,1)S(1)} %select_convert_fusion), channel_id=1, source_target_pairs={{0,1},{1,0},{2,3},{3,2},{4,5},{5,4},{6,7},{7,6},{8,9},{9,8},{10,11... | collective-permute-start | bytes 196616 | tf_op jit(solution)/shard_map/ppermute | solution.py:12

commit v5 on v3

--- a/solution.py
+++ b/solution.py
@@ -96,8 +96,10 @@
     chans = w_gate.shape[1]
     taps = conv_weight.shape[0]
     found = gathered_blocks(tokens)
-    gate_acc = project(found, w_gate)
-    xin_acc = project(found, w_conv_in)
+    both = jnp.concatenate([w_gate, w_conv_in], axis=1)
+    both_acc = project(found, both)
+    gate_acc = both_acc[:, :chans]
+    xin_acc = both_acc[:, chans:]
     gate16 = lax.optimization_barrier(gate_acc.astype(jnp.bfloat16))
     zgate = gate16.astype(jnp.float32)
     xin16 = lax.optimization_barrier(xin_acc.astype(jnp.bfloat16))
@@ -128,11 +130,11 @@
     spec = (((1,), (1,)), ((), ()))
     width = 2 * tokens.shape[1]
 
+    grads16 = jnp.concatenate([dgate16, dxin16], axis=1)
+
     def block_terms(place):
-        gate_rows = lax.dynamic_slice_in_dim(w_gate, place * width, width, 0)
-        conv_rows = lax.dynamic_slice_in_dim(w_conv_in, place * width, width, 0)
-        part = lax.dot_general(dgate16, gate_rows, spec, preferred_element_type=jnp.float32)
-        part = part + lax.dot_general(dxin16, conv_rows, spec, preferred_element_type=jnp.float32)
+        rows_of_both = lax.dynamic_slice_in_dim(both, place * width, width, 0)
+        part = lax.dot_general(grads16, rows_of_both, spec, preferred_element_type=jnp.float32)
         return part.astype(jnp.bfloat16)
 
     d_tokens = scatter_features(block_terms)

time: 192 us -> 207 us (1.078)
  matrix products: 23.2 us -> 42.3 us
  waiting for transfers between devices: 33.7 us -> 24.7 us
  local copies, waits for them, and re-layouts: 0.89 us -> 6.91 us
    dot_general x32 -> x16, matrix products: 7.22 us -> 21.6 us  [block_terms(): lax.dot_general(grads16, rows_of_both, spec, preferred_element_type=jnp.f...]
    ppermute x32, waiting for transfers between devices: 28.5 us -> 18.2 us  [shifted(): lax.ppermute(block, axis, [(i, (i + distance) % size) for i in range(size)])]
    dot_general x32 -> x16, matrix products: 15.8 us -> 20.4 us  [project(): part = jnp.dot(block, rows, preferred_element_type=jnp.float32)]
    unnamed x10 -> x15, local copies, waits for them, and re-layouts: 0.03 us -> 4.59 us
    concatenate x0 -> x1, local copies, waits for them, and re-layouts: none -> 2.29 us  [on_device(): both = jnp.concatenate([w_gate, w_conv_in], axis=1)]
  transfers between devices with their start and end apart: 34 -> 34, of which waited for: 16 -> 10; matrix products, arithmetic and copies ran while one was open for 10% -> 22% of each run, Pallas kernels for 0% -> 0%
where the time goes in v5:
time: 207 us; the launch traced here: 203 us
  starting transfers between devices  126 us (61%)
  matrix products  42.3 us (20%)
  waiting for transfers between devices  24.7 us (12%)
  local copies, waits for them, and re-layouts  6.91 us (3%)
    ppermute x32, starting transfers between devices, shifted(): lax.ppermute(block, axis, [(i, (i + distance) % size) for i in range(size)])  122 us
    dot_general x16, matrix products, block_terms(): lax.dot_general(grads16, rows_of_both, spec, preferred_element_type=jnp.f...  21.6 us
    dot_general x16, matrix products, project(): part = jnp.dot(block, rows, preferred_element_type=jnp.float32)  20.4 us
    ppermute x32, waiting for transfers between devices, shifted(): lax.ppermute(block, axis, [(i, (i + distance) % size) for i in range(size)])  18.2 us
    ppermute x2, waiting for transfers between devices, passed_along(): return lax.ppermute(block, axis, route)  6.54 us
    unnamed x15, local copies, waits for them, and re-layouts  4.59 us
  transfers between devices with their start and end apart: 34, of which 10 were waited for; matrix products, arithmetic and copies ran while one was open for 22% of the time, Pallas kernels for 0%

profile of v5, /device:TPU:56, one launch (start us, length us, event | category | flops | bytes accessed | tf_op | source)
XLA Modules:
  0.0 203.4 jit_solution(4072671322073632696)
XLA Ops:
  0.7 3.7 %collective-permute-start = (bf16[128,256]{1,0:T(8,128)(2,1)}, bf16[128,256]{1,0:T(8,128)(2,1)S(1)}, u32[]{:S(2)}, u32[]{:S(2)}) collective-permute-start(bf16[128,256]{1,0:T(8,128)(2,1)} %param.8), channel_id=1, source_target_pairs={{0,1},{1,0},{2,3},{3,2},{4,5},{5,4},{6,7},{7,6},{8,9},{9,8},{10,11... | collective-permute-start | bytes 196616 | tf_op jit(solution)/shard_map/ppermute | solution.py:12
  4.3 4.5 %constant_dynamic-update-slice_fusion.1 = bf16[8192,512]{1,0:T(8,128)(2,1)} fusion(bf16[8192,256]{1,0:T(8,128)(2,1)} %param.9), kind=kLoop, calls=%fused_computation.169 | loop fusion | bytes 8388608
  8.9 2.3 %constant_dynamic-update-slice_fusion = bf16[8192,512]{1,0:T(8,128)(2,1)} fusion(bf16[8192,512]{1,0:T(8,128)(2,1)} %constant_dynamic-update-slice_fusion.1, bf16[8192,256]{1,0:T(8,128)(2,1)S(1)} %copy-done.1), kind=kLoop, calls=%fused_computation.168 | loop fusion | bytes 8388608 | tf_op jit(solution)/shard_map/concatenate | solution.py:99
  11.2 4.3 %collective-permute-start.1 = (bf16[128,512]{1,0:T(8,128)(2,1)S(1)}, bf16[128,512]{1,0:T(8,128)(2,1)S(1)}, u32[]{:S(2)}, u32[]{:S(2)}) collective-permute-start(bf16[128,512]{1,0:T(8,128)(2,1)S(1)} %maximum_select_fusion), channel_id=1, source_target_pairs={{0,2},{2,4},{4,6},{6,8},{8,10},{10,12},{12,14},{14,16},{16,18},{18... | collective-permute-start | bytes 393224 | tf_op jit(solution)/shard_map/ppermute | solution.py:12
  15.5 15.9 %collective-permute-start.2 = (bf16[128,512]{1,0:T(8,128)(2,1)S(1)}, bf16[128,512]{1,0:T(8,128)(2,1)S(1)}, u32[]{:S(2)}, u32[]{:S(2)}) collective-permute-start(bf16[128,512]{1,0:T(8,128)(2,1)S(1)} %maximum_select_fusion), channel_id=1, source_target_pairs={{0,30},{2,0},{4,2},{6,4},{8,6},{10,8},{12,10},{14,12},{16,14},{18,... | collective-permute-start | bytes 393224 | tf_op jit(solution)/shard_map/ppermute | solution.py:12
  31.4 2.5 %collective-permute-done.2 = bf16[128,512]{1,0:T(8,128)(2,1)S(1)} collective-permute-done((bf16[128,512]{1,0:T(8,128)(2,1)S(1)}, bf16[128,512]{1,0:T(8,128)(2,1)S(1)}, u32[]{:S(2)}, u32[]{:S(2)}) %collective-permute-start.2) | collective-permute-done | bytes 131104 | tf_op jit(solution)/shard_map/ppermute | solution.py:12
  33.9 5.6 %collective-permute-start.4 = (bf16[128,512]{1,0:T(8,128)(2,1)S(1)}, bf16[128,512]{1,0:T(8,128)(2,1)S(1)}, u32[]{:S(2)}, u32[]{:S(2)}) collective-permute-start(bf16[128,512]{1,0:T(8,128)(2,1)S(1)} %collective-permute-done.2), channel_id=1, source_target_pairs={{0,30},{2,0},{4,2},{6,4},{8,6},{10,8},{12,10},{14,12},{16,14},{18,... | collective-permute-start | bytes 393224 | tf_op jit(solution)/shard_map/ppermute | solution.py:12
  39.5 1.9 collective-permute-start.3
  44.0 1.3 fusion
  45.3 5.1 %collective-permute-start.6 = (bf16[128,512]{1,0:T(8,128)(2,1)S(1)}, bf16[128,512]{1,0:T(8,128)(2,1)S(1)}, u32[]{:S(2)}, u32[]{:S(2)}) collective-permute-start(bf16[128,512]{1,0:T(8,128)(2,1)S(1)} %collective-permute-done.4), channel_id=1, source_target_pairs={{0,30},{2,0},{4,2},{6,4},{8,6},{10,8},{12,10},{14,12},{16,14},{18,... | collective-permute-start | bytes 393224 | tf_op jit(solution)/shard_map/ppermute | solution.py:12
  51.7 1.9 collective-permute-start.5
  53.6 1.3 fusion.1
  54.9 5.1 %collective-permute-start.8 = (bf16[128,512]{1,0:T(8,128)(2,1)S(1)}, bf16[128,512]{1,0:T(8,128)(2,1)S(1)}, u32[]{:S(2)}, u32[]{:S(2)}) collective-permute-start(bf16[128,512]{1,0:T(8,128)(2,1)S(1)} %collective-permute-done.6), channel_id=1, source_target_pairs={{0,30},{2,0},{4,2},{6,4},{8,6},{10,8},{12,10},{14,12},{16,14},{18,... | collective-permute-start | bytes 393224 | tf_op jit(solution)/shard_map/ppermute | solution.py:12
  61.4 1.9 collective-permute-start.7
  63.3 1.3 fusion.2
  64.6 5.1 %collective-permute-start.10 = (bf16[128,512]{1,0:T(8,128)(2,1)S(1)}, bf16[128,512]{1,0:T(8,128)(2,1)S(1)}, u32[]{:S(2)}, u32[]{:S(2)}) collective-permute-start(bf16[128,512]{1,0:T(8,128)(2,1)S(1)} %collective-permute-done.8), channel_id=1, source_target_pairs={{0,30},{2,0},{4,2},{6,4},{8,6},{10,8},{12,10},{14,12},{16,14},{18,... | collective-permute-start | bytes 393224 | tf_op jit(solution)/shard_map/ppermute | solution.py:12
  71.0 1.9 collective-permute-start.9
  73.0 1.3 fusion.3
  74.3 5.1 %collective-permute-start.12 = (bf16[128,512]{1,0:T(8,128)(2,1)S(1)}, bf16[128,512]{1,0:T(8,128)(2,1)S(1)}, u32[]{:S(2)}, u32[]{:S(2)}) collective-permute-start(bf16[128,512]{1,0:T(8,128)(2,1)S(1)} %collective-permute-done.10), channel_id=1, source_target_pairs={{0,30},{2,0},{4,2},{6,4},{8,6},{10,8},{12,10},{14,12},{16,14},{18,... | collective-permute-start | bytes 393224 | tf_op jit(solution)/shard_map/ppermute | solution.py:12
  80.7 1.9 collective-permute-start.11
  82.6 1.3 fusion.4
  83.9 5.1 %collective-permute-start.14 = (bf16[128,512]{1,0:T(8,128)(2,1)S(1)}, bf16[128,512]{1,0:T(8,128)(2,1)S(1)}, u32[]{:S(2)}, u32[]{:S(2)}) collective-permute-start(bf16[128,512]{1,0:T(8,128)(2,1)S(1)} %collective-permute-done.12), channel_id=1, source_target_pairs={{0,30},{2,0},{4,2},{6,4},{8,6},{10,8},{12,10},{14,12},{16,14},{18,... | collective-permute-start | bytes 393224 | tf_op jit(solution)/shard_map/ppermute | solution.py:12
  90.4 1.9 collective-permute-start.13
  93.6 5.0 %collective-permute-done.13 = bf16[128,512]{1,0:T(8,128)(2,1)S(1)} collective-permute-done((bf16[128,512]{1,0:T(8,128)(2,1)S(1)}, bf16[128,512]{1,0:T(8,128)(2,1)S(1)}, u32[]{:S(2)}, u32[]{:S(2)}) %collective-permute-start.13) | collective-permute-done | bytes 131104 | tf_op jit(solution)/shard_map/ppermute | solution.py:12
  98.5 1.9 collective-permute-start.15
  101.7 1.3 fusion.6
  103.0 3.6 %collective-permute-done.15 = bf16[128,512]{1,0:T(8,128)(2,1)S(1)} collective-permute-done((bf16[128,512]{1,0:T(8,128)(2,1)S(1)}, bf16[128,512]{1,0:T(8,128)(2,1)S(1)}, u32[]{:S(2)}, u32[]{:S(2)}) %collective-permute-start.15) | collective-permute-done | bytes 131104 | tf_op jit(solution)/shard_map/ppermute | solution.py:12
  107.9 1.9 collective-permute-start.16
  109.9 5.3 %collective-permute-done.16 = bf16[3,256]{1,0:T(4,128)(2,1)S(1)} collective-permute-done((bf16[3,256]{1,0:T(4,128)(2,1)S(1)}, bf16[3,256]{1,0:T(4,128)(2,1)S(1)}, u32[]{:S(2)}, u32[]{:S(2)}) %collective-permute-start.16) | collective-permute-done | bytes 1568 | tf_op jit(solution)/shard_map/ppermute | solution.py:79
  116.3 1.9 collective-permute-start.17
  119.5 1.3 convolution_convert_fusion.8
  120.9 1.9 collective-permute-start.25
  122.9 1.4 convolution_convert_fusion.15
  124.2 3.9 %collective-permute-start.18 = (bf16[128,512]{1,0:T(8,128)(2,1)S(1)}, bf16[128,512]{1,0:T(8,128)(2,1)S(1)}, u32[]{:S(2)}, u32[]{:S(2)}) collective-permute-start(bf16[128,512]{1,0:T(8,128)(2,1)S(1)} %convolution_convert_fusion.15), channel_id=1, source_target_pairs={{0,2},{2,4},{4,6},{6,8},{8,10},{10,12},{12,14},{14,16},{16,18},{18... | collective-permute-start | bytes 393224 | tf_op jit(solution)/shard_map/ppermute | solution.py:12
  128.2 1.3 add_convert_fusion.6
  129.6 3.1 %collective-permute-start.26 = (bf16[128,512]{1,0:T(8,128)(2,1)S(1)}, bf16[128,512]{1,0:T(8,128)(2,1)S(1)}, u32[]{:S(2)}, u32[]{:S(2)}) collective-permute-start(bf16[128,512]{1,0:T(8,128)(2,1)S(1)} %add_convert_fusion.6), channel_id=1, source_target_pairs={{0,30},{2,0},{4,2},{6,4},{8,6},{10,8},{12,10},{14,12},{16,14},{18,... | collective-permute-start | bytes 393224 | tf_op jit(solution)/shard_map/ppermute | solution.py:12
  132.8 1.3 add_convert_fusion.12
  134.2 3.0 %collective-permute-start.19 = (bf16[128,512]{1,0:T(8,128)(2,1)S(1)}, bf16[128,512]{1,0:T(8,128)(2,1)S(1)}, u32[]{:S(2)}, u32[]{:S(2)}) collective-permute-start(bf16[128,512]{1,0:T(8,128)(2,1)S(1)} %add_convert_fusion.12), channel_id=1, source_target_pairs={{0,2},{2,4},{4,6},{6,8},{8,10},{10,12},{12,14},{14,16},{16,18},{18... | collective-permute-start | bytes 393224 | tf_op jit(solution)/shard_map/ppermute | solution.py:12
  137.6 1.3 add_convert_fusion.5
  138.9 4.0 %collective-permute-start.27 = (bf16[128,512]{1,0:T(8,128)(2,1)S(1)}, bf16[128,512]{1,0:T(8,128)(2,1)S(1)}, u32[]{:S(2)}, u32[]{:S(2)}) collective-permute-start(bf16[128,512]{1,0:T(8,128)(2,1)S(1)} %add_convert_fusion.5), channel_id=1, source_target_pairs={{0,30},{2,0},{4,2},{6,4},{8,6},{10,8},{12,10},{14,12},{16,14},{18,... | collective-permute-start | bytes 393224 | tf_op jit(solution)/shard_map/ppermute | solution.py:12
  143.4 1.3 add_convert_fusion.11
  144.7 1.9 collective-permute-start.20
  146.6 1.4 add_convert_fusion.4
  148.0 5.4 %collective-permute-start.28 = (bf16[128,512]{1,0:T(8,128)(2,1)S(1)}, bf16[128,512]{1,0:T(8,128)(2,1)S(1)}, u32[]{:S(2)}, u32[]{:S(2)}) collective-permute-start(bf16[128,512]{1,0:T(8,128)(2,1)S(1)} %add_convert_fusion.4), channel_id=1, source_target_pairs={{0,30},{2,0},{4,2},{6,4},{8,6},{10,8},{12,10},{14,12},{16,14},{18,... | collective-permute-start | bytes 393224 | tf_op jit(solution)/shard_map/ppermute | solution.py:12
  153.4 1.4 add_convert_fusion.10
  154.8 1.9 collective-permute-start.21
  156.7 1.4 add_convert_fusion.3
  158.1 5.1 %collective-permute-start.29 = (bf16[128,512]{1,0:T(8,128)(2,1)S(1)}, bf16[128,512]{1,0:T(8,128)(2,1)S(1)}, u32[]{:S(2)}, u32[]{:S(2)}) collective-permute-start(bf16[128,512]{1,0:T(8,128)(2,1)S(1)} %add_convert_fusion.3), channel_id=1, source_target_pairs={{0,30},{2,0},{4,2},{6,4},{8,6},{10,8},{12,10},{14,12},{16,14},{18,... | collective-permute-start | bytes 393224 | tf_op jit(solution)/shard_map/ppermute | solution.py:12
  163.2 1.4 add_convert_fusion.9
  164.6 1.9 collective-permute-start.22
  166.5 1.4 add_convert_fusion.2
  167.9 5.1 %collective-permute-start.30 = (bf16[128,512]{1,0:T(8,128)(2,1)S(1)}, bf16[128,512]{1,0:T(8,128)(2,1)S(1)}, u32[]{:S(2)}, u32[]{:S(2)}) collective-permute-start(bf16[128,512]{1,0:T(8,128)(2,1)S(1)} %add_convert_fusion.2), channel_id=1, source_target_pairs={{0,30},{2,0},{4,2},{6,4},{8,6},{10,8},{12,10},{14,12},{16,14},{18,... | collective-permute-start | bytes 393224 | tf_op jit(solution)/shard_map/ppermute | solution.py:12
  173.1 1.4 add_convert_fusion.8
  174.4 1.9 collective-permute-start.23
  176.4 1.4 add_convert_fusion.1
  177.7 5.1 %collective-permute-start.31 = (bf16[128,512]{1,0:T(8,128)(2,1)S(1)}, bf16[128,512]{1,0:T(8,128)(2,1)S(1)}, u32[]{:S(2)}, u32[]{:S(2)}) collective-permute-start(bf16[128,512]{1,0:T(8,128)(2,1)S(1)} %add_convert_fusion.1), channel_id=1, source_target_pairs={{0,30},{2,0},{4,2},{6,4},{8,6},{10,8},{12,10},{14,12},{16,14},{18,... | collective-permute-start | bytes 393224 | tf_op jit(solution)/shard_map/ppermute | solution.py:12
  182.9 1.4 add_convert_fusion.7
  184.2 1.9 collective-permute-start.24
  186.2 1.4 add_convert_fusion
  187.5 5.1 %collective-permute-start.32 = (bf16[128,512]{1,0:T(8,128)(2,1)S(1)}, bf16[128,512]{1,0:T(8,128)(2,1)S(1)}, u32[]{:S(2)}, u32[]{:S(2)}) collective-permute-start(bf16[128,512]{1,0:T(8,128)(2,1)S(1)} %add_convert_fusion), channel_id=1, source_target_pairs={{0,30},{2,0},{4,2},{6,4},{8,6},{10,8},{12,10},{14,12},{16,14},{18,... | collective-permute-start | bytes 393224 | tf_op jit(solution)/shard_map/ppermute | solution.py:12
  192.7 2.5 %collective-permute-done.32 = bf16[128,512]{1,0:T(8,128)(2,1)S(1)} collective-permute-done((bf16[128,512]{1,0:T(8,128)(2,1)S(1)}, bf16[128,512]{1,0:T(8,128)(2,1)S(1)}, u32[]{:S(2)}, u32[]{:S(2)}) %collective-permute-start.32) | collective-permute-done | bytes 131104 | tf_op jit(solution)/shard_map/ppermute | solution.py:12
  195.2 1.3 add_add_fusion
  196.6 2.4 %collective-permute-start.33 = (bf16[128,256]{1,0:T(8,128)(2,1)S(1)}, bf16[128,256]{1,0:T(8,128)(2,1)S(1)}, u32[]{:S(2)}, u32[]{:S(2)}) collective-permute-start(bf16[128,256]{1,0:T(8,128)(2,1)S(1)} %select_convert_fusion), channel_id=1, source_target_pairs={{0,1},{1,0},{2,3},{3,2},{4,5},{5,4},{6,7},{7,6},{8,9},{9,8},{10,11... | collective-permute-start | bytes 196616 | tf_op jit(solution)/shard_map/ppermute | solution.py:12
  199.0 3.7 %collective-permute-done.33 = bf16[128,256]{1,0:T(8,128)(2,1)S(1)} collective-permute-done((bf16[128,256]{1,0:T(8,128)(2,1)S(1)}, bf16[128,256]{1,0:T(8,128)(2,1)S(1)}, u32[]{:S(2)}, u32[]{:S(2)}) %collective-permute-start.33) | collective-permute-done | bytes 65568 | tf_op jit(solution)/shard_map/ppermute | solution.py:12
  (68 shorter events, 16.8 us)
Async XLA Ops:
  0.6 114.6 %copy-start = (bf16[10,256]{1,0:T(8,128)(2,1)S(1)}, bf16[10,256]{1,0:T(8,128)(2,1)}, u32[]{:S(2)}) copy-start(bf16[10,256]{1,0:T(8,128)(2,1)} %param.13) | copy-start | bytes 15364
  0.6 10.5 %copy-start.2 = (bf16[128,256]{1,0:T(8,128)(2,1)S(1)}, bf16[128,256]{1,0:T(8,128)(2,1)}, u32[]{:S(2)}) copy-start(bf16[128,256]{1,0:T(8,128)(2,1)} %param.8) | copy-start | bytes 196612
  0.7 8.2 %copy-start.1 = (bf16[8192,256]{1,0:T(8,128)(2,1)S(1)}, bf16[8192,256]{1,0:T(8,128)(2,1)}, u32[]{:S(2)}) copy-start(bf16[8192,256]{1,0:T(8,128)(2,1)} %param.10) | copy-start | bytes 12582916
  0.7 30.7 %copy-start.3 = (f32[4,256]{1,0:T(4,128)S(1)}, f32[4,256]{1,0:T(4,128)}, u32[]{:S(2)}) copy-start(f32[4,256]{1,0:T(4,128)} %param.11) | copy-start | bytes 12292
  0.7 10.5 %collective-permute-start = (bf16[128,256]{1,0:T(8,128)(2,1)}, bf16[128,256]{1,0:T(8,128)(2,1)S(1)}, u32[]{:S(2)}, u32[]{:S(2)}) collective-permute-start(bf16[128,256]{1,0:T(8,128)(2,1)} %param.8), channel_id=1, source_target_pairs={{0,1},{1,0},{2,3},{3,2},{4,5},{5,4},{6,7},{7,6},{8,9},{9,8},{10,11... | collective-permute-start | bytes 196616 | tf_op jit(solution)/shard_map/ppermute | solution.py:12
  11.2 28.2 %collective-permute-start.1 = (bf16[128,512]{1,0:T(8,128)(2,1)S(1)}, bf16[128,512]{1,0:T(8,128)(2,1)S(1)}, u32[]{:S(2)}, u32[]{:S(2)}) collective-permute-start(bf16[128,512]{1,0:T(8,128)(2,1)S(1)} %maximum_select_fusion), channel_id=1, source_target_pairs={{0,2},{2,4},{4,6},{6,8},{8,10},{10,12},{12,14},{14,16},{16,18},{18... | collective-permute-start | bytes 393224 | tf_op jit(solution)/shard_map/ppermute | solution.py:12
  15.5 18.4 %collective-permute-start.2 = (bf16[128,512]{1,0:T(8,128)(2,1)S(1)}, bf16[128,512]{1,0:T(8,128)(2,1)S(1)}, u32[]{:S(2)}, u32[]{:S(2)}) collective-permute-start(bf16[128,512]{1,0:T(8,128)(2,1)S(1)} %maximum_select_fusion), channel_id=1, source_target_pairs={{0,30},{2,0},{4,2},{6,4},{8,6},{10,8},{12,10},{14,12},{16,14},{18,... | collective-permute-start | bytes 393224 | tf_op jit(solution)/shard_map/ppermute | solution.py:12
  33.9 11.4 %collective-permute-start.4 = (bf16[128,512]{1,0:T(8,128)(2,1)S(1)}, bf16[128,512]{1,0:T(8,128)(2,1)S(1)}, u32[]{:S(2)}, u32[]{:S(2)}) collective-permute-start(bf16[128,512]{1,0:T(8,128)(2,1)S(1)} %collective-permute-done.2), channel_id=1, source_target_pairs={{0,30},{2,0},{4,2},{6,4},{8,6},{10,8},{12,10},{14,12},{16,14},{18,... | collective-permute-start | bytes 393224 | tf_op jit(solution)/shard_map/ppermute | solution.py:12
  39.5 12.3 %collective-permute-start.3 = (bf16[128,512]{1,0:T(8,128)(2,1)S(1)}, bf16[128,512]{1,0:T(8,128)(2,1)S(1)}, u32[]{:S(2)}, u32[]{:S(2)}) collective-permute-start(bf16[128,512]{1,0:T(8,128)(2,1)S(1)} %collective-permute-done.1), channel_id=1, source_target_pairs={{0,2},{2,4},{4,6},{6,8},{8,10},{10,12},{12,14},{14,16},{16,18},{18... | collective-permute-start | bytes 393224 | tf_op jit(solution)/shard_map/ppermute | solution.py:12
  43.9 65.9 %copy-start.5 = (s32[128]{0:T(128)S(1)}, s32[128]{0:T(128)}, u32[]{:S(2)}) copy-start(s32[128]{0:T(128)} %param.15) | copy-start | bytes 1540
  44.0 71.3 %copy-start.4 = (f32[256]{0:T(256)S(1)}, f32[256]{0:T(256)}, u32[]{:S(2)}) copy-start(f32[256]{0:T(256)} %param.12) | copy-start | bytes 3076
  44.0 71.3 %copy-start.6 = (s32[128]{0:T(128)S(1)}, s32[128]{0:T(128)}, u32[]{:S(2)}) copy-start(s32[128]{0:T(128)} %param.14) | copy-start | bytes 1540
  45.3 9.7 %collective-permute-start.6 = (bf16[128,512]{1,0:T(8,128)(2,1)S(1)}, bf16[128,512]{1,0:T(8,128)(2,1)S(1)}, u32[]{:S(2)}, u32[]{:S(2)}) collective-permute-start(bf16[128,512]{1,0:T(8,128)(2,1)S(1)} %collective-permute-done.4), channel_id=1, source_target_pairs={{0,30},{2,0},{4,2},{6,4},{8,6},{10,8},{12,10},{14,12},{16,14},{18,... | collective-permute-start | bytes 393224 | tf_op jit(solution)/shard_map/ppermute | solution.py:12
  51.7 9.7 %collective-permute-start.5 = (bf16[128,512]{1,0:T(8,128)(2,1)S(1)}, bf16[128,512]{1,0:T(8,128)(2,1)S(1)}, u32[]{:S(2)}, u32[]{:S(2)}) collective-permute-start(bf16[128,512]{1,0:T(8,128)(2,1)S(1)} %collective-permute-done.3), channel_id=1, source_target_pairs={{0,2},{2,4},{4,6},{6,8},{8,10},{10,12},{12,14},{14,16},{16,18},{18... | collective-permute-start | bytes 393224 | tf_op jit(solution)/shard_map/ppermute | solution.py:12
  54.9 9.7 %collective-permute-start.8 = (bf16[128,512]{1,0:T(8,128)(2,1)S(1)}, bf16[128,512]{1,0:T(8,128)(2,1)S(1)}, u32[]{:S(2)}, u32[]{:S(2)}) collective-permute-start(bf16[128,512]{1,0:T(8,128)(2,1)S(1)} %collective-permute-done.6), channel_id=1, source_target_pairs={{0,30},{2,0},{4,2},{6,4},{8,6},{10,8},{12,10},{14,12},{16,14},{18,... | collective-permute-start | bytes 393224 | tf_op jit(solution)/shard_map/ppermute | solution.py:12
  61.4 9.7 %collective-permute-start.7 = (bf16[128,512]{1,0:T(8,128)(2,1)S(1)}, bf16[128,512]{1,0:T(8,128)(2,1)S(1)}, u32[]{:S(2)}, u32[]{:S(2)}) collective-permute-start(bf16[128,512]{1,0:T(8,128)(2,1)S(1)} %collective-permute-done.5), channel_id=1, source_target_pairs={{0,2},{2,4},{4,6},{6,8},{8,10},{10,12},{12,14},{14,16},{16,18},{18... | collective-permute-start | bytes 393224 | tf_op jit(solution)/shard_map/ppermute | solution.py:12
  64.6 9.7 %collective-permute-start.10 = (bf16[128,512]{1,0:T(8,128)(2,1)S(1)}, bf16[128,512]{1,0:T(8,128)(2,1)S(1)}, u32[]{:S(2)}, u32[]{:S(2)}) collective-permute-start(bf16[128,512]{1,0:T(8,128)(2,1)S(1)} %collective-permute-done.8), channel_id=1, source_target_pairs={{0,30},{2,0},{4,2},{6,4},{8,6},{10,8},{12,10},{14,12},{16,14},{18,... | collective-permute-start | bytes 393224 | tf_op jit(solution)/shard_map/ppermute | solution.py:12
  71.0 9.7 %collective-permute-start.9 = (bf16[128,512]{1,0:T(8,128)(2,1)S(1)}, bf16[128,512]{1,0:T(8,128)(2,1)S(1)}, u32[]{:S(2)}, u32[]{:S(2)}) collective-permute-start(bf16[128,512]{1,0:T(8,128)(2,1)S(1)} %collective-permute-done.7), channel_id=1, source_target_pairs={{0,2},{2,4},{4,6},{6,8},{8,10},{10,12},{12,14},{14,16},{16,18},{18... | collective-permute-start | bytes 393224 | tf_op jit(solution)/shard_map/ppermute | solution.py:12
  74.3 9.7 %collective-permute-start.12 = (bf16[128,512]{1,0:T(8,128)(2,1)S(1)}, bf16[128,512]{1,0:T(8,128)(2,1)S(1)}, u32[]{:S(2)}, u32[]{:S(2)}) collective-permute-start(bf16[128,512]{1,0:T(8,128)(2,1)S(1)} %collective-permute-done.10), channel_id=1, source_target_pairs={{0,30},{2,0},{4,2},{6,4},{8,6},{10,8},{12,10},{14,12},{16,14},{18,... | collective-permute-start | bytes 393224 | tf_op jit(solution)/shard_map/ppermute | solution.py:12
  80.7 9.7 %collective-permute-start.11 = (bf16[128,512]{1,0:T(8,128)(2,1)S(1)}, bf16[128,512]{1,0:T(8,128)(2,1)S(1)}, u32[]{:S(2)}, u32[]{:S(2)}) collective-permute-start(bf16[128,512]{1,0:T(8,128)(2,1)S(1)} %collective-permute-done.9), channel_id=1, source_target_pairs={{0,2},{2,4},{4,6},{6,8},{8,10},{10,12},{12,14},{14,16},{16,18},{18... | collective-permute-start | bytes 393224 | tf_op jit(solution)/shard_map/ppermute | solution.py:12
  83.9 16.5 %collective-permute-start.14 = (bf16[128,512]{1,0:T(8,128)(2,1)S(1)}, bf16[128,512]{1,0:T(8,128)(2,1)S(1)}, u32[]{:S(2)}, u32[]{:S(2)}) collective-permute-start(bf16[128,512]{1,0:T(8,128)(2,1)S(1)} %collective-permute-done.12), channel_id=1, source_target_pairs={{0,30},{2,0},{4,2},{6,4},{8,6},{10,8},{12,10},{14,12},{16,14},{18,... | collective-permute-start | bytes 393224 | tf_op jit(solution)/shard_map/ppermute | solution.py:12
  90.4 8.2 %collective-permute-start.13 = (bf16[128,512]{1,0:T(8,128)(2,1)S(1)}, bf16[128,512]{1,0:T(8,128)(2,1)S(1)}, u32[]{:S(2)}, u32[]{:S(2)}) collective-permute-start(bf16[128,512]{1,0:T(8,128)(2,1)S(1)} %collective-permute-done.11), channel_id=1, source_target_pairs={{0,2},{2,4},{4,6},{6,8},{8,10},{10,12},{12,14},{14,16},{16,18},{18... | collective-permute-start | bytes 393224 | tf_op jit(solution)/shard_map/ppermute | solution.py:12
  98.5 8.1 %collective-permute-start.15 = (bf16[128,512]{1,0:T(8,128)(2,1)S(1)}, bf16[128,512]{1,0:T(8,128)(2,1)S(1)}, u32[]{:S(2)}, u32[]{:S(2)}) collective-permute-start(bf16[128,512]{1,0:T(8,128)(2,1)S(1)} %collective-permute-done.13), channel_id=1, source_target_pairs={{0,2},{2,4},{4,6},{6,8},{8,10},{10,12},{12,14},{14,16},{16,18},{18... | collective-permute-start | bytes 393224 | tf_op jit(solution)/shard_map/ppermute | solution.py:12
  107.9 7.3 %collective-permute-start.16 = (bf16[3,256]{1,0:T(4,128)(2,1)S(1)}, bf16[3,256]{1,0:T(4,128)(2,1)S(1)}, u32[]{:S(2)}, u32[]{:S(2)}) collective-permute-start(bf16[3,256]{1,0:T(4,128)(2,1)S(1)} %slice.98), channel_id=1, source_target_pairs={{0,32},{32,64},{64,96},{96,128},{128,160},{160,192},{192,224},{224... | collective-permute-start | bytes 4616 | tf_op jit(solution)/shard_map/ppermute | solution.py:79
  116.3 3.2 %collective-permute-start.17 = (f32[3,256]{1,0:T(4,128)S(1)}, f32[3,256]{1,0:T(4,128)S(1)}, u32[]{:S(2)}, u32[]{:S(2)}) collective-permute-start(f32[3,256]{1,0:T(4,128)S(1)} %fusion.139), channel_id=1, source_target_pairs={{32,0},{64,32},{96,64},{128,96},{160,128},{192,160},{224,192},{256... | collective-permute-start | bytes 9224 | tf_op jit(solution)/shard_map/ppermute | solution.py:79
  120.9 7.3 %collective-permute-start.25 = (bf16[128,512]{1,0:T(8,128)(2,1)S(1)}, bf16[128,512]{1,0:T(8,128)(2,1)S(1)}, u32[]{:S(2)}, u32[]{:S(2)}) collective-permute-start(bf16[128,512]{1,0:T(8,128)(2,1)S(1)} %convolution_convert_fusion.8), channel_id=1, source_target_pairs={{0,30},{2,0},{4,2},{6,4},{8,6},{10,8},{12,10},{14,12},{16,14},{18,... | collective-permute-start | bytes 393224 | tf_op jit(solution)/shard_map/ppermute | solution.py:12
  124.2 8.6 %collective-permute-start.18 = (bf16[128,512]{1,0:T(8,128)(2,1)S(1)}, bf16[128,512]{1,0:T(8,128)(2,1)S(1)}, u32[]{:S(2)}, u32[]{:S(2)}) collective-permute-start(bf16[128,512]{1,0:T(8,128)(2,1)S(1)} %convolution_convert_fusion.15), channel_id=1, source_target_pairs={{0,2},{2,4},{4,6},{6,8},{8,10},{10,12},{12,14},{14,16},{16,18},{18... | collective-permute-start | bytes 393224 | tf_op jit(solution)/shard_map/ppermute | solution.py:12
  129.6 8.0 %collective-permute-start.26 = (bf16[128,512]{1,0:T(8,128)(2,1)S(1)}, bf16[128,512]{1,0:T(8,128)(2,1)S(1)}, u32[]{:S(2)}, u32[]{:S(2)}) collective-permute-start(bf16[128,512]{1,0:T(8,128)(2,1)S(1)} %add_convert_fusion.6), channel_id=1, source_target_pairs={{0,30},{2,0},{4,2},{6,4},{8,6},{10,8},{12,10},{14,12},{16,14},{18,... | collective-permute-start | bytes 393224 | tf_op jit(solution)/shard_map/ppermute | solution.py:12
  134.2 9.2 %collective-permute-start.19 = (bf16[128,512]{1,0:T(8,128)(2,1)S(1)}, bf16[128,512]{1,0:T(8,128)(2,1)S(1)}, u32[]{:S(2)}, u32[]{:S(2)}) collective-permute-start(bf16[128,512]{1,0:T(8,128)(2,1)S(1)} %add_convert_fusion.12), channel_id=1, source_target_pairs={{0,2},{2,4},{4,6},{6,8},{8,10},{10,12},{12,14},{14,16},{16,18},{18... | collective-permute-start | bytes 393224 | tf_op jit(solution)/shard_map/ppermute | solution.py:12
  138.9 7.7 %collective-permute-start.27 = (bf16[128,512]{1,0:T(8,128)(2,1)S(1)}, bf16[128,512]{1,0:T(8,128)(2,1)S(1)}, u32[]{:S(2)}, u32[]{:S(2)}) collective-permute-start(bf16[128,512]{1,0:T(8,128)(2,1)S(1)} %add_convert_fusion.5), channel_id=1, source_target_pairs={{0,30},{2,0},{4,2},{6,4},{8,6},{10,8},{12,10},{14,12},{16,14},{18,... | collective-permute-start | bytes 393224 | tf_op jit(solution)/shard_map/ppermute | solution.py:12
  144.7 8.7 %collective-permute-start.20 = (bf16[128,512]{1,0:T(8,128)(2,1)S(1)}, bf16[128,512]{1,0:T(8,128)(2,1)S(1)}, u32[]{:S(2)}, u32[]{:S(2)}) collective-permute-start(bf16[128,512]{1,0:T(8,128)(2,1)S(1)} %add_convert_fusion.11), channel_id=1, source_target_pairs={{0,2},{2,4},{4,6},{6,8},{8,10},{10,12},{12,14},{14,16},{16,18},{18... | collective-permute-start | bytes 393224 | tf_op jit(solution)/shard_map/ppermute | solution.py:12
  148.0 8.7 %collective-permute-start.28 = (bf16[128,512]{1,0:T(8,128)(2,1)S(1)}, bf16[128,512]{1,0:T(8,128)(2,1)S(1)}, u32[]{:S(2)}, u32[]{:S(2)}) collective-permute-start(bf16[128,512]{1,0:T(8,128)(2,1)S(1)} %add_convert_fusion.4), channel_id=1, source_target_pairs={{0,30},{2,0},{4,2},{6,4},{8,6},{10,8},{12,10},{14,12},{16,14},{18,... | collective-permute-start | bytes 393224 | tf_op jit(solution)/shard_map/ppermute | solution.py:12
  154.8 8.4 %collective-permute-start.21 = (bf16[128,512]{1,0:T(8,128)(2,1)S(1)}, bf16[128,512]{1,0:T(8,128)(2,1)S(1)}, u32[]{:S(2)}, u32[]{:S(2)}) collective-permute-start(bf16[128,512]{1,0:T(8,128)(2,1)S(1)} %add_convert_fusion.10), channel_id=1, source_target_pairs={{0,2},{2,4},{4,6},{6,8},{8,10},{10,12},{12,14},{14,16},{16,18},{18... | collective-permute-start | bytes 393224 | tf_op jit(solution)/shard_map/ppermute | solution.py:12
  158.1 8.4 %collective-permute-start.29 = (bf16[128,512]{1,0:T(8,128)(2,1)S(1)}, bf16[128,512]{1,0:T(8,128)(2,1)S(1)}, u32[]{:S(2)}, u32[]{:S(2)}) collective-permute-start(bf16[128,512]{1,0:T(8,128)(2,1)S(1)} %add_convert_fusion.3), channel_id=1, source_target_pairs={{0,30},{2,0},{4,2},{6,4},{8,6},{10,8},{12,10},{14,12},{16,14},{18,... | collective-permute-start | bytes 393224 | tf_op jit(solution)/shard_map/ppermute | solution.py:12
  164.6 8.4 %collective-permute-start.22 = (bf16[128,512]{1,0:T(8,128)(2,1)S(1)}, bf16[128,512]{1,0:T(8,128)(2,1)S(1)}, u32[]{:S(2)}, u32[]{:S(2)}) collective-permute-start(bf16[128,512]{1,0:T(8,128)(2,1)S(1)} %add_convert_fusion.9), channel_id=1, source_target_pairs={{0,2},{2,4},{4,6},{6,8},{8,10},{10,12},{12,14},{14,16},{16,18},{18... | collective-permute-start | bytes 393224 | tf_op jit(solution)/shard_map/ppermute | solution.py:12
  167.9 8.4 %collective-permute-start.30 = (bf16[128,512]{1,0:T(8,128)(2,1)S(1)}, bf16[128,512]{1,0:T(8,128)(2,1)S(1)}, u32[]{:S(2)}, u32[]{:S(2)}) collective-permute-start(bf16[128,512]{1,0:T(8,128)(2,1)S(1)} %add_convert_fusion.2), channel_id=1, source_target_pairs={{0,30},{2,0},{4,2},{6,4},{8,6},{10,8},{12,10},{14,12},{16,14},{18,... | collective-permute-start | bytes 393224 | tf_op jit(solution)/shard_map/ppermute | solution.py:12
  174.4 8.4 %collective-permute-start.23 = (bf16[128,512]{1,0:T(8,128)(2,1)S(1)}, bf16[128,512]{1,0:T(8,128)(2,1)S(1)}, u32[]{:S(2)}, u32[]{:S(2)}) collective-permute-start(bf16[128,512]{1,0:T(8,128)(2,1)S(1)} %add_convert_fusion.8), channel_id=1, source_target_pairs={{0,2},{2,4},{4,6},{6,8},{8,10},{10,12},{12,14},{14,16},{16,18},{18... | collective-permute-start | bytes 393224 | tf_op jit(solution)/shard_map/ppermute | solution.py:12
  177.7 8.4 %collective-permute-start.31 = (bf16[128,512]{1,0:T(8,128)(2,1)S(1)}, bf16[128,512]{1,0:T(8,128)(2,1)S(1)}, u32[]{:S(2)}, u32[]{:S(2)}) collective-permute-start(bf16[128,512]{1,0:T(8,128)(2,1)S(1)} %add_convert_fusion.1), channel_id=1, source_target_pairs={{0,30},{2,0},{4,2},{6,4},{8,6},{10,8},{12,10},{14,12},{16,14},{18,... | collective-permute-start | bytes 393224 | tf_op jit(solution)/shard_map/ppermute | solution.py:12
  184.2 8.5 %collective-permute-start.24 = (bf16[128,512]{1,0:T(8,128)(2,1)S(1)}, bf16[128,512]{1,0:T(8,128)(2,1)S(1)}, u32[]{:S(2)}, u32[]{:S(2)}) collective-permute-start(bf16[128,512]{1,0:T(8,128)(2,1)S(1)} %add_convert_fusion.7), channel_id=1, source_target_pairs={{0,2},{2,4},{4,6},{6,8},{8,10},{10,12},{12,14},{14,16},{16,18},{18... | collective-permute-start | bytes 393224 | tf_op jit(solution)/shard_map/ppermute | solution.py:12
  187.5 7.6 %collective-permute-start.32 = (bf16[128,512]{1,0:T(8,128)(2,1)S(1)}, bf16[128,512]{1,0:T(8,128)(2,1)S(1)}, u32[]{:S(2)}, u32[]{:S(2)}) collective-permute-start(bf16[128,512]{1,0:T(8,128)(2,1)S(1)} %add_convert_fusion), channel_id=1, source_target_pairs={{0,30},{2,0},{4,2},{6,4},{8,6},{10,8},{12,10},{14,12},{16,14},{18,... | collective-permute-start | bytes 393224 | tf_op jit(solution)/shard_map/ppermute | solution.py:12
  196.6 6.2 %collective-permute-start.33 = (bf16[128,256]{1,0:T(8,128)(2,1)S(1)}, bf16[128,256]{1,0:T(8,128)(2,1)S(1)}, u32[]{:S(2)}, u32[]{:S(2)}) collective-permute-start(bf16[128,256]{1,0:T(8,128)(2,1)S(1)} %select_convert_fusion), channel_id=1, source_target_pairs={{0,1},{1,0},{2,3},{3,2},{4,5},{5,4},{6,7},{7,6},{8,9},{9,8},{10,11... | collective-permute-start | bytes 196616 | tf_op jit(solution)/shard_map/ppermute | solution.py:12

commit v6 on v3

--- a/solution.py
+++ b/solution.py
@@ -17,30 +17,24 @@
     return jnp.where(first, jnp.concatenate([mine, other], 1), jnp.concatenate([other, mine], 1))
 
 
-def gathered_blocks(tokens):
+def gather_features(tokens):
+    rows = tokens.shape[0]
     pair = halves_in_order(tokens, shifted(tokens, "tx", 1))
     count = lax.axis_size("tz")
-    here = lax.axis_index("tz")
-    found = [(pair, here)]
+    blocks = [pair] * count
     ahead = pair
     behind = pair
     for step in range(1, count // 2 + 1):
         ahead = shifted(ahead, "tz", 1)
-        found.append((ahead, (here - step) % count))
+        blocks[-step % count] = ahead
         if step < count - step:
             behind = shifted(behind, "tz", -1)
-            found.append((behind, (here + step) % count))
-    return found
-
-
-def project(found, weights):
-    width = found[0][0].shape[1]
-    total = None
-    for block, place in found:
-        rows = lax.dynamic_slice_in_dim(weights, place * width, width, 0)
-        part = jnp.dot(block, rows, preferred_element_type=jnp.float32)
-        total = part if total is None else total + part
-    return total
+            blocks[step] = behind
+    stacked = jnp.stack(blocks, 0)
+    doubled = jnp.concatenate([stacked, stacked], 0)
+    start = (count - lax.axis_index("tz")) % count
+    ordered = lax.dynamic_slice_in_dim(doubled, start, count, 0)
+    return ordered.transpose(1, 0, 2).reshape(rows, -1)
 
 
 def scatter_features(make_block):
@@ -95,9 +89,9 @@
     rows = tokens.shape[0]
     chans = w_gate.shape[1]
     taps = conv_weight.shape[0]
-    found = gathered_blocks(tokens)
-    gate_acc = project(found, w_gate)
-    xin_acc = project(found, w_conv_in)
+    piece = gather_features(tokens)
+    gate_acc = jnp.dot(piece, w_gate, preferred_element_type=jnp.float32)
+    xin_acc = jnp.dot(piece, w_conv_in, preferred_element_type=jnp.float32)
     gate16 = lax.optimization_barrier(gate_acc.astype(jnp.bfloat16))
     zgate = gate16.astype(jnp.float32)
     xin16 = lax.optimization_barrier(xin_acc.astype(jnp.bfloat16))

time: 192 us -> 184 us (0.958)
  matrix products: 23.2 us -> 9.49 us
  starting transfers between devices: 126 us -> 131 us
  local copies, waits for them, and re-layouts: 0.89 us -> 4.14 us
    dot_general x32 -> x2, matrix products: 15.8 us -> 1.98 us  [the longest x1 0.99 us: on_device(): gate_acc = jnp.dot(piece, w_gate, preferred_element_type=jnp.float32)]
    ppermute x32, starting transfers between devices: 122 us -> 127 us  [shifted(): lax.ppermute(block, axis, [(i, (i + distance) % size) for i in range(size)])]
    unnamed x10 -> x40, local copies, waits for them, and re-layouts: 0.03 us -> 3.07 us
  transfers between devices with their start and end apart: 34 -> 34, of which waited for: 16 -> 19; matrix products, arithmetic and copies ran while one was open for 10% -> 6% of each run, Pallas kernels for 0% -> 0%
where the time goes in v6:
time: 184 us; the launch traced here: 182 us
  starting transfers between devices  131 us (71%)
  waiting for transfers between devices  32.9 us (18%)
  matrix products  9.49 us (5%)
  local copies, waits for them, and re-layouts  4.14 us (2%)
  other arithmetic  2.26 us (1%)
    ppermute x32, starting transfers between devices, shifted(): lax.ppermute(block, axis, [(i, (i + distance) % size) for i in range(size)])  127 us
    ppermute x32, waiting for transfers between devices, shifted(): lax.ppermute(block, axis, [(i, (i + distance) % size) for i in range(size)])  28.6 us
    ppermute x2, waiting for transfers between devices, passed_along(): return lax.ppermute(block, axis, route)  4.38 us
    ppermute x2, starting transfers between devices, passed_along(): return lax.ppermute(block, axis, route)  3.84 us
  transfers between devices with their start and end apart: 34, of which 19 were waited for; matrix products, arithmetic and copies ran while one was open for 6% of the time, Pallas kernels for 0%

profile of v6, /device:TPU:56, one launch (start us, length us, event | category | flops | bytes accessed | tf_op | source)
XLA Modules:
  0.0 181.8 jit_solution(2581801327038152367)
XLA Ops:
  0.6 1.0 copy.10
  1.6 3.4 %collective-permute-start = (bf16[128,256]{0,1:T(8,128)(2,1)S(1)}, bf16[128,256]{0,1:T(8,128)(2,1)S(1)}, u32[]{:S(2)}, u32[]{:S(2)}) collective-permute-start(bf16[128,256]{0,1:T(8,128)(2,1)S(1)} %copy.10), channel_id=1, source_target_pairs={{0,1},{1,0},{2,3},{3,2},{4,5},{5,4},{6,7},{7,6},{8,9},{9,8},{10,11... | collective-permute-start | bytes 196616 | tf_op jit(solution)/shard_map/ppermute | solution.py:12
  5.0 0.8 fusion.159
  5.9 1.9 %collective-permute-done = bf16[128,256]{0,1:T(8,128)(2,1)S(1)} collective-permute-done((bf16[128,256]{0,1:T(8,128)(2,1)S(1)}, bf16[128,256]{0,1:T(8,128)(2,1)S(1)}, u32[]{:S(2)}, u32[]{:S(2)}) %collective-permute-start) | collective-permute-done | bytes 65568 | tf_op jit(solution)/shard_map/ppermute | solution.py:12
  7.8 18.2 %collective-permute-start.1 = (bf16[128,512]{0,1:T(8,128)(2,1)S(1)}, bf16[128,512]{0,1:T(8,128)(2,1)S(1)}, u32[]{:S(2)}, u32[]{:S(2)}) collective-permute-start(bf16[128,512]{0,1:T(8,128)(2,1)S(1)} %maximum_select_fusion.1), channel_id=1, source_target_pairs={{0,30},{2,0},{4,2},{6,4},{8,6},{10,8},{12,10},{14,12},{16,14},{18,... | collective-permute-start | bytes 393224 | tf_op jit(solution)/shard_map/ppermute | solution.py:12
  26.0 1.9 %collective-permute-start.8 = (bf16[128,512]{0,1:T(8,128)(2,1)S(1)}, bf16[128,512]{0,1:T(8,128)(2,1)S(1)}, u32[]{:S(2)}, u32[]{:S(2)}) collective-permute-start(bf16[128,512]{0,1:T(8,128)(2,1)S(1)} %maximum_select_fusion.1), channel_id=1, source_target_pairs={{0,2},{2,4},{4,6},{6,8},{8,10},{10,12},{12,14},{14,16},{16,18},{18... | collective-permute-start | bytes 393224 | tf_op jit(solution)/shard_map/ppermute | solution.py:12
  28.2 0.7 convert_element_type.215
  28.9 5.2 %collective-permute-start.2 = (bf16[128,512]{0,1:T(8,128)(2,1)S(1)}, bf16[128,512]{0,1:T(8,128)(2,1)S(1)}, u32[]{:S(2)}, u32[]{:S(2)}) collective-permute-start(bf16[128,512]{0,1:T(8,128)(2,1)S(1)} %collective-permute-done.1), channel_id=1, source_target_pairs={{0,30},{2,0},{4,2},{6,4},{8,6},{10,8},{12,10},{14,12},{16,14},{18,... | collective-permute-start | bytes 393224 | tf_op jit(solution)/shard_map/ppermute | solution.py:12
  34.1 1.9 %collective-permute-start.9 = (bf16[128,512]{0,1:T(8,128)(2,1)S(1)}, bf16[128,512]{0,1:T(8,128)(2,1)S(1)}, u32[]{:S(2)}, u32[]{:S(2)}) collective-permute-start(bf16[128,512]{0,1:T(8,128)(2,1)S(1)} %collective-permute-done.8), channel_id=1, source_target_pairs={{0,2},{2,4},{4,6},{6,8},{8,10},{10,12},{12,14},{14,16},{16,18},{18... | collective-permute-start | bytes 393224 | tf_op jit(solution)/shard_map/ppermute | solution.py:12
  36.1 0.5 collective-permute-done.2
  36.6 5.6 %collective-permute-start.3 = (bf16[128,512]{0,1:T(8,128)(2,1)S(1)}, bf16[128,512]{0,1:T(8,128)(2,1)S(1)}, u32[]{:S(2)}, u32[]{:S(2)}) collective-permute-start(bf16[128,512]{0,1:T(8,128)(2,1)S(1)} %collective-permute-done.2), channel_id=1, source_target_pairs={{0,30},{2,0},{4,2},{6,4},{8,6},{10,8},{12,10},{14,12},{16,14},{18,... | collective-permute-start | bytes 393224 | tf_op jit(solution)/shard_map/ppermute | solution.py:12
  42.2 1.9 %collective-permute-start.10 = (bf16[128,512]{0,1:T(8,128)(2,1)S(1)}, bf16[128,512]{0,1:T(8,128)(2,1)S(1)}, u32[]{:S(2)}, u32[]{:S(2)}) collective-permute-start(bf16[128,512]{0,1:T(8,128)(2,1)S(1)} %collective-permute-done.9), channel_id=1, source_target_pairs={{0,2},{2,4},{4,6},{6,8},{8,10},{10,12},{12,14},{14,16},{16,18},{18... | collective-permute-start | bytes 393224 | tf_op jit(solution)/shard_map/ppermute | solution.py:12
  44.1 0.5 collective-permute-done.3
  44.7 5.6 %collective-permute-start.4 = (bf16[128,512]{0,1:T(8,128)(2,1)S(1)}, bf16[128,512]{0,1:T(8,128)(2,1)S(1)}, u32[]{:S(2)}, u32[]{:S(2)}) collective-permute-start(bf16[128,512]{0,1:T(8,128)(2,1)S(1)} %collective-permute-done.3), channel_id=1, source_target_pairs={{0,30},{2,0},{4,2},{6,4},{8,6},{10,8},{12,10},{14,12},{16,14},{18,... | collective-permute-start | bytes 393224 | tf_op jit(solution)/shard_map/ppermute | solution.py:12
  50.2 1.9 %collective-permute-start.11 = (bf16[128,512]{0,1:T(8,128)(2,1)S(1)}, bf16[128,512]{0,1:T(8,128)(2,1)S(1)}, u32[]{:S(2)}, u32[]{:S(2)}) collective-permute-start(bf16[128,512]{0,1:T(8,128)(2,1)S(1)} %collective-permute-done.10), channel_id=1, source_target_pairs={{0,2},{2,4},{4,6},{6,8},{8,10},{10,12},{12,14},{14,16},{16,18},{18... | collective-permute-start | bytes 393224 | tf_op jit(solution)/shard_map/ppermute | solution.py:12
  52.2 0.5 collective-permute-done.4
  52.7 5.6 %collective-permute-start.5 = (bf16[128,512]{0,1:T(8,128)(2,1)S(1)}, bf16[128,512]{0,1:T(8,128)(2,1)S(1)}, u32[]{:S(2)}, u32[]{:S(2)}) collective-permute-start(bf16[128,512]{0,1:T(8,128)(2,1)S(1)} %collective-permute-done.4), channel_id=1, source_target_pairs={{0,30},{2,0},{4,2},{6,4},{8,6},{10,8},{12,10},{14,12},{16,14},{18,... | collective-permute-start | bytes 393224 | tf_op jit(solution)/shard_map/ppermute | solution.py:12
  58.3 1.9 %collective-permute-start.12 = (bf16[128,512]{0,1:T(8,128)(2,1)S(1)}, bf16[128,512]{0,1:T(8,128)(2,1)S(1)}, u32[]{:S(2)}, u32[]{:S(2)}) collective-permute-start(bf16[128,512]{0,1:T(8,128)(2,1)S(1)} %collective-permute-done.11), channel_id=1, source_target_pairs={{0,2},{2,4},{4,6},{6,8},{8,10},{10,12},{12,14},{14,16},{16,18},{18... | collective-permute-start | bytes 393224 | tf_op jit(solution)/shard_map/ppermute | solution.py:12
  60.2 1.4 collective-permute-done.5
  61.7 5.6 %collective-permute-start.6 = (bf16[128,512]{0,1:T(8,128)(2,1)S(1)}, bf16[128,512]{0,1:T(8,128)(2,1)S(1)}, u32[]{:S(2)}, u32[]{:S(2)}) collective-permute-start(bf16[128,512]{0,1:T(8,128)(2,1)S(1)} %collective-permute-done.5), channel_id=1, source_target_pairs={{0,30},{2,0},{4,2},{6,4},{8,6},{10,8},{12,10},{14,12},{16,14},{18,... | collective-permute-start | bytes 393224 | tf_op jit(solution)/shard_map/ppermute | solution.py:12
  67.2 0.2 collective-permute-done.12
  67.5 1.9 %collective-permute-start.13 = (bf16[128,512]{0,1:T(8,128)(2,1)S(1)}, bf16[128,512]{0,1:T(8,128)(2,1)S(1)}, u32[]{:S(2)}, u32[]{:S(2)}) collective-permute-start(bf16[128,512]{0,1:T(8,128)(2,1)S(1)} %collective-permute-done.12), channel_id=1, source_target_pairs={{0,2},{2,4},{4,6},{6,8},{8,10},{10,12},{12,14},{14,16},{16,18},{18... | collective-permute-start | bytes 393224 | tf_op jit(solution)/shard_map/ppermute | solution.py:12
  69.4 1.0 collective-permute-done.6
  70.5 5.6 %collective-permute-start.7 = (bf16[128,512]{0,1:T(8,128)(2,1)S(1)}, bf16[128,512]{0,1:T(8,128)(2,1)S(1)}, u32[]{:S(2)}, u32[]{:S(2)}) collective-permute-start(bf16[128,512]{0,1:T(8,128)(2,1)S(1)} %collective-permute-done.6), channel_id=1, source_target_pairs={{0,30},{2,0},{4,2},{6,4},{8,6},{10,8},{12,10},{14,12},{16,14},{18,... | collective-permute-start | bytes 393224 | tf_op jit(solution)/shard_map/ppermute | solution.py:12
  76.1 1.9 %collective-permute-start.14 = (bf16[128,512]{0,1:T(8,128)(2,1)S(1)}, bf16[128,512]{0,1:T(8,128)(2,1)S(1)}, u32[]{:S(2)}, u32[]{:S(2)}) collective-permute-start(bf16[128,512]{0,1:T(8,128)(2,1)S(1)} %collective-permute-done.13), channel_id=1, source_target_pairs={{0,2},{2,4},{4,6},{6,8},{8,10},{10,12},{12,14},{14,16},{16,18},{18... | collective-permute-start | bytes 393224 | tf_op jit(solution)/shard_map/ppermute | solution.py:12
  78.0 6.1 %collective-permute-done.14 = bf16[128,512]{0,1:T(8,128)(2,1)S(1)} collective-permute-done((bf16[128,512]{0,1:T(8,128)(2,1)S(1)}, bf16[128,512]{0,1:T(8,128)(2,1)S(1)}, u32[]{:S(2)}, u32[]{:S(2)}) %collective-permute-start.14) | collective-permute-done | bytes 131104 | tf_op jit(solution)/shard_map/ppermute | solution.py:12
  84.2 1.9 %collective-permute-start.15 = (bf16[128,512]{0,1:T(8,128)(2,1)S(1)}, bf16[128,512]{0,1:T(8,128)(2,1)S(1)}, u32[]{:S(2)}, u32[]{:S(2)}) collective-permute-start(bf16[128,512]{0,1:T(8,128)(2,1)S(1)} %collective-permute-done.14), channel_id=1, source_target_pairs={{0,2},{2,4},{4,6},{6,8},{8,10},{10,12},{12,14},{14,16},{16,18},{18... | collective-permute-start | bytes 393224 | tf_op jit(solution)/shard_map/ppermute | solution.py:12
  86.1 6.1 %collective-permute-done.15 = bf16[128,512]{0,1:T(8,128)(2,1)S(1)} collective-permute-done((bf16[128,512]{0,1:T(8,128)(2,1)S(1)}, bf16[128,512]{0,1:T(8,128)(2,1)S(1)}, u32[]{:S(2)}, u32[]{:S(2)}) %collective-permute-start.15) | collective-permute-done | bytes 131104 | tf_op jit(solution)/shard_map/ppermute | solution.py:12
  93.1 1.5 copy-done.2
  94.6 1.0 convolution_convert_fusion.1
  95.7 1.9 %collective-permute-start.16 = (bf16[3,256]{1,0:T(4,128)(2,1)S(1)}, bf16[3,256]{1,0:T(4,128)(2,1)S(1)}, u32[]{:S(2)}, u32[]{:S(2)}) collective-permute-start(bf16[3,256]{1,0:T(4,128)(2,1)S(1)} %slice.87), channel_id=1, source_target_pairs={{0,32},{32,64},{64,96},{96,128},{128,160},{160,192},{192,224},{224... | collective-permute-start | bytes 4616 | tf_op jit(solution)/shard_map/ppermute | solution.py:73
  97.6 1.0 convolution_convert_fusion
  98.6 4.4 %collective-permute-done.16 = bf16[3,256]{1,0:T(4,128)(2,1)S(1)} collective-permute-done((bf16[3,256]{1,0:T(4,128)(2,1)S(1)}, bf16[3,256]{1,0:T(4,128)(2,1)S(1)}, u32[]{:S(2)}, u32[]{:S(2)}) %collective-permute-start.16) | collective-permute-done | bytes 1568 | tf_op jit(solution)/shard_map/ppermute | solution.py:73
  103.0 0.3 multiply_multiply_fusion
  103.3 1.9 %collective-permute-start.17 = (f32[3,256]{1,0:T(4,128)S(1)}, f32[3,256]{1,0:T(4,128)S(1)}, u32[]{:S(2)}, u32[]{:S(2)}) collective-permute-start(f32[3,256]{1,0:T(4,128)S(1)} %fusion.155), channel_id=1, source_target_pairs={{32,0},{64,32},{96,64},{128,96},{160,128},{192,160},{224,192},{256... | collective-permute-start | bytes 9224 | tf_op jit(solution)/shard_map/ppermute | solution.py:73
  105.2 0.8 fusion.84
  109.8 1.9 %collective-permute-start.25 = (bf16[128,512]{1,0:T(8,128)(2,1)S(1)}, bf16[128,512]{1,0:T(8,128)(2,1)S(1)}, u32[]{:S(2)}, u32[]{:S(2)}) collective-permute-start(bf16[128,512]{1,0:T(8,128)(2,1)S(1)} %fusion.13), channel_id=1, source_target_pairs={{0,30},{2,0},{4,2},{6,4},{8,6},{10,8},{12,10},{14,12},{16,14},{18,... | collective-permute-start | bytes 393224 | tf_op jit(solution)/shard_map/ppermute | solution.py:12
  111.7 0.2 fusion
  112.0 3.9 %collective-permute-start.18 = (bf16[128,512]{1,0:T(8,128)(2,1)S(1)}, bf16[128,512]{1,0:T(8,128)(2,1)S(1)}, u32[]{:S(2)}, u32[]{:S(2)}) collective-permute-start(bf16[128,512]{1,0:T(8,128)(2,1)S(1)} %fusion), channel_id=1, source_target_pairs={{0,2},{2,4},{4,6},{6,8},{8,10},{10,12},{12,14},{14,16},{16,18},{18... | collective-permute-start | bytes 393224 | tf_op jit(solution)/shard_map/ppermute | solution.py:12
  115.9 1.7 collective-permute-done.25
  117.8 3.4 %collective-permute-start.26 = (bf16[128,512]{1,0:T(8,128)(2,1)S(1)}, bf16[128,512]{1,0:T(8,128)(2,1)S(1)}, u32[]{:S(2)}, u32[]{:S(2)}) collective-permute-start(bf16[128,512]{1,0:T(8,128)(2,1)S(1)} %add_convert_fusion.6), channel_id=1, source_target_pairs={{0,30},{2,0},{4,2},{6,4},{8,6},{10,8},{12,10},{14,12},{16,14},{18,... | collective-permute-start | bytes 393224 | tf_op jit(solution)/shard_map/ppermute | solution.py:12
  121.5 2.4 %collective-permute-start.19 = (bf16[128,512]{1,0:T(8,128)(2,1)S(1)}, bf16[128,512]{1,0:T(8,128)(2,1)S(1)}, u32[]{:S(2)}, u32[]{:S(2)}) collective-permute-start(bf16[128,512]{1,0:T(8,128)(2,1)S(1)} %add_convert_fusion.12), channel_id=1, source_target_pairs={{0,2},{2,4},{4,6},{6,8},{8,10},{10,12},{12,14},{14,16},{16,18},{18... | collective-permute-start | bytes 393224 | tf_op jit(solution)/shard_map/ppermute | solution.py:12
  123.9 0.9 collective-permute-done.26
  125.1 4.8 %collective-permute-start.27 = (bf16[128,512]{1,0:T(8,128)(2,1)S(1)}, bf16[128,512]{1,0:T(8,128)(2,1)S(1)}, u32[]{:S(2)}, u32[]{:S(2)}) collective-permute-start(bf16[128,512]{1,0:T(8,128)(2,1)S(1)} %add_convert_fusion.5), channel_id=1, source_target_pairs={{0,30},{2,0},{4,2},{6,4},{8,6},{10,8},{12,10},{14,12},{16,14},{18,... | collective-permute-start | bytes 393224 | tf_op jit(solution)/shard_map/ppermute | solution.py:12
  129.9 0.2 add_convert_fusion.11
  130.2 1.9 %collective-permute-start.20 = (bf16[128,512]{1,0:T(8,128)(2,1)S(1)}, bf16[128,512]{1,0:T(8,128)(2,1)S(1)}, u32[]{:S(2)}, u32[]{:S(2)}) collective-permute-start(bf16[128,512]{1,0:T(8,128)(2,1)S(1)} %add_convert_fusion.11), channel_id=1, source_target_pairs={{0,2},{2,4},{4,6},{6,8},{8,10},{10,12},{12,14},{14,16},{16,18},{18... | collective-permute-start | bytes 393224 | tf_op jit(solution)/shard_map/ppermute | solution.py:12
  132.1 0.3 collective-permute-done.27
  132.7 5.6 %collective-permute-start.28 = (bf16[128,512]{1,0:T(8,128)(2,1)S(1)}, bf16[128,512]{1,0:T(8,128)(2,1)S(1)}, u32[]{:S(2)}, u32[]{:S(2)}) collective-permute-start(bf16[128,512]{1,0:T(8,128)(2,1)S(1)} %add_convert_fusion.4), channel_id=1, source_target_pairs={{0,30},{2,0},{4,2},{6,4},{8,6},{10,8},{12,10},{14,12},{16,14},{18,... | collective-permute-start | bytes 393224 | tf_op jit(solution)/shard_map/ppermute | solution.py:12
  138.5 1.9 %collective-permute-start.21 = (bf16[128,512]{1,0:T(8,128)(2,1)S(1)}, bf16[128,512]{1,0:T(8,128)(2,1)S(1)}, u32[]{:S(2)}, u32[]{:S(2)}) collective-permute-start(bf16[128,512]{1,0:T(8,128)(2,1)S(1)} %add_convert_fusion.10), channel_id=1, source_target_pairs={{0,2},{2,4},{4,6},{6,8},{8,10},{10,12},{12,14},{14,16},{16,18},{18... | collective-permute-start | bytes 393224 | tf_op jit(solution)/shard_map/ppermute | solution.py:12
  140.4 0.3 collective-permute-done.28
  141.0 5.6 %collective-permute-start.29 = (bf16[128,512]{1,0:T(8,128)(2,1)S(1)}, bf16[128,512]{1,0:T(8,128)(2,1)S(1)}, u32[]{:S(2)}, u32[]{:S(2)}) collective-permute-start(bf16[128,512]{1,0:T(8,128)(2,1)S(1)} %add_convert_fusion.3), channel_id=1, source_target_pairs={{0,30},{2,0},{4,2},{6,4},{8,6},{10,8},{12,10},{14,12},{16,14},{18,... | collective-permute-start | bytes 393224 | tf_op jit(solution)/shard_map/ppermute | solution.py:12
  146.8 1.9 %collective-permute-start.22 = (bf16[128,512]{1,0:T(8,128)(2,1)S(1)}, bf16[128,512]{1,0:T(8,128)(2,1)S(1)}, u32[]{:S(2)}, u32[]{:S(2)}) collective-permute-start(bf16[128,512]{1,0:T(8,128)(2,1)S(1)} %add_convert_fusion.9), channel_id=1, source_target_pairs={{0,2},{2,4},{4,6},{6,8},{8,10},{10,12},{12,14},{14,16},{16,18},{18... | collective-permute-start | bytes 393224 | tf_op jit(solution)/shard_map/ppermute | solution.py:12
  148.7 0.3 collective-permute-done.29
  149.3 5.6 %collective-permute-start.30 = (bf16[128,512]{1,0:T(8,128)(2,1)S(1)}, bf16[128,512]{1,0:T(8,128)(2,1)S(1)}, u32[]{:S(2)}, u32[]{:S(2)}) collective-permute-start(bf16[128,512]{1,0:T(8,128)(2,1)S(1)} %add_convert_fusion.2), channel_id=1, source_target_pairs={{0,30},{2,0},{4,2},{6,4},{8,6},{10,8},{12,10},{14,12},{16,14},{18,... | collective-permute-start | bytes 393224 | tf_op jit(solution)/shard_map/ppermute | solution.py:12
  155.1 1.9 %collective-permute-start.23 = (bf16[128,512]{1,0:T(8,128)(2,1)S(1)}, bf16[128,512]{1,0:T(8,128)(2,1)S(1)}, u32[]{:S(2)}, u32[]{:S(2)}) collective-permute-start(bf16[128,512]{1,0:T(8,128)(2,1)S(1)} %add_convert_fusion.8), channel_id=1, source_target_pairs={{0,2},{2,4},{4,6},{6,8},{8,10},{10,12},{12,14},{14,16},{16,18},{18... | collective-permute-start | bytes 393224 | tf_op jit(solution)/shard_map/ppermute | solution.py:12
  157.0 0.3 collective-permute-done.30
  157.6 5.6 %collective-permute-start.31 = (bf16[128,512]{1,0:T(8,128)(2,1)S(1)}, bf16[128,512]{1,0:T(8,128)(2,1)S(1)}, u32[]{:S(2)}, u32[]{:S(2)}) collective-permute-start(bf16[128,512]{1,0:T(8,128)(2,1)S(1)} %add_convert_fusion.1), channel_id=1, source_target_pairs={{0,30},{2,0},{4,2},{6,4},{8,6},{10,8},{12,10},{14,12},{16,14},{18,... | collective-permute-start | bytes 393224 | tf_op jit(solution)/shard_map/ppermute | solution.py:12
  163.4 1.9 %collective-permute-start.24 = (bf16[128,512]{1,0:T(8,128)(2,1)S(1)}, bf16[128,512]{1,0:T(8,128)(2,1)S(1)}, u32[]{:S(2)}, u32[]{:S(2)}) collective-permute-start(bf16[128,512]{1,0:T(8,128)(2,1)S(1)} %add_convert_fusion.7), channel_id=1, source_target_pairs={{0,2},{2,4},{4,6},{6,8},{8,10},{10,12},{12,14},{14,16},{16,18},{18... | collective-permute-start | bytes 393224 | tf_op jit(solution)/shard_map/ppermute | solution.py:12
  165.3 1.1 collective-permute-done.31
  166.6 5.6 %collective-permute-start.32 = (bf16[128,512]{1,0:T(8,128)(2,1)S(1)}, bf16[128,512]{1,0:T(8,128)(2,1)S(1)}, u32[]{:S(2)}, u32[]{:S(2)}) collective-permute-start(bf16[128,512]{1,0:T(8,128)(2,1)S(1)} %add_convert_fusion), channel_id=1, source_target_pairs={{0,30},{2,0},{4,2},{6,4},{8,6},{10,8},{12,10},{14,12},{16,14},{18,... | collective-permute-start | bytes 393224 | tf_op jit(solution)/shard_map/ppermute | solution.py:12
  172.5 2.3 %collective-permute-done.32 = bf16[128,512]{1,0:T(8,128)(2,1)S(1)} collective-permute-done((bf16[128,512]{1,0:T(8,128)(2,1)S(1)}, bf16[128,512]{1,0:T(8,128)(2,1)S(1)}, u32[]{:S(2)}, u32[]{:S(2)}) %collective-permute-start.32) | collective-permute-done | bytes 131104 | tf_op jit(solution)/shard_map/ppermute | solution.py:12
  175.0 3.4 %collective-permute-start.33 = (bf16[128,256]{1,0:T(8,128)(2,1)S(1)}, bf16[128,256]{1,0:T(8,128)(2,1)S(1)}, u32[]{:S(2)}, u32[]{:S(2)}) collective-permute-start(bf16[128,256]{1,0:T(8,128)(2,1)S(1)} %select_convert_fusion), channel_id=1, source_target_pairs={{0,1},{1,0},{2,3},{3,2},{4,5},{5,4},{6,7},{7,6},{8,9},{9,8},{10,11... | collective-permute-start | bytes 196616 | tf_op jit(solution)/shard_map/ppermute | solution.py:12
  178.4 2.7 %collective-permute-done.33 = bf16[128,256]{1,0:T(8,128)(2,1)S(1)} collective-permute-done((bf16[128,256]{1,0:T(8,128)(2,1)S(1)}, bf16[128,256]{1,0:T(8,128)(2,1)S(1)}, u32[]{:S(2)}, u32[]{:S(2)}) %collective-permute-start.33) | collective-permute-done | bytes 65568 | tf_op jit(solution)/shard_map/ppermute | solution.py:12
  181.2 0.7 add_convert_fusion.13
  (96 shorter events, 8.0 us)
Async XLA Ops:
  0.6 102.4 %copy-start = (bf16[10,256]{1,0:T(8,128)(2,1)S(1)}, bf16[10,256]{1,0:T(8,128)(2,1)}, u32[]{:S(2)}) copy-start(bf16[10,256]{1,0:T(8,128)(2,1)} %param.13) | copy-start | bytes 15364
  1.6 6.2 %collective-permute-start = (bf16[128,256]{0,1:T(8,128)(2,1)S(1)}, bf16[128,256]{0,1:T(8,128)(2,1)S(1)}, u32[]{:S(2)}, u32[]{:S(2)}) collective-permute-start(bf16[128,256]{0,1:T(8,128)(2,1)S(1)} %copy.10), channel_id=1, source_target_pairs={{0,1},{1,0},{2,3},{3,2},{4,5},{5,4},{6,7},{7,6},{8,9},{9,8},{10,11... | collective-permute-start | bytes 196616 | tf_op jit(solution)/shard_map/ppermute | solution.py:12
  7.8 21.1 %collective-permute-start.1 = (bf16[128,512]{0,1:T(8,128)(2,1)S(1)}, bf16[128,512]{0,1:T(8,128)(2,1)S(1)}, u32[]{:S(2)}, u32[]{:S(2)}) collective-permute-start(bf16[128,512]{0,1:T(8,128)(2,1)S(1)} %maximum_select_fusion.1), channel_id=1, source_target_pairs={{0,30},{2,0},{4,2},{6,4},{8,6},{10,8},{12,10},{14,12},{16,14},{18,... | collective-permute-start | bytes 393224 | tf_op jit(solution)/shard_map/ppermute | solution.py:12
  26.0 8.1 %collective-permute-start.8 = (bf16[128,512]{0,1:T(8,128)(2,1)S(1)}, bf16[128,512]{0,1:T(8,128)(2,1)S(1)}, u32[]{:S(2)}, u32[]{:S(2)}) collective-permute-start(bf16[128,512]{0,1:T(8,128)(2,1)S(1)} %maximum_select_fusion.1), channel_id=1, source_target_pairs={{0,2},{2,4},{4,6},{6,8},{8,10},{10,12},{12,14},{14,16},{16,18},{18... | collective-permute-start | bytes 393224 | tf_op jit(solution)/shard_map/ppermute | solution.py:12
  28.9 7.7 %collective-permute-start.2 = (bf16[128,512]{0,1:T(8,128)(2,1)S(1)}, bf16[128,512]{0,1:T(8,128)(2,1)S(1)}, u32[]{:S(2)}, u32[]{:S(2)}) collective-permute-start(bf16[128,512]{0,1:T(8,128)(2,1)S(1)} %collective-permute-done.1), channel_id=1, source_target_pairs={{0,30},{2,0},{4,2},{6,4},{8,6},{10,8},{12,10},{14,12},{16,14},{18,... | collective-permute-start | bytes 393224 | tf_op jit(solution)/shard_map/ppermute | solution.py:12
  34.1 8.1 %collective-permute-start.9 = (bf16[128,512]{0,1:T(8,128)(2,1)S(1)}, bf16[128,512]{0,1:T(8,128)(2,1)S(1)}, u32[]{:S(2)}, u32[]{:S(2)}) collective-permute-start(bf16[128,512]{0,1:T(8,128)(2,1)S(1)} %collective-permute-done.8), channel_id=1, source_target_pairs={{0,2},{2,4},{4,6},{6,8},{8,10},{10,12},{12,14},{14,16},{16,18},{18... | collective-permute-start | bytes 393224 | tf_op jit(solution)/shard_map/ppermute | solution.py:12
  36.6 8.1 %collective-permute-start.3 = (bf16[128,512]{0,1:T(8,128)(2,1)S(1)}, bf16[128,512]{0,1:T(8,128)(2,1)S(1)}, u32[]{:S(2)}, u32[]{:S(2)}) collective-permute-start(bf16[128,512]{0,1:T(8,128)(2,1)S(1)} %collective-permute-done.2), channel_id=1, source_target_pairs={{0,30},{2,0},{4,2},{6,4},{8,6},{10,8},{12,10},{14,12},{16,14},{18,... | collective-permute-start | bytes 393224 | tf_op jit(solution)/shard_map/ppermute | solution.py:12
  42.2 8.1 %collective-permute-start.10 = (bf16[128,512]{0,1:T(8,128)(2,1)S(1)}, bf16[128,512]{0,1:T(8,128)(2,1)S(1)}, u32[]{:S(2)}, u32[]{:S(2)}) collective-permute-start(bf16[128,512]{0,1:T(8,128)(2,1)S(1)} %collective-permute-done.9), channel_id=1, source_target_pairs={{0,2},{2,4},{4,6},{6,8},{8,10},{10,12},{12,14},{14,16},{16,18},{18... | collective-permute-start | bytes 393224 | tf_op jit(solution)/shard_map/ppermute | solution.py:12
  44.7 8.1 %collective-permute-start.4 = (bf16[128,512]{0,1:T(8,128)(2,1)S(1)}, bf16[128,512]{0,1:T(8,128)(2,1)S(1)}, u32[]{:S(2)}, u32[]{:S(2)}) collective-permute-start(bf16[128,512]{0,1:T(8,128)(2,1)S(1)} %collective-permute-done.3), channel_id=1, source_target_pairs={{0,30},{2,0},{4,2},{6,4},{8,6},{10,8},{12,10},{14,12},{16,14},{18,... | collective-permute-start | bytes 393224 | tf_op jit(solution)/shard_map/ppermute | solution.py:12
  50.2 8.1 %collective-permute-start.11 = (bf16[128,512]{0,1:T(8,128)(2,1)S(1)}, bf16[128,512]{0,1:T(8,128)(2,1)S(1)}, u32[]{:S(2)}, u32[]{:S(2)}) collective-permute-start(bf16[128,512]{0,1:T(8,128)(2,1)S(1)} %collective-permute-done.10), channel_id=1, source_target_pairs={{0,2},{2,4},{4,6},{6,8},{8,10},{10,12},{12,14},{14,16},{16,18},{18... | collective-permute-start | bytes 393224 | tf_op jit(solution)/shard_map/ppermute | solution.py:12
  52.7 8.9 %collective-permute-start.5 = (bf16[128,512]{0,1:T(8,128)(2,1)S(1)}, bf16[128,512]{0,1:T(8,128)(2,1)S(1)}, u32[]{:S(2)}, u32[]{:S(2)}) collective-permute-start(bf16[128,512]{0,1:T(8,128)(2,1)S(1)} %collective-permute-done.4), channel_id=1, source_target_pairs={{0,30},{2,0},{4,2},{6,4},{8,6},{10,8},{12,10},{14,12},{16,14},{18,... | collective-permute-start | bytes 393224 | tf_op jit(solution)/shard_map/ppermute | solution.py:12
  58.3 9.2 %collective-permute-start.12 = (bf16[128,512]{0,1:T(8,128)(2,1)S(1)}, bf16[128,512]{0,1:T(8,128)(2,1)S(1)}, u32[]{:S(2)}, u32[]{:S(2)}) collective-permute-start(bf16[128,512]{0,1:T(8,128)(2,1)S(1)} %collective-permute-done.11), channel_id=1, source_target_pairs={{0,2},{2,4},{4,6},{6,8},{8,10},{10,12},{12,14},{14,16},{16,18},{18... | collective-permute-start | bytes 393224 | tf_op jit(solution)/shard_map/ppermute | solution.py:12
  61.7 8.8 %collective-permute-start.6 = (bf16[128,512]{0,1:T(8,128)(2,1)S(1)}, bf16[128,512]{0,1:T(8,128)(2,1)S(1)}, u32[]{:S(2)}, u32[]{:S(2)}) collective-permute-start(bf16[128,512]{0,1:T(8,128)(2,1)S(1)} %collective-permute-done.5), channel_id=1, source_target_pairs={{0,30},{2,0},{4,2},{6,4},{8,6},{10,8},{12,10},{14,12},{16,14},{18,... | collective-permute-start | bytes 393224 | tf_op jit(solution)/shard_map/ppermute | solution.py:12
  67.5 8.6 %collective-permute-start.13 = (bf16[128,512]{0,1:T(8,128)(2,1)S(1)}, bf16[128,512]{0,1:T(8,128)(2,1)S(1)}, u32[]{:S(2)}, u32[]{:S(2)}) collective-permute-start(bf16[128,512]{0,1:T(8,128)(2,1)S(1)} %collective-permute-done.12), channel_id=1, source_target_pairs={{0,2},{2,4},{4,6},{6,8},{8,10},{10,12},{12,14},{14,16},{16,18},{18... | collective-permute-start | bytes 393224 | tf_op jit(solution)/shard_map/ppermute | solution.py:12
  70.5 15.6 %collective-permute-start.7 = (bf16[128,512]{0,1:T(8,128)(2,1)S(1)}, bf16[128,512]{0,1:T(8,128)(2,1)S(1)}, u32[]{:S(2)}, u32[]{:S(2)}) collective-permute-start(bf16[128,512]{0,1:T(8,128)(2,1)S(1)} %collective-permute-done.6), channel_id=1, source_target_pairs={{0,30},{2,0},{4,2},{6,4},{8,6},{10,8},{12,10},{14,12},{16,14},{18,... | collective-permute-start | bytes 393224 | tf_op jit(solution)/shard_map/ppermute | solution.py:12
  76.1 8.1 %collective-permute-start.14 = (bf16[128,512]{0,1:T(8,128)(2,1)S(1)}, bf16[128,512]{0,1:T(8,128)(2,1)S(1)}, u32[]{:S(2)}, u32[]{:S(2)}) collective-permute-start(bf16[128,512]{0,1:T(8,128)(2,1)S(1)} %collective-permute-done.13), channel_id=1, source_target_pairs={{0,2},{2,4},{4,6},{6,8},{8,10},{10,12},{12,14},{14,16},{16,18},{18... | collective-permute-start | bytes 393224 | tf_op jit(solution)/shard_map/ppermute | solution.py:12
  84.2 8.1 %collective-permute-start.15 = (bf16[128,512]{0,1:T(8,128)(2,1)S(1)}, bf16[128,512]{0,1:T(8,128)(2,1)S(1)}, u32[]{:S(2)}, u32[]{:S(2)}) collective-permute-start(bf16[128,512]{0,1:T(8,128)(2,1)S(1)} %collective-permute-done.14), channel_id=1, source_target_pairs={{0,2},{2,4},{4,6},{6,8},{8,10},{10,12},{12,14},{14,16},{16,18},{18... | collective-permute-start | bytes 393224 | tf_op jit(solution)/shard_map/ppermute | solution.py:12
  92.4 2.2 %copy-start.2 = (bf16[8192,256]{1,0:T(8,128)(2,1)S(1)}, bf16[8192,256]{1,0:T(8,128)(2,1)}, u32[]{:S(2)}) copy-start(bf16[8192,256]{1,0:T(8,128)(2,1)} %param.10) | copy-start | bytes 12582916
  93.1 4.5 %copy-start.1 = (bf16[8192,256]{1,0:T(8,128)(2,1)S(1)}, bf16[8192,256]{1,0:T(8,128)(2,1)}, u32[]{:S(2)}) copy-start(bf16[8192,256]{1,0:T(8,128)(2,1)} %param.9) | copy-start | bytes 12582916
  95.6 7.4 %copy-start.3 = (f32[256]{0:T(256)S(1)}, f32[256]{0:T(256)}, u32[]{:S(2)}) copy-start(f32[256]{0:T(256)} %param.12) | copy-start | bytes 3076
  95.6 7.4 %copy-start.4 = (s32[128]{0:T(128)S(1)}, s32[128]{0:T(128)}, u32[]{:S(2)}) copy-start(s32[128]{0:T(128)} %param.14) | copy-start | bytes 1540
  95.7 7.3 %collective-permute-start.16 = (bf16[3,256]{1,0:T(4,128)(2,1)S(1)}, bf16[3,256]{1,0:T(4,128)(2,1)S(1)}, u32[]{:S(2)}, u32[]{:S(2)}) collective-permute-start(bf16[3,256]{1,0:T(4,128)(2,1)S(1)} %slice.87), channel_id=1, source_target_pairs={{0,32},{32,64},{64,96},{96,128},{128,160},{160,192},{192,224},{224... | collective-permute-start | bytes 4616 | tf_op jit(solution)/shard_map/ppermute | solution.py:73
  103.3 6.2 %collective-permute-start.17 = (f32[3,256]{1,0:T(4,128)S(1)}, f32[3,256]{1,0:T(4,128)S(1)}, u32[]{:S(2)}, u32[]{:S(2)}) collective-permute-start(f32[3,256]{1,0:T(4,128)S(1)} %fusion.155), channel_id=1, source_target_pairs={{32,0},{64,32},{96,64},{128,96},{160,128},{192,160},{224,192},{256... | collective-permute-start | bytes 9224 | tf_op jit(solution)/shard_map/ppermute | solution.py:73
  109.8 7.8 %collective-permute-start.25 = (bf16[128,512]{1,0:T(8,128)(2,1)S(1)}, bf16[128,512]{1,0:T(8,128)(2,1)S(1)}, u32[]{:S(2)}, u32[]{:S(2)}) collective-permute-start(bf16[128,512]{1,0:T(8,128)(2,1)S(1)} %fusion.13), channel_id=1, source_target_pairs={{0,30},{2,0},{4,2},{6,4},{8,6},{10,8},{12,10},{14,12},{16,14},{18,... | collective-permute-start | bytes 393224 | tf_op jit(solution)/shard_map/ppermute | solution.py:12
  112.0 9.3 %collective-permute-start.18 = (bf16[128,512]{1,0:T(8,128)(2,1)S(1)}, bf16[128,512]{1,0:T(8,128)(2,1)S(1)}, u32[]{:S(2)}, u32[]{:S(2)}) collective-permute-start(bf16[128,512]{1,0:T(8,128)(2,1)S(1)} %fusion), channel_id=1, source_target_pairs={{0,2},{2,4},{4,6},{6,8},{8,10},{10,12},{12,14},{14,16},{16,18},{18... | collective-permute-start | bytes 393224 | tf_op jit(solution)/shard_map/ppermute | solution.py:12
  117.8 7.0 %collective-permute-start.26 = (bf16[128,512]{1,0:T(8,128)(2,1)S(1)}, bf16[128,512]{1,0:T(8,128)(2,1)S(1)}, u32[]{:S(2)}, u32[]{:S(2)}) collective-permute-start(bf16[128,512]{1,0:T(8,128)(2,1)S(1)} %add_convert_fusion.6), channel_id=1, source_target_pairs={{0,30},{2,0},{4,2},{6,4},{8,6},{10,8},{12,10},{14,12},{16,14},{18,... | collective-permute-start | bytes 393224 | tf_op jit(solution)/shard_map/ppermute | solution.py:12
  121.5 8.4 %collective-permute-start.19 = (bf16[128,512]{1,0:T(8,128)(2,1)S(1)}, bf16[128,512]{1,0:T(8,128)(2,1)S(1)}, u32[]{:S(2)}, u32[]{:S(2)}) collective-permute-start(bf16[128,512]{1,0:T(8,128)(2,1)S(1)} %add_convert_fusion.12), channel_id=1, source_target_pairs={{0,2},{2,4},{4,6},{6,8},{8,10},{10,12},{12,14},{14,16},{16,18},{18... | collective-permute-start | bytes 393224 | tf_op jit(solution)/shard_map/ppermute | solution.py:12
  125.1 7.3 %collective-permute-start.27 = (bf16[128,512]{1,0:T(8,128)(2,1)S(1)}, bf16[128,512]{1,0:T(8,128)(2,1)S(1)}, u32[]{:S(2)}, u32[]{:S(2)}) collective-permute-start(bf16[128,512]{1,0:T(8,128)(2,1)S(1)} %add_convert_fusion.5), channel_id=1, source_target_pairs={{0,30},{2,0},{4,2},{6,4},{8,6},{10,8},{12,10},{14,12},{16,14},{18,... | collective-permute-start | bytes 393224 | tf_op jit(solution)/shard_map/ppermute | solution.py:12
  130.2 8.1 %collective-permute-start.20 = (bf16[128,512]{1,0:T(8,128)(2,1)S(1)}, bf16[128,512]{1,0:T(8,128)(2,1)S(1)}, u32[]{:S(2)}, u32[]{:S(2)}) collective-permute-start(bf16[128,512]{1,0:T(8,128)(2,1)S(1)} %add_convert_fusion.11), channel_id=1, source_target_pairs={{0,2},{2,4},{4,6},{6,8},{8,10},{10,12},{12,14},{14,16},{16,18},{18... | collective-permute-start | bytes 393224 | tf_op jit(solution)/shard_map/ppermute | solution.py:12
  132.7 8.1 %collective-permute-start.28 = (bf16[128,512]{1,0:T(8,128)(2,1)S(1)}, bf16[128,512]{1,0:T(8,128)(2,1)S(1)}, u32[]{:S(2)}, u32[]{:S(2)}) collective-permute-start(bf16[128,512]{1,0:T(8,128)(2,1)S(1)} %add_convert_fusion.4), channel_id=1, source_target_pairs={{0,30},{2,0},{4,2},{6,4},{8,6},{10,8},{12,10},{14,12},{16,14},{18,... | collective-permute-start | bytes 393224 | tf_op jit(solution)/shard_map/ppermute | solution.py:12
  138.5 8.1 %collective-permute-start.21 = (bf16[128,512]{1,0:T(8,128)(2,1)S(1)}, bf16[128,512]{1,0:T(8,128)(2,1)S(1)}, u32[]{:S(2)}, u32[]{:S(2)}) collective-permute-start(bf16[128,512]{1,0:T(8,128)(2,1)S(1)} %add_convert_fusion.10), channel_id=1, source_target_pairs={{0,2},{2,4},{4,6},{6,8},{8,10},{10,12},{12,14},{14,16},{16,18},{18... | collective-permute-start | bytes 393224 | tf_op jit(solution)/shard_map/ppermute | solution.py:12
  141.0 8.1 %collective-permute-start.29 = (bf16[128,512]{1,0:T(8,128)(2,1)S(1)}, bf16[128,512]{1,0:T(8,128)(2,1)S(1)}, u32[]{:S(2)}, u32[]{:S(2)}) collective-permute-start(bf16[128,512]{1,0:T(8,128)(2,1)S(1)} %add_convert_fusion.3), channel_id=1, source_target_pairs={{0,30},{2,0},{4,2},{6,4},{8,6},{10,8},{12,10},{14,12},{16,14},{18,... | collective-permute-start | bytes 393224 | tf_op jit(solution)/shard_map/ppermute | solution.py:12
  146.8 8.1 %collective-permute-start.22 = (bf16[128,512]{1,0:T(8,128)(2,1)S(1)}, bf16[128,512]{1,0:T(8,128)(2,1)S(1)}, u32[]{:S(2)}, u32[]{:S(2)}) collective-permute-start(bf16[128,512]{1,0:T(8,128)(2,1)S(1)} %add_convert_fusion.9), channel_id=1, source_target_pairs={{0,2},{2,4},{4,6},{6,8},{8,10},{10,12},{12,14},{14,16},{16,18},{18... | collective-permute-start | bytes 393224 | tf_op jit(solution)/shard_map/ppermute | solution.py:12
  149.3 8.1 %collective-permute-start.30 = (bf16[128,512]{1,0:T(8,128)(2,1)S(1)}, bf16[128,512]{1,0:T(8,128)(2,1)S(1)}, u32[]{:S(2)}, u32[]{:S(2)}) collective-permute-start(bf16[128,512]{1,0:T(8,128)(2,1)S(1)} %add_convert_fusion.2), channel_id=1, source_target_pairs={{0,30},{2,0},{4,2},{6,4},{8,6},{10,8},{12,10},{14,12},{16,14},{18,... | collective-permute-start | bytes 393224 | tf_op jit(solution)/shard_map/ppermute | solution.py:12
  155.1 8.1 %collective-permute-start.23 = (bf16[128,512]{1,0:T(8,128)(2,1)S(1)}, bf16[128,512]{1,0:T(8,128)(2,1)S(1)}, u32[]{:S(2)}, u32[]{:S(2)}) collective-permute-start(bf16[128,512]{1,0:T(8,128)(2,1)S(1)} %add_convert_fusion.8), channel_id=1, source_target_pairs={{0,2},{2,4},{4,6},{6,8},{8,10},{10,12},{12,14},{14,16},{16,18},{18... | collective-permute-start | bytes 393224 | tf_op jit(solution)/shard_map/ppermute | solution.py:12
  157.6 8.8 %collective-permute-start.31 = (bf16[128,512]{1,0:T(8,128)(2,1)S(1)}, bf16[128,512]{1,0:T(8,128)(2,1)S(1)}, u32[]{:S(2)}, u32[]{:S(2)}) collective-permute-start(bf16[128,512]{1,0:T(8,128)(2,1)S(1)} %add_convert_fusion.1), channel_id=1, source_target_pairs={{0,30},{2,0},{4,2},{6,4},{8,6},{10,8},{12,10},{14,12},{16,14},{18,... | collective-permute-start | bytes 393224 | tf_op jit(solution)/shard_map/ppermute | solution.py:12
  163.4 9.1 %collective-permute-start.24 = (bf16[128,512]{1,0:T(8,128)(2,1)S(1)}, bf16[128,512]{1,0:T(8,128)(2,1)S(1)}, u32[]{:S(2)}, u32[]{:S(2)}) collective-permute-start(bf16[128,512]{1,0:T(8,128)(2,1)S(1)} %add_convert_fusion.7), channel_id=1, source_target_pairs={{0,2},{2,4},{4,6},{6,8},{8,10},{10,12},{12,14},{14,16},{16,18},{18... | collective-permute-start | bytes 393224 | tf_op jit(solution)/shard_map/ppermute | solution.py:12
  166.6 8.1 %collective-permute-start.32 = (bf16[128,512]{1,0:T(8,128)(2,1)S(1)}, bf16[128,512]{1,0:T(8,128)(2,1)S(1)}, u32[]{:S(2)}, u32[]{:S(2)}) collective-permute-start(bf16[128,512]{1,0:T(8,128)(2,1)S(1)} %add_convert_fusion), channel_id=1, source_target_pairs={{0,30},{2,0},{4,2},{6,4},{8,6},{10,8},{12,10},{14,12},{16,14},{18,... | collective-permute-start | bytes 393224 | tf_op jit(solution)/shard_map/ppermute | solution.py:12
  175.0 6.2 %collective-permute-start.33 = (bf16[128,256]{1,0:T(8,128)(2,1)S(1)}, bf16[128,256]{1,0:T(8,128)(2,1)S(1)}, u32[]{:S(2)}, u32[]{:S(2)}) collective-permute-start(bf16[128,256]{1,0:T(8,128)(2,1)S(1)} %select_convert_fusion), channel_id=1, source_target_pairs={{0,1},{1,0},{2,3},{3,2},{4,5},{5,4},{6,7},{7,6},{8,9},{9,8},{10,11... | collective-permute-start | bytes 196616 | tf_op jit(solution)/shard_map/ppermute | solution.py:12

commit v7 on v6

--- a/solution.py
+++ b/solution.py
@@ -17,14 +17,24 @@
     return jnp.where(first, jnp.concatenate([mine, other], 1), jnp.concatenate([other, mine], 1))
 
 
+def across(block, dz):
+    count = lax.axis_size("tz")
+    route = [(z * 2 + x, (z + dz) % count * 2 + 1 - x) for z in range(count) for x in range(2)]
+    return lax.ppermute(block, TP, route)
+
+
 def gather_features(tokens):
     rows = tokens.shape[0]
+    count = lax.axis_size("tz")
     pair = halves_in_order(tokens, shifted(tokens, "tx", 1))
-    count = lax.axis_size("tz")
     blocks = [pair] * count
-    ahead = pair
-    behind = pair
-    for step in range(1, count // 2 + 1):
+    ahead = halves_in_order(shifted(tokens, "tz", 1), across(tokens, 1))
+    blocks[-1 % count] = ahead
+    behind = None
+    if 1 < count - 1:
+        behind = halves_in_order(shifted(tokens, "tz", -1), across(tokens, -1))
+        blocks[1] = behind
+    for step in range(2, count // 2 + 1):
         ahead = shifted(ahead, "tz", 1)
         blocks[-step % count] = ahead
         if step < count - step:

time: 184 us -> 189 us (1.027)
  starting transfers between devices: 131 us -> 137 us
    ppermute x0 -> x2, starting transfers between devices: none -> 6.74 us  [across(): return lax.ppermute(block, TP, route)]
  transfers between devices with their start and end apart: 34 -> 36, of which waited for: 19 -> 22; matrix products, arithmetic and copies ran while one was open for 6% -> 6% of each run, Pallas kernels for 0% -> 0%
where the time goes in v7:
time: 189 us; the launch traced here: 187 us
  starting transfers between devices  137 us (72%)
  waiting for transfers between devices  32 us (17%)
  matrix products  9.48 us (5%)
  local copies, waits for them, and re-layouts  4.01 us (2%)
  other arithmetic  2.51 us (1%)
    ppermute x32, starting transfers between devices, shifted(): lax.ppermute(block, axis, [(i, (i + distance) % size) for i in range(size)])  126 us
    ppermute x32, waiting for transfers between devices, shifted(): lax.ppermute(block, axis, [(i, (i + distance) % size) for i in range(size)])  27.6 us
    ppermute x2, starting transfers between devices, across(): return lax.ppermute(block, TP, route)  6.74 us
    ppermute x2, waiting for transfers between devices, passed_along(): return lax.ppermute(block, axis, route)  4.38 us
    ppermute x2, starting transfers between devices, passed_along(): return lax.ppermute(block, axis, route)  3.84 us
  transfers between devices with their start and end apart: 36, of which 22 were waited for; matrix products, arithmetic and copies ran while one was open for 6% of the time, Pallas kernels for 0%

profile of v7, /device:TPU:56, one launch (start us, length us, event | category | flops | bytes accessed | tf_op | source)
XLA Modules:
  0.0 186.7 jit_solution(15969449413362572714)
XLA Ops:
  0.6 1.0 copy.10
  1.6 3.4 %collective-permute-start = (bf16[128,256]{0,1:T(8,128)(2,1)S(1)}, bf16[128,256]{0,1:T(8,128)(2,1)S(1)}, u32[]{:S(2)}, u32[]{:S(2)}) collective-permute-start(bf16[128,256]{0,1:T(8,128)(2,1)S(1)} %copy.10), channel_id=1, source_target_pairs={{0,1},{1,0},{2,3},{3,2},{4,5},{5,4},{6,7},{7,6},{8,9},{9,8},{10,11... | collective-permute-start | bytes 196616 | tf_op jit(solution)/shard_map/ppermute | solution.py:12
  5.0 18.2 %collective-permute-start.1 = (bf16[128,256]{0,1:T(8,128)(2,1)S(1)}, bf16[128,256]{0,1:T(8,128)(2,1)S(1)}, u32[]{:S(2)}, u32[]{:S(2)}) collective-permute-start(bf16[128,256]{0,1:T(8,128)(2,1)S(1)} %copy.10), channel_id=1, source_target_pairs={{0,30},{2,0},{4,2},{6,4},{8,6},{10,8},{12,10},{14,12},{16,14},{18,... | collective-permute-start | bytes 196616 | tf_op jit(solution)/shard_map/ppermute | solution.py:12
  23.2 2.4 %collective-permute-start.2 = (bf16[128,256]{0,1:T(8,128)(2,1)S(1)}, bf16[128,256]{0,1:T(8,128)(2,1)S(1)}, u32[]{:S(2)}, u32[]{:S(2)}) collective-permute-start(bf16[128,256]{0,1:T(8,128)(2,1)S(1)} %copy.10), channel_id=1, source_target_pairs={{0,31},{1,30},{2,1},{3,0},{4,3},{5,2},{6,5},{7,4},{8,7},{9,6},{10,... | collective-permute-start | bytes 196616 | tf_op jit(solution)/shard_map/ppermute | solution.py:23
  25.7 4.3 %collective-permute-start.10 = (bf16[128,256]{0,1:T(8,128)(2,1)S(1)}, bf16[128,256]{0,1:T(8,128)(2,1)S(1)}, u32[]{:S(2)}, u32[]{:S(2)}) collective-permute-start(bf16[128,256]{0,1:T(8,128)(2,1)S(1)} %copy.10), channel_id=1, source_target_pairs={{0,3},{1,2},{2,5},{3,4},{4,7},{5,6},{6,9},{7,8},{8,11},{9,10},{10,... | collective-permute-start | bytes 196616 | tf_op jit(solution)/shard_map/ppermute | solution.py:23
  30.0 1.9 %collective-permute-start.9 = (bf16[128,256]{0,1:T(8,128)(2,1)S(1)}, bf16[128,256]{0,1:T(8,128)(2,1)S(1)}, u32[]{:S(2)}, u32[]{:S(2)}) collective-permute-start(bf16[128,256]{0,1:T(8,128)(2,1)S(1)} %copy.10), channel_id=1, source_target_pairs={{0,2},{2,4},{4,6},{6,8},{8,10},{10,12},{12,14},{14,16},{16,18},{18... | collective-permute-start | bytes 196616 | tf_op jit(solution)/shard_map/ppermute | solution.py:12
  31.9 0.8 fusion.159
  33.0 0.7 convert_element_type.215
  33.7 5.1 %collective-permute-start.3 = (bf16[128,512]{0,1:T(8,128)(2,1)S(1)}, bf16[128,512]{0,1:T(8,128)(2,1)S(1)}, u32[]{:S(2)}, u32[]{:S(2)}) collective-permute-start(bf16[128,512]{0,1:T(8,128)(2,1)S(1)} %maximum_select_fusion.2), channel_id=1, source_target_pairs={{0,30},{2,0},{4,2},{6,4},{8,6},{10,8},{12,10},{14,12},{16,14},{18,... | collective-permute-start | bytes 393224 | tf_op jit(solution)/shard_map/ppermute | solution.py:12
  38.9 1.9 %collective-permute-start.11 = (bf16[128,512]{0,1:T(8,128)(2,1)S(1)}, bf16[128,512]{0,1:T(8,128)(2,1)S(1)}, u32[]{:S(2)}, u32[]{:S(2)}) collective-permute-start(bf16[128,512]{0,1:T(8,128)(2,1)S(1)} %maximum_select_fusion.3), channel_id=1, source_target_pairs={{0,2},{2,4},{4,6},{6,8},{8,10},{10,12},{12,14},{14,16},{16,18},{18... | collective-permute-start | bytes 393224 | tf_op jit(solution)/shard_map/ppermute | solution.py:12
  40.9 0.4 collective-permute-done.3
  41.3 5.6 %collective-permute-start.4 = (bf16[128,512]{0,1:T(8,128)(2,1)S(1)}, bf16[128,512]{0,1:T(8,128)(2,1)S(1)}, u32[]{:S(2)}, u32[]{:S(2)}) collective-permute-start(bf16[128,512]{0,1:T(8,128)(2,1)S(1)} %collective-permute-done.3), channel_id=1, source_target_pairs={{0,30},{2,0},{4,2},{6,4},{8,6},{10,8},{12,10},{14,12},{16,14},{18,... | collective-permute-start | bytes 393224 | tf_op jit(solution)/shard_map/ppermute | solution.py:12
  47.0 1.9 %collective-permute-start.12 = (bf16[128,512]{0,1:T(8,128)(2,1)S(1)}, bf16[128,512]{0,1:T(8,128)(2,1)S(1)}, u32[]{:S(2)}, u32[]{:S(2)}) collective-permute-start(bf16[128,512]{0,1:T(8,128)(2,1)S(1)} %collective-permute-done.11), channel_id=1, source_target_pairs={{0,2},{2,4},{4,6},{6,8},{8,10},{10,12},{12,14},{14,16},{16,18},{18... | collective-permute-start | bytes 393224 | tf_op jit(solution)/shard_map/ppermute | solution.py:12
  48.9 0.5 collective-permute-done.4
  49.4 5.6 %collective-permute-start.5 = (bf16[128,512]{0,1:T(8,128)(2,1)S(1)}, bf16[128,512]{0,1:T(8,128)(2,1)S(1)}, u32[]{:S(2)}, u32[]{:S(2)}) collective-permute-start(bf16[128,512]{0,1:T(8,128)(2,1)S(1)} %collective-permute-done.4), channel_id=1, source_target_pairs={{0,30},{2,0},{4,2},{6,4},{8,6},{10,8},{12,10},{14,12},{16,14},{18,... | collective-permute-start | bytes 393224 | tf_op jit(solution)/shard_map/ppermute | solution.py:12
  55.0 1.9 %collective-permute-start.13 = (bf16[128,512]{0,1:T(8,128)(2,1)S(1)}, bf16[128,512]{0,1:T(8,128)(2,1)S(1)}, u32[]{:S(2)}, u32[]{:S(2)}) collective-permute-start(bf16[128,512]{0,1:T(8,128)(2,1)S(1)} %collective-permute-done.12), channel_id=1, source_target_pairs={{0,2},{2,4},{4,6},{6,8},{8,10},{10,12},{12,14},{14,16},{16,18},{18... | collective-permute-start | bytes 393224 | tf_op jit(solution)/shard_map/ppermute | solution.py:12
  57.0 0.5 collective-permute-done.5
  57.5 5.6 %collective-permute-start.6 = (bf16[128,512]{0,1:T(8,128)(2,1)S(1)}, bf16[128,512]{0,1:T(8,128)(2,1)S(1)}, u32[]{:S(2)}, u32[]{:S(2)}) collective-permute-start(bf16[128,512]{0,1:T(8,128)(2,1)S(1)} %collective-permute-done.5), channel_id=1, source_target_pairs={{0,30},{2,0},{4,2},{6,4},{8,6},{10,8},{12,10},{14,12},{16,14},{18,... | collective-permute-start | bytes 393224 | tf_op jit(solution)/shard_map/ppermute | solution.py:12
  63.1 1.9 %collective-permute-start.14 = (bf16[128,512]{0,1:T(8,128)(2,1)S(1)}, bf16[128,512]{0,1:T(8,128)(2,1)S(1)}, u32[]{:S(2)}, u32[]{:S(2)}) collective-permute-start(bf16[128,512]{0,1:T(8,128)(2,1)S(1)} %collective-permute-done.13), channel_id=1, source_target_pairs={{0,2},{2,4},{4,6},{6,8},{8,10},{10,12},{12,14},{14,16},{16,18},{18... | collective-permute-start | bytes 393224 | tf_op jit(solution)/shard_map/ppermute | solution.py:12
  65.0 0.9 collective-permute-done.6
  66.0 5.6 %collective-permute-start.7 = (bf16[128,512]{0,1:T(8,128)(2,1)S(1)}, bf16[128,512]{0,1:T(8,128)(2,1)S(1)}, u32[]{:S(2)}, u32[]{:S(2)}) collective-permute-start(bf16[128,512]{0,1:T(8,128)(2,1)S(1)} %collective-permute-done.6), channel_id=1, source_target_pairs={{0,30},{2,0},{4,2},{6,4},{8,6},{10,8},{12,10},{14,12},{16,14},{18,... | collective-permute-start | bytes 393224 | tf_op jit(solution)/shard_map/ppermute | solution.py:12
  71.6 0.4 collective-permute-done.14
  72.0 1.9 %collective-permute-start.15 = (bf16[128,512]{0,1:T(8,128)(2,1)S(1)}, bf16[128,512]{0,1:T(8,128)(2,1)S(1)}, u32[]{:S(2)}, u32[]{:S(2)}) collective-permute-start(bf16[128,512]{0,1:T(8,128)(2,1)S(1)} %collective-permute-done.14), channel_id=1, source_target_pairs={{0,2},{2,4},{4,6},{6,8},{8,10},{10,12},{12,14},{14,16},{16,18},{18... | collective-permute-start | bytes 393224 | tf_op jit(solution)/shard_map/ppermute | solution.py:12
  73.9 1.3 collective-permute-done.7
  75.2 5.6 %collective-permute-start.8 = (bf16[128,512]{0,1:T(8,128)(2,1)S(1)}, bf16[128,512]{0,1:T(8,128)(2,1)S(1)}, u32[]{:S(2)}, u32[]{:S(2)}) collective-permute-start(bf16[128,512]{0,1:T(8,128)(2,1)S(1)} %collective-permute-done.7), channel_id=1, source_target_pairs={{0,30},{2,0},{4,2},{6,4},{8,6},{10,8},{12,10},{14,12},{16,14},{18,... | collective-permute-start | bytes 393224 | tf_op jit(solution)/shard_map/ppermute | solution.py:12
  80.9 1.9 %collective-permute-start.16 = (bf16[128,512]{0,1:T(8,128)(2,1)S(1)}, bf16[128,512]{0,1:T(8,128)(2,1)S(1)}, u32[]{:S(2)}, u32[]{:S(2)}) collective-permute-start(bf16[128,512]{0,1:T(8,128)(2,1)S(1)} %collective-permute-done.15), channel_id=1, source_target_pairs={{0,2},{2,4},{4,6},{6,8},{8,10},{10,12},{12,14},{14,16},{16,18},{18... | collective-permute-start | bytes 393224 | tf_op jit(solution)/shard_map/ppermute | solution.py:12
  82.8 6.2 %collective-permute-done.16 = bf16[128,512]{0,1:T(8,128)(2,1)S(1)} collective-permute-done((bf16[128,512]{0,1:T(8,128)(2,1)S(1)}, bf16[128,512]{0,1:T(8,128)(2,1)S(1)}, u32[]{:S(2)}, u32[]{:S(2)}) %collective-permute-start.16) | collective-permute-done | bytes 131104 | tf_op jit(solution)/shard_map/ppermute | solution.py:12
  89.0 1.9 %collective-permute-start.17 = (bf16[128,512]{0,1:T(8,128)(2,1)S(1)}, bf16[128,512]{0,1:T(8,128)(2,1)S(1)}, u32[]{:S(2)}, u32[]{:S(2)}) collective-permute-start(bf16[128,512]{0,1:T(8,128)(2,1)S(1)} %collective-permute-done.16), channel_id=1, source_target_pairs={{0,2},{2,4},{4,6},{6,8},{8,10},{10,12},{12,14},{14,16},{16,18},{18... | collective-permute-start | bytes 393224 | tf_op jit(solution)/shard_map/ppermute | solution.py:12
  91.0 6.1 %collective-permute-done.17 = bf16[128,512]{0,1:T(8,128)(2,1)S(1)} collective-permute-done((bf16[128,512]{0,1:T(8,128)(2,1)S(1)}, bf16[128,512]{0,1:T(8,128)(2,1)S(1)}, u32[]{:S(2)}, u32[]{:S(2)}) %collective-permute-start.17) | collective-permute-done | bytes 131104 | tf_op jit(solution)/shard_map/ppermute | solution.py:12
  98.1 1.5 copy-done.2
  99.5 1.0 convolution_convert_fusion.1
  100.6 1.9 %collective-permute-start.18 = (bf16[3,256]{1,0:T(4,128)(2,1)S(1)}, bf16[3,256]{1,0:T(4,128)(2,1)S(1)}, u32[]{:S(2)}, u32[]{:S(2)}) collective-permute-start(bf16[3,256]{1,0:T(4,128)(2,1)S(1)} %slice.87), channel_id=1, source_target_pairs={{0,32},{32,64},{64,96},{96,128},{128,160},{160,192},{192,224},{224... | collective-permute-start | bytes 4616 | tf_op jit(solution)/shard_map/ppermute | solution.py:83
  102.5 1.0 convolution_convert_fusion
  103.5 4.4 %collective-permute-done.18 = bf16[3,256]{1,0:T(4,128)(2,1)S(1)} collective-permute-done((bf16[3,256]{1,0:T(4,128)(2,1)S(1)}, bf16[3,256]{1,0:T(4,128)(2,1)S(1)}, u32[]{:S(2)}, u32[]{:S(2)}) %collective-permute-start.18) | collective-permute-done | bytes 1568 | tf_op jit(solution)/shard_map/ppermute | solution.py:83
  107.9 0.3 multiply_multiply_fusion
  108.2 1.9 %collective-permute-start.19 = (f32[3,256]{1,0:T(4,128)S(1)}, f32[3,256]{1,0:T(4,128)S(1)}, u32[]{:S(2)}, u32[]{:S(2)}) collective-permute-start(f32[3,256]{1,0:T(4,128)S(1)} %fusion.155), channel_id=1, source_target_pairs={{32,0},{64,32},{96,64},{128,96},{160,128},{192,160},{224,192},{256... | collective-permute-start | bytes 9224 | tf_op jit(solution)/shard_map/ppermute | solution.py:83
  110.1 0.8 fusion.84
  114.7 1.9 %collective-permute-start.27 = (bf16[128,512]{1,0:T(8,128)(2,1)S(1)}, bf16[128,512]{1,0:T(8,128)(2,1)S(1)}, u32[]{:S(2)}, u32[]{:S(2)}) collective-permute-start(bf16[128,512]{1,0:T(8,128)(2,1)S(1)} %fusion.13), channel_id=1, source_target_pairs={{0,30},{2,0},{4,2},{6,4},{8,6},{10,8},{12,10},{14,12},{16,14},{18,... | collective-permute-start | bytes 393224 | tf_op jit(solution)/shard_map/ppermute | solution.py:12
  116.6 0.2 fusion
  116.9 3.9 %collective-permute-start.20 = (bf16[128,512]{1,0:T(8,128)(2,1)S(1)}, bf16[128,512]{1,0:T(8,128)(2,1)S(1)}, u32[]{:S(2)}, u32[]{:S(2)}) collective-permute-start(bf16[128,512]{1,0:T(8,128)(2,1)S(1)} %fusion), channel_id=1, source_target_pairs={{0,2},{2,4},{4,6},{6,8},{8,10},{10,12},{12,14},{14,16},{16,18},{18... | collective-permute-start | bytes 393224 | tf_op jit(solution)/shard_map/ppermute | solution.py:12
  120.8 1.7 collective-permute-done.27
  122.7 3.4 %collective-permute-start.28 = (bf16[128,512]{1,0:T(8,128)(2,1)S(1)}, bf16[128,512]{1,0:T(8,128)(2,1)S(1)}, u32[]{:S(2)}, u32[]{:S(2)}) collective-permute-start(bf16[128,512]{1,0:T(8,128)(2,1)S(1)} %add_convert_fusion.6), channel_id=1, source_target_pairs={{0,30},{2,0},{4,2},{6,4},{8,6},{10,8},{12,10},{14,12},{16,14},{18,... | collective-permute-start | bytes 393224 | tf_op jit(solution)/shard_map/ppermute | solution.py:12
  126.4 2.4 %collective-permute-start.21 = (bf16[128,512]{1,0:T(8,128)(2,1)S(1)}, bf16[128,512]{1,0:T(8,128)(2,1)S(1)}, u32[]{:S(2)}, u32[]{:S(2)}) collective-permute-start(bf16[128,512]{1,0:T(8,128)(2,1)S(1)} %add_convert_fusion.12), channel_id=1, source_target_pairs={{0,2},{2,4},{4,6},{6,8},{8,10},{10,12},{12,14},{14,16},{16,18},{18... | collective-permute-start | bytes 393224 | tf_op jit(solution)/shard_map/ppermute | solution.py:12
  128.8 0.9 collective-permute-done.28
  130.0 4.8 %collective-permute-start.29 = (bf16[128,512]{1,0:T(8,128)(2,1)S(1)}, bf16[128,512]{1,0:T(8,128)(2,1)S(1)}, u32[]{:S(2)}, u32[]{:S(2)}) collective-permute-start(bf16[128,512]{1,0:T(8,128)(2,1)S(1)} %add_convert_fusion.5), channel_id=1, source_target_pairs={{0,30},{2,0},{4,2},{6,4},{8,6},{10,8},{12,10},{14,12},{16,14},{18,... | collective-permute-start | bytes 393224 | tf_op jit(solution)/shard_map/ppermute | solution.py:12
  135.1 1.9 %collective-permute-start.22 = (bf16[128,512]{1,0:T(8,128)(2,1)S(1)}, bf16[128,512]{1,0:T(8,128)(2,1)S(1)}, u32[]{:S(2)}, u32[]{:S(2)}) collective-permute-start(bf16[128,512]{1,0:T(8,128)(2,1)S(1)} %add_convert_fusion.11), channel_id=1, source_target_pairs={{0,2},{2,4},{4,6},{6,8},{8,10},{10,12},{12,14},{14,16},{16,18},{18... | collective-permute-start | bytes 393224 | tf_op jit(solution)/shard_map/ppermute | solution.py:12
  137.0 0.3 collective-permute-done.29
  137.6 5.6 %collective-permute-start.30 = (bf16[128,512]{1,0:T(8,128)(2,1)S(1)}, bf16[128,512]{1,0:T(8,128)(2,1)S(1)}, u32[]{:S(2)}, u32[]{:S(2)}) collective-permute-start(bf16[128,512]{1,0:T(8,128)(2,1)S(1)} %add_convert_fusion.4), channel_id=1, source_target_pairs={{0,30},{2,0},{4,2},{6,4},{8,6},{10,8},{12,10},{14,12},{16,14},{18,... | collective-permute-start | bytes 393224 | tf_op jit(solution)/shard_map/ppermute | solution.py:12
  143.4 1.9 %collective-permute-start.23 = (bf16[128,512]{1,0:T(8,128)(2,1)S(1)}, bf16[128,512]{1,0:T(8,128)(2,1)S(1)}, u32[]{:S(2)}, u32[]{:S(2)}) collective-permute-start(bf16[128,512]{1,0:T(8,128)(2,1)S(1)} %add_convert_fusion.10), channel_id=1, source_target_pairs={{0,2},{2,4},{4,6},{6,8},{8,10},{10,12},{12,14},{14,16},{16,18},{18... | collective-permute-start | bytes 393224 | tf_op jit(solution)/shard_map/ppermute | solution.py:12
  145.3 0.3 collective-permute-done.30
  145.9 5.6 %collective-permute-start.31 = (bf16[128,512]{1,0:T(8,128)(2,1)S(1)}, bf16[128,512]{1,0:T(8,128)(2,1)S(1)}, u32[]{:S(2)}, u32[]{:S(2)}) collective-permute-start(bf16[128,512]{1,0:T(8,128)(2,1)S(1)} %add_convert_fusion.3), channel_id=1, source_target_pairs={{0,30},{2,0},{4,2},{6,4},{8,6},{10,8},{12,10},{14,12},{16,14},{18,... | collective-permute-start | bytes 393224 | tf_op jit(solution)/shard_map/ppermute | solution.py:12
  151.7 1.9 %collective-permute-start.24 = (bf16[128,512]{1,0:T(8,128)(2,1)S(1)}, bf16[128,512]{1,0:T(8,128)(2,1)S(1)}, u32[]{:S(2)}, u32[]{:S(2)}) collective-permute-start(bf16[128,512]{1,0:T(8,128)(2,1)S(1)} %add_convert_fusion.9), channel_id=1, source_target_pairs={{0,2},{2,4},{4,6},{6,8},{8,10},{10,12},{12,14},{14,16},{16,18},{18... | collective-permute-start | bytes 393224 | tf_op jit(solution)/shard_map/ppermute | solution.py:12
  153.6 0.3 collective-permute-done.31
  154.2 5.6 %collective-permute-start.32 = (bf16[128,512]{1,0:T(8,128)(2,1)S(1)}, bf16[128,512]{1,0:T(8,128)(2,1)S(1)}, u32[]{:S(2)}, u32[]{:S(2)}) collective-permute-start(bf16[128,512]{1,0:T(8,128)(2,1)S(1)} %add_convert_fusion.2), channel_id=1, source_target_pairs={{0,30},{2,0},{4,2},{6,4},{8,6},{10,8},{12,10},{14,12},{16,14},{18,... | collective-permute-start | bytes 393224 | tf_op jit(solution)/shard_map/ppermute | solution.py:12
  160.0 1.9 %collective-permute-start.25 = (bf16[128,512]{1,0:T(8,128)(2,1)S(1)}, bf16[128,512]{1,0:T(8,128)(2,1)S(1)}, u32[]{:S(2)}, u32[]{:S(2)}) collective-permute-start(bf16[128,512]{1,0:T(8,128)(2,1)S(1)} %add_convert_fusion.8), channel_id=1, source_target_pairs={{0,2},{2,4},{4,6},{6,8},{8,10},{10,12},{12,14},{14,16},{16,18},{18... | collective-permute-start | bytes 393224 | tf_op jit(solution)/shard_map/ppermute | solution.py:12
  161.9 0.3 collective-permute-done.32
  162.5 5.6 %collective-permute-start.33 = (bf16[128,512]{1,0:T(8,128)(2,1)S(1)}, bf16[128,512]{1,0:T(8,128)(2,1)S(1)}, u32[]{:S(2)}, u32[]{:S(2)}) collective-permute-start(bf16[128,512]{1,0:T(8,128)(2,1)S(1)} %add_convert_fusion.1), channel_id=1, source_target_pairs={{0,30},{2,0},{4,2},{6,4},{8,6},{10,8},{12,10},{14,12},{16,14},{18,... | collective-permute-start | bytes 393224 | tf_op jit(solution)/shard_map/ppermute | solution.py:12
  168.3 1.9 %collective-permute-start.26 = (bf16[128,512]{1,0:T(8,128)(2,1)S(1)}, bf16[128,512]{1,0:T(8,128)(2,1)S(1)}, u32[]{:S(2)}, u32[]{:S(2)}) collective-permute-start(bf16[128,512]{1,0:T(8,128)(2,1)S(1)} %add_convert_fusion.7), channel_id=1, source_target_pairs={{0,2},{2,4},{4,6},{6,8},{8,10},{10,12},{12,14},{14,16},{16,18},{18... | collective-permute-start | bytes 393224 | tf_op jit(solution)/shard_map/ppermute | solution.py:12
  170.2 1.1 collective-permute-done.33
  171.5 5.6 %collective-permute-start.34 = (bf16[128,512]{1,0:T(8,128)(2,1)S(1)}, bf16[128,512]{1,0:T(8,128)(2,1)S(1)}, u32[]{:S(2)}, u32[]{:S(2)}) collective-permute-start(bf16[128,512]{1,0:T(8,128)(2,1)S(1)} %add_convert_fusion), channel_id=1, source_target_pairs={{0,30},{2,0},{4,2},{6,4},{8,6},{10,8},{12,10},{14,12},{16,14},{18,... | collective-permute-start | bytes 393224 | tf_op jit(solution)/shard_map/ppermute | solution.py:12
  177.4 2.3 %collective-permute-done.34 = bf16[128,512]{1,0:T(8,128)(2,1)S(1)} collective-permute-done((bf16[128,512]{1,0:T(8,128)(2,1)S(1)}, bf16[128,512]{1,0:T(8,128)(2,1)S(1)}, u32[]{:S(2)}, u32[]{:S(2)}) %collective-permute-start.34) | collective-permute-done | bytes 131104 | tf_op jit(solution)/shard_map/ppermute | solution.py:12
  179.9 2.4 %collective-permute-start.35 = (bf16[128,256]{1,0:T(8,128)(2,1)S(1)}, bf16[128,256]{1,0:T(8,128)(2,1)S(1)}, u32[]{:S(2)}, u32[]{:S(2)}) collective-permute-start(bf16[128,256]{1,0:T(8,128)(2,1)S(1)} %select_convert_fusion), channel_id=1, source_target_pairs={{0,1},{1,0},{2,3},{3,2},{4,5},{5,4},{6,7},{7,6},{8,9},{9,8},{10,11... | collective-permute-start | bytes 196616 | tf_op jit(solution)/shard_map/ppermute | solution.py:12
  182.4 3.7 %collective-permute-done.35 = bf16[128,256]{1,0:T(8,128)(2,1)S(1)} collective-permute-done((bf16[128,256]{1,0:T(8,128)(2,1)S(1)}, bf16[128,256]{1,0:T(8,128)(2,1)S(1)}, u32[]{:S(2)}, u32[]{:S(2)}) %collective-permute-start.35) | collective-permute-done | bytes 65568 | tf_op jit(solution)/shard_map/ppermute | solution.py:12
  186.1 0.7 add_convert_fusion.13
  (101 shorter events, 8.6 us)
Async XLA Ops:
  0.6 107.3 %copy-start = (bf16[10,256]{1,0:T(8,128)(2,1)S(1)}, bf16[10,256]{1,0:T(8,128)(2,1)}, u32[]{:S(2)}) copy-start(bf16[10,256]{1,0:T(8,128)(2,1)} %param.13) | copy-start | bytes 15364
  1.6 39.2 %collective-permute-start = (bf16[128,256]{0,1:T(8,128)(2,1)S(1)}, bf16[128,256]{0,1:T(8,128)(2,1)S(1)}, u32[]{:S(2)}, u32[]{:S(2)}) collective-permute-start(bf16[128,256]{0,1:T(8,128)(2,1)S(1)} %copy.10), channel_id=1, source_target_pairs={{0,1},{1,0},{2,3},{3,2},{4,5},{5,4},{6,7},{7,6},{8,9},{9,8},{10,11... | collective-permute-start | bytes 196616 | tf_op jit(solution)/shard_map/ppermute | solution.py:12
  5.0 28.6 %collective-permute-start.1 = (bf16[128,256]{0,1:T(8,128)(2,1)S(1)}, bf16[128,256]{0,1:T(8,128)(2,1)S(1)}, u32[]{:S(2)}, u32[]{:S(2)}) collective-permute-start(bf16[128,256]{0,1:T(8,128)(2,1)S(1)} %copy.10), channel_id=1, source_target_pairs={{0,30},{2,0},{4,2},{6,4},{8,6},{10,8},{12,10},{14,12},{16,14},{18,... | collective-permute-start | bytes 196616 | tf_op jit(solution)/shard_map/ppermute | solution.py:12
  23.2 10.4 %collective-permute-start.2 = (bf16[128,256]{0,1:T(8,128)(2,1)S(1)}, bf16[128,256]{0,1:T(8,128)(2,1)S(1)}, u32[]{:S(2)}, u32[]{:S(2)}) collective-permute-start(bf16[128,256]{0,1:T(8,128)(2,1)S(1)} %copy.10), channel_id=1, source_target_pairs={{0,31},{1,30},{2,1},{3,0},{4,3},{5,2},{6,5},{7,4},{8,7},{9,6},{10,... | collective-permute-start | bytes 196616 | tf_op jit(solution)/shard_map/ppermute | solution.py:23
  25.7 13.2 %collective-permute-start.10 = (bf16[128,256]{0,1:T(8,128)(2,1)S(1)}, bf16[128,256]{0,1:T(8,128)(2,1)S(1)}, u32[]{:S(2)}, u32[]{:S(2)}) collective-permute-start(bf16[128,256]{0,1:T(8,128)(2,1)S(1)} %copy.10), channel_id=1, source_target_pairs={{0,3},{1,2},{2,5},{3,4},{4,7},{5,6},{6,9},{7,8},{8,11},{9,10},{10,... | collective-permute-start | bytes 196616 | tf_op jit(solution)/shard_map/ppermute | solution.py:23
  30.0 8.9 %collective-permute-start.9 = (bf16[128,256]{0,1:T(8,128)(2,1)S(1)}, bf16[128,256]{0,1:T(8,128)(2,1)S(1)}, u32[]{:S(2)}, u32[]{:S(2)}) collective-permute-start(bf16[128,256]{0,1:T(8,128)(2,1)S(1)} %copy.10), channel_id=1, source_target_pairs={{0,2},{2,4},{4,6},{6,8},{8,10},{10,12},{12,14},{14,16},{16,18},{18... | collective-permute-start | bytes 196616 | tf_op jit(solution)/shard_map/ppermute | solution.py:12
  33.7 7.6 %collective-permute-start.3 = (bf16[128,512]{0,1:T(8,128)(2,1)S(1)}, bf16[128,512]{0,1:T(8,128)(2,1)S(1)}, u32[]{:S(2)}, u32[]{:S(2)}) collective-permute-start(bf16[128,512]{0,1:T(8,128)(2,1)S(1)} %maximum_select_fusion.2), channel_id=1, source_target_pairs={{0,30},{2,0},{4,2},{6,4},{8,6},{10,8},{12,10},{14,12},{16,14},{18,... | collective-permute-start | bytes 393224 | tf_op jit(solution)/shard_map/ppermute | solution.py:12
  38.9 8.1 %collective-permute-start.11 = (bf16[128,512]{0,1:T(8,128)(2,1)S(1)}, bf16[128,512]{0,1:T(8,128)(2,1)S(1)}, u32[]{:S(2)}, u32[]{:S(2)}) collective-permute-start(bf16[128,512]{0,1:T(8,128)(2,1)S(1)} %maximum_select_fusion.3), channel_id=1, source_target_pairs={{0,2},{2,4},{4,6},{6,8},{8,10},{10,12},{12,14},{14,16},{16,18},{18... | collective-permute-start | bytes 393224 | tf_op jit(solution)/shard_map/ppermute | solution.py:12
  41.3 8.1 %collective-permute-start.4 = (bf16[128,512]{0,1:T(8,128)(2,1)S(1)}, bf16[128,512]{0,1:T(8,128)(2,1)S(1)}, u32[]{:S(2)}, u32[]{:S(2)}) collective-permute-start(bf16[128,512]{0,1:T(8,128)(2,1)S(1)} %collective-permute-done.3), channel_id=1, source_target_pairs={{0,30},{2,0},{4,2},{6,4},{8,6},{10,8},{12,10},{14,12},{16,14},{18,... | collective-permute-start | bytes 393224 | tf_op jit(solution)/shard_map/ppermute | solution.py:12
  47.0 8.1 %collective-permute-start.12 = (bf16[128,512]{0,1:T(8,128)(2,1)S(1)}, bf16[128,512]{0,1:T(8,128)(2,1)S(1)}, u32[]{:S(2)}, u32[]{:S(2)}) collective-permute-start(bf16[128,512]{0,1:T(8,128)(2,1)S(1)} %collective-permute-done.11), channel_id=1, source_target_pairs={{0,2},{2,4},{4,6},{6,8},{8,10},{10,12},{12,14},{14,16},{16,18},{18... | collective-permute-start | bytes 393224 | tf_op jit(solution)/shard_map/ppermute | solution.py:12
  49.4 8.1 %collective-permute-start.5 = (bf16[128,512]{0,1:T(8,128)(2,1)S(1)}, bf16[128,512]{0,1:T(8,128)(2,1)S(1)}, u32[]{:S(2)}, u32[]{:S(2)}) collective-permute-start(bf16[128,512]{0,1:T(8,128)(2,1)S(1)} %collective-permute-done.4), channel_id=1, source_target_pairs={{0,30},{2,0},{4,2},{6,4},{8,6},{10,8},{12,10},{14,12},{16,14},{18,... | collective-permute-start | bytes 393224 | tf_op jit(solution)/shard_map/ppermute | solution.py:12
  55.0 8.1 %collective-permute-start.13 = (bf16[128,512]{0,1:T(8,128)(2,1)S(1)}, bf16[128,512]{0,1:T(8,128)(2,1)S(1)}, u32[]{:S(2)}, u32[]{:S(2)}) collective-permute-start(bf16[128,512]{0,1:T(8,128)(2,1)S(1)} %collective-permute-done.12), channel_id=1, source_target_pairs={{0,2},{2,4},{4,6},{6,8},{8,10},{10,12},{12,14},{14,16},{16,18},{18... | collective-permute-start | bytes 393224 | tf_op jit(solution)/shard_map/ppermute | solution.py:12
  57.5 8.5 %collective-permute-start.6 = (bf16[128,512]{0,1:T(8,128)(2,1)S(1)}, bf16[128,512]{0,1:T(8,128)(2,1)S(1)}, u32[]{:S(2)}, u32[]{:S(2)}) collective-permute-start(bf16[128,512]{0,1:T(8,128)(2,1)S(1)} %collective-permute-done.5), channel_id=1, source_target_pairs={{0,30},{2,0},{4,2},{6,4},{8,6},{10,8},{12,10},{14,12},{16,14},{18,... | collective-permute-start | bytes 393224 | tf_op jit(solution)/shard_map/ppermute | solution.py:12
  63.1 8.9 %collective-permute-start.14 = (bf16[128,512]{0,1:T(8,128)(2,1)S(1)}, bf16[128,512]{0,1:T(8,128)(2,1)S(1)}, u32[]{:S(2)}, u32[]{:S(2)}) collective-permute-start(bf16[128,512]{0,1:T(8,128)(2,1)S(1)} %collective-permute-done.13), channel_id=1, source_target_pairs={{0,2},{2,4},{4,6},{6,8},{8,10},{10,12},{12,14},{14,16},{16,18},{18... | collective-permute-start | bytes 393224 | tf_op jit(solution)/shard_map/ppermute | solution.py:12
  66.0 9.2 %collective-permute-start.7 = (bf16[128,512]{0,1:T(8,128)(2,1)S(1)}, bf16[128,512]{0,1:T(8,128)(2,1)S(1)}, u32[]{:S(2)}, u32[]{:S(2)}) collective-permute-start(bf16[128,512]{0,1:T(8,128)(2,1)S(1)} %collective-permute-done.6), channel_id=1, source_target_pairs={{0,30},{2,0},{4,2},{6,4},{8,6},{10,8},{12,10},{14,12},{16,14},{18,... | collective-permute-start | bytes 393224 | tf_op jit(solution)/shard_map/ppermute | solution.py:12
  72.0 8.9 %collective-permute-start.15 = (bf16[128,512]{0,1:T(8,128)(2,1)S(1)}, bf16[128,512]{0,1:T(8,128)(2,1)S(1)}, u32[]{:S(2)}, u32[]{:S(2)}) collective-permute-start(bf16[128,512]{0,1:T(8,128)(2,1)S(1)} %collective-permute-done.14), channel_id=1, source_target_pairs={{0,2},{2,4},{4,6},{6,8},{8,10},{10,12},{12,14},{14,16},{16,18},{18... | collective-permute-start | bytes 393224 | tf_op jit(solution)/shard_map/ppermute | solution.py:12
  75.2 15.7 %collective-permute-start.8 = (bf16[128,512]{0,1:T(8,128)(2,1)S(1)}, bf16[128,512]{0,1:T(8,128)(2,1)S(1)}, u32[]{:S(2)}, u32[]{:S(2)}) collective-permute-start(bf16[128,512]{0,1:T(8,128)(2,1)S(1)} %collective-permute-done.7), channel_id=1, source_target_pairs={{0,30},{2,0},{4,2},{6,4},{8,6},{10,8},{12,10},{14,12},{16,14},{18,... | collective-permute-start | bytes 393224 | tf_op jit(solution)/shard_map/ppermute | solution.py:12
  80.9 8.1 %collective-permute-start.16 = (bf16[128,512]{0,1:T(8,128)(2,1)S(1)}, bf16[128,512]{0,1:T(8,128)(2,1)S(1)}, u32[]{:S(2)}, u32[]{:S(2)}) collective-permute-start(bf16[128,512]{0,1:T(8,128)(2,1)S(1)} %collective-permute-done.15), channel_id=1, source_target_pairs={{0,2},{2,4},{4,6},{6,8},{8,10},{10,12},{12,14},{14,16},{16,18},{18... | collective-permute-start | bytes 393224 | tf_op jit(solution)/shard_map/ppermute | solution.py:12
  89.0 8.1 %collective-permute-start.17 = (bf16[128,512]{0,1:T(8,128)(2,1)S(1)}, bf16[128,512]{0,1:T(8,128)(2,1)S(1)}, u32[]{:S(2)}, u32[]{:S(2)}) collective-permute-start(bf16[128,512]{0,1:T(8,128)(2,1)S(1)} %collective-permute-done.16), channel_id=1, source_target_pairs={{0,2},{2,4},{4,6},{6,8},{8,10},{10,12},{12,14},{14,16},{16,18},{18... | collective-permute-start | bytes 393224 | tf_op jit(solution)/shard_map/ppermute | solution.py:12
  97.3 2.2 %copy-start.2 = (bf16[8192,256]{1,0:T(8,128)(2,1)S(1)}, bf16[8192,256]{1,0:T(8,128)(2,1)}, u32[]{:S(2)}) copy-start(bf16[8192,256]{1,0:T(8,128)(2,1)} %param.10) | copy-start | bytes 12582916
  98.1 4.4 %copy-start.1 = (bf16[8192,256]{1,0:T(8,128)(2,1)S(1)}, bf16[8192,256]{1,0:T(8,128)(2,1)}, u32[]{:S(2)}) copy-start(bf16[8192,256]{1,0:T(8,128)(2,1)} %param.9) | copy-start | bytes 12582916
  100.5 7.4 %copy-start.3 = (f32[256]{0:T(256)S(1)}, f32[256]{0:T(256)}, u32[]{:S(2)}) copy-start(f32[256]{0:T(256)} %param.12) | copy-start | bytes 3076
  100.5 7.4 %copy-start.4 = (s32[128]{0:T(128)S(1)}, s32[128]{0:T(128)}, u32[]{:S(2)}) copy-start(s32[128]{0:T(128)} %param.14) | copy-start | bytes 1540
  100.6 7.3 %collective-permute-start.18 = (bf16[3,256]{1,0:T(4,128)(2,1)S(1)}, bf16[3,256]{1,0:T(4,128)(2,1)S(1)}, u32[]{:S(2)}, u32[]{:S(2)}) collective-permute-start(bf16[3,256]{1,0:T(4,128)(2,1)S(1)} %slice.87), channel_id=1, source_target_pairs={{0,32},{32,64},{64,96},{96,128},{128,160},{160,192},{192,224},{224... | collective-permute-start | bytes 4616 | tf_op jit(solution)/shard_map/ppermute | solution.py:83
  108.2 6.2 %collective-permute-start.19 = (f32[3,256]{1,0:T(4,128)S(1)}, f32[3,256]{1,0:T(4,128)S(1)}, u32[]{:S(2)}, u32[]{:S(2)}) collective-permute-start(f32[3,256]{1,0:T(4,128)S(1)} %fusion.155), channel_id=1, source_target_pairs={{32,0},{64,32},{96,64},{128,96},{160,128},{192,160},{224,192},{256... | collective-permute-start | bytes 9224 | tf_op jit(solution)/shard_map/ppermute | solution.py:83
  114.7 7.8 %collective-permute-start.27 = (bf16[128,512]{1,0:T(8,128)(2,1)S(1)}, bf16[128,512]{1,0:T(8,128)(2,1)S(1)}, u32[]{:S(2)}, u32[]{:S(2)}) collective-permute-start(bf16[128,512]{1,0:T(8,128)(2,1)S(1)} %fusion.13), channel_id=1, source_target_pairs={{0,30},{2,0},{4,2},{6,4},{8,6},{10,8},{12,10},{14,12},{16,14},{18,... | collective-permute-start | bytes 393224 | tf_op jit(solution)/shard_map/ppermute | solution.py:12
  116.9 9.3 %collective-permute-start.20 = (bf16[128,512]{1,0:T(8,128)(2,1)S(1)}, bf16[128,512]{1,0:T(8,128)(2,1)S(1)}, u32[]{:S(2)}, u32[]{:S(2)}) collective-permute-start(bf16[128,512]{1,0:T(8,128)(2,1)S(1)} %fusion), channel_id=1, source_target_pairs={{0,2},{2,4},{4,6},{6,8},{8,10},{10,12},{12,14},{14,16},{16,18},{18... | collective-permute-start | bytes 393224 | tf_op jit(solution)/shard_map/ppermute | solution.py:12
  122.7 7.0 %collective-permute-start.28 = (bf16[128,512]{1,0:T(8,128)(2,1)S(1)}, bf16[128,512]{1,0:T(8,128)(2,1)S(1)}, u32[]{:S(2)}, u32[]{:S(2)}) collective-permute-start(bf16[128,512]{1,0:T(8,128)(2,1)S(1)} %add_convert_fusion.6), channel_id=1, source_target_pairs={{0,30},{2,0},{4,2},{6,4},{8,6},{10,8},{12,10},{14,12},{16,14},{18,... | collective-permute-start | bytes 393224 | tf_op jit(solution)/shard_map/ppermute | solution.py:12
  126.4 8.4 %collective-permute-start.21 = (bf16[128,512]{1,0:T(8,128)(2,1)S(1)}, bf16[128,512]{1,0:T(8,128)(2,1)S(1)}, u32[]{:S(2)}, u32[]{:S(2)}) collective-permute-start(bf16[128,512]{1,0:T(8,128)(2,1)S(1)} %add_convert_fusion.12), channel_id=1, source_target_pairs={{0,2},{2,4},{4,6},{6,8},{8,10},{10,12},{12,14},{14,16},{16,18},{18... | collective-permute-start | bytes 393224 | tf_op jit(solution)/shard_map/ppermute | solution.py:12
  130.0 7.3 %collective-permute-start.29 = (bf16[128,512]{1,0:T(8,128)(2,1)S(1)}, bf16[128,512]{1,0:T(8,128)(2,1)S(1)}, u32[]{:S(2)}, u32[]{:S(2)}) collective-permute-start(bf16[128,512]{1,0:T(8,128)(2,1)S(1)} %add_convert_fusion.5), channel_id=1, source_target_pairs={{0,30},{2,0},{4,2},{6,4},{8,6},{10,8},{12,10},{14,12},{16,14},{18,... | collective-permute-start | bytes 393224 | tf_op jit(solution)/shard_map/ppermute | solution.py:12
  135.1 8.1 %collective-permute-start.22 = (bf16[128,512]{1,0:T(8,128)(2,1)S(1)}, bf16[128,512]{1,0:T(8,128)(2,1)S(1)}, u32[]{:S(2)}, u32[]{:S(2)}) collective-permute-start(bf16[128,512]{1,0:T(8,128)(2,1)S(1)} %add_convert_fusion.11), channel_id=1, source_target_pairs={{0,2},{2,4},{4,6},{6,8},{8,10},{10,12},{12,14},{14,16},{16,18},{18... | collective-permute-start | bytes 393224 | tf_op jit(solution)/shard_map/ppermute | solution.py:12
  137.6 8.1 %collective-permute-start.30 = (bf16[128,512]{1,0:T(8,128)(2,1)S(1)}, bf16[128,512]{1,0:T(8,128)(2,1)S(1)}, u32[]{:S(2)}, u32[]{:S(2)}) collective-permute-start(bf16[128,512]{1,0:T(8,128)(2,1)S(1)} %add_convert_fusion.4), channel_id=1, source_target_pairs={{0,30},{2,0},{4,2},{6,4},{8,6},{10,8},{12,10},{14,12},{16,14},{18,... | collective-permute-start | bytes 393224 | tf_op jit(solution)/shard_map/ppermute | solution.py:12
  143.4 8.1 %collective-permute-start.23 = (bf16[128,512]{1,0:T(8,128)(2,1)S(1)}, bf16[128,512]{1,0:T(8,128)(2,1)S(1)}, u32[]{:S(2)}, u32[]{:S(2)}) collective-permute-start(bf16[128,512]{1,0:T(8,128)(2,1)S(1)} %add_convert_fusion.10), channel_id=1, source_target_pairs={{0,2},{2,4},{4,6},{6,8},{8,10},{10,12},{12,14},{14,16},{16,18},{18... | collective-permute-start | bytes 393224 | tf_op jit(solution)/shard_map/ppermute | solution.py:12
  145.9 8.1 %collective-permute-start.31 = (bf16[128,512]{1,0:T(8,128)(2,1)S(1)}, bf16[128,512]{1,0:T(8,128)(2,1)S(1)}, u32[]{:S(2)}, u32[]{:S(2)}) collective-permute-start(bf16[128,512]{1,0:T(8,128)(2,1)S(1)} %add_convert_fusion.3), channel_id=1, source_target_pairs={{0,30},{2,0},{4,2},{6,4},{8,6},{10,8},{12,10},{14,12},{16,14},{18,... | collective-permute-start | bytes 393224 | tf_op jit(solution)/shard_map/ppermute | solution.py:12
  151.7 8.1 %collective-permute-start.24 = (bf16[128,512]{1,0:T(8,128)(2,1)S(1)}, bf16[128,512]{1,0:T(8,128)(2,1)S(1)}, u32[]{:S(2)}, u32[]{:S(2)}) collective-permute-start(bf16[128,512]{1,0:T(8,128)(2,1)S(1)} %add_convert_fusion.9), channel_id=1, source_target_pairs={{0,2},{2,4},{4,6},{6,8},{8,10},{10,12},{12,14},{14,16},{16,18},{18... | collective-permute-start | bytes 393224 | tf_op jit(solution)/shard_map/ppermute | solution.py:12
  154.2 8.1 %collective-permute-start.32 = (bf16[128,512]{1,0:T(8,128)(2,1)S(1)}, bf16[128,512]{1,0:T(8,128)(2,1)S(1)}, u32[]{:S(2)}, u32[]{:S(2)}) collective-permute-start(bf16[128,512]{1,0:T(8,128)(2,1)S(1)} %add_convert_fusion.2), channel_id=1, source_target_pairs={{0,30},{2,0},{4,2},{6,4},{8,6},{10,8},{12,10},{14,12},{16,14},{18,... | collective-permute-start | bytes 393224 | tf_op jit(solution)/shard_map/ppermute | solution.py:12
  160.0 8.1 %collective-permute-start.25 = (bf16[128,512]{1,0:T(8,128)(2,1)S(1)}, bf16[128,512]{1,0:T(8,128)(2,1)S(1)}, u32[]{:S(2)}, u32[]{:S(2)}) collective-permute-start(bf16[128,512]{1,0:T(8,128)(2,1)S(1)} %add_convert_fusion.8), channel_id=1, source_target_pairs={{0,2},{2,4},{4,6},{6,8},{8,10},{10,12},{12,14},{14,16},{16,18},{18... | collective-permute-start | bytes 393224 | tf_op jit(solution)/shard_map/ppermute | solution.py:12
  162.5 8.8 %collective-permute-start.33 = (bf16[128,512]{1,0:T(8,128)(2,1)S(1)}, bf16[128,512]{1,0:T(8,128)(2,1)S(1)}, u32[]{:S(2)}, u32[]{:S(2)}) collective-permute-start(bf16[128,512]{1,0:T(8,128)(2,1)S(1)} %add_convert_fusion.1), channel_id=1, source_target_pairs={{0,30},{2,0},{4,2},{6,4},{8,6},{10,8},{12,10},{14,12},{16,14},{18,... | collective-permute-start | bytes 393224 | tf_op jit(solution)/shard_map/ppermute | solution.py:12
  168.3 9.1 %collective-permute-start.26 = (bf16[128,512]{1,0:T(8,128)(2,1)S(1)}, bf16[128,512]{1,0:T(8,128)(2,1)S(1)}, u32[]{:S(2)}, u32[]{:S(2)}) collective-permute-start(bf16[128,512]{1,0:T(8,128)(2,1)S(1)} %add_convert_fusion.7), channel_id=1, source_target_pairs={{0,2},{2,4},{4,6},{6,8},{8,10},{10,12},{12,14},{14,16},{16,18},{18... | collective-permute-start | bytes 393224 | tf_op jit(solution)/shard_map/ppermute | solution.py:12
  171.5 8.1 %collective-permute-start.34 = (bf16[128,512]{1,0:T(8,128)(2,1)S(1)}, bf16[128,512]{1,0:T(8,128)(2,1)S(1)}, u32[]{:S(2)}, u32[]{:S(2)}) collective-permute-start(bf16[128,512]{1,0:T(8,128)(2,1)S(1)} %add_convert_fusion), channel_id=1, source_target_pairs={{0,30},{2,0},{4,2},{6,4},{8,6},{10,8},{12,10},{14,12},{16,14},{18,... | collective-permute-start | bytes 393224 | tf_op jit(solution)/shard_map/ppermute | solution.py:12
  179.9 6.2 %collective-permute-start.35 = (bf16[128,256]{1,0:T(8,128)(2,1)S(1)}, bf16[128,256]{1,0:T(8,128)(2,1)S(1)}, u32[]{:S(2)}, u32[]{:S(2)}) collective-permute-start(bf16[128,256]{1,0:T(8,128)(2,1)S(1)} %select_convert_fusion), channel_id=1, source_target_pairs={{0,1},{1,0},{2,3},{3,2},{4,5},{5,4},{6,7},{7,6},{8,9},{9,8},{10,11... | collective-permute-start | bytes 196616 | tf_op jit(solution)/shard_map/ppermute | solution.py:12

commit v8 on v6

--- a/solution.py
+++ b/solution.py
@@ -37,24 +37,40 @@
     return ordered.transpose(1, 0, 2).reshape(rows, -1)
 
 
-def scatter_features(make_block):
+def scatter_features(make_block, operands):
     count = lax.axis_size("tz")
     here = lax.axis_index("tz")
-    own = lambda offset: make_block((here + offset) % count).astype(jnp.float32)
+
+    def own(offset, after=None):
+        used = operands if after is None else lax.optimization_barrier((operands, after))[0]
+        return make_block((here + offset) % count, *used).astype(jnp.float32)
+
     right = count - 1 - count // 2
     left = count // 2
     total = None
+    last = None
     if right > 0:
         acc = own(right)
+        coming = own(right - 1) if right > 1 else None
         for step in range(1, right):
-            acc = hop(acc, 1) + own(right - step)
+            got = hop(acc, 1)
+            acc = got + coming
+            if step + 1 < right:
+                coming = own(right - step - 1, got)
         total = hop(acc, 1)
+        last = total
     if left > 0:
         acc = own(left)
+        coming = own(left + 1) if left > 1 else None
         for step in range(1, left):
-            acc = hop(acc, -1) + own(left + step)
-        total = hop(acc, -1) if total is None else total + hop(acc, -1)
-    total = own(0) if total is None else total + own(0)
+            got = hop(acc, -1)
+            acc = got + coming
+            if step + 1 < left:
+                coming = own(left + step + 1, got)
+        arrived_left = hop(acc, -1)
+        total = arrived_left if total is None else total + arrived_left
+        last = acc
+    total = own(0, last) + (0.0 if total is None else total)
     half = total.shape[1] // 2
     first = lax.axis_index("tx") == 0
     mine = jnp.where(first, total[:, :half], total[:, half:])
@@ -122,14 +138,14 @@
     spec = (((1,), (1,)), ((), ()))
     width = 2 * tokens.shape[1]
 
-    def block_terms(place):
+    def block_terms(place, dgate16, dxin16):
         gate_rows = lax.dynamic_slice_in_dim(w_gate, place * width, width, 0)
         conv_rows = lax.dynamic_slice_in_dim(w_conv_in, place * width, width, 0)
         part = lax.dot_general(dgate16, gate_rows, spec, preferred_element_type=jnp.float32)
         part = part + lax.dot_general(dxin16, conv_rows, spec, preferred_element_type=jnp.float32)
         return part.astype(jnp.bfloat16)
 
-    d_tokens = scatter_features(block_terms)
+    d_tokens = scatter_features(block_terms, (dgate16, dxin16))
     return (gated, d_tokens)
 
 

time: 184 us -> 182 us (0.989)
  transfers between devices with their start and end apart: 34 -> 34, of which waited for: 19 -> 21; matrix products, arithmetic and copies ran while one was open for 6% -> 6% of each run, Pallas kernels for 0% -> 0%
where the time goes in v8:
time: 182 us; the launch traced here: 180 us
  starting transfers between devices  130 us (71%)
  waiting for transfers between devices  33.1 us (18%)
  matrix products  9.52 us (5%)
  local copies, waits for them, and re-layouts  4.14 us (2%)
  other arithmetic  2.27 us (1%)
  between operations  1.83 us (1%)
    ppermute x32, starting transfers between devices, shifted(): lax.ppermute(block, axis, [(i, (i + distance) % size) for i in range(size)])  126 us
    ppermute x32, waiting for transfers between devices, shifted(): lax.ppermute(block, axis, [(i, (i + distance) % size) for i in range(size)])  28.7 us
    ppermute x2, waiting for transfers between devices, passed_along(): return lax.ppermute(block, axis, route)  4.38 us
    ppermute x2, starting transfers between devices, passed_along(): return lax.ppermute(block, axis, route)  3.84 us
    dot_general x16, matrix products, block_terms(): lax.dot_general(dxin16, conv_rows, spec, preferred_element_type=jnp.float32)  3.65 us
  transfers between devices with their start and end apart: 34, of which 21 were waited for; matrix products, arithmetic and copies ran while one was open for 6% of the time, Pallas kernels for 0%

profile of v8, /device:TPU:56, one launch (start us, length us, event | category | flops | bytes accessed | tf_op | source)
XLA Modules:
  0.0 180.4 jit_solution(17310989419181939034)
XLA Ops:
  0.6 1.0 copy.10
  1.6 3.4 %collective-permute-start = (bf16[128,256]{0,1:T(8,128)(2,1)S(1)}, bf16[128,256]{0,1:T(8,128)(2,1)S(1)}, u32[]{:S(2)}, u32[]{:S(2)}) collective-permute-start(bf16[128,256]{0,1:T(8,128)(2,1)S(1)} %copy.10), channel_id=1, source_target_pairs={{0,1},{1,0},{2,3},{3,2},{4,5},{5,4},{6,7},{7,6},{8,9},{9,8},{10,11... | collective-permute-start | bytes 196616 | tf_op jit(solution)/shard_map/ppermute | solution.py:12
  5.0 0.8 fusion.159
  5.9 1.9 %collective-permute-done = bf16[128,256]{0,1:T(8,128)(2,1)S(1)} collective-permute-done((bf16[128,256]{0,1:T(8,128)(2,1)S(1)}, bf16[128,256]{0,1:T(8,128)(2,1)S(1)}, u32[]{:S(2)}, u32[]{:S(2)}) %collective-permute-start) | collective-permute-done | bytes 65568 | tf_op jit(solution)/shard_map/ppermute | solution.py:12
  7.8 18.2 %collective-permute-start.1 = (bf16[128,512]{0,1:T(8,128)(2,1)S(1)}, bf16[128,512]{0,1:T(8,128)(2,1)S(1)}, u32[]{:S(2)}, u32[]{:S(2)}) collective-permute-start(bf16[128,512]{0,1:T(8,128)(2,1)S(1)} %maximum_select_fusion.1), channel_id=1, source_target_pairs={{0,30},{2,0},{4,2},{6,4},{8,6},{10,8},{12,10},{14,12},{16,14},{18,... | collective-permute-start | bytes 393224 | tf_op jit(solution)/shard_map/ppermute | solution.py:12
  26.0 1.9 %collective-permute-start.8 = (bf16[128,512]{0,1:T(8,128)(2,1)S(1)}, bf16[128,512]{0,1:T(8,128)(2,1)S(1)}, u32[]{:S(2)}, u32[]{:S(2)}) collective-permute-start(bf16[128,512]{0,1:T(8,128)(2,1)S(1)} %maximum_select_fusion.1), channel_id=1, source_target_pairs={{0,2},{2,4},{4,6},{6,8},{8,10},{10,12},{12,14},{14,16},{16,18},{18... | collective-permute-start | bytes 393224 | tf_op jit(solution)/shard_map/ppermute | solution.py:12
  28.2 0.7 convert_element_type.215
  28.9 5.2 %collective-permute-start.2 = (bf16[128,512]{0,1:T(8,128)(2,1)S(1)}, bf16[128,512]{0,1:T(8,128)(2,1)S(1)}, u32[]{:S(2)}, u32[]{:S(2)}) collective-permute-start(bf16[128,512]{0,1:T(8,128)(2,1)S(1)} %collective-permute-done.1), channel_id=1, source_target_pairs={{0,30},{2,0},{4,2},{6,4},{8,6},{10,8},{12,10},{14,12},{16,14},{18,... | collective-permute-start | bytes 393224 | tf_op jit(solution)/shard_map/ppermute | solution.py:12
  34.1 1.9 %collective-permute-start.9 = (bf16[128,512]{0,1:T(8,128)(2,1)S(1)}, bf16[128,512]{0,1:T(8,128)(2,1)S(1)}, u32[]{:S(2)}, u32[]{:S(2)}) collective-permute-start(bf16[128,512]{0,1:T(8,128)(2,1)S(1)} %collective-permute-done.8), channel_id=1, source_target_pairs={{0,2},{2,4},{4,6},{6,8},{8,10},{10,12},{12,14},{14,16},{16,18},{18... | collective-permute-start | bytes 393224 | tf_op jit(solution)/shard_map/ppermute | solution.py:12
  36.1 0.5 collective-permute-done.2
  36.6 5.6 %collective-permute-start.3 = (bf16[128,512]{0,1:T(8,128)(2,1)S(1)}, bf16[128,512]{0,1:T(8,128)(2,1)S(1)}, u32[]{:S(2)}, u32[]{:S(2)}) collective-permute-start(bf16[128,512]{0,1:T(8,128)(2,1)S(1)} %collective-permute-done.2), channel_id=1, source_target_pairs={{0,30},{2,0},{4,2},{6,4},{8,6},{10,8},{12,10},{14,12},{16,14},{18,... | collective-permute-start | bytes 393224 | tf_op jit(solution)/shard_map/ppermute | solution.py:12
  42.2 1.9 %collective-permute-start.10 = (bf16[128,512]{0,1:T(8,128)(2,1)S(1)}, bf16[128,512]{0,1:T(8,128)(2,1)S(1)}, u32[]{:S(2)}, u32[]{:S(2)}) collective-permute-start(bf16[128,512]{0,1:T(8,128)(2,1)S(1)} %collective-permute-done.9), channel_id=1, source_target_pairs={{0,2},{2,4},{4,6},{6,8},{8,10},{10,12},{12,14},{14,16},{16,18},{18... | collective-permute-start | bytes 393224 | tf_op jit(solution)/shard_map/ppermute | solution.py:12
  44.1 0.5 collective-permute-done.3
  44.7 5.6 %collective-permute-start.4 = (bf16[128,512]{0,1:T(8,128)(2,1)S(1)}, bf16[128,512]{0,1:T(8,128)(2,1)S(1)}, u32[]{:S(2)}, u32[]{:S(2)}) collective-permute-start(bf16[128,512]{0,1:T(8,128)(2,1)S(1)} %collective-permute-done.3), channel_id=1, source_target_pairs={{0,30},{2,0},{4,2},{6,4},{8,6},{10,8},{12,10},{14,12},{16,14},{18,... | collective-permute-start | bytes 393224 | tf_op jit(solution)/shard_map/ppermute | solution.py:12
  50.2 1.9 %collective-permute-start.11 = (bf16[128,512]{0,1:T(8,128)(2,1)S(1)}, bf16[128,512]{0,1:T(8,128)(2,1)S(1)}, u32[]{:S(2)}, u32[]{:S(2)}) collective-permute-start(bf16[128,512]{0,1:T(8,128)(2,1)S(1)} %collective-permute-done.10), channel_id=1, source_target_pairs={{0,2},{2,4},{4,6},{6,8},{8,10},{10,12},{12,14},{14,16},{16,18},{18... | collective-permute-start | bytes 393224 | tf_op jit(solution)/shard_map/ppermute | solution.py:12
  52.2 0.5 collective-permute-done.4
  52.7 5.6 %collective-permute-start.5 = (bf16[128,512]{0,1:T(8,128)(2,1)S(1)}, bf16[128,512]{0,1:T(8,128)(2,1)S(1)}, u32[]{:S(2)}, u32[]{:S(2)}) collective-permute-start(bf16[128,512]{0,1:T(8,128)(2,1)S(1)} %collective-permute-done.4), channel_id=1, source_target_pairs={{0,30},{2,0},{4,2},{6,4},{8,6},{10,8},{12,10},{14,12},{16,14},{18,... | collective-permute-start | bytes 393224 | tf_op jit(solution)/shard_map/ppermute | solution.py:12
  58.3 1.9 %collective-permute-start.12 = (bf16[128,512]{0,1:T(8,128)(2,1)S(1)}, bf16[128,512]{0,1:T(8,128)(2,1)S(1)}, u32[]{:S(2)}, u32[]{:S(2)}) collective-permute-start(bf16[128,512]{0,1:T(8,128)(2,1)S(1)} %collective-permute-done.11), channel_id=1, source_target_pairs={{0,2},{2,4},{4,6},{6,8},{8,10},{10,12},{12,14},{14,16},{16,18},{18... | collective-permute-start | bytes 393224 | tf_op jit(solution)/shard_map/ppermute | solution.py:12
  60.2 1.4 collective-permute-done.5
  61.7 5.6 %collective-permute-start.6 = (bf16[128,512]{0,1:T(8,128)(2,1)S(1)}, bf16[128,512]{0,1:T(8,128)(2,1)S(1)}, u32[]{:S(2)}, u32[]{:S(2)}) collective-permute-start(bf16[128,512]{0,1:T(8,128)(2,1)S(1)} %collective-permute-done.5), channel_id=1, source_target_pairs={{0,30},{2,0},{4,2},{6,4},{8,6},{10,8},{12,10},{14,12},{16,14},{18,... | collective-permute-start | bytes 393224 | tf_op jit(solution)/shard_map/ppermute | solution.py:12
  67.2 0.2 collective-permute-done.12
  67.5 1.9 %collective-permute-start.13 = (bf16[128,512]{0,1:T(8,128)(2,1)S(1)}, bf16[128,512]{0,1:T(8,128)(2,1)S(1)}, u32[]{:S(2)}, u32[]{:S(2)}) collective-permute-start(bf16[128,512]{0,1:T(8,128)(2,1)S(1)} %collective-permute-done.12), channel_id=1, source_target_pairs={{0,2},{2,4},{4,6},{6,8},{8,10},{10,12},{12,14},{14,16},{16,18},{18... | collective-permute-start | bytes 393224 | tf_op jit(solution)/shard_map/ppermute | solution.py:12
  69.4 1.0 collective-permute-done.6
  70.5 5.6 %collective-permute-start.7 = (bf16[128,512]{0,1:T(8,128)(2,1)S(1)}, bf16[128,512]{0,1:T(8,128)(2,1)S(1)}, u32[]{:S(2)}, u32[]{:S(2)}) collective-permute-start(bf16[128,512]{0,1:T(8,128)(2,1)S(1)} %collective-permute-done.6), channel_id=1, source_target_pairs={{0,30},{2,0},{4,2},{6,4},{8,6},{10,8},{12,10},{14,12},{16,14},{18,... | collective-permute-start | bytes 393224 | tf_op jit(solution)/shard_map/ppermute | solution.py:12
  76.1 1.9 %collective-permute-start.14 = (bf16[128,512]{0,1:T(8,128)(2,1)S(1)}, bf16[128,512]{0,1:T(8,128)(2,1)S(1)}, u32[]{:S(2)}, u32[]{:S(2)}) collective-permute-start(bf16[128,512]{0,1:T(8,128)(2,1)S(1)} %collective-permute-done.13), channel_id=1, source_target_pairs={{0,2},{2,4},{4,6},{6,8},{8,10},{10,12},{12,14},{14,16},{16,18},{18... | collective-permute-start | bytes 393224 | tf_op jit(solution)/shard_map/ppermute | solution.py:12
  78.0 6.1 %collective-permute-done.14 = bf16[128,512]{0,1:T(8,128)(2,1)S(1)} collective-permute-done((bf16[128,512]{0,1:T(8,128)(2,1)S(1)}, bf16[128,512]{0,1:T(8,128)(2,1)S(1)}, u32[]{:S(2)}, u32[]{:S(2)}) %collective-permute-start.14) | collective-permute-done | bytes 131104 | tf_op jit(solution)/shard_map/ppermute | solution.py:12
  84.2 1.9 %collective-permute-start.15 = (bf16[128,512]{0,1:T(8,128)(2,1)S(1)}, bf16[128,512]{0,1:T(8,128)(2,1)S(1)}, u32[]{:S(2)}, u32[]{:S(2)}) collective-permute-start(bf16[128,512]{0,1:T(8,128)(2,1)S(1)} %collective-permute-done.14), channel_id=1, source_target_pairs={{0,2},{2,4},{4,6},{6,8},{8,10},{10,12},{12,14},{14,16},{16,18},{18... | collective-permute-start | bytes 393224 | tf_op jit(solution)/shard_map/ppermute | solution.py:12
  86.1 6.1 %collective-permute-done.15 = bf16[128,512]{0,1:T(8,128)(2,1)S(1)} collective-permute-done((bf16[128,512]{0,1:T(8,128)(2,1)S(1)}, bf16[128,512]{0,1:T(8,128)(2,1)S(1)}, u32[]{:S(2)}, u32[]{:S(2)}) %collective-permute-start.15) | collective-permute-done | bytes 131104 | tf_op jit(solution)/shard_map/ppermute | solution.py:12
  93.1 1.5 copy-done.2
  94.6 1.0 convolution_convert_fusion.1
  95.7 1.9 %collective-permute-start.16 = (bf16[3,256]{1,0:T(4,128)(2,1)S(1)}, bf16[3,256]{1,0:T(4,128)(2,1)S(1)}, u32[]{:S(2)}, u32[]{:S(2)}) collective-permute-start(bf16[3,256]{1,0:T(4,128)(2,1)S(1)} %slice.87), channel_id=1, source_target_pairs={{0,32},{32,64},{64,96},{96,128},{128,160},{160,192},{192,224},{224... | collective-permute-start | bytes 4616 | tf_op jit(solution)/shard_map/ppermute | solution.py:89
  97.6 1.0 convolution_convert_fusion
  98.6 4.4 %collective-permute-done.16 = bf16[3,256]{1,0:T(4,128)(2,1)S(1)} collective-permute-done((bf16[3,256]{1,0:T(4,128)(2,1)S(1)}, bf16[3,256]{1,0:T(4,128)(2,1)S(1)}, u32[]{:S(2)}, u32[]{:S(2)}) %collective-permute-start.16) | collective-permute-done | bytes 1568 | tf_op jit(solution)/shard_map/ppermute | solution.py:89
  103.0 0.3 multiply_multiply_fusion
  103.3 1.9 %collective-permute-start.17 = (f32[3,256]{1,0:T(4,128)S(1)}, f32[3,256]{1,0:T(4,128)S(1)}, u32[]{:S(2)}, u32[]{:S(2)}) collective-permute-start(f32[3,256]{1,0:T(4,128)S(1)} %fusion.155), channel_id=1, source_target_pairs={{32,0},{64,32},{96,64},{128,96},{160,128},{192,160},{224,192},{256... | collective-permute-start | bytes 9224 | tf_op jit(solution)/shard_map/ppermute | solution.py:89
  105.2 0.8 fusion.106
  107.2 1.9 %collective-permute-start.18 = (bf16[128,512]{1,0:T(8,128)(2,1)S(1)}, bf16[128,512]{1,0:T(8,128)(2,1)S(1)}, u32[]{:S(2)}, u32[]{:S(2)}) collective-permute-start(bf16[128,512]{1,0:T(8,128)(2,1)S(1)} %fusion), channel_id=1, source_target_pairs={{0,30},{2,0},{4,2},{6,4},{8,6},{10,8},{12,10},{14,12},{16,14},{18,... | collective-permute-start | bytes 393224 | tf_op jit(solution)/shard_map/ppermute | solution.py:12
  110.8 3.9 %collective-permute-start.25 = (bf16[128,512]{1,0:T(8,128)(2,1)S(1)}, bf16[128,512]{1,0:T(8,128)(2,1)S(1)}, u32[]{:S(2)}, u32[]{:S(2)}) collective-permute-start(bf16[128,512]{1,0:T(8,128)(2,1)S(1)} %fusion.29), channel_id=1, source_target_pairs={{0,2},{2,4},{4,6},{6,8},{8,10},{10,12},{12,14},{14,16},{16,18},{18... | collective-permute-start | bytes 393224 | tf_op jit(solution)/shard_map/ppermute | solution.py:12
  116.2 3.1 %collective-permute-start.19 = (bf16[128,512]{1,0:T(8,128)(2,1)S(1)}, bf16[128,512]{1,0:T(8,128)(2,1)S(1)}, u32[]{:S(2)}, u32[]{:S(2)}) collective-permute-start(bf16[128,512]{1,0:T(8,128)(2,1)S(1)} %fusion.4), channel_id=1, source_target_pairs={{0,30},{2,0},{4,2},{6,4},{8,6},{10,8},{12,10},{14,12},{16,14},{18,... | collective-permute-start | bytes 393224 | tf_op jit(solution)/shard_map/ppermute | solution.py:12
  119.8 3.1 %collective-permute-start.26 = (bf16[128,512]{1,0:T(8,128)(2,1)S(1)}, bf16[128,512]{1,0:T(8,128)(2,1)S(1)}, u32[]{:S(2)}, u32[]{:S(2)}) collective-permute-start(bf16[128,512]{1,0:T(8,128)(2,1)S(1)} %fusion.33), channel_id=1, source_target_pairs={{0,2},{2,4},{4,6},{6,8},{8,10},{10,12},{12,14},{14,16},{16,18},{18... | collective-permute-start | bytes 393224 | tf_op jit(solution)/shard_map/ppermute | solution.py:12
  122.8 1.4 collective-permute-done.19
  124.5 4.1 %collective-permute-start.20 = (bf16[128,512]{1,0:T(8,128)(2,1)S(1)}, bf16[128,512]{1,0:T(8,128)(2,1)S(1)}, u32[]{:S(2)}, u32[]{:S(2)}) collective-permute-start(bf16[128,512]{1,0:T(8,128)(2,1)S(1)} %fusion.8), channel_id=1, source_target_pairs={{0,30},{2,0},{4,2},{6,4},{8,6},{10,8},{12,10},{14,12},{16,14},{18,... | collective-permute-start | bytes 393224 | tf_op jit(solution)/shard_map/ppermute | solution.py:12
  128.6 0.6 collective-permute-done.26
  129.5 1.9 %collective-permute-start.27 = (bf16[128,512]{1,0:T(8,128)(2,1)S(1)}, bf16[128,512]{1,0:T(8,128)(2,1)S(1)}, u32[]{:S(2)}, u32[]{:S(2)}) collective-permute-start(bf16[128,512]{1,0:T(8,128)(2,1)S(1)} %fusion.37), channel_id=1, source_target_pairs={{0,2},{2,4},{4,6},{6,8},{8,10},{10,12},{12,14},{14,16},{16,18},{18... | collective-permute-start | bytes 393224 | tf_op jit(solution)/shard_map/ppermute | solution.py:12
  131.4 0.5 collective-permute-done.20
  132.1 5.5 %collective-permute-start.21 = (bf16[128,512]{1,0:T(8,128)(2,1)S(1)}, bf16[128,512]{1,0:T(8,128)(2,1)S(1)}, u32[]{:S(2)}, u32[]{:S(2)}) collective-permute-start(bf16[128,512]{1,0:T(8,128)(2,1)S(1)} %fusion.12), channel_id=1, source_target_pairs={{0,30},{2,0},{4,2},{6,4},{8,6},{10,8},{12,10},{14,12},{16,14},{18,... | collective-permute-start | bytes 393224 | tf_op jit(solution)/shard_map/ppermute | solution.py:12
  137.6 0.5 collective-permute-done.27
  138.3 1.9 %collective-permute-start.28 = (bf16[128,512]{1,0:T(8,128)(2,1)S(1)}, bf16[128,512]{1,0:T(8,128)(2,1)S(1)}, u32[]{:S(2)}, u32[]{:S(2)}) collective-permute-start(bf16[128,512]{1,0:T(8,128)(2,1)S(1)} %fusion.41), channel_id=1, source_target_pairs={{0,2},{2,4},{4,6},{6,8},{8,10},{10,12},{12,14},{14,16},{16,18},{18... | collective-permute-start | bytes 393224 | tf_op jit(solution)/shard_map/ppermute | solution.py:12
  140.5 5.4 %collective-permute-start.22 = (bf16[128,512]{1,0:T(8,128)(2,1)S(1)}, bf16[128,512]{1,0:T(8,128)(2,1)S(1)}, u32[]{:S(2)}, u32[]{:S(2)}) collective-permute-start(bf16[128,512]{1,0:T(8,128)(2,1)S(1)} %fusion.16), channel_id=1, source_target_pairs={{0,30},{2,0},{4,2},{6,4},{8,6},{10,8},{12,10},{14,12},{16,14},{18,... | collective-permute-start | bytes 393224 | tf_op jit(solution)/shard_map/ppermute | solution.py:12
  145.9 0.5 collective-permute-done.28
  146.6 1.9 %collective-permute-start.29 = (bf16[128,512]{1,0:T(8,128)(2,1)S(1)}, bf16[128,512]{1,0:T(8,128)(2,1)S(1)}, u32[]{:S(2)}, u32[]{:S(2)}) collective-permute-start(bf16[128,512]{1,0:T(8,128)(2,1)S(1)} %fusion.45), channel_id=1, source_target_pairs={{0,2},{2,4},{4,6},{6,8},{8,10},{10,12},{12,14},{14,16},{16,18},{18... | collective-permute-start | bytes 393224 | tf_op jit(solution)/shard_map/ppermute | solution.py:12
  148.6 0.2 fusion.20
  148.8 5.4 %collective-permute-start.23 = (bf16[128,512]{1,0:T(8,128)(2,1)S(1)}, bf16[128,512]{1,0:T(8,128)(2,1)S(1)}, u32[]{:S(2)}, u32[]{:S(2)}) collective-permute-start(bf16[128,512]{1,0:T(8,128)(2,1)S(1)} %fusion.20), channel_id=1, source_target_pairs={{0,30},{2,0},{4,2},{6,4},{8,6},{10,8},{12,10},{14,12},{16,14},{18,... | collective-permute-start | bytes 393224 | tf_op jit(solution)/shard_map/ppermute | solution.py:12
  154.2 0.5 collective-permute-done.29
  154.9 1.9 %collective-permute-start.30 = (bf16[128,512]{1,0:T(8,128)(2,1)S(1)}, bf16[128,512]{1,0:T(8,128)(2,1)S(1)}, u32[]{:S(2)}, u32[]{:S(2)}) collective-permute-start(bf16[128,512]{1,0:T(8,128)(2,1)S(1)} %fusion.49), channel_id=1, source_target_pairs={{0,2},{2,4},{4,6},{6,8},{8,10},{10,12},{12,14},{14,16},{16,18},{18... | collective-permute-start | bytes 393224 | tf_op jit(solution)/shard_map/ppermute | solution.py:12
  157.1 5.4 %collective-permute-start.24 = (bf16[128,512]{1,0:T(8,128)(2,1)S(1)}, bf16[128,512]{1,0:T(8,128)(2,1)S(1)}, u32[]{:S(2)}, u32[]{:S(2)}) collective-permute-start(bf16[128,512]{1,0:T(8,128)(2,1)S(1)} %fusion.24), channel_id=1, source_target_pairs={{0,30},{2,0},{4,2},{6,4},{8,6},{10,8},{12,10},{14,12},{16,14},{18,... | collective-permute-start | bytes 393224 | tf_op jit(solution)/shard_map/ppermute | solution.py:12
  162.5 0.5 collective-permute-done.30
  163.2 1.9 %collective-permute-start.31 = (bf16[128,512]{1,0:T(8,128)(2,1)S(1)}, bf16[128,512]{1,0:T(8,128)(2,1)S(1)}, u32[]{:S(2)}, u32[]{:S(2)}) collective-permute-start(bf16[128,512]{1,0:T(8,128)(2,1)S(1)} %add_convert_fusion), channel_id=1, source_target_pairs={{0,2},{2,4},{4,6},{6,8},{8,10},{10,12},{12,14},{14,16},{16,18},{18... | collective-permute-start | bytes 393224 | tf_op jit(solution)/shard_map/ppermute | solution.py:12
  165.4 5.4 %collective-permute-start.32 = (bf16[128,512]{1,0:T(8,128)(2,1)S(1)}, bf16[128,512]{1,0:T(8,128)(2,1)S(1)}, u32[]{:S(2)}, u32[]{:S(2)}) collective-permute-start(bf16[128,512]{1,0:T(8,128)(2,1)S(1)} %convert_add_fusion), channel_id=1, source_target_pairs={{0,30},{2,0},{4,2},{6,4},{8,6},{10,8},{12,10},{14,12},{16,14},{18,... | collective-permute-start | bytes 393224 | tf_op jit(solution)/shard_map/ppermute | solution.py:12
  171.0 0.3 collective-permute-done.31
  171.3 2.0 %collective-permute-done.32 = bf16[128,512]{1,0:T(8,128)(2,1)S(1)} collective-permute-done((bf16[128,512]{1,0:T(8,128)(2,1)S(1)}, bf16[128,512]{1,0:T(8,128)(2,1)S(1)}, u32[]{:S(2)}, u32[]{:S(2)}) %collective-permute-start.32) | collective-permute-done | bytes 131104 | tf_op jit(solution)/shard_map/ppermute | solution.py:12
  173.6 3.0 %collective-permute-start.33 = (bf16[128,256]{1,0:T(8,128)(2,1)S(1)}, bf16[128,256]{1,0:T(8,128)(2,1)S(1)}, u32[]{:S(2)}, u32[]{:S(2)}) collective-permute-start(bf16[128,256]{1,0:T(8,128)(2,1)S(1)} %select_convert_fusion), channel_id=1, source_target_pairs={{0,1},{1,0},{2,3},{3,2},{4,5},{5,4},{6,7},{7,6},{8,9},{9,8},{10,11... | collective-permute-start | bytes 196616 | tf_op jit(solution)/shard_map/ppermute | solution.py:12
  176.6 3.2 %collective-permute-done.33 = bf16[128,256]{1,0:T(8,128)(2,1)S(1)} collective-permute-done((bf16[128,256]{1,0:T(8,128)(2,1)S(1)}, bf16[128,256]{1,0:T(8,128)(2,1)S(1)}, u32[]{:S(2)}, u32[]{:S(2)}) %collective-permute-start.33) | collective-permute-done | bytes 65568 | tf_op jit(solution)/shard_map/ppermute | solution.py:12
  179.7 0.7 add_convert_fusion.1
  (97 shorter events, 8.4 us)
Async XLA Ops:
  0.6 102.4 %copy-start = (bf16[10,256]{1,0:T(8,128)(2,1)S(1)}, bf16[10,256]{1,0:T(8,128)(2,1)}, u32[]{:S(2)}) copy-start(bf16[10,256]{1,0:T(8,128)(2,1)} %param.13) | copy-start | bytes 15364
  1.6 6.2 %collective-permute-start = (bf16[128,256]{0,1:T(8,128)(2,1)S(1)}, bf16[128,256]{0,1:T(8,128)(2,1)S(1)}, u32[]{:S(2)}, u32[]{:S(2)}) collective-permute-start(bf16[128,256]{0,1:T(8,128)(2,1)S(1)} %copy.10), channel_id=1, source_target_pairs={{0,1},{1,0},{2,3},{3,2},{4,5},{5,4},{6,7},{7,6},{8,9},{9,8},{10,11... | collective-permute-start | bytes 196616 | tf_op jit(solution)/shard_map/ppermute | solution.py:12
  7.8 21.1 %collective-permute-start.1 = (bf16[128,512]{0,1:T(8,128)(2,1)S(1)}, bf16[128,512]{0,1:T(8,128)(2,1)S(1)}, u32[]{:S(2)}, u32[]{:S(2)}) collective-permute-start(bf16[128,512]{0,1:T(8,128)(2,1)S(1)} %maximum_select_fusion.1), channel_id=1, source_target_pairs={{0,30},{2,0},{4,2},{6,4},{8,6},{10,8},{12,10},{14,12},{16,14},{18,... | collective-permute-start | bytes 393224 | tf_op jit(solution)/shard_map/ppermute | solution.py:12
  26.0 8.1 %collective-permute-start.8 = (bf16[128,512]{0,1:T(8,128)(2,1)S(1)}, bf16[128,512]{0,1:T(8,128)(2,1)S(1)}, u32[]{:S(2)}, u32[]{:S(2)}) collective-permute-start(bf16[128,512]{0,1:T(8,128)(2,1)S(1)} %maximum_select_fusion.1), channel_id=1, source_target_pairs={{0,2},{2,4},{4,6},{6,8},{8,10},{10,12},{12,14},{14,16},{16,18},{18... | collective-permute-start | bytes 393224 | tf_op jit(solution)/shard_map/ppermute | solution.py:12
  28.9 7.7 %collective-permute-start.2 = (bf16[128,512]{0,1:T(8,128)(2,1)S(1)}, bf16[128,512]{0,1:T(8,128)(2,1)S(1)}, u32[]{:S(2)}, u32[]{:S(2)}) collective-permute-start(bf16[128,512]{0,1:T(8,128)(2,1)S(1)} %collective-permute-done.1), channel_id=1, source_target_pairs={{0,30},{2,0},{4,2},{6,4},{8,6},{10,8},{12,10},{14,12},{16,14},{18,... | collective-permute-start | bytes 393224 | tf_op jit(solution)/shard_map/ppermute | solution.py:12
  34.1 8.1 %collective-permute-start.9 = (bf16[128,512]{0,1:T(8,128)(2,1)S(1)}, bf16[128,512]{0,1:T(8,128)(2,1)S(1)}, u32[]{:S(2)}, u32[]{:S(2)}) collective-permute-start(bf16[128,512]{0,1:T(8,128)(2,1)S(1)} %collective-permute-done.8), channel_id=1, source_target_pairs={{0,2},{2,4},{4,6},{6,8},{8,10},{10,12},{12,14},{14,16},{16,18},{18... | collective-permute-start | bytes 393224 | tf_op jit(solution)/shard_map/ppermute | solution.py:12
  36.6 8.1 %collective-permute-start.3 = (bf16[128,512]{0,1:T(8,128)(2,1)S(1)}, bf16[128,512]{0,1:T(8,128)(2,1)S(1)}, u32[]{:S(2)}, u32[]{:S(2)}) collective-permute-start(bf16[128,512]{0,1:T(8,128)(2,1)S(1)} %collective-permute-done.2), channel_id=1, source_target_pairs={{0,30},{2,0},{4,2},{6,4},{8,6},{10,8},{12,10},{14,12},{16,14},{18,... | collective-permute-start | bytes 393224 | tf_op jit(solution)/shard_map/ppermute | solution.py:12
  42.2 8.1 %collective-permute-start.10 = (bf16[128,512]{0,1:T(8,128)(2,1)S(1)}, bf16[128,512]{0,1:T(8,128)(2,1)S(1)}, u32[]{:S(2)}, u32[]{:S(2)}) collective-permute-start(bf16[128,512]{0,1:T(8,128)(2,1)S(1)} %collective-permute-done.9), channel_id=1, source_target_pairs={{0,2},{2,4},{4,6},{6,8},{8,10},{10,12},{12,14},{14,16},{16,18},{18... | collective-permute-start | bytes 393224 | tf_op jit(solution)/shard_map/ppermute | solution.py:12
  44.7 8.1 %collective-permute-start.4 = (bf16[128,512]{0,1:T(8,128)(2,1)S(1)}, bf16[128,512]{0,1:T(8,128)(2,1)S(1)}, u32[]{:S(2)}, u32[]{:S(2)}) collective-permute-start(bf16[128,512]{0,1:T(8,128)(2,1)S(1)} %collective-permute-done.3), channel_id=1, source_target_pairs={{0,30},{2,0},{4,2},{6,4},{8,6},{10,8},{12,10},{14,12},{16,14},{18,... | collective-permute-start | bytes 393224 | tf_op jit(solution)/shard_map/ppermute | solution.py:12
  50.2 8.1 %collective-permute-start.11 = (bf16[128,512]{0,1:T(8,128)(2,1)S(1)}, bf16[128,512]{0,1:T(8,128)(2,1)S(1)}, u32[]{:S(2)}, u32[]{:S(2)}) collective-permute-start(bf16[128,512]{0,1:T(8,128)(2,1)S(1)} %collective-permute-done.10), channel_id=1, source_target_pairs={{0,2},{2,4},{4,6},{6,8},{8,10},{10,12},{12,14},{14,16},{16,18},{18... | collective-permute-start | bytes 393224 | tf_op jit(solution)/shard_map/ppermute | solution.py:12
  52.7 8.9 %collective-permute-start.5 = (bf16[128,512]{0,1:T(8,128)(2,1)S(1)}, bf16[128,512]{0,1:T(8,128)(2,1)S(1)}, u32[]{:S(2)}, u32[]{:S(2)}) collective-permute-start(bf16[128,512]{0,1:T(8,128)(2,1)S(1)} %collective-permute-done.4), channel_id=1, source_target_pairs={{0,30},{2,0},{4,2},{6,4},{8,6},{10,8},{12,10},{14,12},{16,14},{18,... | collective-permute-start | bytes 393224 | tf_op jit(solution)/shard_map/ppermute | solution.py:12
  58.3 9.2 %collective-permute-start.12 = (bf16[128,512]{0,1:T(8,128)(2,1)S(1)}, bf16[128,512]{0,1:T(8,128)(2,1)S(1)}, u32[]{:S(2)}, u32[]{:S(2)}) collective-permute-start(bf16[128,512]{0,1:T(8,128)(2,1)S(1)} %collective-permute-done.11), channel_id=1, source_target_pairs={{0,2},{2,4},{4,6},{6,8},{8,10},{10,12},{12,14},{14,16},{16,18},{18... | collective-permute-start | bytes 393224 | tf_op jit(solution)/shard_map/ppermute | solution.py:12
  61.7 8.8 %collective-permute-start.6 = (bf16[128,512]{0,1:T(8,128)(2,1)S(1)}, bf16[128,512]{0,1:T(8,128)(2,1)S(1)}, u32[]{:S(2)}, u32[]{:S(2)}) collective-permute-start(bf16[128,512]{0,1:T(8,128)(2,1)S(1)} %collective-permute-done.5), channel_id=1, source_target_pairs={{0,30},{2,0},{4,2},{6,4},{8,6},{10,8},{12,10},{14,12},{16,14},{18,... | collective-permute-start | bytes 393224 | tf_op jit(solution)/shard_map/ppermute | solution.py:12
  67.5 8.6 %collective-permute-start.13 = (bf16[128,512]{0,1:T(8,128)(2,1)S(1)}, bf16[128,512]{0,1:T(8,128)(2,1)S(1)}, u32[]{:S(2)}, u32[]{:S(2)}) collective-permute-start(bf16[128,512]{0,1:T(8,128)(2,1)S(1)} %collective-permute-done.12), channel_id=1, source_target_pairs={{0,2},{2,4},{4,6},{6,8},{8,10},{10,12},{12,14},{14,16},{16,18},{18... | collective-permute-start | bytes 393224 | tf_op jit(solution)/shard_map/ppermute | solution.py:12
  70.5 15.6 %collective-permute-start.7 = (bf16[128,512]{0,1:T(8,128)(2,1)S(1)}, bf16[128,512]{0,1:T(8,128)(2,1)S(1)}, u32[]{:S(2)}, u32[]{:S(2)}) collective-permute-start(bf16[128,512]{0,1:T(8,128)(2,1)S(1)} %collective-permute-done.6), channel_id=1, source_target_pairs={{0,30},{2,0},{4,2},{6,4},{8,6},{10,8},{12,10},{14,12},{16,14},{18,... | collective-permute-start | bytes 393224 | tf_op jit(solution)/shard_map/ppermute | solution.py:12
  76.1 8.1 %collective-permute-start.14 = (bf16[128,512]{0,1:T(8,128)(2,1)S(1)}, bf16[128,512]{0,1:T(8,128)(2,1)S(1)}, u32[]{:S(2)}, u32[]{:S(2)}) collective-permute-start(bf16[128,512]{0,1:T(8,128)(2,1)S(1)} %collective-permute-done.13), channel_id=1, source_target_pairs={{0,2},{2,4},{4,6},{6,8},{8,10},{10,12},{12,14},{14,16},{16,18},{18... | collective-permute-start | bytes 393224 | tf_op jit(solution)/shard_map/ppermute | solution.py:12
  84.2 8.1 %collective-permute-start.15 = (bf16[128,512]{0,1:T(8,128)(2,1)S(1)}, bf16[128,512]{0,1:T(8,128)(2,1)S(1)}, u32[]{:S(2)}, u32[]{:S(2)}) collective-permute-start(bf16[128,512]{0,1:T(8,128)(2,1)S(1)} %collective-permute-done.14), channel_id=1, source_target_pairs={{0,2},{2,4},{4,6},{6,8},{8,10},{10,12},{12,14},{14,16},{16,18},{18... | collective-permute-start | bytes 393224 | tf_op jit(solution)/shard_map/ppermute | solution.py:12
  92.4 2.2 %copy-start.2 = (bf16[8192,256]{1,0:T(8,128)(2,1)S(1)}, bf16[8192,256]{1,0:T(8,128)(2,1)}, u32[]{:S(2)}) copy-start(bf16[8192,256]{1,0:T(8,128)(2,1)} %param.10) | copy-start | bytes 12582916
  93.1 4.5 %copy-start.1 = (bf16[8192,256]{1,0:T(8,128)(2,1)S(1)}, bf16[8192,256]{1,0:T(8,128)(2,1)}, u32[]{:S(2)}) copy-start(bf16[8192,256]{1,0:T(8,128)(2,1)} %param.9) | copy-start | bytes 12582916
  95.6 7.4 %copy-start.3 = (f32[256]{0:T(256)S(1)}, f32[256]{0:T(256)}, u32[]{:S(2)}) copy-start(f32[256]{0:T(256)} %param.12) | copy-start | bytes 3076
  95.6 7.4 %copy-start.4 = (s32[128]{0:T(128)S(1)}, s32[128]{0:T(128)}, u32[]{:S(2)}) copy-start(s32[128]{0:T(128)} %param.14) | copy-start | bytes 1540
  95.7 7.3 %collective-permute-start.16 = (bf16[3,256]{1,0:T(4,128)(2,1)S(1)}, bf16[3,256]{1,0:T(4,128)(2,1)S(1)}, u32[]{:S(2)}, u32[]{:S(2)}) collective-permute-start(bf16[3,256]{1,0:T(4,128)(2,1)S(1)} %slice.87), channel_id=1, source_target_pairs={{0,32},{32,64},{64,96},{96,128},{128,160},{160,192},{192,224},{224... | collective-permute-start | bytes 4616 | tf_op jit(solution)/shard_map/ppermute | solution.py:89
  103.3 3.7 %collective-permute-start.17 = (f32[3,256]{1,0:T(4,128)S(1)}, f32[3,256]{1,0:T(4,128)S(1)}, u32[]{:S(2)}, u32[]{:S(2)}) collective-permute-start(f32[3,256]{1,0:T(4,128)S(1)} %fusion.155), channel_id=1, source_target_pairs={{32,0},{64,32},{96,64},{128,96},{160,128},{192,160},{224,192},{256... | collective-permute-start | bytes 9224 | tf_op jit(solution)/shard_map/ppermute | solution.py:89
  107.2 8.7 %collective-permute-start.18 = (bf16[128,512]{1,0:T(8,128)(2,1)S(1)}, bf16[128,512]{1,0:T(8,128)(2,1)S(1)}, u32[]{:S(2)}, u32[]{:S(2)}) collective-permute-start(bf16[128,512]{1,0:T(8,128)(2,1)S(1)} %fusion), channel_id=1, source_target_pairs={{0,30},{2,0},{4,2},{6,4},{8,6},{10,8},{12,10},{14,12},{16,14},{18,... | collective-permute-start | bytes 393224 | tf_op jit(solution)/shard_map/ppermute | solution.py:12
  110.8 8.7 %collective-permute-start.25 = (bf16[128,512]{1,0:T(8,128)(2,1)S(1)}, bf16[128,512]{1,0:T(8,128)(2,1)S(1)}, u32[]{:S(2)}, u32[]{:S(2)}) collective-permute-start(bf16[128,512]{1,0:T(8,128)(2,1)S(1)} %fusion.29), channel_id=1, source_target_pairs={{0,2},{2,4},{4,6},{6,8},{8,10},{10,12},{12,14},{14,16},{16,18},{18... | collective-permute-start | bytes 393224 | tf_op jit(solution)/shard_map/ppermute | solution.py:12
  116.2 8.0 %collective-permute-start.19 = (bf16[128,512]{1,0:T(8,128)(2,1)S(1)}, bf16[128,512]{1,0:T(8,128)(2,1)S(1)}, u32[]{:S(2)}, u32[]{:S(2)}) collective-permute-start(bf16[128,512]{1,0:T(8,128)(2,1)S(1)} %fusion.4), channel_id=1, source_target_pairs={{0,30},{2,0},{4,2},{6,4},{8,6},{10,8},{12,10},{14,12},{16,14},{18,... | collective-permute-start | bytes 393224 | tf_op jit(solution)/shard_map/ppermute | solution.py:12
  119.8 9.5 %collective-permute-start.26 = (bf16[128,512]{1,0:T(8,128)(2,1)S(1)}, bf16[128,512]{1,0:T(8,128)(2,1)S(1)}, u32[]{:S(2)}, u32[]{:S(2)}) collective-permute-start(bf16[128,512]{1,0:T(8,128)(2,1)S(1)} %fusion.33), channel_id=1, source_target_pairs={{0,2},{2,4},{4,6},{6,8},{8,10},{10,12},{12,14},{14,16},{16,18},{18... | collective-permute-start | bytes 393224 | tf_op jit(solution)/shard_map/ppermute | solution.py:12
  124.5 7.4 %collective-permute-start.20 = (bf16[128,512]{1,0:T(8,128)(2,1)S(1)}, bf16[128,512]{1,0:T(8,128)(2,1)S(1)}, u32[]{:S(2)}, u32[]{:S(2)}) collective-permute-start(bf16[128,512]{1,0:T(8,128)(2,1)S(1)} %fusion.8), channel_id=1, source_target_pairs={{0,30},{2,0},{4,2},{6,4},{8,6},{10,8},{12,10},{14,12},{16,14},{18,... | collective-permute-start | bytes 393224 | tf_op jit(solution)/shard_map/ppermute | solution.py:12
  129.5 8.6 %collective-permute-start.27 = (bf16[128,512]{1,0:T(8,128)(2,1)S(1)}, bf16[128,512]{1,0:T(8,128)(2,1)S(1)}, u32[]{:S(2)}, u32[]{:S(2)}) collective-permute-start(bf16[128,512]{1,0:T(8,128)(2,1)S(1)} %fusion.37), channel_id=1, source_target_pairs={{0,2},{2,4},{4,6},{6,8},{8,10},{10,12},{12,14},{14,16},{16,18},{18... | collective-permute-start | bytes 393224 | tf_op jit(solution)/shard_map/ppermute | solution.py:12
  132.1 8.2 %collective-permute-start.21 = (bf16[128,512]{1,0:T(8,128)(2,1)S(1)}, bf16[128,512]{1,0:T(8,128)(2,1)S(1)}, u32[]{:S(2)}, u32[]{:S(2)}) collective-permute-start(bf16[128,512]{1,0:T(8,128)(2,1)S(1)} %fusion.12), channel_id=1, source_target_pairs={{0,30},{2,0},{4,2},{6,4},{8,6},{10,8},{12,10},{14,12},{16,14},{18,... | collective-permute-start | bytes 393224 | tf_op jit(solution)/shard_map/ppermute | solution.py:12
  138.3 8.1 %collective-permute-start.28 = (bf16[128,512]{1,0:T(8,128)(2,1)S(1)}, bf16[128,512]{1,0:T(8,128)(2,1)S(1)}, u32[]{:S(2)}, u32[]{:S(2)}) collective-permute-start(bf16[128,512]{1,0:T(8,128)(2,1)S(1)} %fusion.41), channel_id=1, source_target_pairs={{0,2},{2,4},{4,6},{6,8},{8,10},{10,12},{12,14},{14,16},{16,18},{18... | collective-permute-start | bytes 393224 | tf_op jit(solution)/shard_map/ppermute | solution.py:12
  140.5 8.1 %collective-permute-start.22 = (bf16[128,512]{1,0:T(8,128)(2,1)S(1)}, bf16[128,512]{1,0:T(8,128)(2,1)S(1)}, u32[]{:S(2)}, u32[]{:S(2)}) collective-permute-start(bf16[128,512]{1,0:T(8,128)(2,1)S(1)} %fusion.16), channel_id=1, source_target_pairs={{0,30},{2,0},{4,2},{6,4},{8,6},{10,8},{12,10},{14,12},{16,14},{18,... | collective-permute-start | bytes 393224 | tf_op jit(solution)/shard_map/ppermute | solution.py:12
  146.6 8.1 %collective-permute-start.29 = (bf16[128,512]{1,0:T(8,128)(2,1)S(1)}, bf16[128,512]{1,0:T(8,128)(2,1)S(1)}, u32[]{:S(2)}, u32[]{:S(2)}) collective-permute-start(bf16[128,512]{1,0:T(8,128)(2,1)S(1)} %fusion.45), channel_id=1, source_target_pairs={{0,2},{2,4},{4,6},{6,8},{8,10},{10,12},{12,14},{14,16},{16,18},{18... | collective-permute-start | bytes 393224 | tf_op jit(solution)/shard_map/ppermute | solution.py:12
  148.8 8.1 %collective-permute-start.23 = (bf16[128,512]{1,0:T(8,128)(2,1)S(1)}, bf16[128,512]{1,0:T(8,128)(2,1)S(1)}, u32[]{:S(2)}, u32[]{:S(2)}) collective-permute-start(bf16[128,512]{1,0:T(8,128)(2,1)S(1)} %fusion.20), channel_id=1, source_target_pairs={{0,30},{2,0},{4,2},{6,4},{8,6},{10,8},{12,10},{14,12},{16,14},{18,... | collective-permute-start | bytes 393224 | tf_op jit(solution)/shard_map/ppermute | solution.py:12
  154.9 8.1 %collective-permute-start.30 = (bf16[128,512]{1,0:T(8,128)(2,1)S(1)}, bf16[128,512]{1,0:T(8,128)(2,1)S(1)}, u32[]{:S(2)}, u32[]{:S(2)}) collective-permute-start(bf16[128,512]{1,0:T(8,128)(2,1)S(1)} %fusion.49), channel_id=1, source_target_pairs={{0,2},{2,4},{4,6},{6,8},{8,10},{10,12},{12,14},{14,16},{16,18},{18... | collective-permute-start | bytes 393224 | tf_op jit(solution)/shard_map/ppermute | solution.py:12
  157.1 8.1 %collective-permute-start.24 = (bf16[128,512]{1,0:T(8,128)(2,1)S(1)}, bf16[128,512]{1,0:T(8,128)(2,1)S(1)}, u32[]{:S(2)}, u32[]{:S(2)}) collective-permute-start(bf16[128,512]{1,0:T(8,128)(2,1)S(1)} %fusion.24), channel_id=1, source_target_pairs={{0,30},{2,0},{4,2},{6,4},{8,6},{10,8},{12,10},{14,12},{16,14},{18,... | collective-permute-start | bytes 393224 | tf_op jit(solution)/shard_map/ppermute | solution.py:12
  163.2 8.1 %collective-permute-start.31 = (bf16[128,512]{1,0:T(8,128)(2,1)S(1)}, bf16[128,512]{1,0:T(8,128)(2,1)S(1)}, u32[]{:S(2)}, u32[]{:S(2)}) collective-permute-start(bf16[128,512]{1,0:T(8,128)(2,1)S(1)} %add_convert_fusion), channel_id=1, source_target_pairs={{0,2},{2,4},{4,6},{6,8},{8,10},{10,12},{12,14},{14,16},{16,18},{18... | collective-permute-start | bytes 393224 | tf_op jit(solution)/shard_map/ppermute | solution.py:12
  165.4 7.9 %collective-permute-start.32 = (bf16[128,512]{1,0:T(8,128)(2,1)S(1)}, bf16[128,512]{1,0:T(8,128)(2,1)S(1)}, u32[]{:S(2)}, u32[]{:S(2)}) collective-permute-start(bf16[128,512]{1,0:T(8,128)(2,1)S(1)} %convert_add_fusion), channel_id=1, source_target_pairs={{0,30},{2,0},{4,2},{6,4},{8,6},{10,8},{12,10},{14,12},{16,14},{18,... | collective-permute-start | bytes 393224 | tf_op jit(solution)/shard_map/ppermute | solution.py:12
  173.6 6.2 %collective-permute-start.33 = (bf16[128,256]{1,0:T(8,128)(2,1)S(1)}, bf16[128,256]{1,0:T(8,128)(2,1)S(1)}, u32[]{:S(2)}, u32[]{:S(2)}) collective-permute-start(bf16[128,256]{1,0:T(8,128)(2,1)S(1)} %select_convert_fusion), channel_id=1, source_target_pairs={{0,1},{1,0},{2,3},{3,2},{4,5},{5,4},{6,7},{7,6},{8,9},{9,8},{10,11... | collective-permute-start | bytes 196616 | tf_op jit(solution)/shard_map/ppermute | solution.py:12

commit v9 on v8

--- a/solution.py
+++ b/solution.py
@@ -37,6 +37,12 @@
     return ordered.transpose(1, 0, 2).reshape(rows, -1)
 
 
+def across(block, dz):
+    count = lax.axis_size("tz")
+    route = [(z * 2 + x, (z + dz) % count * 2 + 1 - x) for z in range(count) for x in range(2)]
+    return lax.ppermute(block, TP, route)
+
+
 def scatter_features(make_block, operands):
     count = lax.axis_size("tz")
     here = lax.axis_index("tz")
@@ -45,10 +51,17 @@
         used = operands if after is None else lax.optimization_barrier((operands, after))[0]
         return make_block((here + offset) % count, *used).astype(jnp.float32)
 
+    first = lax.axis_index("tx") == 0
+
+    def split(block):
+        half = block.shape[1] // 2
+        mine = jnp.where(first, block[:, :half], block[:, half:])
+        other = jnp.where(first, block[:, half:], block[:, :half])
+        return mine, other
+
     right = count - 1 - count // 2
     left = count // 2
-    total = None
-    last = None
+    partial = None
     if right > 0:
         acc = own(right)
         coming = own(right - 1) if right > 1 else None
@@ -57,8 +70,10 @@
             acc = got + coming
             if step + 1 < right:
                 coming = own(right - step - 1, got)
-        total = hop(acc, 1)
-        last = total
+        partial = hop(acc, 1)
+    partial = own(0, partial) if partial is None else own(0, partial) + partial
+    mine, other = split(partial)
+    mine = mine + shifted(other.astype(jnp.bfloat16), "tx", 1).astype(jnp.float32)
     if left > 0:
         acc = own(left)
         coming = own(left + 1) if left > 1 else None
@@ -67,16 +82,10 @@
             acc = got + coming
             if step + 1 < left:
                 coming = own(left + step + 1, got)
-        arrived_left = hop(acc, -1)
-        total = arrived_left if total is None else total + arrived_left
-        last = acc
-    total = own(0, last) + (0.0 if total is None else total)
-    half = total.shape[1] // 2
-    first = lax.axis_index("tx") == 0
-    mine = jnp.where(first, total[:, :half], total[:, half:])
-    other = jnp.where(first, total[:, half:], total[:, :half])
-    arrived = shifted(other.astype(jnp.bfloat16), "tx", 1).astype(jnp.float32)
-    return (mine + arrived).astype(jnp.bfloat16)
+        ahead_mine, ahead_other = split(acc.astype(jnp.bfloat16))
+        mine = mine + shifted(ahead_mine, "tz", -1).astype(jnp.float32)
+        mine = mine + across(ahead_other, -1).astype(jnp.float32)
+    return mine.astype(jnp.bfloat16)
 
 
 def hop(acc, distance):

time: 182 us -> 186 us (1.022)
  starting transfers between devices: 130 us -> 133 us
    ppermute x0 -> x1, waiting for transfers between devices: none -> 4.57 us  [across(): return lax.ppermute(block, TP, route)]
    ppermute x32, waiting for transfers between devices: 28.7 us -> 24.3 us  [shifted(): lax.ppermute(block, axis, [(i, (i + distance) % size) for i in range(size)])]
    ppermute x0 -> x1, starting transfers between devices: none -> 2.46 us  [across(): return lax.ppermute(block, TP, route)]
  transfers between devices with their start and end apart: 34 -> 35, of which waited for: 21 -> 17; matrix products, arithmetic and copies ran while one was open for 6% -> 6% of each run, Pallas kernels for 0% -> 0%
where the time goes in v9:
time: 186 us; the launch traced here: 184 us
  starting transfers between devices  133 us (72%)
  waiting for transfers between devices  33.3 us (18%)
  matrix products  9.54 us (5%)
  local copies, waits for them, and re-layouts  4.14 us (2%)
  other arithmetic  2.31 us (1%)
  between operations  1.88 us (1%)
    ppermute x32, starting transfers between devices, shifted(): lax.ppermute(block, axis, [(i, (i + distance) % size) for i in range(size)])  127 us
    ppermute x32, waiting for transfers between devices, shifted(): lax.ppermute(block, axis, [(i, (i + distance) % size) for i in range(size)])  24.3 us
    ppermute x1, waiting for transfers between devices, across(): return lax.ppermute(block, TP, route)  4.57 us
    ppermute x2, waiting for transfers between devices, passed_along(): return lax.ppermute(block, axis, route)  4.38 us
    ppermute x2, starting transfers between devices, passed_along(): return lax.ppermute(block, axis, route)  3.84 us
  transfers between devices with their start and end apart: 35, of which 17 were waited for; matrix products, arithmetic and copies ran while one was open for 6% of the time, Pallas kernels for 0%

profile of v9, /device:TPU:56, one launch (start us, length us, event | category | flops | bytes accessed | tf_op | source)
XLA Modules:
  0.0 184.3 jit_solution(5539851746876421699)
XLA Ops:
  0.6 1.0 copy.10
  1.6 3.4 %collective-permute-start = (bf16[128,256]{0,1:T(8,128)(2,1)S(1)}, bf16[128,256]{0,1:T(8,128)(2,1)S(1)}, u32[]{:S(2)}, u32[]{:S(2)}) collective-permute-start(bf16[128,256]{0,1:T(8,128)(2,1)S(1)} %copy.10), channel_id=1, source_target_pairs={{0,1},{1,0},{2,3},{3,2},{4,5},{5,4},{6,7},{7,6},{8,9},{9,8},{10,11... | collective-permute-start | bytes 196616 | tf_op jit(solution)/shard_map/ppermute | solution.py:12
  5.0 0.8 fusion.158
  5.9 1.9 %collective-permute-done = bf16[128,256]{0,1:T(8,128)(2,1)S(1)} collective-permute-done((bf16[128,256]{0,1:T(8,128)(2,1)S(1)}, bf16[128,256]{0,1:T(8,128)(2,1)S(1)}, u32[]{:S(2)}, u32[]{:S(2)}) %collective-permute-start) | collective-permute-done | bytes 65568 | tf_op jit(solution)/shard_map/ppermute | solution.py:12
  7.8 18.2 %collective-permute-start.1 = (bf16[128,512]{0,1:T(8,128)(2,1)S(1)}, bf16[128,512]{0,1:T(8,128)(2,1)S(1)}, u32[]{:S(2)}, u32[]{:S(2)}) collective-permute-start(bf16[128,512]{0,1:T(8,128)(2,1)S(1)} %maximum_select_fusion.1), channel_id=1, source_target_pairs={{0,30},{2,0},{4,2},{6,4},{8,6},{10,8},{12,10},{14,12},{16,14},{18,... | collective-permute-start | bytes 393224 | tf_op jit(solution)/shard_map/ppermute | solution.py:12
  26.0 1.9 %collective-permute-start.8 = (bf16[128,512]{0,1:T(8,128)(2,1)S(1)}, bf16[128,512]{0,1:T(8,128)(2,1)S(1)}, u32[]{:S(2)}, u32[]{:S(2)}) collective-permute-start(bf16[128,512]{0,1:T(8,128)(2,1)S(1)} %maximum_select_fusion.1), channel_id=1, source_target_pairs={{0,2},{2,4},{4,6},{6,8},{8,10},{10,12},{12,14},{14,16},{16,18},{18... | collective-permute-start | bytes 393224 | tf_op jit(solution)/shard_map/ppermute | solution.py:12
  28.2 0.7 convert_element_type.218
  28.9 5.2 %collective-permute-start.2 = (bf16[128,512]{0,1:T(8,128)(2,1)S(1)}, bf16[128,512]{0,1:T(8,128)(2,1)S(1)}, u32[]{:S(2)}, u32[]{:S(2)}) collective-permute-start(bf16[128,512]{0,1:T(8,128)(2,1)S(1)} %collective-permute-done.1), channel_id=1, source_target_pairs={{0,30},{2,0},{4,2},{6,4},{8,6},{10,8},{12,10},{14,12},{16,14},{18,... | collective-permute-start | bytes 393224 | tf_op jit(solution)/shard_map/ppermute | solution.py:12
  34.1 1.9 %collective-permute-start.9 = (bf16[128,512]{0,1:T(8,128)(2,1)S(1)}, bf16[128,512]{0,1:T(8,128)(2,1)S(1)}, u32[]{:S(2)}, u32[]{:S(2)}) collective-permute-start(bf16[128,512]{0,1:T(8,128)(2,1)S(1)} %collective-permute-done.8), channel_id=1, source_target_pairs={{0,2},{2,4},{4,6},{6,8},{8,10},{10,12},{12,14},{14,16},{16,18},{18... | collective-permute-start | bytes 393224 | tf_op jit(solution)/shard_map/ppermute | solution.py:12
  36.1 0.5 collective-permute-done.2
  36.6 5.6 %collective-permute-start.3 = (bf16[128,512]{0,1:T(8,128)(2,1)S(1)}, bf16[128,512]{0,1:T(8,128)(2,1)S(1)}, u32[]{:S(2)}, u32[]{:S(2)}) collective-permute-start(bf16[128,512]{0,1:T(8,128)(2,1)S(1)} %collective-permute-done.2), channel_id=1, source_target_pairs={{0,30},{2,0},{4,2},{6,4},{8,6},{10,8},{12,10},{14,12},{16,14},{18,... | collective-permute-start | bytes 393224 | tf_op jit(solution)/shard_map/ppermute | solution.py:12
  42.2 1.9 %collective-permute-start.10 = (bf16[128,512]{0,1:T(8,128)(2,1)S(1)}, bf16[128,512]{0,1:T(8,128)(2,1)S(1)}, u32[]{:S(2)}, u32[]{:S(2)}) collective-permute-start(bf16[128,512]{0,1:T(8,128)(2,1)S(1)} %collective-permute-done.9), channel_id=1, source_target_pairs={{0,2},{2,4},{4,6},{6,8},{8,10},{10,12},{12,14},{14,16},{16,18},{18... | collective-permute-start | bytes 393224 | tf_op jit(solution)/shard_map/ppermute | solution.py:12
  44.1 0.5 collective-permute-done.3
  44.7 5.6 %collective-permute-start.4 = (bf16[128,512]{0,1:T(8,128)(2,1)S(1)}, bf16[128,512]{0,1:T(8,128)(2,1)S(1)}, u32[]{:S(2)}, u32[]{:S(2)}) collective-permute-start(bf16[128,512]{0,1:T(8,128)(2,1)S(1)} %collective-permute-done.3), channel_id=1, source_target_pairs={{0,30},{2,0},{4,2},{6,4},{8,6},{10,8},{12,10},{14,12},{16,14},{18,... | collective-permute-start | bytes 393224 | tf_op jit(solution)/shard_map/ppermute | solution.py:12
  50.2 1.9 %collective-permute-start.11 = (bf16[128,512]{0,1:T(8,128)(2,1)S(1)}, bf16[128,512]{0,1:T(8,128)(2,1)S(1)}, u32[]{:S(2)}, u32[]{:S(2)}) collective-permute-start(bf16[128,512]{0,1:T(8,128)(2,1)S(1)} %collective-permute-done.10), channel_id=1, source_target_pairs={{0,2},{2,4},{4,6},{6,8},{8,10},{10,12},{12,14},{14,16},{16,18},{18... | collective-permute-start | bytes 393224 | tf_op jit(solution)/shard_map/ppermute | solution.py:12
  52.2 0.5 collective-permute-done.4
  52.7 5.6 %collective-permute-start.5 = (bf16[128,512]{0,1:T(8,128)(2,1)S(1)}, bf16[128,512]{0,1:T(8,128)(2,1)S(1)}, u32[]{:S(2)}, u32[]{:S(2)}) collective-permute-start(bf16[128,512]{0,1:T(8,128)(2,1)S(1)} %collective-permute-done.4), channel_id=1, source_target_pairs={{0,30},{2,0},{4,2},{6,4},{8,6},{10,8},{12,10},{14,12},{16,14},{18,... | collective-permute-start | bytes 393224 | tf_op jit(solution)/shard_map/ppermute | solution.py:12
  58.3 1.9 %collective-permute-start.12 = (bf16[128,512]{0,1:T(8,128)(2,1)S(1)}, bf16[128,512]{0,1:T(8,128)(2,1)S(1)}, u32[]{:S(2)}, u32[]{:S(2)}) collective-permute-start(bf16[128,512]{0,1:T(8,128)(2,1)S(1)} %collective-permute-done.11), channel_id=1, source_target_pairs={{0,2},{2,4},{4,6},{6,8},{8,10},{10,12},{12,14},{14,16},{16,18},{18... | collective-permute-start | bytes 393224 | tf_op jit(solution)/shard_map/ppermute | solution.py:12
  60.2 1.4 collective-permute-done.5
  61.7 5.6 %collective-permute-start.6 = (bf16[128,512]{0,1:T(8,128)(2,1)S(1)}, bf16[128,512]{0,1:T(8,128)(2,1)S(1)}, u32[]{:S(2)}, u32[]{:S(2)}) collective-permute-start(bf16[128,512]{0,1:T(8,128)(2,1)S(1)} %collective-permute-done.5), channel_id=1, source_target_pairs={{0,30},{2,0},{4,2},{6,4},{8,6},{10,8},{12,10},{14,12},{16,14},{18,... | collective-permute-start | bytes 393224 | tf_op jit(solution)/shard_map/ppermute | solution.py:12
  67.2 0.2 collective-permute-done.12
  67.5 1.9 %collective-permute-start.13 = (bf16[128,512]{0,1:T(8,128)(2,1)S(1)}, bf16[128,512]{0,1:T(8,128)(2,1)S(1)}, u32[]{:S(2)}, u32[]{:S(2)}) collective-permute-start(bf16[128,512]{0,1:T(8,128)(2,1)S(1)} %collective-permute-done.12), channel_id=1, source_target_pairs={{0,2},{2,4},{4,6},{6,8},{8,10},{10,12},{12,14},{14,16},{16,18},{18... | collective-permute-start | bytes 393224 | tf_op jit(solution)/shard_map/ppermute | solution.py:12
  69.4 1.0 collective-permute-done.6
  70.5 5.6 %collective-permute-start.7 = (bf16[128,512]{0,1:T(8,128)(2,1)S(1)}, bf16[128,512]{0,1:T(8,128)(2,1)S(1)}, u32[]{:S(2)}, u32[]{:S(2)}) collective-permute-start(bf16[128,512]{0,1:T(8,128)(2,1)S(1)} %collective-permute-done.6), channel_id=1, source_target_pairs={{0,30},{2,0},{4,2},{6,4},{8,6},{10,8},{12,10},{14,12},{16,14},{18,... | collective-permute-start | bytes 393224 | tf_op jit(solution)/shard_map/ppermute | solution.py:12
  76.1 1.9 %collective-permute-start.14 = (bf16[128,512]{0,1:T(8,128)(2,1)S(1)}, bf16[128,512]{0,1:T(8,128)(2,1)S(1)}, u32[]{:S(2)}, u32[]{:S(2)}) collective-permute-start(bf16[128,512]{0,1:T(8,128)(2,1)S(1)} %collective-permute-done.13), channel_id=1, source_target_pairs={{0,2},{2,4},{4,6},{6,8},{8,10},{10,12},{12,14},{14,16},{16,18},{18... | collective-permute-start | bytes 393224 | tf_op jit(solution)/shard_map/ppermute | solution.py:12
  78.0 6.1 %collective-permute-done.14 = bf16[128,512]{0,1:T(8,128)(2,1)S(1)} collective-permute-done((bf16[128,512]{0,1:T(8,128)(2,1)S(1)}, bf16[128,512]{0,1:T(8,128)(2,1)S(1)}, u32[]{:S(2)}, u32[]{:S(2)}) %collective-permute-start.14) | collective-permute-done | bytes 131104 | tf_op jit(solution)/shard_map/ppermute | solution.py:12
  84.2 1.9 %collective-permute-start.15 = (bf16[128,512]{0,1:T(8,128)(2,1)S(1)}, bf16[128,512]{0,1:T(8,128)(2,1)S(1)}, u32[]{:S(2)}, u32[]{:S(2)}) collective-permute-start(bf16[128,512]{0,1:T(8,128)(2,1)S(1)} %collective-permute-done.14), channel_id=1, source_target_pairs={{0,2},{2,4},{4,6},{6,8},{8,10},{10,12},{12,14},{14,16},{16,18},{18... | collective-permute-start | bytes 393224 | tf_op jit(solution)/shard_map/ppermute | solution.py:12
  86.1 6.1 %collective-permute-done.15 = bf16[128,512]{0,1:T(8,128)(2,1)S(1)} collective-permute-done((bf16[128,512]{0,1:T(8,128)(2,1)S(1)}, bf16[128,512]{0,1:T(8,128)(2,1)S(1)}, u32[]{:S(2)}, u32[]{:S(2)}) %collective-permute-start.15) | collective-permute-done | bytes 131104 | tf_op jit(solution)/shard_map/ppermute | solution.py:12
  93.1 1.5 copy-done.1
  94.6 1.0 convolution_convert_fusion.1
  95.7 1.9 %collective-permute-start.16 = (bf16[3,256]{1,0:T(4,128)(2,1)S(1)}, bf16[3,256]{1,0:T(4,128)(2,1)S(1)}, u32[]{:S(2)}, u32[]{:S(2)}) collective-permute-start(bf16[3,256]{1,0:T(4,128)(2,1)S(1)} %slice.97), channel_id=1, source_target_pairs={{0,32},{32,64},{64,96},{96,128},{128,160},{160,192},{192,224},{224... | collective-permute-start | bytes 4616 | tf_op jit(solution)/shard_map/ppermute | solution.py:98
  97.6 1.0 convolution_convert_fusion
  98.6 4.4 %collective-permute-done.16 = bf16[3,256]{1,0:T(4,128)(2,1)S(1)} collective-permute-done((bf16[3,256]{1,0:T(4,128)(2,1)S(1)}, bf16[3,256]{1,0:T(4,128)(2,1)S(1)}, u32[]{:S(2)}, u32[]{:S(2)}) %collective-permute-start.16) | collective-permute-done | bytes 1568 | tf_op jit(solution)/shard_map/ppermute | solution.py:98
  103.0 0.3 multiply_multiply_fusion
  103.3 1.9 %collective-permute-start.17 = (f32[3,256]{1,0:T(4,128)S(1)}, f32[3,256]{1,0:T(4,128)S(1)}, u32[]{:S(2)}, u32[]{:S(2)}) collective-permute-start(f32[3,256]{1,0:T(4,128)S(1)} %fusion.154), channel_id=1, source_target_pairs={{32,0},{64,32},{96,64},{128,96},{160,128},{192,160},{224,192},{256... | collective-permute-start | bytes 9224 | tf_op jit(solution)/shard_map/ppermute | solution.py:98
  105.2 0.8 fusion.107
  107.2 1.9 %collective-permute-start.18 = (bf16[128,512]{1,0:T(8,128)(2,1)S(1)}, bf16[128,512]{1,0:T(8,128)(2,1)S(1)}, u32[]{:S(2)}, u32[]{:S(2)}) collective-permute-start(bf16[128,512]{1,0:T(8,128)(2,1)S(1)} %fusion), channel_id=1, source_target_pairs={{0,2},{2,4},{4,6},{6,8},{8,10},{10,12},{12,14},{14,16},{16,18},{18... | collective-permute-start | bytes 393224 | tf_op jit(solution)/shard_map/ppermute | solution.py:12
  110.8 5.1 %collective-permute-start.26 = (bf16[128,512]{1,0:T(8,128)(2,1)S(1)}, bf16[128,512]{1,0:T(8,128)(2,1)S(1)}, u32[]{:S(2)}, u32[]{:S(2)}) collective-permute-start(bf16[128,512]{1,0:T(8,128)(2,1)S(1)} %fusion.26), channel_id=1, source_target_pairs={{0,30},{2,0},{4,2},{6,4},{8,6},{10,8},{12,10},{14,12},{16,14},{18,... | collective-permute-start | bytes 393224 | tf_op jit(solution)/shard_map/ppermute | solution.py:12
  117.4 0.2 fusion.4
  117.6 1.9 %collective-permute-start.19 = (bf16[128,512]{1,0:T(8,128)(2,1)S(1)}, bf16[128,512]{1,0:T(8,128)(2,1)S(1)}, u32[]{:S(2)}, u32[]{:S(2)}) collective-permute-start(bf16[128,512]{1,0:T(8,128)(2,1)S(1)} %fusion.4), channel_id=1, source_target_pairs={{0,2},{2,4},{4,6},{6,8},{8,10},{10,12},{12,14},{14,16},{16,18},{18... | collective-permute-start | bytes 393224 | tf_op jit(solution)/shard_map/ppermute | solution.py:12
  119.6 0.2 fusion.30
  119.8 5.4 %collective-permute-start.27 = (bf16[128,512]{1,0:T(8,128)(2,1)S(1)}, bf16[128,512]{1,0:T(8,128)(2,1)S(1)}, u32[]{:S(2)}, u32[]{:S(2)}) collective-permute-start(bf16[128,512]{1,0:T(8,128)(2,1)S(1)} %fusion.30), channel_id=1, source_target_pairs={{0,30},{2,0},{4,2},{6,4},{8,6},{10,8},{12,10},{14,12},{16,14},{18,... | collective-permute-start | bytes 393224 | tf_op jit(solution)/shard_map/ppermute | solution.py:12
  125.2 1.6 collective-permute-done.19
  127.1 1.9 %collective-permute-start.20 = (bf16[128,512]{1,0:T(8,128)(2,1)S(1)}, bf16[128,512]{1,0:T(8,128)(2,1)S(1)}, u32[]{:S(2)}, u32[]{:S(2)}) collective-permute-start(bf16[128,512]{1,0:T(8,128)(2,1)S(1)} %fusion.8), channel_id=1, source_target_pairs={{0,2},{2,4},{4,6},{6,8},{8,10},{10,12},{12,14},{14,16},{16,18},{18... | collective-permute-start | bytes 393224 | tf_op jit(solution)/shard_map/ppermute | solution.py:12
  129.3 5.3 %collective-permute-start.28 = (bf16[128,512]{1,0:T(8,128)(2,1)S(1)}, bf16[128,512]{1,0:T(8,128)(2,1)S(1)}, u32[]{:S(2)}, u32[]{:S(2)}) collective-permute-start(bf16[128,512]{1,0:T(8,128)(2,1)S(1)} %fusion.34), channel_id=1, source_target_pairs={{0,30},{2,0},{4,2},{6,4},{8,6},{10,8},{12,10},{14,12},{16,14},{18,... | collective-permute-start | bytes 393224 | tf_op jit(solution)/shard_map/ppermute | solution.py:12
  134.6 1.1 collective-permute-done.20
  136.0 1.9 %collective-permute-start.21 = (bf16[128,512]{1,0:T(8,128)(2,1)S(1)}, bf16[128,512]{1,0:T(8,128)(2,1)S(1)}, u32[]{:S(2)}, u32[]{:S(2)}) collective-permute-start(bf16[128,512]{1,0:T(8,128)(2,1)S(1)} %fusion.12), channel_id=1, source_target_pairs={{0,2},{2,4},{4,6},{6,8},{8,10},{10,12},{12,14},{14,16},{16,18},{18... | collective-permute-start | bytes 393224 | tf_op jit(solution)/shard_map/ppermute | solution.py:12
  137.9 0.2 fusion.38
  138.1 5.1 %collective-permute-start.29 = (bf16[128,512]{1,0:T(8,128)(2,1)S(1)}, bf16[128,512]{1,0:T(8,128)(2,1)S(1)}, u32[]{:S(2)}, u32[]{:S(2)}) collective-permute-start(bf16[128,512]{1,0:T(8,128)(2,1)S(1)} %fusion.38), channel_id=1, source_target_pairs={{0,30},{2,0},{4,2},{6,4},{8,6},{10,8},{12,10},{14,12},{16,14},{18,... | collective-permute-start | bytes 393224 | tf_op jit(solution)/shard_map/ppermute | solution.py:12
  143.3 0.8 collective-permute-done.21
  144.3 1.9 %collective-permute-start.22 = (bf16[128,512]{1,0:T(8,128)(2,1)S(1)}, bf16[128,512]{1,0:T(8,128)(2,1)S(1)}, u32[]{:S(2)}, u32[]{:S(2)}) collective-permute-start(bf16[128,512]{1,0:T(8,128)(2,1)S(1)} %fusion.16), channel_id=1, source_target_pairs={{0,2},{2,4},{4,6},{6,8},{8,10},{10,12},{12,14},{14,16},{16,18},{18... | collective-permute-start | bytes 393224 | tf_op jit(solution)/shard_map/ppermute | solution.py:12
  146.5 5.1 %collective-permute-start.30 = (bf16[128,512]{1,0:T(8,128)(2,1)S(1)}, bf16[128,512]{1,0:T(8,128)(2,1)S(1)}, u32[]{:S(2)}, u32[]{:S(2)}) collective-permute-start(bf16[128,512]{1,0:T(8,128)(2,1)S(1)} %fusion.42), channel_id=1, source_target_pairs={{0,30},{2,0},{4,2},{6,4},{8,6},{10,8},{12,10},{14,12},{16,14},{18,... | collective-permute-start | bytes 393224 | tf_op jit(solution)/shard_map/ppermute | solution.py:12
  151.6 0.8 collective-permute-done.22
  152.6 1.9 %collective-permute-start.23 = (bf16[128,512]{1,0:T(8,128)(2,1)S(1)}, bf16[128,512]{1,0:T(8,128)(2,1)S(1)}, u32[]{:S(2)}, u32[]{:S(2)}) collective-permute-start(bf16[128,512]{1,0:T(8,128)(2,1)S(1)} %fusion.20), channel_id=1, source_target_pairs={{0,2},{2,4},{4,6},{6,8},{8,10},{10,12},{12,14},{14,16},{16,18},{18... | collective-permute-start | bytes 393224 | tf_op jit(solution)/shard_map/ppermute | solution.py:12
  154.8 5.1 %collective-permute-start.31 = (bf16[128,512]{1,0:T(8,128)(2,1)S(1)}, bf16[128,512]{1,0:T(8,128)(2,1)S(1)}, u32[]{:S(2)}, u32[]{:S(2)}) collective-permute-start(bf16[128,512]{1,0:T(8,128)(2,1)S(1)} %fusion.46), channel_id=1, source_target_pairs={{0,30},{2,0},{4,2},{6,4},{8,6},{10,8},{12,10},{14,12},{16,14},{18,... | collective-permute-start | bytes 393224 | tf_op jit(solution)/shard_map/ppermute | solution.py:12
  159.9 0.7 collective-permute-done.23
  160.9 1.9 %collective-permute-start.24 = (bf16[128,512]{1,0:T(8,128)(2,1)S(1)}, bf16[128,512]{1,0:T(8,128)(2,1)S(1)}, u32[]{:S(2)}, u32[]{:S(2)}) collective-permute-start(bf16[128,512]{1,0:T(8,128)(2,1)S(1)} %add_convert_fusion.1), channel_id=1, source_target_pairs={{0,2},{2,4},{4,6},{6,8},{8,10},{10,12},{12,14},{14,16},{16,18},{18... | collective-permute-start | bytes 393224 | tf_op jit(solution)/shard_map/ppermute | solution.py:12
  163.1 5.1 %collective-permute-start.32 = (bf16[128,512]{1,0:T(8,128)(2,1)S(1)}, bf16[128,512]{1,0:T(8,128)(2,1)S(1)}, u32[]{:S(2)}, u32[]{:S(2)}) collective-permute-start(bf16[128,512]{1,0:T(8,128)(2,1)S(1)} %fusion.50), channel_id=1, source_target_pairs={{0,30},{2,0},{4,2},{6,4},{8,6},{10,8},{12,10},{14,12},{16,14},{18,... | collective-permute-start | bytes 393224 | tf_op jit(solution)/shard_map/ppermute | solution.py:12
  168.2 0.7 collective-permute-done.24
  169.2 2.4 %collective-permute-start.25 = (bf16[128,256]{1,0:T(8,128)(2,1)S(1)}, bf16[128,256]{1,0:T(8,128)(2,1)S(1)}, u32[]{:S(2)}, u32[]{:S(2)}) collective-permute-start(bf16[128,256]{1,0:T(8,128)(2,1)S(1)} %select_convert_fusion), channel_id=1, source_target_pairs={{0,1},{1,0},{2,3},{3,2},{4,5},{5,4},{6,7},{7,6},{8,9},{9,8},{10,11... | collective-permute-start | bytes 196616 | tf_op jit(solution)/shard_map/ppermute | solution.py:12
  171.9 4.6 %collective-permute-start.33 = (bf16[128,256]{1,0:T(8,128)(2,1)S(1)}, bf16[128,256]{1,0:T(8,128)(2,1)S(1)}, u32[]{:S(2)}, u32[]{:S(2)}) collective-permute-start(bf16[128,256]{1,0:T(8,128)(2,1)S(1)} %get-tuple-element.54), channel_id=1, source_target_pairs={{0,30},{2,0},{4,2},{6,4},{8,6},{10,8},{12,10},{14,12},{16,14},{18,... | collective-permute-start | bytes 196616 | tf_op jit(solution)/shard_map/ppermute | solution.py:12
  176.5 2.5 %collective-permute-start.34 = (bf16[128,256]{1,0:T(8,128)(2,1)S(1)}, bf16[128,256]{1,0:T(8,128)(2,1)S(1)}, u32[]{:S(2)}, u32[]{:S(2)}) collective-permute-start(bf16[128,256]{1,0:T(8,128)(2,1)S(1)} %get-tuple-element.55), channel_id=1, source_target_pairs={{0,31},{1,30},{2,1},{3,0},{4,3},{5,2},{6,5},{7,4},{8,7},{9,6},{10,... | collective-permute-start | bytes 196616 | tf_op jit(solution)/shard_map/ppermute | solution.py:43
  179.0 4.6 %collective-permute-done.34 = bf16[128,256]{1,0:T(8,128)(2,1)S(1)} collective-permute-done((bf16[128,256]{1,0:T(8,128)(2,1)S(1)}, bf16[128,256]{1,0:T(8,128)(2,1)S(1)}, u32[]{:S(2)}, u32[]{:S(2)}) %collective-permute-start.34) | collective-permute-done | bytes 65568 | tf_op jit(solution)/shard_map/ppermute | solution.py:43
  183.6 0.7 add_convert_fusion.2
  (100 shorter events, 7.8 us)
Async XLA Ops:
  0.6 102.4 %copy-start = (bf16[10,256]{1,0:T(8,128)(2,1)S(1)}, bf16[10,256]{1,0:T(8,128)(2,1)}, u32[]{:S(2)}) copy-start(bf16[10,256]{1,0:T(8,128)(2,1)} %param.13) | copy-start | bytes 15364
  1.6 6.2 %collective-permute-start = (bf16[128,256]{0,1:T(8,128)(2,1)S(1)}, bf16[128,256]{0,1:T(8,128)(2,1)S(1)}, u32[]{:S(2)}, u32[]{:S(2)}) collective-permute-start(bf16[128,256]{0,1:T(8,128)(2,1)S(1)} %copy.10), channel_id=1, source_target_pairs={{0,1},{1,0},{2,3},{3,2},{4,5},{5,4},{6,7},{7,6},{8,9},{9,8},{10,11... | collective-permute-start | bytes 196616 | tf_op jit(solution)/shard_map/ppermute | solution.py:12
  7.8 21.1 %collective-permute-start.1 = (bf16[128,512]{0,1:T(8,128)(2,1)S(1)}, bf16[128,512]{0,1:T(8,128)(2,1)S(1)}, u32[]{:S(2)}, u32[]{:S(2)}) collective-permute-start(bf16[128,512]{0,1:T(8,128)(2,1)S(1)} %maximum_select_fusion.1), channel_id=1, source_target_pairs={{0,30},{2,0},{4,2},{6,4},{8,6},{10,8},{12,10},{14,12},{16,14},{18,... | collective-permute-start | bytes 393224 | tf_op jit(solution)/shard_map/ppermute | solution.py:12
  26.0 8.1 %collective-permute-start.8 = (bf16[128,512]{0,1:T(8,128)(2,1)S(1)}, bf16[128,512]{0,1:T(8,128)(2,1)S(1)}, u32[]{:S(2)}, u32[]{:S(2)}) collective-permute-start(bf16[128,512]{0,1:T(8,128)(2,1)S(1)} %maximum_select_fusion.1), channel_id=1, source_target_pairs={{0,2},{2,4},{4,6},{6,8},{8,10},{10,12},{12,14},{14,16},{16,18},{18... | collective-permute-start | bytes 393224 | tf_op jit(solution)/shard_map/ppermute | solution.py:12
  28.9 7.7 %collective-permute-start.2 = (bf16[128,512]{0,1:T(8,128)(2,1)S(1)}, bf16[128,512]{0,1:T(8,128)(2,1)S(1)}, u32[]{:S(2)}, u32[]{:S(2)}) collective-permute-start(bf16[128,512]{0,1:T(8,128)(2,1)S(1)} %collective-permute-done.1), channel_id=1, source_target_pairs={{0,30},{2,0},{4,2},{6,4},{8,6},{10,8},{12,10},{14,12},{16,14},{18,... | collective-permute-start | bytes 393224 | tf_op jit(solution)/shard_map/ppermute | solution.py:12
  34.1 8.1 %collective-permute-start.9 = (bf16[128,512]{0,1:T(8,128)(2,1)S(1)}, bf16[128,512]{0,1:T(8,128)(2,1)S(1)}, u32[]{:S(2)}, u32[]{:S(2)}) collective-permute-start(bf16[128,512]{0,1:T(8,128)(2,1)S(1)} %collective-permute-done.8), channel_id=1, source_target_pairs={{0,2},{2,4},{4,6},{6,8},{8,10},{10,12},{12,14},{14,16},{16,18},{18... | collective-permute-start | bytes 393224 | tf_op jit(solution)/shard_map/ppermute | solution.py:12
  36.6 8.1 %collective-permute-start.3 = (bf16[128,512]{0,1:T(8,128)(2,1)S(1)}, bf16[128,512]{0,1:T(8,128)(2,1)S(1)}, u32[]{:S(2)}, u32[]{:S(2)}) collective-permute-start(bf16[128,512]{0,1:T(8,128)(2,1)S(1)} %collective-permute-done.2), channel_id=1, source_target_pairs={{0,30},{2,0},{4,2},{6,4},{8,6},{10,8},{12,10},{14,12},{16,14},{18,... | collective-permute-start | bytes 393224 | tf_op jit(solution)/shard_map/ppermute | solution.py:12
  42.2 8.1 %collective-permute-start.10 = (bf16[128,512]{0,1:T(8,128)(2,1)S(1)}, bf16[128,512]{0,1:T(8,128)(2,1)S(1)}, u32[]{:S(2)}, u32[]{:S(2)}) collective-permute-start(bf16[128,512]{0,1:T(8,128)(2,1)S(1)} %collective-permute-done.9), channel_id=1, source_target_pairs={{0,2},{2,4},{4,6},{6,8},{8,10},{10,12},{12,14},{14,16},{16,18},{18... | collective-permute-start | bytes 393224 | tf_op jit(solution)/shard_map/ppermute | solution.py:12
  44.7 8.1 %collective-permute-start.4 = (bf16[128,512]{0,1:T(8,128)(2,1)S(1)}, bf16[128,512]{0,1:T(8,128)(2,1)S(1)}, u32[]{:S(2)}, u32[]{:S(2)}) collective-permute-start(bf16[128,512]{0,1:T(8,128)(2,1)S(1)} %collective-permute-done.3), channel_id=1, source_target_pairs={{0,30},{2,0},{4,2},{6,4},{8,6},{10,8},{12,10},{14,12},{16,14},{18,... | collective-permute-start | bytes 393224 | tf_op jit(solution)/shard_map/ppermute | solution.py:12
  50.2 8.1 %collective-permute-start.11 = (bf16[128,512]{0,1:T(8,128)(2,1)S(1)}, bf16[128,512]{0,1:T(8,128)(2,1)S(1)}, u32[]{:S(2)}, u32[]{:S(2)}) collective-permute-start(bf16[128,512]{0,1:T(8,128)(2,1)S(1)} %collective-permute-done.10), channel_id=1, source_target_pairs={{0,2},{2,4},{4,6},{6,8},{8,10},{10,12},{12,14},{14,16},{16,18},{18... | collective-permute-start | bytes 393224 | tf_op jit(solution)/shard_map/ppermute | solution.py:12
  52.7 8.9 %collective-permute-start.5 = (bf16[128,512]{0,1:T(8,128)(2,1)S(1)}, bf16[128,512]{0,1:T(8,128)(2,1)S(1)}, u32[]{:S(2)}, u32[]{:S(2)}) collective-permute-start(bf16[128,512]{0,1:T(8,128)(2,1)S(1)} %collective-permute-done.4), channel_id=1, source_target_pairs={{0,30},{2,0},{4,2},{6,4},{8,6},{10,8},{12,10},{14,12},{16,14},{18,... | collective-permute-start | bytes 393224 | tf_op jit(solution)/shard_map/ppermute | solution.py:12
  58.3 9.2 %collective-permute-start.12 = (bf16[128,512]{0,1:T(8,128)(2,1)S(1)}, bf16[128,512]{0,1:T(8,128)(2,1)S(1)}, u32[]{:S(2)}, u32[]{:S(2)}) collective-permute-start(bf16[128,512]{0,1:T(8,128)(2,1)S(1)} %collective-permute-done.11), channel_id=1, source_target_pairs={{0,2},{2,4},{4,6},{6,8},{8,10},{10,12},{12,14},{14,16},{16,18},{18... | collective-permute-start | bytes 393224 | tf_op jit(solution)/shard_map/ppermute | solution.py:12
  61.7 8.8 %collective-permute-start.6 = (bf16[128,512]{0,1:T(8,128)(2,1)S(1)}, bf16[128,512]{0,1:T(8,128)(2,1)S(1)}, u32[]{:S(2)}, u32[]{:S(2)}) collective-permute-start(bf16[128,512]{0,1:T(8,128)(2,1)S(1)} %collective-permute-done.5), channel_id=1, source_target_pairs={{0,30},{2,0},{4,2},{6,4},{8,6},{10,8},{12,10},{14,12},{16,14},{18,... | collective-permute-start | bytes 393224 | tf_op jit(solution)/shard_map/ppermute | solution.py:12
  67.5 8.6 %collective-permute-start.13 = (bf16[128,512]{0,1:T(8,128)(2,1)S(1)}, bf16[128,512]{0,1:T(8,128)(2,1)S(1)}, u32[]{:S(2)}, u32[]{:S(2)}) collective-permute-start(bf16[128,512]{0,1:T(8,128)(2,1)S(1)} %collective-permute-done.12), channel_id=1, source_target_pairs={{0,2},{2,4},{4,6},{6,8},{8,10},{10,12},{12,14},{14,16},{16,18},{18... | collective-permute-start | bytes 393224 | tf_op jit(solution)/shard_map/ppermute | solution.py:12
  70.5 15.6 %collective-permute-start.7 = (bf16[128,512]{0,1:T(8,128)(2,1)S(1)}, bf16[128,512]{0,1:T(8,128)(2,1)S(1)}, u32[]{:S(2)}, u32[]{:S(2)}) collective-permute-start(bf16[128,512]{0,1:T(8,128)(2,1)S(1)} %collective-permute-done.6), channel_id=1, source_target_pairs={{0,30},{2,0},{4,2},{6,4},{8,6},{10,8},{12,10},{14,12},{16,14},{18,... | collective-permute-start | bytes 393224 | tf_op jit(solution)/shard_map/ppermute | solution.py:12
  76.1 8.1 %collective-permute-start.14 = (bf16[128,512]{0,1:T(8,128)(2,1)S(1)}, bf16[128,512]{0,1:T(8,128)(2,1)S(1)}, u32[]{:S(2)}, u32[]{:S(2)}) collective-permute-start(bf16[128,512]{0,1:T(8,128)(2,1)S(1)} %collective-permute-done.13), channel_id=1, source_target_pairs={{0,2},{2,4},{4,6},{6,8},{8,10},{10,12},{12,14},{14,16},{16,18},{18... | collective-permute-start | bytes 393224 | tf_op jit(solution)/shard_map/ppermute | solution.py:12
  84.2 8.1 %collective-permute-start.15 = (bf16[128,512]{0,1:T(8,128)(2,1)S(1)}, bf16[128,512]{0,1:T(8,128)(2,1)S(1)}, u32[]{:S(2)}, u32[]{:S(2)}) collective-permute-start(bf16[128,512]{0,1:T(8,128)(2,1)S(1)} %collective-permute-done.14), channel_id=1, source_target_pairs={{0,2},{2,4},{4,6},{6,8},{8,10},{10,12},{12,14},{14,16},{16,18},{18... | collective-permute-start | bytes 393224 | tf_op jit(solution)/shard_map/ppermute | solution.py:12
  92.4 2.2 %copy-start.1 = (bf16[8192,256]{1,0:T(8,128)(2,1)S(1)}, bf16[8192,256]{1,0:T(8,128)(2,1)}, u32[]{:S(2)}) copy-start(bf16[8192,256]{1,0:T(8,128)(2,1)} %param.10) | copy-start | bytes 12582916
  93.1 4.5 %copy-start.2 = (bf16[8192,256]{1,0:T(8,128)(2,1)S(1)}, bf16[8192,256]{1,0:T(8,128)(2,1)}, u32[]{:S(2)}) copy-start(bf16[8192,256]{1,0:T(8,128)(2,1)} %param.9) | copy-start | bytes 12582916
  95.6 7.4 %copy-start.3 = (f32[256]{0:T(256)S(1)}, f32[256]{0:T(256)}, u32[]{:S(2)}) copy-start(f32[256]{0:T(256)} %param.12) | copy-start | bytes 3076
  95.6 7.4 %copy-start.4 = (s32[128]{0:T(128)S(1)}, s32[128]{0:T(128)}, u32[]{:S(2)}) copy-start(s32[128]{0:T(128)} %param.14) | copy-start | bytes 1540
  95.7 7.3 %collective-permute-start.16 = (bf16[3,256]{1,0:T(4,128)(2,1)S(1)}, bf16[3,256]{1,0:T(4,128)(2,1)S(1)}, u32[]{:S(2)}, u32[]{:S(2)}) collective-permute-start(bf16[3,256]{1,0:T(4,128)(2,1)S(1)} %slice.97), channel_id=1, source_target_pairs={{0,32},{32,64},{64,96},{96,128},{128,160},{160,192},{192,224},{224... | collective-permute-start | bytes 4616 | tf_op jit(solution)/shard_map/ppermute | solution.py:98
  103.3 3.7 %collective-permute-start.17 = (f32[3,256]{1,0:T(4,128)S(1)}, f32[3,256]{1,0:T(4,128)S(1)}, u32[]{:S(2)}, u32[]{:S(2)}) collective-permute-start(f32[3,256]{1,0:T(4,128)S(1)} %fusion.154), channel_id=1, source_target_pairs={{32,0},{64,32},{96,64},{128,96},{160,128},{192,160},{224,192},{256... | collective-permute-start | bytes 9224 | tf_op jit(solution)/shard_map/ppermute | solution.py:98
  107.2 10.1 %collective-permute-start.18 = (bf16[128,512]{1,0:T(8,128)(2,1)S(1)}, bf16[128,512]{1,0:T(8,128)(2,1)S(1)}, u32[]{:S(2)}, u32[]{:S(2)}) collective-permute-start(bf16[128,512]{1,0:T(8,128)(2,1)S(1)} %fusion), channel_id=1, source_target_pairs={{0,2},{2,4},{4,6},{6,8},{8,10},{10,12},{12,14},{14,16},{16,18},{18... | collective-permute-start | bytes 393224 | tf_op jit(solution)/shard_map/ppermute | solution.py:12
  110.8 8.7 %collective-permute-start.26 = (bf16[128,512]{1,0:T(8,128)(2,1)S(1)}, bf16[128,512]{1,0:T(8,128)(2,1)S(1)}, u32[]{:S(2)}, u32[]{:S(2)}) collective-permute-start(bf16[128,512]{1,0:T(8,128)(2,1)S(1)} %fusion.26), channel_id=1, source_target_pairs={{0,30},{2,0},{4,2},{6,4},{8,6},{10,8},{12,10},{14,12},{16,14},{18,... | collective-permute-start | bytes 393224 | tf_op jit(solution)/shard_map/ppermute | solution.py:12
  117.6 9.3 %collective-permute-start.19 = (bf16[128,512]{1,0:T(8,128)(2,1)S(1)}, bf16[128,512]{1,0:T(8,128)(2,1)S(1)}, u32[]{:S(2)}, u32[]{:S(2)}) collective-permute-start(bf16[128,512]{1,0:T(8,128)(2,1)S(1)} %fusion.4), channel_id=1, source_target_pairs={{0,2},{2,4},{4,6},{6,8},{8,10},{10,12},{12,14},{14,16},{16,18},{18... | collective-permute-start | bytes 393224 | tf_op jit(solution)/shard_map/ppermute | solution.py:12
  119.8 9.2 %collective-permute-start.27 = (bf16[128,512]{1,0:T(8,128)(2,1)S(1)}, bf16[128,512]{1,0:T(8,128)(2,1)S(1)}, u32[]{:S(2)}, u32[]{:S(2)}) collective-permute-start(bf16[128,512]{1,0:T(8,128)(2,1)S(1)} %fusion.30), channel_id=1, source_target_pairs={{0,30},{2,0},{4,2},{6,4},{8,6},{10,8},{12,10},{14,12},{16,14},{18,... | collective-permute-start | bytes 393224 | tf_op jit(solution)/shard_map/ppermute | solution.py:12
  127.1 8.6 %collective-permute-start.20 = (bf16[128,512]{1,0:T(8,128)(2,1)S(1)}, bf16[128,512]{1,0:T(8,128)(2,1)S(1)}, u32[]{:S(2)}, u32[]{:S(2)}) collective-permute-start(bf16[128,512]{1,0:T(8,128)(2,1)S(1)} %fusion.8), channel_id=1, source_target_pairs={{0,2},{2,4},{4,6},{6,8},{8,10},{10,12},{12,14},{14,16},{16,18},{18... | collective-permute-start | bytes 393224 | tf_op jit(solution)/shard_map/ppermute | solution.py:12
  129.3 8.6 %collective-permute-start.28 = (bf16[128,512]{1,0:T(8,128)(2,1)S(1)}, bf16[128,512]{1,0:T(8,128)(2,1)S(1)}, u32[]{:S(2)}, u32[]{:S(2)}) collective-permute-start(bf16[128,512]{1,0:T(8,128)(2,1)S(1)} %fusion.34), channel_id=1, source_target_pairs={{0,30},{2,0},{4,2},{6,4},{8,6},{10,8},{12,10},{14,12},{16,14},{18,... | collective-permute-start | bytes 393224 | tf_op jit(solution)/shard_map/ppermute | solution.py:12
  136.0 8.1 %collective-permute-start.21 = (bf16[128,512]{1,0:T(8,128)(2,1)S(1)}, bf16[128,512]{1,0:T(8,128)(2,1)S(1)}, u32[]{:S(2)}, u32[]{:S(2)}) collective-permute-start(bf16[128,512]{1,0:T(8,128)(2,1)S(1)} %fusion.12), channel_id=1, source_target_pairs={{0,2},{2,4},{4,6},{6,8},{8,10},{10,12},{12,14},{14,16},{16,18},{18... | collective-permute-start | bytes 393224 | tf_op jit(solution)/shard_map/ppermute | solution.py:12
  138.1 8.1 %collective-permute-start.29 = (bf16[128,512]{1,0:T(8,128)(2,1)S(1)}, bf16[128,512]{1,0:T(8,128)(2,1)S(1)}, u32[]{:S(2)}, u32[]{:S(2)}) collective-permute-start(bf16[128,512]{1,0:T(8,128)(2,1)S(1)} %fusion.38), channel_id=1, source_target_pairs={{0,30},{2,0},{4,2},{6,4},{8,6},{10,8},{12,10},{14,12},{16,14},{18,... | collective-permute-start | bytes 393224 | tf_op jit(solution)/shard_map/ppermute | solution.py:12
  144.3 8.1 %collective-permute-start.22 = (bf16[128,512]{1,0:T(8,128)(2,1)S(1)}, bf16[128,512]{1,0:T(8,128)(2,1)S(1)}, u32[]{:S(2)}, u32[]{:S(2)}) collective-permute-start(bf16[128,512]{1,0:T(8,128)(2,1)S(1)} %fusion.16), channel_id=1, source_target_pairs={{0,2},{2,4},{4,6},{6,8},{8,10},{10,12},{12,14},{14,16},{16,18},{18... | collective-permute-start | bytes 393224 | tf_op jit(solution)/shard_map/ppermute | solution.py:12
  146.5 8.1 %collective-permute-start.30 = (bf16[128,512]{1,0:T(8,128)(2,1)S(1)}, bf16[128,512]{1,0:T(8,128)(2,1)S(1)}, u32[]{:S(2)}, u32[]{:S(2)}) collective-permute-start(bf16[128,512]{1,0:T(8,128)(2,1)S(1)} %fusion.42), channel_id=1, source_target_pairs={{0,30},{2,0},{4,2},{6,4},{8,6},{10,8},{12,10},{14,12},{16,14},{18,... | collective-permute-start | bytes 393224 | tf_op jit(solution)/shard_map/ppermute | solution.py:12
  152.6 8.1 %collective-permute-start.23 = (bf16[128,512]{1,0:T(8,128)(2,1)S(1)}, bf16[128,512]{1,0:T(8,128)(2,1)S(1)}, u32[]{:S(2)}, u32[]{:S(2)}) collective-permute-start(bf16[128,512]{1,0:T(8,128)(2,1)S(1)} %fusion.20), channel_id=1, source_target_pairs={{0,2},{2,4},{4,6},{6,8},{8,10},{10,12},{12,14},{14,16},{16,18},{18... | collective-permute-start | bytes 393224 | tf_op jit(solution)/shard_map/ppermute | solution.py:12
  154.8 8.1 %collective-permute-start.31 = (bf16[128,512]{1,0:T(8,128)(2,1)S(1)}, bf16[128,512]{1,0:T(8,128)(2,1)S(1)}, u32[]{:S(2)}, u32[]{:S(2)}) collective-permute-start(bf16[128,512]{1,0:T(8,128)(2,1)S(1)} %fusion.46), channel_id=1, source_target_pairs={{0,30},{2,0},{4,2},{6,4},{8,6},{10,8},{12,10},{14,12},{16,14},{18,... | collective-permute-start | bytes 393224 | tf_op jit(solution)/shard_map/ppermute | solution.py:12
  160.9 8.1 %collective-permute-start.24 = (bf16[128,512]{1,0:T(8,128)(2,1)S(1)}, bf16[128,512]{1,0:T(8,128)(2,1)S(1)}, u32[]{:S(2)}, u32[]{:S(2)}) collective-permute-start(bf16[128,512]{1,0:T(8,128)(2,1)S(1)} %add_convert_fusion.1), channel_id=1, source_target_pairs={{0,2},{2,4},{4,6},{6,8},{8,10},{10,12},{12,14},{14,16},{16,18},{18... | collective-permute-start | bytes 393224 | tf_op jit(solution)/shard_map/ppermute | solution.py:12
  163.1 8.6 %collective-permute-start.32 = (bf16[128,512]{1,0:T(8,128)(2,1)S(1)}, bf16[128,512]{1,0:T(8,128)(2,1)S(1)}, u32[]{:S(2)}, u32[]{:S(2)}) collective-permute-start(bf16[128,512]{1,0:T(8,128)(2,1)S(1)} %fusion.50), channel_id=1, source_target_pairs={{0,30},{2,0},{4,2},{6,4},{8,6},{10,8},{12,10},{14,12},{16,14},{18,... | collective-permute-start | bytes 393224 | tf_op jit(solution)/shard_map/ppermute | solution.py:12
  169.2 9.8 %collective-permute-start.25 = (bf16[128,256]{1,0:T(8,128)(2,1)S(1)}, bf16[128,256]{1,0:T(8,128)(2,1)S(1)}, u32[]{:S(2)}, u32[]{:S(2)}) collective-permute-start(bf16[128,256]{1,0:T(8,128)(2,1)S(1)} %select_convert_fusion), channel_id=1, source_target_pairs={{0,1},{1,0},{2,3},{3,2},{4,5},{5,4},{6,7},{7,6},{8,9},{9,8},{10,11... | collective-permute-start | bytes 196616 | tf_op jit(solution)/shard_map/ppermute | solution.py:12
  171.9 7.1 %collective-permute-start.33 = (bf16[128,256]{1,0:T(8,128)(2,1)S(1)}, bf16[128,256]{1,0:T(8,128)(2,1)S(1)}, u32[]{:S(2)}, u32[]{:S(2)}) collective-permute-start(bf16[128,256]{1,0:T(8,128)(2,1)S(1)} %get-tuple-element.54), channel_id=1, source_target_pairs={{0,30},{2,0},{4,2},{6,4},{8,6},{10,8},{12,10},{14,12},{16,14},{18,... | collective-permute-start | bytes 196616 | tf_op jit(solution)/shard_map/ppermute | solution.py:12
  176.5 7.1 %collective-permute-start.34 = (bf16[128,256]{1,0:T(8,128)(2,1)S(1)}, bf16[128,256]{1,0:T(8,128)(2,1)S(1)}, u32[]{:S(2)}, u32[]{:S(2)}) collective-permute-start(bf16[128,256]{1,0:T(8,128)(2,1)S(1)} %get-tuple-element.55), channel_id=1, source_target_pairs={{0,31},{1,30},{2,1},{3,0},{4,3},{5,2},{6,5},{7,4},{8,7},{9,6},{10,... | collective-permute-start | bytes 196616 | tf_op jit(solution)/shard_map/ppermute | solution.py:43

commit v10 on v8

--- a/solution.py
+++ b/solution.py
@@ -141,7 +141,7 @@
     def block_terms(place, dgate16, dxin16):
         gate_rows = lax.dynamic_slice_in_dim(w_gate, place * width, width, 0)
         conv_rows = lax.dynamic_slice_in_dim(w_conv_in, place * width, width, 0)
-        part = lax.dot_general(dgate16, gate_rows, spec, preferred_element_type=jnp.float32)
+        part = lax.optimization_barrier(lax.dot_general(dgate16, gate_rows, spec, preferred_element_type=jnp.float32))
         part = part + lax.dot_general(dxin16, conv_rows, spec, preferred_element_type=jnp.float32)
         return part.astype(jnp.bfloat16)
 

time: 182 us -> 182 us (level)
  no operation moved by 1% of the time
where the time goes in v10:
time: 182 us; the launch traced here: 180 us
  starting transfers between devices  130 us (71%)
  waiting for transfers between devices  33.1 us (18%)
  matrix products  9.52 us (5%)
  local copies, waits for them, and re-layouts  4.14 us (2%)
  other arithmetic  2.27 us (1%)
  between operations  1.83 us (1%)
    ppermute x32, starting transfers between devices, shifted(): lax.ppermute(block, axis, [(i, (i + distance) % size) for i in range(size)])  126 us
    ppermute x32, waiting for transfers between devices, shifted(): lax.ppermute(block, axis, [(i, (i + distance) % size) for i in range(size)])  28.7 us
    ppermute x2, waiting for transfers between devices, passed_along(): return lax.ppermute(block, axis, route)  4.38 us
    ppermute x2, starting transfers between devices, passed_along(): return lax.ppermute(block, axis, route)  3.84 us
    dot_general x16, matrix products, block_terms(): lax.dot_general(dxin16, conv_rows, spec, preferred_element_type=jnp.float32)  3.66 us
  transfers between devices with their start and end apart: 34, of which 21 were waited for; matrix products, arithmetic and copies ran while one was open for 6% of the time, Pallas kernels for 0%

profile of v10, /device:TPU:56, one launch (start us, length us, event | category | flops | bytes accessed | tf_op | source)
XLA Modules:
  0.0 180.4 jit_solution(15319171575145876411)
XLA Ops:
  0.6 1.0 copy.10
  1.6 3.4 %collective-permute-start = (bf16[128,256]{0,1:T(8,128)(2,1)S(1)}, bf16[128,256]{0,1:T(8,128)(2,1)S(1)}, u32[]{:S(2)}, u32[]{:S(2)}) collective-permute-start(bf16[128,256]{0,1:T(8,128)(2,1)S(1)} %copy.10), channel_id=1, source_target_pairs={{0,1},{1,0},{2,3},{3,2},{4,5},{5,4},{6,7},{7,6},{8,9},{9,8},{10,11... | collective-permute-start | bytes 196616 | tf_op jit(solution)/shard_map/ppermute | solution.py:12
  5.0 0.8 fusion.159
  5.9 1.9 %collective-permute-done = bf16[128,256]{0,1:T(8,128)(2,1)S(1)} collective-permute-done((bf16[128,256]{0,1:T(8,128)(2,1)S(1)}, bf16[128,256]{0,1:T(8,128)(2,1)S(1)}, u32[]{:S(2)}, u32[]{:S(2)}) %collective-permute-start) | collective-permute-done | bytes 65568 | tf_op jit(solution)/shard_map/ppermute | solution.py:12
  7.8 18.2 %collective-permute-start.1 = (bf16[128,512]{0,1:T(8,128)(2,1)S(1)}, bf16[128,512]{0,1:T(8,128)(2,1)S(1)}, u32[]{:S(2)}, u32[]{:S(2)}) collective-permute-start(bf16[128,512]{0,1:T(8,128)(2,1)S(1)} %maximum_select_fusion.1), channel_id=1, source_target_pairs={{0,30},{2,0},{4,2},{6,4},{8,6},{10,8},{12,10},{14,12},{16,14},{18,... | collective-permute-start | bytes 393224 | tf_op jit(solution)/shard_map/ppermute | solution.py:12
  26.0 1.9 %collective-permute-start.8 = (bf16[128,512]{0,1:T(8,128)(2,1)S(1)}, bf16[128,512]{0,1:T(8,128)(2,1)S(1)}, u32[]{:S(2)}, u32[]{:S(2)}) collective-permute-start(bf16[128,512]{0,1:T(8,128)(2,1)S(1)} %maximum_select_fusion.1), channel_id=1, source_target_pairs={{0,2},{2,4},{4,6},{6,8},{8,10},{10,12},{12,14},{14,16},{16,18},{18... | collective-permute-start | bytes 393224 | tf_op jit(solution)/shard_map/ppermute | solution.py:12
  28.2 0.7 convert_element_type.215
  28.9 5.2 %collective-permute-start.2 = (bf16[128,512]{0,1:T(8,128)(2,1)S(1)}, bf16[128,512]{0,1:T(8,128)(2,1)S(1)}, u32[]{:S(2)}, u32[]{:S(2)}) collective-permute-start(bf16[128,512]{0,1:T(8,128)(2,1)S(1)} %collective-permute-done.1), channel_id=1, source_target_pairs={{0,30},{2,0},{4,2},{6,4},{8,6},{10,8},{12,10},{14,12},{16,14},{18,... | collective-permute-start | bytes 393224 | tf_op jit(solution)/shard_map/ppermute | solution.py:12
  34.1 1.9 %collective-permute-start.9 = (bf16[128,512]{0,1:T(8,128)(2,1)S(1)}, bf16[128,512]{0,1:T(8,128)(2,1)S(1)}, u32[]{:S(2)}, u32[]{:S(2)}) collective-permute-start(bf16[128,512]{0,1:T(8,128)(2,1)S(1)} %collective-permute-done.8), channel_id=1, source_target_pairs={{0,2},{2,4},{4,6},{6,8},{8,10},{10,12},{12,14},{14,16},{16,18},{18... | collective-permute-start | bytes 393224 | tf_op jit(solution)/shard_map/ppermute | solution.py:12
  36.1 0.5 collective-permute-done.2
  36.6 5.6 %collective-permute-start.3 = (bf16[128,512]{0,1:T(8,128)(2,1)S(1)}, bf16[128,512]{0,1:T(8,128)(2,1)S(1)}, u32[]{:S(2)}, u32[]{:S(2)}) collective-permute-start(bf16[128,512]{0,1:T(8,128)(2,1)S(1)} %collective-permute-done.2), channel_id=1, source_target_pairs={{0,30},{2,0},{4,2},{6,4},{8,6},{10,8},{12,10},{14,12},{16,14},{18,... | collective-permute-start | bytes 393224 | tf_op jit(solution)/shard_map/ppermute | solution.py:12
  42.2 1.9 %collective-permute-start.10 = (bf16[128,512]{0,1:T(8,128)(2,1)S(1)}, bf16[128,512]{0,1:T(8,128)(2,1)S(1)}, u32[]{:S(2)}, u32[]{:S(2)}) collective-permute-start(bf16[128,512]{0,1:T(8,128)(2,1)S(1)} %collective-permute-done.9), channel_id=1, source_target_pairs={{0,2},{2,4},{4,6},{6,8},{8,10},{10,12},{12,14},{14,16},{16,18},{18... | collective-permute-start | bytes 393224 | tf_op jit(solution)/shard_map/ppermute | solution.py:12
  44.1 0.5 collective-permute-done.3
  44.7 5.6 %collective-permute-start.4 = (bf16[128,512]{0,1:T(8,128)(2,1)S(1)}, bf16[128,512]{0,1:T(8,128)(2,1)S(1)}, u32[]{:S(2)}, u32[]{:S(2)}) collective-permute-start(bf16[128,512]{0,1:T(8,128)(2,1)S(1)} %collective-permute-done.3), channel_id=1, source_target_pairs={{0,30},{2,0},{4,2},{6,4},{8,6},{10,8},{12,10},{14,12},{16,14},{18,... | collective-permute-start | bytes 393224 | tf_op jit(solution)/shard_map/ppermute | solution.py:12
  50.2 1.9 %collective-permute-start.11 = (bf16[128,512]{0,1:T(8,128)(2,1)S(1)}, bf16[128,512]{0,1:T(8,128)(2,1)S(1)}, u32[]{:S(2)}, u32[]{:S(2)}) collective-permute-start(bf16[128,512]{0,1:T(8,128)(2,1)S(1)} %collective-permute-done.10), channel_id=1, source_target_pairs={{0,2},{2,4},{4,6},{6,8},{8,10},{10,12},{12,14},{14,16},{16,18},{18... | collective-permute-start | bytes 393224 | tf_op jit(solution)/shard_map/ppermute | solution.py:12
  52.2 0.5 collective-permute-done.4
  52.7 5.6 %collective-permute-start.5 = (bf16[128,512]{0,1:T(8,128)(2,1)S(1)}, bf16[128,512]{0,1:T(8,128)(2,1)S(1)}, u32[]{:S(2)}, u32[]{:S(2)}) collective-permute-start(bf16[128,512]{0,1:T(8,128)(2,1)S(1)} %collective-permute-done.4), channel_id=1, source_target_pairs={{0,30},{2,0},{4,2},{6,4},{8,6},{10,8},{12,10},{14,12},{16,14},{18,... | collective-permute-start | bytes 393224 | tf_op jit(solution)/shard_map/ppermute | solution.py:12
  58.3 1.9 %collective-permute-start.12 = (bf16[128,512]{0,1:T(8,128)(2,1)S(1)}, bf16[128,512]{0,1:T(8,128)(2,1)S(1)}, u32[]{:S(2)}, u32[]{:S(2)}) collective-permute-start(bf16[128,512]{0,1:T(8,128)(2,1)S(1)} %collective-permute-done.11), channel_id=1, source_target_pairs={{0,2},{2,4},{4,6},{6,8},{8,10},{10,12},{12,14},{14,16},{16,18},{18... | collective-permute-start | bytes 393224 | tf_op jit(solution)/shard_map/ppermute | solution.py:12
  60.2 1.4 collective-permute-done.5
  61.7 5.6 %collective-permute-start.6 = (bf16[128,512]{0,1:T(8,128)(2,1)S(1)}, bf16[128,512]{0,1:T(8,128)(2,1)S(1)}, u32[]{:S(2)}, u32[]{:S(2)}) collective-permute-start(bf16[128,512]{0,1:T(8,128)(2,1)S(1)} %collective-permute-done.5), channel_id=1, source_target_pairs={{0,30},{2,0},{4,2},{6,4},{8,6},{10,8},{12,10},{14,12},{16,14},{18,... | collective-permute-start | bytes 393224 | tf_op jit(solution)/shard_map/ppermute | solution.py:12
  67.2 0.2 collective-permute-done.12
  67.5 1.9 %collective-permute-start.13 = (bf16[128,512]{0,1:T(8,128)(2,1)S(1)}, bf16[128,512]{0,1:T(8,128)(2,1)S(1)}, u32[]{:S(2)}, u32[]{:S(2)}) collective-permute-start(bf16[128,512]{0,1:T(8,128)(2,1)S(1)} %collective-permute-done.12), channel_id=1, source_target_pairs={{0,2},{2,4},{4,6},{6,8},{8,10},{10,12},{12,14},{14,16},{16,18},{18... | collective-permute-start | bytes 393224 | tf_op jit(solution)/shard_map/ppermute | solution.py:12
  69.4 1.0 collective-permute-done.6
  70.5 5.6 %collective-permute-start.7 = (bf16[128,512]{0,1:T(8,128)(2,1)S(1)}, bf16[128,512]{0,1:T(8,128)(2,1)S(1)}, u32[]{:S(2)}, u32[]{:S(2)}) collective-permute-start(bf16[128,512]{0,1:T(8,128)(2,1)S(1)} %collective-permute-done.6), channel_id=1, source_target_pairs={{0,30},{2,0},{4,2},{6,4},{8,6},{10,8},{12,10},{14,12},{16,14},{18,... | collective-permute-start | bytes 393224 | tf_op jit(solution)/shard_map/ppermute | solution.py:12
  76.1 1.9 %collective-permute-start.14 = (bf16[128,512]{0,1:T(8,128)(2,1)S(1)}, bf16[128,512]{0,1:T(8,128)(2,1)S(1)}, u32[]{:S(2)}, u32[]{:S(2)}) collective-permute-start(bf16[128,512]{0,1:T(8,128)(2,1)S(1)} %collective-permute-done.13), channel_id=1, source_target_pairs={{0,2},{2,4},{4,6},{6,8},{8,10},{10,12},{12,14},{14,16},{16,18},{18... | collective-permute-start | bytes 393224 | tf_op jit(solution)/shard_map/ppermute | solution.py:12
  78.0 6.1 %collective-permute-done.14 = bf16[128,512]{0,1:T(8,128)(2,1)S(1)} collective-permute-done((bf16[128,512]{0,1:T(8,128)(2,1)S(1)}, bf16[128,512]{0,1:T(8,128)(2,1)S(1)}, u32[]{:S(2)}, u32[]{:S(2)}) %collective-permute-start.14) | collective-permute-done | bytes 131104 | tf_op jit(solution)/shard_map/ppermute | solution.py:12
  84.2 1.9 %collective-permute-start.15 = (bf16[128,512]{0,1:T(8,128)(2,1)S(1)}, bf16[128,512]{0,1:T(8,128)(2,1)S(1)}, u32[]{:S(2)}, u32[]{:S(2)}) collective-permute-start(bf16[128,512]{0,1:T(8,128)(2,1)S(1)} %collective-permute-done.14), channel_id=1, source_target_pairs={{0,2},{2,4},{4,6},{6,8},{8,10},{10,12},{12,14},{14,16},{16,18},{18... | collective-permute-start | bytes 393224 | tf_op jit(solution)/shard_map/ppermute | solution.py:12
  86.1 6.1 %collective-permute-done.15 = bf16[128,512]{0,1:T(8,128)(2,1)S(1)} collective-permute-done((bf16[128,512]{0,1:T(8,128)(2,1)S(1)}, bf16[128,512]{0,1:T(8,128)(2,1)S(1)}, u32[]{:S(2)}, u32[]{:S(2)}) %collective-permute-start.15) | collective-permute-done | bytes 131104 | tf_op jit(solution)/shard_map/ppermute | solution.py:12
  93.1 1.5 copy-done.2
  94.6 1.0 convolution_convert_fusion.1
  95.7 1.9 %collective-permute-start.16 = (bf16[3,256]{1,0:T(4,128)(2,1)S(1)}, bf16[3,256]{1,0:T(4,128)(2,1)S(1)}, u32[]{:S(2)}, u32[]{:S(2)}) collective-permute-start(bf16[3,256]{1,0:T(4,128)(2,1)S(1)} %slice.87), channel_id=1, source_target_pairs={{0,32},{32,64},{64,96},{96,128},{128,160},{160,192},{192,224},{224... | collective-permute-start | bytes 4616 | tf_op jit(solution)/shard_map/ppermute | solution.py:89
  97.6 1.0 convolution_convert_fusion
  98.6 4.4 %collective-permute-done.16 = bf16[3,256]{1,0:T(4,128)(2,1)S(1)} collective-permute-done((bf16[3,256]{1,0:T(4,128)(2,1)S(1)}, bf16[3,256]{1,0:T(4,128)(2,1)S(1)}, u32[]{:S(2)}, u32[]{:S(2)}) %collective-permute-start.16) | collective-permute-done | bytes 1568 | tf_op jit(solution)/shard_map/ppermute | solution.py:89
  103.0 0.3 multiply_multiply_fusion
  103.3 1.9 %collective-permute-start.17 = (f32[3,256]{1,0:T(4,128)S(1)}, f32[3,256]{1,0:T(4,128)S(1)}, u32[]{:S(2)}, u32[]{:S(2)}) collective-permute-start(f32[3,256]{1,0:T(4,128)S(1)} %fusion.155), channel_id=1, source_target_pairs={{32,0},{64,32},{96,64},{128,96},{160,128},{192,160},{224,192},{256... | collective-permute-start | bytes 9224 | tf_op jit(solution)/shard_map/ppermute | solution.py:89
  105.2 0.8 fusion.106
  107.2 1.9 %collective-permute-start.18 = (bf16[128,512]{1,0:T(8,128)(2,1)S(1)}, bf16[128,512]{1,0:T(8,128)(2,1)S(1)}, u32[]{:S(2)}, u32[]{:S(2)}) collective-permute-start(bf16[128,512]{1,0:T(8,128)(2,1)S(1)} %fusion), channel_id=1, source_target_pairs={{0,30},{2,0},{4,2},{6,4},{8,6},{10,8},{12,10},{14,12},{16,14},{18,... | collective-permute-start | bytes 393224 | tf_op jit(solution)/shard_map/ppermute | solution.py:12
  110.8 3.9 %collective-permute-start.25 = (bf16[128,512]{1,0:T(8,128)(2,1)S(1)}, bf16[128,512]{1,0:T(8,128)(2,1)S(1)}, u32[]{:S(2)}, u32[]{:S(2)}) collective-permute-start(bf16[128,512]{1,0:T(8,128)(2,1)S(1)} %fusion.29), channel_id=1, source_target_pairs={{0,2},{2,4},{4,6},{6,8},{8,10},{10,12},{12,14},{14,16},{16,18},{18... | collective-permute-start | bytes 393224 | tf_op jit(solution)/shard_map/ppermute | solution.py:12
  116.2 3.1 %collective-permute-start.19 = (bf16[128,512]{1,0:T(8,128)(2,1)S(1)}, bf16[128,512]{1,0:T(8,128)(2,1)S(1)}, u32[]{:S(2)}, u32[]{:S(2)}) collective-permute-start(bf16[128,512]{1,0:T(8,128)(2,1)S(1)} %fusion.4), channel_id=1, source_target_pairs={{0,30},{2,0},{4,2},{6,4},{8,6},{10,8},{12,10},{14,12},{16,14},{18,... | collective-permute-start | bytes 393224 | tf_op jit(solution)/shard_map/ppermute | solution.py:12
  119.8 3.1 %collective-permute-start.26 = (bf16[128,512]{1,0:T(8,128)(2,1)S(1)}, bf16[128,512]{1,0:T(8,128)(2,1)S(1)}, u32[]{:S(2)}, u32[]{:S(2)}) collective-permute-start(bf16[128,512]{1,0:T(8,128)(2,1)S(1)} %fusion.33), channel_id=1, source_target_pairs={{0,2},{2,4},{4,6},{6,8},{8,10},{10,12},{12,14},{14,16},{16,18},{18... | collective-permute-start | bytes 393224 | tf_op jit(solution)/shard_map/ppermute | solution.py:12
  122.8 1.4 collective-permute-done.19
  124.5 4.1 %collective-permute-start.20 = (bf16[128,512]{1,0:T(8,128)(2,1)S(1)}, bf16[128,512]{1,0:T(8,128)(2,1)S(1)}, u32[]{:S(2)}, u32[]{:S(2)}) collective-permute-start(bf16[128,512]{1,0:T(8,128)(2,1)S(1)} %fusion.8), channel_id=1, source_target_pairs={{0,30},{2,0},{4,2},{6,4},{8,6},{10,8},{12,10},{14,12},{16,14},{18,... | collective-permute-start | bytes 393224 | tf_op jit(solution)/shard_map/ppermute | solution.py:12
  128.6 0.6 collective-permute-done.26
  129.5 1.9 %collective-permute-start.27 = (bf16[128,512]{1,0:T(8,128)(2,1)S(1)}, bf16[128,512]{1,0:T(8,128)(2,1)S(1)}, u32[]{:S(2)}, u32[]{:S(2)}) collective-permute-start(bf16[128,512]{1,0:T(8,128)(2,1)S(1)} %fusion.37), channel_id=1, source_target_pairs={{0,2},{2,4},{4,6},{6,8},{8,10},{10,12},{12,14},{14,16},{16,18},{18... | collective-permute-start | bytes 393224 | tf_op jit(solution)/shard_map/ppermute | solution.py:12
  131.4 0.5 collective-permute-done.20
  132.1 5.5 %collective-permute-start.21 = (bf16[128,512]{1,0:T(8,128)(2,1)S(1)}, bf16[128,512]{1,0:T(8,128)(2,1)S(1)}, u32[]{:S(2)}, u32[]{:S(2)}) collective-permute-start(bf16[128,512]{1,0:T(8,128)(2,1)S(1)} %fusion.12), channel_id=1, source_target_pairs={{0,30},{2,0},{4,2},{6,4},{8,6},{10,8},{12,10},{14,12},{16,14},{18,... | collective-permute-start | bytes 393224 | tf_op jit(solution)/shard_map/ppermute | solution.py:12
  137.6 0.5 collective-permute-done.27
  138.3 1.9 %collective-permute-start.28 = (bf16[128,512]{1,0:T(8,128)(2,1)S(1)}, bf16[128,512]{1,0:T(8,128)(2,1)S(1)}, u32[]{:S(2)}, u32[]{:S(2)}) collective-permute-start(bf16[128,512]{1,0:T(8,128)(2,1)S(1)} %fusion.41), channel_id=1, source_target_pairs={{0,2},{2,4},{4,6},{6,8},{8,10},{10,12},{12,14},{14,16},{16,18},{18... | collective-permute-start | bytes 393224 | tf_op jit(solution)/shard_map/ppermute | solution.py:12
  140.3 0.2 fusion.16
  140.5 5.4 %collective-permute-start.22 = (bf16[128,512]{1,0:T(8,128)(2,1)S(1)}, bf16[128,512]{1,0:T(8,128)(2,1)S(1)}, u32[]{:S(2)}, u32[]{:S(2)}) collective-permute-start(bf16[128,512]{1,0:T(8,128)(2,1)S(1)} %fusion.16), channel_id=1, source_target_pairs={{0,30},{2,0},{4,2},{6,4},{8,6},{10,8},{12,10},{14,12},{16,14},{18,... | collective-permute-start | bytes 393224 | tf_op jit(solution)/shard_map/ppermute | solution.py:12
  145.9 0.5 collective-permute-done.28
  146.6 1.9 %collective-permute-start.29 = (bf16[128,512]{1,0:T(8,128)(2,1)S(1)}, bf16[128,512]{1,0:T(8,128)(2,1)S(1)}, u32[]{:S(2)}, u32[]{:S(2)}) collective-permute-start(bf16[128,512]{1,0:T(8,128)(2,1)S(1)} %fusion.45), channel_id=1, source_target_pairs={{0,2},{2,4},{4,6},{6,8},{8,10},{10,12},{12,14},{14,16},{16,18},{18... | collective-permute-start | bytes 393224 | tf_op jit(solution)/shard_map/ppermute | solution.py:12
  148.8 5.4 %collective-permute-start.23 = (bf16[128,512]{1,0:T(8,128)(2,1)S(1)}, bf16[128,512]{1,0:T(8,128)(2,1)S(1)}, u32[]{:S(2)}, u32[]{:S(2)}) collective-permute-start(bf16[128,512]{1,0:T(8,128)(2,1)S(1)} %fusion.20), channel_id=1, source_target_pairs={{0,30},{2,0},{4,2},{6,4},{8,6},{10,8},{12,10},{14,12},{16,14},{18,... | collective-permute-start | bytes 393224 | tf_op jit(solution)/shard_map/ppermute | solution.py:12
  154.2 0.5 collective-permute-done.29
  154.9 1.9 %collective-permute-start.30 = (bf16[128,512]{1,0:T(8,128)(2,1)S(1)}, bf16[128,512]{1,0:T(8,128)(2,1)S(1)}, u32[]{:S(2)}, u32[]{:S(2)}) collective-permute-start(bf16[128,512]{1,0:T(8,128)(2,1)S(1)} %fusion.49), channel_id=1, source_target_pairs={{0,2},{2,4},{4,6},{6,8},{8,10},{10,12},{12,14},{14,16},{16,18},{18... | collective-permute-start | bytes 393224 | tf_op jit(solution)/shard_map/ppermute | solution.py:12
  157.1 5.4 %collective-permute-start.24 = (bf16[128,512]{1,0:T(8,128)(2,1)S(1)}, bf16[128,512]{1,0:T(8,128)(2,1)S(1)}, u32[]{:S(2)}, u32[]{:S(2)}) collective-permute-start(bf16[128,512]{1,0:T(8,128)(2,1)S(1)} %fusion.24), channel_id=1, source_target_pairs={{0,30},{2,0},{4,2},{6,4},{8,6},{10,8},{12,10},{14,12},{16,14},{18,... | collective-permute-start | bytes 393224 | tf_op jit(solution)/shard_map/ppermute | solution.py:12
  162.5 0.5 collective-permute-done.30
  163.2 1.9 %collective-permute-start.31 = (bf16[128,512]{1,0:T(8,128)(2,1)S(1)}, bf16[128,512]{1,0:T(8,128)(2,1)S(1)}, u32[]{:S(2)}, u32[]{:S(2)}) collective-permute-start(bf16[128,512]{1,0:T(8,128)(2,1)S(1)} %add_convert_fusion), channel_id=1, source_target_pairs={{0,2},{2,4},{4,6},{6,8},{8,10},{10,12},{12,14},{14,16},{16,18},{18... | collective-permute-start | bytes 393224 | tf_op jit(solution)/shard_map/ppermute | solution.py:12
  165.4 5.4 %collective-permute-start.32 = (bf16[128,512]{1,0:T(8,128)(2,1)S(1)}, bf16[128,512]{1,0:T(8,128)(2,1)S(1)}, u32[]{:S(2)}, u32[]{:S(2)}) collective-permute-start(bf16[128,512]{1,0:T(8,128)(2,1)S(1)} %convert_add_fusion), channel_id=1, source_target_pairs={{0,30},{2,0},{4,2},{6,4},{8,6},{10,8},{12,10},{14,12},{16,14},{18,... | collective-permute-start | bytes 393224 | tf_op jit(solution)/shard_map/ppermute | solution.py:12
  171.0 0.3 collective-permute-done.31
  171.3 2.0 %collective-permute-done.32 = bf16[128,512]{1,0:T(8,128)(2,1)S(1)} collective-permute-done((bf16[128,512]{1,0:T(8,128)(2,1)S(1)}, bf16[128,512]{1,0:T(8,128)(2,1)S(1)}, u32[]{:S(2)}, u32[]{:S(2)}) %collective-permute-start.32) | collective-permute-done | bytes 131104 | tf_op jit(solution)/shard_map/ppermute | solution.py:12
  173.6 3.0 %collective-permute-start.33 = (bf16[128,256]{1,0:T(8,128)(2,1)S(1)}, bf16[128,256]{1,0:T(8,128)(2,1)S(1)}, u32[]{:S(2)}, u32[]{:S(2)}) collective-permute-start(bf16[128,256]{1,0:T(8,128)(2,1)S(1)} %select_convert_fusion), channel_id=1, source_target_pairs={{0,1},{1,0},{2,3},{3,2},{4,5},{5,4},{6,7},{7,6},{8,9},{9,8},{10,11... | collective-permute-start | bytes 196616 | tf_op jit(solution)/shard_map/ppermute | solution.py:12
  176.6 3.2 %collective-permute-done.33 = bf16[128,256]{1,0:T(8,128)(2,1)S(1)} collective-permute-done((bf16[128,256]{1,0:T(8,128)(2,1)S(1)}, bf16[128,256]{1,0:T(8,128)(2,1)S(1)}, u32[]{:S(2)}, u32[]{:S(2)}) %collective-permute-start.33) | collective-permute-done | bytes 65568 | tf_op jit(solution)/shard_map/ppermute | solution.py:12
  179.7 0.7 add_convert_fusion.1
  (97 shorter events, 8.4 us)
Async XLA Ops:
  0.6 102.4 %copy-start = (bf16[10,256]{1,0:T(8,128)(2,1)S(1)}, bf16[10,256]{1,0:T(8,128)(2,1)}, u32[]{:S(2)}) copy-start(bf16[10,256]{1,0:T(8,128)(2,1)} %param.13) | copy-start | bytes 15364
  1.6 6.2 %collective-permute-start = (bf16[128,256]{0,1:T(8,128)(2,1)S(1)}, bf16[128,256]{0,1:T(8,128)(2,1)S(1)}, u32[]{:S(2)}, u32[]{:S(2)}) collective-permute-start(bf16[128,256]{0,1:T(8,128)(2,1)S(1)} %copy.10), channel_id=1, source_target_pairs={{0,1},{1,0},{2,3},{3,2},{4,5},{5,4},{6,7},{7,6},{8,9},{9,8},{10,11... | collective-permute-start | bytes 196616 | tf_op jit(solution)/shard_map/ppermute | solution.py:12
  7.8 21.1 %collective-permute-start.1 = (bf16[128,512]{0,1:T(8,128)(2,1)S(1)}, bf16[128,512]{0,1:T(8,128)(2,1)S(1)}, u32[]{:S(2)}, u32[]{:S(2)}) collective-permute-start(bf16[128,512]{0,1:T(8,128)(2,1)S(1)} %maximum_select_fusion.1), channel_id=1, source_target_pairs={{0,30},{2,0},{4,2},{6,4},{8,6},{10,8},{12,10},{14,12},{16,14},{18,... | collective-permute-start | bytes 393224 | tf_op jit(solution)/shard_map/ppermute | solution.py:12
  26.0 8.1 %collective-permute-start.8 = (bf16[128,512]{0,1:T(8,128)(2,1)S(1)}, bf16[128,512]{0,1:T(8,128)(2,1)S(1)}, u32[]{:S(2)}, u32[]{:S(2)}) collective-permute-start(bf16[128,512]{0,1:T(8,128)(2,1)S(1)} %maximum_select_fusion.1), channel_id=1, source_target_pairs={{0,2},{2,4},{4,6},{6,8},{8,10},{10,12},{12,14},{14,16},{16,18},{18... | collective-permute-start | bytes 393224 | tf_op jit(solution)/shard_map/ppermute | solution.py:12
  28.9 7.7 %collective-permute-start.2 = (bf16[128,512]{0,1:T(8,128)(2,1)S(1)}, bf16[128,512]{0,1:T(8,128)(2,1)S(1)}, u32[]{:S(2)}, u32[]{:S(2)}) collective-permute-start(bf16[128,512]{0,1:T(8,128)(2,1)S(1)} %collective-permute-done.1), channel_id=1, source_target_pairs={{0,30},{2,0},{4,2},{6,4},{8,6},{10,8},{12,10},{14,12},{16,14},{18,... | collective-permute-start | bytes 393224 | tf_op jit(solution)/shard_map/ppermute | solution.py:12
  34.1 8.1 %collective-permute-start.9 = (bf16[128,512]{0,1:T(8,128)(2,1)S(1)}, bf16[128,512]{0,1:T(8,128)(2,1)S(1)}, u32[]{:S(2)}, u32[]{:S(2)}) collective-permute-start(bf16[128,512]{0,1:T(8,128)(2,1)S(1)} %collective-permute-done.8), channel_id=1, source_target_pairs={{0,2},{2,4},{4,6},{6,8},{8,10},{10,12},{12,14},{14,16},{16,18},{18... | collective-permute-start | bytes 393224 | tf_op jit(solution)/shard_map/ppermute | solution.py:12
  36.6 8.1 %collective-permute-start.3 = (bf16[128,512]{0,1:T(8,128)(2,1)S(1)}, bf16[128,512]{0,1:T(8,128)(2,1)S(1)}, u32[]{:S(2)}, u32[]{:S(2)}) collective-permute-start(bf16[128,512]{0,1:T(8,128)(2,1)S(1)} %collective-permute-done.2), channel_id=1, source_target_pairs={{0,30},{2,0},{4,2},{6,4},{8,6},{10,8},{12,10},{14,12},{16,14},{18,... | collective-permute-start | bytes 393224 | tf_op jit(solution)/shard_map/ppermute | solution.py:12
  42.2 8.1 %collective-permute-start.10 = (bf16[128,512]{0,1:T(8,128)(2,1)S(1)}, bf16[128,512]{0,1:T(8,128)(2,1)S(1)}, u32[]{:S(2)}, u32[]{:S(2)}) collective-permute-start(bf16[128,512]{0,1:T(8,128)(2,1)S(1)} %collective-permute-done.9), channel_id=1, source_target_pairs={{0,2},{2,4},{4,6},{6,8},{8,10},{10,12},{12,14},{14,16},{16,18},{18... | collective-permute-start | bytes 393224 | tf_op jit(solution)/shard_map/ppermute | solution.py:12
  44.7 8.1 %collective-permute-start.4 = (bf16[128,512]{0,1:T(8,128)(2,1)S(1)}, bf16[128,512]{0,1:T(8,128)(2,1)S(1)}, u32[]{:S(2)}, u32[]{:S(2)}) collective-permute-start(bf16[128,512]{0,1:T(8,128)(2,1)S(1)} %collective-permute-done.3), channel_id=1, source_target_pairs={{0,30},{2,0},{4,2},{6,4},{8,6},{10,8},{12,10},{14,12},{16,14},{18,... | collective-permute-start | bytes 393224 | tf_op jit(solution)/shard_map/ppermute | solution.py:12
  50.2 8.1 %collective-permute-start.11 = (bf16[128,512]{0,1:T(8,128)(2,1)S(1)}, bf16[128,512]{0,1:T(8,128)(2,1)S(1)}, u32[]{:S(2)}, u32[]{:S(2)}) collective-permute-start(bf16[128,512]{0,1:T(8,128)(2,1)S(1)} %collective-permute-done.10), channel_id=1, source_target_pairs={{0,2},{2,4},{4,6},{6,8},{8,10},{10,12},{12,14},{14,16},{16,18},{18... | collective-permute-start | bytes 393224 | tf_op jit(solution)/shard_map/ppermute | solution.py:12
  52.7 8.9 %collective-permute-start.5 = (bf16[128,512]{0,1:T(8,128)(2,1)S(1)}, bf16[128,512]{0,1:T(8,128)(2,1)S(1)}, u32[]{:S(2)}, u32[]{:S(2)}) collective-permute-start(bf16[128,512]{0,1:T(8,128)(2,1)S(1)} %collective-permute-done.4), channel_id=1, source_target_pairs={{0,30},{2,0},{4,2},{6,4},{8,6},{10,8},{12,10},{14,12},{16,14},{18,... | collective-permute-start | bytes 393224 | tf_op jit(solution)/shard_map/ppermute | solution.py:12
  58.3 9.2 %collective-permute-start.12 = (bf16[128,512]{0,1:T(8,128)(2,1)S(1)}, bf16[128,512]{0,1:T(8,128)(2,1)S(1)}, u32[]{:S(2)}, u32[]{:S(2)}) collective-permute-start(bf16[128,512]{0,1:T(8,128)(2,1)S(1)} %collective-permute-done.11), channel_id=1, source_target_pairs={{0,2},{2,4},{4,6},{6,8},{8,10},{10,12},{12,14},{14,16},{16,18},{18... | collective-permute-start | bytes 393224 | tf_op jit(solution)/shard_map/ppermute | solution.py:12
  61.7 8.8 %collective-permute-start.6 = (bf16[128,512]{0,1:T(8,128)(2,1)S(1)}, bf16[128,512]{0,1:T(8,128)(2,1)S(1)}, u32[]{:S(2)}, u32[]{:S(2)}) collective-permute-start(bf16[128,512]{0,1:T(8,128)(2,1)S(1)} %collective-permute-done.5), channel_id=1, source_target_pairs={{0,30},{2,0},{4,2},{6,4},{8,6},{10,8},{12,10},{14,12},{16,14},{18,... | collective-permute-start | bytes 393224 | tf_op jit(solution)/shard_map/ppermute | solution.py:12
  67.5 8.6 %collective-permute-start.13 = (bf16[128,512]{0,1:T(8,128)(2,1)S(1)}, bf16[128,512]{0,1:T(8,128)(2,1)S(1)}, u32[]{:S(2)}, u32[]{:S(2)}) collective-permute-start(bf16[128,512]{0,1:T(8,128)(2,1)S(1)} %collective-permute-done.12), channel_id=1, source_target_pairs={{0,2},{2,4},{4,6},{6,8},{8,10},{10,12},{12,14},{14,16},{16,18},{18... | collective-permute-start | bytes 393224 | tf_op jit(solution)/shard_map/ppermute | solution.py:12
  70.5 15.6 %collective-permute-start.7 = (bf16[128,512]{0,1:T(8,128)(2,1)S(1)}, bf16[128,512]{0,1:T(8,128)(2,1)S(1)}, u32[]{:S(2)}, u32[]{:S(2)}) collective-permute-start(bf16[128,512]{0,1:T(8,128)(2,1)S(1)} %collective-permute-done.6), channel_id=1, source_target_pairs={{0,30},{2,0},{4,2},{6,4},{8,6},{10,8},{12,10},{14,12},{16,14},{18,... | collective-permute-start | bytes 393224 | tf_op jit(solution)/shard_map/ppermute | solution.py:12
  76.1 8.1 %collective-permute-start.14 = (bf16[128,512]{0,1:T(8,128)(2,1)S(1)}, bf16[128,512]{0,1:T(8,128)(2,1)S(1)}, u32[]{:S(2)}, u32[]{:S(2)}) collective-permute-start(bf16[128,512]{0,1:T(8,128)(2,1)S(1)} %collective-permute-done.13), channel_id=1, source_target_pairs={{0,2},{2,4},{4,6},{6,8},{8,10},{10,12},{12,14},{14,16},{16,18},{18... | collective-permute-start | bytes 393224 | tf_op jit(solution)/shard_map/ppermute | solution.py:12
  84.2 8.1 %collective-permute-start.15 = (bf16[128,512]{0,1:T(8,128)(2,1)S(1)}, bf16[128,512]{0,1:T(8,128)(2,1)S(1)}, u32[]{:S(2)}, u32[]{:S(2)}) collective-permute-start(bf16[128,512]{0,1:T(8,128)(2,1)S(1)} %collective-permute-done.14), channel_id=1, source_target_pairs={{0,2},{2,4},{4,6},{6,8},{8,10},{10,12},{12,14},{14,16},{16,18},{18... | collective-permute-start | bytes 393224 | tf_op jit(solution)/shard_map/ppermute | solution.py:12
  92.4 2.2 %copy-start.2 = (bf16[8192,256]{1,0:T(8,128)(2,1)S(1)}, bf16[8192,256]{1,0:T(8,128)(2,1)}, u32[]{:S(2)}) copy-start(bf16[8192,256]{1,0:T(8,128)(2,1)} %param.10) | copy-start | bytes 12582916
  93.1 4.5 %copy-start.1 = (bf16[8192,256]{1,0:T(8,128)(2,1)S(1)}, bf16[8192,256]{1,0:T(8,128)(2,1)}, u32[]{:S(2)}) copy-start(bf16[8192,256]{1,0:T(8,128)(2,1)} %param.9) | copy-start | bytes 12582916
  95.6 7.4 %copy-start.3 = (f32[256]{0:T(256)S(1)}, f32[256]{0:T(256)}, u32[]{:S(2)}) copy-start(f32[256]{0:T(256)} %param.12) | copy-start | bytes 3076
  95.6 7.4 %copy-start.4 = (s32[128]{0:T(128)S(1)}, s32[128]{0:T(128)}, u32[]{:S(2)}) copy-start(s32[128]{0:T(128)} %param.14) | copy-start | bytes 1540
  95.7 7.3 %collective-permute-start.16 = (bf16[3,256]{1,0:T(4,128)(2,1)S(1)}, bf16[3,256]{1,0:T(4,128)(2,1)S(1)}, u32[]{:S(2)}, u32[]{:S(2)}) collective-permute-start(bf16[3,256]{1,0:T(4,128)(2,1)S(1)} %slice.87), channel_id=1, source_target_pairs={{0,32},{32,64},{64,96},{96,128},{128,160},{160,192},{192,224},{224... | collective-permute-start | bytes 4616 | tf_op jit(solution)/shard_map/ppermute | solution.py:89
  103.3 3.7 %collective-permute-start.17 = (f32[3,256]{1,0:T(4,128)S(1)}, f32[3,256]{1,0:T(4,128)S(1)}, u32[]{:S(2)}, u32[]{:S(2)}) collective-permute-start(f32[3,256]{1,0:T(4,128)S(1)} %fusion.155), channel_id=1, source_target_pairs={{32,0},{64,32},{96,64},{128,96},{160,128},{192,160},{224,192},{256... | collective-permute-start | bytes 9224 | tf_op jit(solution)/shard_map/ppermute | solution.py:89
  107.2 8.7 %collective-permute-start.18 = (bf16[128,512]{1,0:T(8,128)(2,1)S(1)}, bf16[128,512]{1,0:T(8,128)(2,1)S(1)}, u32[]{:S(2)}, u32[]{:S(2)}) collective-permute-start(bf16[128,512]{1,0:T(8,128)(2,1)S(1)} %fusion), channel_id=1, source_target_pairs={{0,30},{2,0},{4,2},{6,4},{8,6},{10,8},{12,10},{14,12},{16,14},{18,... | collective-permute-start | bytes 393224 | tf_op jit(solution)/shard_map/ppermute | solution.py:12
  110.8 8.7 %collective-permute-start.25 = (bf16[128,512]{1,0:T(8,128)(2,1)S(1)}, bf16[128,512]{1,0:T(8,128)(2,1)S(1)}, u32[]{:S(2)}, u32[]{:S(2)}) collective-permute-start(bf16[128,512]{1,0:T(8,128)(2,1)S(1)} %fusion.29), channel_id=1, source_target_pairs={{0,2},{2,4},{4,6},{6,8},{8,10},{10,12},{12,14},{14,16},{16,18},{18... | collective-permute-start | bytes 393224 | tf_op jit(solution)/shard_map/ppermute | solution.py:12
  116.2 8.0 %collective-permute-start.19 = (bf16[128,512]{1,0:T(8,128)(2,1)S(1)}, bf16[128,512]{1,0:T(8,128)(2,1)S(1)}, u32[]{:S(2)}, u32[]{:S(2)}) collective-permute-start(bf16[128,512]{1,0:T(8,128)(2,1)S(1)} %fusion.4), channel_id=1, source_target_pairs={{0,30},{2,0},{4,2},{6,4},{8,6},{10,8},{12,10},{14,12},{16,14},{18,... | collective-permute-start | bytes 393224 | tf_op jit(solution)/shard_map/ppermute | solution.py:12
  119.8 9.5 %collective-permute-start.26 = (bf16[128,512]{1,0:T(8,128)(2,1)S(1)}, bf16[128,512]{1,0:T(8,128)(2,1)S(1)}, u32[]{:S(2)}, u32[]{:S(2)}) collective-permute-start(bf16[128,512]{1,0:T(8,128)(2,1)S(1)} %fusion.33), channel_id=1, source_target_pairs={{0,2},{2,4},{4,6},{6,8},{8,10},{10,12},{12,14},{14,16},{16,18},{18... | collective-permute-start | bytes 393224 | tf_op jit(solution)/shard_map/ppermute | solution.py:12
  124.5 7.4 %collective-permute-start.20 = (bf16[128,512]{1,0:T(8,128)(2,1)S(1)}, bf16[128,512]{1,0:T(8,128)(2,1)S(1)}, u32[]{:S(2)}, u32[]{:S(2)}) collective-permute-start(bf16[128,512]{1,0:T(8,128)(2,1)S(1)} %fusion.8), channel_id=1, source_target_pairs={{0,30},{2,0},{4,2},{6,4},{8,6},{10,8},{12,10},{14,12},{16,14},{18,... | collective-permute-start | bytes 393224 | tf_op jit(solution)/shard_map/ppermute | solution.py:12
  129.5 8.6 %collective-permute-start.27 = (bf16[128,512]{1,0:T(8,128)(2,1)S(1)}, bf16[128,512]{1,0:T(8,128)(2,1)S(1)}, u32[]{:S(2)}, u32[]{:S(2)}) collective-permute-start(bf16[128,512]{1,0:T(8,128)(2,1)S(1)} %fusion.37), channel_id=1, source_target_pairs={{0,2},{2,4},{4,6},{6,8},{8,10},{10,12},{12,14},{14,16},{16,18},{18... | collective-permute-start | bytes 393224 | tf_op jit(solution)/shard_map/ppermute | solution.py:12
  132.1 8.2 %collective-permute-start.21 = (bf16[128,512]{1,0:T(8,128)(2,1)S(1)}, bf16[128,512]{1,0:T(8,128)(2,1)S(1)}, u32[]{:S(2)}, u32[]{:S(2)}) collective-permute-start(bf16[128,512]{1,0:T(8,128)(2,1)S(1)} %fusion.12), channel_id=1, source_target_pairs={{0,30},{2,0},{4,2},{6,4},{8,6},{10,8},{12,10},{14,12},{16,14},{18,... | collective-permute-start | bytes 393224 | tf_op jit(solution)/shard_map/ppermute | solution.py:12
  138.3 8.1 %collective-permute-start.28 = (bf16[128,512]{1,0:T(8,128)(2,1)S(1)}, bf16[128,512]{1,0:T(8,128)(2,1)S(1)}, u32[]{:S(2)}, u32[]{:S(2)}) collective-permute-start(bf16[128,512]{1,0:T(8,128)(2,1)S(1)} %fusion.41), channel_id=1, source_target_pairs={{0,2},{2,4},{4,6},{6,8},{8,10},{10,12},{12,14},{14,16},{16,18},{18... | collective-permute-start | bytes 393224 | tf_op jit(solution)/shard_map/ppermute | solution.py:12
  140.5 8.1 %collective-permute-start.22 = (bf16[128,512]{1,0:T(8,128)(2,1)S(1)}, bf16[128,512]{1,0:T(8,128)(2,1)S(1)}, u32[]{:S(2)}, u32[]{:S(2)}) collective-permute-start(bf16[128,512]{1,0:T(8,128)(2,1)S(1)} %fusion.16), channel_id=1, source_target_pairs={{0,30},{2,0},{4,2},{6,4},{8,6},{10,8},{12,10},{14,12},{16,14},{18,... | collective-permute-start | bytes 393224 | tf_op jit(solution)/shard_map/ppermute | solution.py:12
  146.6 8.1 %collective-permute-start.29 = (bf16[128,512]{1,0:T(8,128)(2,1)S(1)}, bf16[128,512]{1,0:T(8,128)(2,1)S(1)}, u32[]{:S(2)}, u32[]{:S(2)}) collective-permute-start(bf16[128,512]{1,0:T(8,128)(2,1)S(1)} %fusion.45), channel_id=1, source_target_pairs={{0,2},{2,4},{4,6},{6,8},{8,10},{10,12},{12,14},{14,16},{16,18},{18... | collective-permute-start | bytes 393224 | tf_op jit(solution)/shard_map/ppermute | solution.py:12
  148.8 8.1 %collective-permute-start.23 = (bf16[128,512]{1,0:T(8,128)(2,1)S(1)}, bf16[128,512]{1,0:T(8,128)(2,1)S(1)}, u32[]{:S(2)}, u32[]{:S(2)}) collective-permute-start(bf16[128,512]{1,0:T(8,128)(2,1)S(1)} %fusion.20), channel_id=1, source_target_pairs={{0,30},{2,0},{4,2},{6,4},{8,6},{10,8},{12,10},{14,12},{16,14},{18,... | collective-permute-start | bytes 393224 | tf_op jit(solution)/shard_map/ppermute | solution.py:12
  154.9 8.1 %collective-permute-start.30 = (bf16[128,512]{1,0:T(8,128)(2,1)S(1)}, bf16[128,512]{1,0:T(8,128)(2,1)S(1)}, u32[]{:S(2)}, u32[]{:S(2)}) collective-permute-start(bf16[128,512]{1,0:T(8,128)(2,1)S(1)} %fusion.49), channel_id=1, source_target_pairs={{0,2},{2,4},{4,6},{6,8},{8,10},{10,12},{12,14},{14,16},{16,18},{18... | collective-permute-start | bytes 393224 | tf_op jit(solution)/shard_map/ppermute | solution.py:12
  157.1 8.1 %collective-permute-start.24 = (bf16[128,512]{1,0:T(8,128)(2,1)S(1)}, bf16[128,512]{1,0:T(8,128)(2,1)S(1)}, u32[]{:S(2)}, u32[]{:S(2)}) collective-permute-start(bf16[128,512]{1,0:T(8,128)(2,1)S(1)} %fusion.24), channel_id=1, source_target_pairs={{0,30},{2,0},{4,2},{6,4},{8,6},{10,8},{12,10},{14,12},{16,14},{18,... | collective-permute-start | bytes 393224 | tf_op jit(solution)/shard_map/ppermute | solution.py:12
  163.2 8.1 %collective-permute-start.31 = (bf16[128,512]{1,0:T(8,128)(2,1)S(1)}, bf16[128,512]{1,0:T(8,128)(2,1)S(1)}, u32[]{:S(2)}, u32[]{:S(2)}) collective-permute-start(bf16[128,512]{1,0:T(8,128)(2,1)S(1)} %add_convert_fusion), channel_id=1, source_target_pairs={{0,2},{2,4},{4,6},{6,8},{8,10},{10,12},{12,14},{14,16},{16,18},{18... | collective-permute-start | bytes 393224 | tf_op jit(solution)/shard_map/ppermute | solution.py:12
  165.4 7.9 %collective-permute-start.32 = (bf16[128,512]{1,0:T(8,128)(2,1)S(1)}, bf16[128,512]{1,0:T(8,128)(2,1)S(1)}, u32[]{:S(2)}, u32[]{:S(2)}) collective-permute-start(bf16[128,512]{1,0:T(8,128)(2,1)S(1)} %convert_add_fusion), channel_id=1, source_target_pairs={{0,30},{2,0},{4,2},{6,4},{8,6},{10,8},{12,10},{14,12},{16,14},{18,... | collective-permute-start | bytes 393224 | tf_op jit(solution)/shard_map/ppermute | solution.py:12
  173.6 6.2 %collective-permute-start.33 = (bf16[128,256]{1,0:T(8,128)(2,1)S(1)}, bf16[128,256]{1,0:T(8,128)(2,1)S(1)}, u32[]{:S(2)}, u32[]{:S(2)}) collective-permute-start(bf16[128,256]{1,0:T(8,128)(2,1)S(1)} %select_convert_fusion), channel_id=1, source_target_pairs={{0,1},{1,0},{2,3},{3,2},{4,5},{5,4},{6,7},{7,6},{8,9},{9,8},{10,11... | collective-permute-start | bytes 196616 | tf_op jit(solution)/shard_map/ppermute | solution.py:12

commit v11 on v8

--- a/solution.py
+++ b/solution.py
@@ -111,7 +111,8 @@
     gate16 = lax.optimization_barrier(gate_acc.astype(jnp.bfloat16))
     zgate = gate16.astype(jnp.float32)
     xin16 = lax.optimization_barrier(xin_acc.astype(jnp.bfloat16))
-    before = passed_along(xin16[rows - (taps - 1) :], "seq", 1)
+    tail = jnp.dot(piece[rows - (taps - 1) :], w_conv_in, preferred_element_type=jnp.float32)
+    before = passed_along(tail.astype(jnp.bfloat16), "seq", 1)
     padded = jnp.concatenate([before, xin16], axis=0).astype(jnp.float32)
     conv_out = conv_bias[None, :] + sum(
         (conv_weight[k][None, :] * padded[k : k + rows] for k in range(taps))

time: 182 us -> 184 us (1.011)
  no operation moved by 1% of the time
where the time goes in v11:
time: 184 us; the launch traced here: 182 us
  starting transfers between devices  131 us (71%)
  waiting for transfers between devices  32 us (17%)
  matrix products  10.4 us (6%)
  local copies, waits for them, and re-layouts  4.8 us (3%)
  other arithmetic  2.27 us (1%)
    ppermute x32, starting transfers between devices, shifted(): lax.ppermute(block, axis, [(i, (i + distance) % size) for i in range(size)])  126 us
    ppermute x32, waiting for transfers between devices, shifted(): lax.ppermute(block, axis, [(i, (i + distance) % size) for i in range(size)])  28.7 us
    ppermute x2, starting transfers between devices, passed_along(): return lax.ppermute(block, axis, route)  4.89 us
  transfers between devices with their start and end apart: 34, of which 21 were waited for; matrix products, arithmetic and copies ran while one was open for 6% of the time, Pallas kernels for 0%

profile of v11, /device:TPU:56, one launch (start us, length us, event | category | flops | bytes accessed | tf_op | source)
XLA Modules:
  0.0 182.0 jit_solution(7833789487551664474)
XLA Ops:
  0.6 1.0 copy.10
  1.6 3.4 %collective-permute-start = (bf16[128,256]{0,1:T(8,128)(2,1)S(1)}, bf16[128,256]{0,1:T(8,128)(2,1)S(1)}, u32[]{:S(2)}, u32[]{:S(2)}) collective-permute-start(bf16[128,256]{0,1:T(8,128)(2,1)S(1)} %copy.10), channel_id=1, source_target_pairs={{0,1},{1,0},{2,3},{3,2},{4,5},{5,4},{6,7},{7,6},{8,9},{9,8},{10,11... | collective-permute-start | bytes 196616 | tf_op jit(solution)/shard_map/ppermute | solution.py:12
  5.0 0.8 fusion.159
  5.9 1.9 %collective-permute-done = bf16[128,256]{0,1:T(8,128)(2,1)S(1)} collective-permute-done((bf16[128,256]{0,1:T(8,128)(2,1)S(1)}, bf16[128,256]{0,1:T(8,128)(2,1)S(1)}, u32[]{:S(2)}, u32[]{:S(2)}) %collective-permute-start) | collective-permute-done | bytes 65568 | tf_op jit(solution)/shard_map/ppermute | solution.py:12
  7.8 18.2 %collective-permute-start.1 = (bf16[128,512]{0,1:T(8,128)(2,1)S(1)}, bf16[128,512]{0,1:T(8,128)(2,1)S(1)}, u32[]{:S(2)}, u32[]{:S(2)}) collective-permute-start(bf16[128,512]{0,1:T(8,128)(2,1)S(1)} %maximum_select_fusion.1), channel_id=1, source_target_pairs={{0,30},{2,0},{4,2},{6,4},{8,6},{10,8},{12,10},{14,12},{16,14},{18,... | collective-permute-start | bytes 393224 | tf_op jit(solution)/shard_map/ppermute | solution.py:12
  26.0 1.9 %collective-permute-start.8 = (bf16[128,512]{0,1:T(8,128)(2,1)S(1)}, bf16[128,512]{0,1:T(8,128)(2,1)S(1)}, u32[]{:S(2)}, u32[]{:S(2)}) collective-permute-start(bf16[128,512]{0,1:T(8,128)(2,1)S(1)} %maximum_select_fusion.1), channel_id=1, source_target_pairs={{0,2},{2,4},{4,6},{6,8},{8,10},{10,12},{12,14},{14,16},{16,18},{18... | collective-permute-start | bytes 393224 | tf_op jit(solution)/shard_map/ppermute | solution.py:12
  28.2 0.7 convert_element_type.219
  28.9 5.2 %collective-permute-start.2 = (bf16[128,512]{0,1:T(8,128)(2,1)S(1)}, bf16[128,512]{0,1:T(8,128)(2,1)S(1)}, u32[]{:S(2)}, u32[]{:S(2)}) collective-permute-start(bf16[128,512]{0,1:T(8,128)(2,1)S(1)} %collective-permute-done.1), channel_id=1, source_target_pairs={{0,30},{2,0},{4,2},{6,4},{8,6},{10,8},{12,10},{14,12},{16,14},{18,... | collective-permute-start | bytes 393224 | tf_op jit(solution)/shard_map/ppermute | solution.py:12
  34.1 1.9 %collective-permute-start.9 = (bf16[128,512]{0,1:T(8,128)(2,1)S(1)}, bf16[128,512]{0,1:T(8,128)(2,1)S(1)}, u32[]{:S(2)}, u32[]{:S(2)}) collective-permute-start(bf16[128,512]{0,1:T(8,128)(2,1)S(1)} %collective-permute-done.8), channel_id=1, source_target_pairs={{0,2},{2,4},{4,6},{6,8},{8,10},{10,12},{12,14},{14,16},{16,18},{18... | collective-permute-start | bytes 393224 | tf_op jit(solution)/shard_map/ppermute | solution.py:12
  36.1 0.5 collective-permute-done.2
  36.6 5.6 %collective-permute-start.3 = (bf16[128,512]{0,1:T(8,128)(2,1)S(1)}, bf16[128,512]{0,1:T(8,128)(2,1)S(1)}, u32[]{:S(2)}, u32[]{:S(2)}) collective-permute-start(bf16[128,512]{0,1:T(8,128)(2,1)S(1)} %collective-permute-done.2), channel_id=1, source_target_pairs={{0,30},{2,0},{4,2},{6,4},{8,6},{10,8},{12,10},{14,12},{16,14},{18,... | collective-permute-start | bytes 393224 | tf_op jit(solution)/shard_map/ppermute | solution.py:12
  42.2 1.9 %collective-permute-start.10 = (bf16[128,512]{0,1:T(8,128)(2,1)S(1)}, bf16[128,512]{0,1:T(8,128)(2,1)S(1)}, u32[]{:S(2)}, u32[]{:S(2)}) collective-permute-start(bf16[128,512]{0,1:T(8,128)(2,1)S(1)} %collective-permute-done.9), channel_id=1, source_target_pairs={{0,2},{2,4},{4,6},{6,8},{8,10},{10,12},{12,14},{14,16},{16,18},{18... | collective-permute-start | bytes 393224 | tf_op jit(solution)/shard_map/ppermute | solution.py:12
  44.1 0.5 collective-permute-done.3
  44.7 5.6 %collective-permute-start.4 = (bf16[128,512]{0,1:T(8,128)(2,1)S(1)}, bf16[128,512]{0,1:T(8,128)(2,1)S(1)}, u32[]{:S(2)}, u32[]{:S(2)}) collective-permute-start(bf16[128,512]{0,1:T(8,128)(2,1)S(1)} %collective-permute-done.3), channel_id=1, source_target_pairs={{0,30},{2,0},{4,2},{6,4},{8,6},{10,8},{12,10},{14,12},{16,14},{18,... | collective-permute-start | bytes 393224 | tf_op jit(solution)/shard_map/ppermute | solution.py:12
  50.2 1.9 %collective-permute-start.11 = (bf16[128,512]{0,1:T(8,128)(2,1)S(1)}, bf16[128,512]{0,1:T(8,128)(2,1)S(1)}, u32[]{:S(2)}, u32[]{:S(2)}) collective-permute-start(bf16[128,512]{0,1:T(8,128)(2,1)S(1)} %collective-permute-done.10), channel_id=1, source_target_pairs={{0,2},{2,4},{4,6},{6,8},{8,10},{10,12},{12,14},{14,16},{16,18},{18... | collective-permute-start | bytes 393224 | tf_op jit(solution)/shard_map/ppermute | solution.py:12
  52.2 0.5 collective-permute-done.4
  52.7 5.6 %collective-permute-start.5 = (bf16[128,512]{0,1:T(8,128)(2,1)S(1)}, bf16[128,512]{0,1:T(8,128)(2,1)S(1)}, u32[]{:S(2)}, u32[]{:S(2)}) collective-permute-start(bf16[128,512]{0,1:T(8,128)(2,1)S(1)} %collective-permute-done.4), channel_id=1, source_target_pairs={{0,30},{2,0},{4,2},{6,4},{8,6},{10,8},{12,10},{14,12},{16,14},{18,... | collective-permute-start | bytes 393224 | tf_op jit(solution)/shard_map/ppermute | solution.py:12
  58.3 1.9 %collective-permute-start.12 = (bf16[128,512]{0,1:T(8,128)(2,1)S(1)}, bf16[128,512]{0,1:T(8,128)(2,1)S(1)}, u32[]{:S(2)}, u32[]{:S(2)}) collective-permute-start(bf16[128,512]{0,1:T(8,128)(2,1)S(1)} %collective-permute-done.11), channel_id=1, source_target_pairs={{0,2},{2,4},{4,6},{6,8},{8,10},{10,12},{12,14},{14,16},{16,18},{18... | collective-permute-start | bytes 393224 | tf_op jit(solution)/shard_map/ppermute | solution.py:12
  60.2 1.4 collective-permute-done.5
  61.7 5.6 %collective-permute-start.6 = (bf16[128,512]{0,1:T(8,128)(2,1)S(1)}, bf16[128,512]{0,1:T(8,128)(2,1)S(1)}, u32[]{:S(2)}, u32[]{:S(2)}) collective-permute-start(bf16[128,512]{0,1:T(8,128)(2,1)S(1)} %collective-permute-done.5), channel_id=1, source_target_pairs={{0,30},{2,0},{4,2},{6,4},{8,6},{10,8},{12,10},{14,12},{16,14},{18,... | collective-permute-start | bytes 393224 | tf_op jit(solution)/shard_map/ppermute | solution.py:12
  67.5 1.9 %collective-permute-start.13 = (bf16[128,512]{0,1:T(8,128)(2,1)S(1)}, bf16[128,512]{0,1:T(8,128)(2,1)S(1)}, u32[]{:S(2)}, u32[]{:S(2)}) collective-permute-start(bf16[128,512]{0,1:T(8,128)(2,1)S(1)} %collective-permute-done.12), channel_id=1, source_target_pairs={{0,2},{2,4},{4,6},{6,8},{8,10},{10,12},{12,14},{14,16},{16,18},{18... | collective-permute-start | bytes 393224 | tf_op jit(solution)/shard_map/ppermute | solution.py:12
  69.4 1.0 collective-permute-done.6
  70.5 5.6 %collective-permute-start.7 = (bf16[128,512]{0,1:T(8,128)(2,1)S(1)}, bf16[128,512]{0,1:T(8,128)(2,1)S(1)}, u32[]{:S(2)}, u32[]{:S(2)}) collective-permute-start(bf16[128,512]{0,1:T(8,128)(2,1)S(1)} %collective-permute-done.6), channel_id=1, source_target_pairs={{0,30},{2,0},{4,2},{6,4},{8,6},{10,8},{12,10},{14,12},{16,14},{18,... | collective-permute-start | bytes 393224 | tf_op jit(solution)/shard_map/ppermute | solution.py:12
  76.1 1.9 %collective-permute-start.14 = (bf16[128,512]{0,1:T(8,128)(2,1)S(1)}, bf16[128,512]{0,1:T(8,128)(2,1)S(1)}, u32[]{:S(2)}, u32[]{:S(2)}) collective-permute-start(bf16[128,512]{0,1:T(8,128)(2,1)S(1)} %collective-permute-done.13), channel_id=1, source_target_pairs={{0,2},{2,4},{4,6},{6,8},{8,10},{10,12},{12,14},{14,16},{16,18},{18... | collective-permute-start | bytes 393224 | tf_op jit(solution)/shard_map/ppermute | solution.py:12
  78.0 6.1 %collective-permute-done.14 = bf16[128,512]{0,1:T(8,128)(2,1)S(1)} collective-permute-done((bf16[128,512]{0,1:T(8,128)(2,1)S(1)}, bf16[128,512]{0,1:T(8,128)(2,1)S(1)}, u32[]{:S(2)}, u32[]{:S(2)}) %collective-permute-start.14) | collective-permute-done | bytes 131104 | tf_op jit(solution)/shard_map/ppermute | solution.py:12
  84.2 1.9 %collective-permute-start.15 = (bf16[128,512]{0,1:T(8,128)(2,1)S(1)}, bf16[128,512]{0,1:T(8,128)(2,1)S(1)}, u32[]{:S(2)}, u32[]{:S(2)}) collective-permute-start(bf16[128,512]{0,1:T(8,128)(2,1)S(1)} %collective-permute-done.14), channel_id=1, source_target_pairs={{0,2},{2,4},{4,6},{6,8},{8,10},{10,12},{12,14},{14,16},{16,18},{18... | collective-permute-start | bytes 393224 | tf_op jit(solution)/shard_map/ppermute | solution.py:12
  86.1 6.1 %collective-permute-done.15 = bf16[128,512]{0,1:T(8,128)(2,1)S(1)} collective-permute-done((bf16[128,512]{0,1:T(8,128)(2,1)S(1)}, bf16[128,512]{0,1:T(8,128)(2,1)S(1)}, u32[]{:S(2)}, u32[]{:S(2)}) %collective-permute-start.15) | collective-permute-done | bytes 131104 | tf_op jit(solution)/shard_map/ppermute | solution.py:12
  93.3 0.7 slice.91
  94.0 1.3 copy-done.1
  95.3 0.9 convolution_convert_fusion.2
  96.2 2.2 %collective-permute-start.16 = (bf16[3,256]{1,0:T(4,128)(2,1)S(1)}, bf16[3,256]{1,0:T(4,128)(2,1)S(1)}, u32[]{:S(2)}, u32[]{:S(2)}) collective-permute-start(bf16[3,256]{1,0:T(4,128)(2,1)S(1)} %convolution_convert_fusion.2), channel_id=1, source_target_pairs={{0,32},{32,64},{64,96},{96,128},{128,160},{160,192},{192,224},{224... | collective-permute-start | bytes 4616 | tf_op jit(solution)/shard_map/ppermute | solution.py:89
  98.4 1.0 convolution_convert_fusion.1
  99.4 1.0 convolution_convert_fusion
  100.4 3.4 %collective-permute-done.16 = bf16[3,256]{1,0:T(4,128)(2,1)S(1)} collective-permute-done((bf16[3,256]{1,0:T(4,128)(2,1)S(1)}, bf16[3,256]{1,0:T(4,128)(2,1)S(1)}, u32[]{:S(2)}, u32[]{:S(2)}) %collective-permute-start.16) | collective-permute-done | bytes 1568 | tf_op jit(solution)/shard_map/ppermute | solution.py:89
  103.8 0.3 multiply_multiply_fusion
  104.1 2.7 %collective-permute-start.17 = (f32[3,256]{1,0:T(4,128)S(1)}, f32[3,256]{1,0:T(4,128)S(1)}, u32[]{:S(2)}, u32[]{:S(2)}) collective-permute-start(f32[3,256]{1,0:T(4,128)S(1)} %fusion.155), channel_id=1, source_target_pairs={{32,0},{64,32},{96,64},{128,96},{160,128},{192,160},{224,192},{256... | collective-permute-start | bytes 9224 | tf_op jit(solution)/shard_map/ppermute | solution.py:89
  106.8 0.8 fusion.106
  108.8 1.9 %collective-permute-start.18 = (bf16[128,512]{1,0:T(8,128)(2,1)S(1)}, bf16[128,512]{1,0:T(8,128)(2,1)S(1)}, u32[]{:S(2)}, u32[]{:S(2)}) collective-permute-start(bf16[128,512]{1,0:T(8,128)(2,1)S(1)} %fusion), channel_id=1, source_target_pairs={{0,30},{2,0},{4,2},{6,4},{8,6},{10,8},{12,10},{14,12},{16,14},{18,... | collective-permute-start | bytes 393224 | tf_op jit(solution)/shard_map/ppermute | solution.py:12
  112.4 3.9 %collective-permute-start.25 = (bf16[128,512]{1,0:T(8,128)(2,1)S(1)}, bf16[128,512]{1,0:T(8,128)(2,1)S(1)}, u32[]{:S(2)}, u32[]{:S(2)}) collective-permute-start(bf16[128,512]{1,0:T(8,128)(2,1)S(1)} %fusion.29), channel_id=1, source_target_pairs={{0,2},{2,4},{4,6},{6,8},{8,10},{10,12},{12,14},{14,16},{16,18},{18... | collective-permute-start | bytes 393224 | tf_op jit(solution)/shard_map/ppermute | solution.py:12
  117.8 3.1 %collective-permute-start.19 = (bf16[128,512]{1,0:T(8,128)(2,1)S(1)}, bf16[128,512]{1,0:T(8,128)(2,1)S(1)}, u32[]{:S(2)}, u32[]{:S(2)}) collective-permute-start(bf16[128,512]{1,0:T(8,128)(2,1)S(1)} %fusion.4), channel_id=1, source_target_pairs={{0,30},{2,0},{4,2},{6,4},{8,6},{10,8},{12,10},{14,12},{16,14},{18,... | collective-permute-start | bytes 393224 | tf_op jit(solution)/shard_map/ppermute | solution.py:12
  121.4 3.1 %collective-permute-start.26 = (bf16[128,512]{1,0:T(8,128)(2,1)S(1)}, bf16[128,512]{1,0:T(8,128)(2,1)S(1)}, u32[]{:S(2)}, u32[]{:S(2)}) collective-permute-start(bf16[128,512]{1,0:T(8,128)(2,1)S(1)} %fusion.33), channel_id=1, source_target_pairs={{0,2},{2,4},{4,6},{6,8},{8,10},{10,12},{12,14},{14,16},{16,18},{18... | collective-permute-start | bytes 393224 | tf_op jit(solution)/shard_map/ppermute | solution.py:12
  124.4 1.4 collective-permute-done.19
  126.1 4.1 %collective-permute-start.20 = (bf16[128,512]{1,0:T(8,128)(2,1)S(1)}, bf16[128,512]{1,0:T(8,128)(2,1)S(1)}, u32[]{:S(2)}, u32[]{:S(2)}) collective-permute-start(bf16[128,512]{1,0:T(8,128)(2,1)S(1)} %fusion.8), channel_id=1, source_target_pairs={{0,30},{2,0},{4,2},{6,4},{8,6},{10,8},{12,10},{14,12},{16,14},{18,... | collective-permute-start | bytes 393224 | tf_op jit(solution)/shard_map/ppermute | solution.py:12
  130.2 0.6 collective-permute-done.26
  131.1 1.9 %collective-permute-start.27 = (bf16[128,512]{1,0:T(8,128)(2,1)S(1)}, bf16[128,512]{1,0:T(8,128)(2,1)S(1)}, u32[]{:S(2)}, u32[]{:S(2)}) collective-permute-start(bf16[128,512]{1,0:T(8,128)(2,1)S(1)} %fusion.37), channel_id=1, source_target_pairs={{0,2},{2,4},{4,6},{6,8},{8,10},{10,12},{12,14},{14,16},{16,18},{18... | collective-permute-start | bytes 393224 | tf_op jit(solution)/shard_map/ppermute | solution.py:12
  133.0 0.5 collective-permute-done.20
  133.7 5.5 %collective-permute-start.21 = (bf16[128,512]{1,0:T(8,128)(2,1)S(1)}, bf16[128,512]{1,0:T(8,128)(2,1)S(1)}, u32[]{:S(2)}, u32[]{:S(2)}) collective-permute-start(bf16[128,512]{1,0:T(8,128)(2,1)S(1)} %fusion.12), channel_id=1, source_target_pairs={{0,30},{2,0},{4,2},{6,4},{8,6},{10,8},{12,10},{14,12},{16,14},{18,... | collective-permute-start | bytes 393224 | tf_op jit(solution)/shard_map/ppermute | solution.py:12
  139.2 0.5 collective-permute-done.27
  139.9 1.9 %collective-permute-start.28 = (bf16[128,512]{1,0:T(8,128)(2,1)S(1)}, bf16[128,512]{1,0:T(8,128)(2,1)S(1)}, u32[]{:S(2)}, u32[]{:S(2)}) collective-permute-start(bf16[128,512]{1,0:T(8,128)(2,1)S(1)} %fusion.41), channel_id=1, source_target_pairs={{0,2},{2,4},{4,6},{6,8},{8,10},{10,12},{12,14},{14,16},{16,18},{18... | collective-permute-start | bytes 393224 | tf_op jit(solution)/shard_map/ppermute | solution.py:12
  142.1 5.4 %collective-permute-start.22 = (bf16[128,512]{1,0:T(8,128)(2,1)S(1)}, bf16[128,512]{1,0:T(8,128)(2,1)S(1)}, u32[]{:S(2)}, u32[]{:S(2)}) collective-permute-start(bf16[128,512]{1,0:T(8,128)(2,1)S(1)} %fusion.16), channel_id=1, source_target_pairs={{0,30},{2,0},{4,2},{6,4},{8,6},{10,8},{12,10},{14,12},{16,14},{18,... | collective-permute-start | bytes 393224 | tf_op jit(solution)/shard_map/ppermute | solution.py:12
  147.5 0.5 collective-permute-done.28
  148.2 1.9 %collective-permute-start.29 = (bf16[128,512]{1,0:T(8,128)(2,1)S(1)}, bf16[128,512]{1,0:T(8,128)(2,1)S(1)}, u32[]{:S(2)}, u32[]{:S(2)}) collective-permute-start(bf16[128,512]{1,0:T(8,128)(2,1)S(1)} %fusion.45), channel_id=1, source_target_pairs={{0,2},{2,4},{4,6},{6,8},{8,10},{10,12},{12,14},{14,16},{16,18},{18... | collective-permute-start | bytes 393224 | tf_op jit(solution)/shard_map/ppermute | solution.py:12
  150.4 5.4 %collective-permute-start.23 = (bf16[128,512]{1,0:T(8,128)(2,1)S(1)}, bf16[128,512]{1,0:T(8,128)(2,1)S(1)}, u32[]{:S(2)}, u32[]{:S(2)}) collective-permute-start(bf16[128,512]{1,0:T(8,128)(2,1)S(1)} %fusion.20), channel_id=1, source_target_pairs={{0,30},{2,0},{4,2},{6,4},{8,6},{10,8},{12,10},{14,12},{16,14},{18,... | collective-permute-start | bytes 393224 | tf_op jit(solution)/shard_map/ppermute | solution.py:12
  155.8 0.5 collective-permute-done.29
  156.5 1.9 %collective-permute-start.30 = (bf16[128,512]{1,0:T(8,128)(2,1)S(1)}, bf16[128,512]{1,0:T(8,128)(2,1)S(1)}, u32[]{:S(2)}, u32[]{:S(2)}) collective-permute-start(bf16[128,512]{1,0:T(8,128)(2,1)S(1)} %fusion.49), channel_id=1, source_target_pairs={{0,2},{2,4},{4,6},{6,8},{8,10},{10,12},{12,14},{14,16},{16,18},{18... | collective-permute-start | bytes 393224 | tf_op jit(solution)/shard_map/ppermute | solution.py:12
  158.7 5.4 %collective-permute-start.24 = (bf16[128,512]{1,0:T(8,128)(2,1)S(1)}, bf16[128,512]{1,0:T(8,128)(2,1)S(1)}, u32[]{:S(2)}, u32[]{:S(2)}) collective-permute-start(bf16[128,512]{1,0:T(8,128)(2,1)S(1)} %fusion.24), channel_id=1, source_target_pairs={{0,30},{2,0},{4,2},{6,4},{8,6},{10,8},{12,10},{14,12},{16,14},{18,... | collective-permute-start | bytes 393224 | tf_op jit(solution)/shard_map/ppermute | solution.py:12
  164.1 0.5 collective-permute-done.30
  164.8 1.9 %collective-permute-start.31 = (bf16[128,512]{1,0:T(8,128)(2,1)S(1)}, bf16[128,512]{1,0:T(8,128)(2,1)S(1)}, u32[]{:S(2)}, u32[]{:S(2)}) collective-permute-start(bf16[128,512]{1,0:T(8,128)(2,1)S(1)} %add_convert_fusion), channel_id=1, source_target_pairs={{0,2},{2,4},{4,6},{6,8},{8,10},{10,12},{12,14},{14,16},{16,18},{18... | collective-permute-start | bytes 393224 | tf_op jit(solution)/shard_map/ppermute | solution.py:12
  167.0 5.4 %collective-permute-start.32 = (bf16[128,512]{1,0:T(8,128)(2,1)S(1)}, bf16[128,512]{1,0:T(8,128)(2,1)S(1)}, u32[]{:S(2)}, u32[]{:S(2)}) collective-permute-start(bf16[128,512]{1,0:T(8,128)(2,1)S(1)} %convert_add_fusion), channel_id=1, source_target_pairs={{0,30},{2,0},{4,2},{6,4},{8,6},{10,8},{12,10},{14,12},{16,14},{18,... | collective-permute-start | bytes 393224 | tf_op jit(solution)/shard_map/ppermute | solution.py:12
  172.7 0.3 collective-permute-done.31
  172.9 2.0 %collective-permute-done.32 = bf16[128,512]{1,0:T(8,128)(2,1)S(1)} collective-permute-done((bf16[128,512]{1,0:T(8,128)(2,1)S(1)}, bf16[128,512]{1,0:T(8,128)(2,1)S(1)}, u32[]{:S(2)}, u32[]{:S(2)}) %collective-permute-start.32) | collective-permute-done | bytes 131104 | tf_op jit(solution)/shard_map/ppermute | solution.py:12
  175.2 3.0 %collective-permute-start.33 = (bf16[128,256]{1,0:T(8,128)(2,1)S(1)}, bf16[128,256]{1,0:T(8,128)(2,1)S(1)}, u32[]{:S(2)}, u32[]{:S(2)}) collective-permute-start(bf16[128,256]{1,0:T(8,128)(2,1)S(1)} %select_convert_fusion), channel_id=1, source_target_pairs={{0,1},{1,0},{2,3},{3,2},{4,5},{5,4},{6,7},{7,6},{8,9},{9,8},{10,11... | collective-permute-start | bytes 196616 | tf_op jit(solution)/shard_map/ppermute | solution.py:12
  178.2 3.2 %collective-permute-done.33 = bf16[128,256]{1,0:T(8,128)(2,1)S(1)} collective-permute-done((bf16[128,256]{1,0:T(8,128)(2,1)S(1)}, bf16[128,256]{1,0:T(8,128)(2,1)S(1)}, u32[]{:S(2)}, u32[]{:S(2)}) %collective-permute-start.33) | collective-permute-done | bytes 65568 | tf_op jit(solution)/shard_map/ppermute | solution.py:12
  181.3 0.7 add_convert_fusion.1
  (99 shorter events, 9.1 us)
Async XLA Ops:
  0.6 103.2 %copy-start = (bf16[10,256]{1,0:T(8,128)(2,1)S(1)}, bf16[10,256]{1,0:T(8,128)(2,1)}, u32[]{:S(2)}) copy-start(bf16[10,256]{1,0:T(8,128)(2,1)} %param.13) | copy-start | bytes 15364
  1.6 6.2 %collective-permute-start = (bf16[128,256]{0,1:T(8,128)(2,1)S(1)}, bf16[128,256]{0,1:T(8,128)(2,1)S(1)}, u32[]{:S(2)}, u32[]{:S(2)}) collective-permute-start(bf16[128,256]{0,1:T(8,128)(2,1)S(1)} %copy.10), channel_id=1, source_target_pairs={{0,1},{1,0},{2,3},{3,2},{4,5},{5,4},{6,7},{7,6},{8,9},{9,8},{10,11... | collective-permute-start | bytes 196616 | tf_op jit(solution)/shard_map/ppermute | solution.py:12
  7.8 21.1 %collective-permute-start.1 = (bf16[128,512]{0,1:T(8,128)(2,1)S(1)}, bf16[128,512]{0,1:T(8,128)(2,1)S(1)}, u32[]{:S(2)}, u32[]{:S(2)}) collective-permute-start(bf16[128,512]{0,1:T(8,128)(2,1)S(1)} %maximum_select_fusion.1), channel_id=1, source_target_pairs={{0,30},{2,0},{4,2},{6,4},{8,6},{10,8},{12,10},{14,12},{16,14},{18,... | collective-permute-start | bytes 393224 | tf_op jit(solution)/shard_map/ppermute | solution.py:12
  26.0 8.1 %collective-permute-start.8 = (bf16[128,512]{0,1:T(8,128)(2,1)S(1)}, bf16[128,512]{0,1:T(8,128)(2,1)S(1)}, u32[]{:S(2)}, u32[]{:S(2)}) collective-permute-start(bf16[128,512]{0,1:T(8,128)(2,1)S(1)} %maximum_select_fusion.1), channel_id=1, source_target_pairs={{0,2},{2,4},{4,6},{6,8},{8,10},{10,12},{12,14},{14,16},{16,18},{18... | collective-permute-start | bytes 393224 | tf_op jit(solution)/shard_map/ppermute | solution.py:12
  28.9 7.7 %collective-permute-start.2 = (bf16[128,512]{0,1:T(8,128)(2,1)S(1)}, bf16[128,512]{0,1:T(8,128)(2,1)S(1)}, u32[]{:S(2)}, u32[]{:S(2)}) collective-permute-start(bf16[128,512]{0,1:T(8,128)(2,1)S(1)} %collective-permute-done.1), channel_id=1, source_target_pairs={{0,30},{2,0},{4,2},{6,4},{8,6},{10,8},{12,10},{14,12},{16,14},{18,... | collective-permute-start | bytes 393224 | tf_op jit(solution)/shard_map/ppermute | solution.py:12
  34.1 8.1 %collective-permute-start.9 = (bf16[128,512]{0,1:T(8,128)(2,1)S(1)}, bf16[128,512]{0,1:T(8,128)(2,1)S(1)}, u32[]{:S(2)}, u32[]{:S(2)}) collective-permute-start(bf16[128,512]{0,1:T(8,128)(2,1)S(1)} %collective-permute-done.8), channel_id=1, source_target_pairs={{0,2},{2,4},{4,6},{6,8},{8,10},{10,12},{12,14},{14,16},{16,18},{18... | collective-permute-start | bytes 393224 | tf_op jit(solution)/shard_map/ppermute | solution.py:12
  36.6 8.1 %collective-permute-start.3 = (bf16[128,512]{0,1:T(8,128)(2,1)S(1)}, bf16[128,512]{0,1:T(8,128)(2,1)S(1)}, u32[]{:S(2)}, u32[]{:S(2)}) collective-permute-start(bf16[128,512]{0,1:T(8,128)(2,1)S(1)} %collective-permute-done.2), channel_id=1, source_target_pairs={{0,30},{2,0},{4,2},{6,4},{8,6},{10,8},{12,10},{14,12},{16,14},{18,... | collective-permute-start | bytes 393224 | tf_op jit(solution)/shard_map/ppermute | solution.py:12
  42.2 8.1 %collective-permute-start.10 = (bf16[128,512]{0,1:T(8,128)(2,1)S(1)}, bf16[128,512]{0,1:T(8,128)(2,1)S(1)}, u32[]{:S(2)}, u32[]{:S(2)}) collective-permute-start(bf16[128,512]{0,1:T(8,128)(2,1)S(1)} %collective-permute-done.9), channel_id=1, source_target_pairs={{0,2},{2,4},{4,6},{6,8},{8,10},{10,12},{12,14},{14,16},{16,18},{18... | collective-permute-start | bytes 393224 | tf_op jit(solution)/shard_map/ppermute | solution.py:12
  44.7 8.1 %collective-permute-start.4 = (bf16[128,512]{0,1:T(8,128)(2,1)S(1)}, bf16[128,512]{0,1:T(8,128)(2,1)S(1)}, u32[]{:S(2)}, u32[]{:S(2)}) collective-permute-start(bf16[128,512]{0,1:T(8,128)(2,1)S(1)} %collective-permute-done.3), channel_id=1, source_target_pairs={{0,30},{2,0},{4,2},{6,4},{8,6},{10,8},{12,10},{14,12},{16,14},{18,... | collective-permute-start | bytes 393224 | tf_op jit(solution)/shard_map/ppermute | solution.py:12
  50.2 8.1 %collective-permute-start.11 = (bf16[128,512]{0,1:T(8,128)(2,1)S(1)}, bf16[128,512]{0,1:T(8,128)(2,1)S(1)}, u32[]{:S(2)}, u32[]{:S(2)}) collective-permute-start(bf16[128,512]{0,1:T(8,128)(2,1)S(1)} %collective-permute-done.10), channel_id=1, source_target_pairs={{0,2},{2,4},{4,6},{6,8},{8,10},{10,12},{12,14},{14,16},{16,18},{18... | collective-permute-start | bytes 393224 | tf_op jit(solution)/shard_map/ppermute | solution.py:12
  52.7 8.9 %collective-permute-start.5 = (bf16[128,512]{0,1:T(8,128)(2,1)S(1)}, bf16[128,512]{0,1:T(8,128)(2,1)S(1)}, u32[]{:S(2)}, u32[]{:S(2)}) collective-permute-start(bf16[128,512]{0,1:T(8,128)(2,1)S(1)} %collective-permute-done.4), channel_id=1, source_target_pairs={{0,30},{2,0},{4,2},{6,4},{8,6},{10,8},{12,10},{14,12},{16,14},{18,... | collective-permute-start | bytes 393224 | tf_op jit(solution)/shard_map/ppermute | solution.py:12
  58.3 9.2 %collective-permute-start.12 = (bf16[128,512]{0,1:T(8,128)(2,1)S(1)}, bf16[128,512]{0,1:T(8,128)(2,1)S(1)}, u32[]{:S(2)}, u32[]{:S(2)}) collective-permute-start(bf16[128,512]{0,1:T(8,128)(2,1)S(1)} %collective-permute-done.11), channel_id=1, source_target_pairs={{0,2},{2,4},{4,6},{6,8},{8,10},{10,12},{12,14},{14,16},{16,18},{18... | collective-permute-start | bytes 393224 | tf_op jit(solution)/shard_map/ppermute | solution.py:12
  61.7 8.8 %collective-permute-start.6 = (bf16[128,512]{0,1:T(8,128)(2,1)S(1)}, bf16[128,512]{0,1:T(8,128)(2,1)S(1)}, u32[]{:S(2)}, u32[]{:S(2)}) collective-permute-start(bf16[128,512]{0,1:T(8,128)(2,1)S(1)} %collective-permute-done.5), channel_id=1, source_target_pairs={{0,30},{2,0},{4,2},{6,4},{8,6},{10,8},{12,10},{14,12},{16,14},{18,... | collective-permute-start | bytes 393224 | tf_op jit(solution)/shard_map/ppermute | solution.py:12
  67.5 8.6 %collective-permute-start.13 = (bf16[128,512]{0,1:T(8,128)(2,1)S(1)}, bf16[128,512]{0,1:T(8,128)(2,1)S(1)}, u32[]{:S(2)}, u32[]{:S(2)}) collective-permute-start(bf16[128,512]{0,1:T(8,128)(2,1)S(1)} %collective-permute-done.12), channel_id=1, source_target_pairs={{0,2},{2,4},{4,6},{6,8},{8,10},{10,12},{12,14},{14,16},{16,18},{18... | collective-permute-start | bytes 393224 | tf_op jit(solution)/shard_map/ppermute | solution.py:12
  70.5 15.6 %collective-permute-start.7 = (bf16[128,512]{0,1:T(8,128)(2,1)S(1)}, bf16[128,512]{0,1:T(8,128)(2,1)S(1)}, u32[]{:S(2)}, u32[]{:S(2)}) collective-permute-start(bf16[128,512]{0,1:T(8,128)(2,1)S(1)} %collective-permute-done.6), channel_id=1, source_target_pairs={{0,30},{2,0},{4,2},{6,4},{8,6},{10,8},{12,10},{14,12},{16,14},{18,... | collective-permute-start | bytes 393224 | tf_op jit(solution)/shard_map/ppermute | solution.py:12
  76.1 8.1 %collective-permute-start.14 = (bf16[128,512]{0,1:T(8,128)(2,1)S(1)}, bf16[128,512]{0,1:T(8,128)(2,1)S(1)}, u32[]{:S(2)}, u32[]{:S(2)}) collective-permute-start(bf16[128,512]{0,1:T(8,128)(2,1)S(1)} %collective-permute-done.13), channel_id=1, source_target_pairs={{0,2},{2,4},{4,6},{6,8},{8,10},{10,12},{12,14},{14,16},{16,18},{18... | collective-permute-start | bytes 393224 | tf_op jit(solution)/shard_map/ppermute | solution.py:12
  84.2 8.1 %collective-permute-start.15 = (bf16[128,512]{0,1:T(8,128)(2,1)S(1)}, bf16[128,512]{0,1:T(8,128)(2,1)S(1)}, u32[]{:S(2)}, u32[]{:S(2)}) collective-permute-start(bf16[128,512]{0,1:T(8,128)(2,1)S(1)} %collective-permute-done.14), channel_id=1, source_target_pairs={{0,2},{2,4},{4,6},{6,8},{8,10},{10,12},{12,14},{14,16},{16,18},{18... | collective-permute-start | bytes 393224 | tf_op jit(solution)/shard_map/ppermute | solution.py:12
  93.1 2.2 %copy-start.1 = (bf16[8192,256]{1,0:T(8,128)(2,1)S(1)}, bf16[8192,256]{1,0:T(8,128)(2,1)}, u32[]{:S(2)}) copy-start(bf16[8192,256]{1,0:T(8,128)(2,1)} %param.10) | copy-start | bytes 12582916
  96.2 3.2 %copy-start.2 = (bf16[8192,256]{1,0:T(8,128)(2,1)S(1)}, bf16[8192,256]{1,0:T(8,128)(2,1)}, u32[]{:S(2)}) copy-start(bf16[8192,256]{1,0:T(8,128)(2,1)} %param.9) | copy-start | bytes 12582916
  96.2 7.6 %collective-permute-start.16 = (bf16[3,256]{1,0:T(4,128)(2,1)S(1)}, bf16[3,256]{1,0:T(4,128)(2,1)S(1)}, u32[]{:S(2)}, u32[]{:S(2)}) collective-permute-start(bf16[3,256]{1,0:T(4,128)(2,1)S(1)} %convolution_convert_fusion.2), channel_id=1, source_target_pairs={{0,32},{32,64},{64,96},{96,128},{128,160},{160,192},{192,224},{224... | collective-permute-start | bytes 4616 | tf_op jit(solution)/shard_map/ppermute | solution.py:89
  99.4 4.4 %copy-start.3 = (f32[256]{0:T(256)S(1)}, f32[256]{0:T(256)}, u32[]{:S(2)}) copy-start(f32[256]{0:T(256)} %param.12) | copy-start | bytes 3076
  99.4 4.4 %copy-start.4 = (s32[128]{0:T(128)S(1)}, s32[128]{0:T(128)}, u32[]{:S(2)}) copy-start(s32[128]{0:T(128)} %param.14) | copy-start | bytes 1540
  104.1 4.4 %collective-permute-start.17 = (f32[3,256]{1,0:T(4,128)S(1)}, f32[3,256]{1,0:T(4,128)S(1)}, u32[]{:S(2)}, u32[]{:S(2)}) collective-permute-start(f32[3,256]{1,0:T(4,128)S(1)} %fusion.155), channel_id=1, source_target_pairs={{32,0},{64,32},{96,64},{128,96},{160,128},{192,160},{224,192},{256... | collective-permute-start | bytes 9224 | tf_op jit(solution)/shard_map/ppermute | solution.py:89
  108.8 8.7 %collective-permute-start.18 = (bf16[128,512]{1,0:T(8,128)(2,1)S(1)}, bf16[128,512]{1,0:T(8,128)(2,1)S(1)}, u32[]{:S(2)}, u32[]{:S(2)}) collective-permute-start(bf16[128,512]{1,0:T(8,128)(2,1)S(1)} %fusion), channel_id=1, source_target_pairs={{0,30},{2,0},{4,2},{6,4},{8,6},{10,8},{12,10},{14,12},{16,14},{18,... | collective-permute-start | bytes 393224 | tf_op jit(solution)/shard_map/ppermute | solution.py:12
  112.4 8.7 %collective-permute-start.25 = (bf16[128,512]{1,0:T(8,128)(2,1)S(1)}, bf16[128,512]{1,0:T(8,128)(2,1)S(1)}, u32[]{:S(2)}, u32[]{:S(2)}) collective-permute-start(bf16[128,512]{1,0:T(8,128)(2,1)S(1)} %fusion.29), channel_id=1, source_target_pairs={{0,2},{2,4},{4,6},{6,8},{8,10},{10,12},{12,14},{14,16},{16,18},{18... | collective-permute-start | bytes 393224 | tf_op jit(solution)/shard_map/ppermute | solution.py:12
  117.8 8.0 %collective-permute-start.19 = (bf16[128,512]{1,0:T(8,128)(2,1)S(1)}, bf16[128,512]{1,0:T(8,128)(2,1)S(1)}, u32[]{:S(2)}, u32[]{:S(2)}) collective-permute-start(bf16[128,512]{1,0:T(8,128)(2,1)S(1)} %fusion.4), channel_id=1, source_target_pairs={{0,30},{2,0},{4,2},{6,4},{8,6},{10,8},{12,10},{14,12},{16,14},{18,... | collective-permute-start | bytes 393224 | tf_op jit(solution)/shard_map/ppermute | solution.py:12
  121.4 9.5 %collective-permute-start.26 = (bf16[128,512]{1,0:T(8,128)(2,1)S(1)}, bf16[128,512]{1,0:T(8,128)(2,1)S(1)}, u32[]{:S(2)}, u32[]{:S(2)}) collective-permute-start(bf16[128,512]{1,0:T(8,128)(2,1)S(1)} %fusion.33), channel_id=1, source_target_pairs={{0,2},{2,4},{4,6},{6,8},{8,10},{10,12},{12,14},{14,16},{16,18},{18... | collective-permute-start | bytes 393224 | tf_op jit(solution)/shard_map/ppermute | solution.py:12
  126.1 7.4 %collective-permute-start.20 = (bf16[128,512]{1,0:T(8,128)(2,1)S(1)}, bf16[128,512]{1,0:T(8,128)(2,1)S(1)}, u32[]{:S(2)}, u32[]{:S(2)}) collective-permute-start(bf16[128,512]{1,0:T(8,128)(2,1)S(1)} %fusion.8), channel_id=1, source_target_pairs={{0,30},{2,0},{4,2},{6,4},{8,6},{10,8},{12,10},{14,12},{16,14},{18,... | collective-permute-start | bytes 393224 | tf_op jit(solution)/shard_map/ppermute | solution.py:12
  131.1 8.6 %collective-permute-start.27 = (bf16[128,512]{1,0:T(8,128)(2,1)S(1)}, bf16[128,512]{1,0:T(8,128)(2,1)S(1)}, u32[]{:S(2)}, u32[]{:S(2)}) collective-permute-start(bf16[128,512]{1,0:T(8,128)(2,1)S(1)} %fusion.37), channel_id=1, source_target_pairs={{0,2},{2,4},{4,6},{6,8},{8,10},{10,12},{12,14},{14,16},{16,18},{18... | collective-permute-start | bytes 393224 | tf_op jit(solution)/shard_map/ppermute | solution.py:12
  133.7 8.1 %collective-permute-start.21 = (bf16[128,512]{1,0:T(8,128)(2,1)S(1)}, bf16[128,512]{1,0:T(8,128)(2,1)S(1)}, u32[]{:S(2)}, u32[]{:S(2)}) collective-permute-start(bf16[128,512]{1,0:T(8,128)(2,1)S(1)} %fusion.12), channel_id=1, source_target_pairs={{0,30},{2,0},{4,2},{6,4},{8,6},{10,8},{12,10},{14,12},{16,14},{18,... | collective-permute-start | bytes 393224 | tf_op jit(solution)/shard_map/ppermute | solution.py:12
  139.9 8.1 %collective-permute-start.28 = (bf16[128,512]{1,0:T(8,128)(2,1)S(1)}, bf16[128,512]{1,0:T(8,128)(2,1)S(1)}, u32[]{:S(2)}, u32[]{:S(2)}) collective-permute-start(bf16[128,512]{1,0:T(8,128)(2,1)S(1)} %fusion.41), channel_id=1, source_target_pairs={{0,2},{2,4},{4,6},{6,8},{8,10},{10,12},{12,14},{14,16},{16,18},{18... | collective-permute-start | bytes 393224 | tf_op jit(solution)/shard_map/ppermute | solution.py:12
  142.1 8.1 %collective-permute-start.22 = (bf16[128,512]{1,0:T(8,128)(2,1)S(1)}, bf16[128,512]{1,0:T(8,128)(2,1)S(1)}, u32[]{:S(2)}, u32[]{:S(2)}) collective-permute-start(bf16[128,512]{1,0:T(8,128)(2,1)S(1)} %fusion.16), channel_id=1, source_target_pairs={{0,30},{2,0},{4,2},{6,4},{8,6},{10,8},{12,10},{14,12},{16,14},{18,... | collective-permute-start | bytes 393224 | tf_op jit(solution)/shard_map/ppermute | solution.py:12
  148.2 8.1 %collective-permute-start.29 = (bf16[128,512]{1,0:T(8,128)(2,1)S(1)}, bf16[128,512]{1,0:T(8,128)(2,1)S(1)}, u32[]{:S(2)}, u32[]{:S(2)}) collective-permute-start(bf16[128,512]{1,0:T(8,128)(2,1)S(1)} %fusion.45), channel_id=1, source_target_pairs={{0,2},{2,4},{4,6},{6,8},{8,10},{10,12},{12,14},{14,16},{16,18},{18... | collective-permute-start | bytes 393224 | tf_op jit(solution)/shard_map/ppermute | solution.py:12
  150.4 8.1 %collective-permute-start.23 = (bf16[128,512]{1,0:T(8,128)(2,1)S(1)}, bf16[128,512]{1,0:T(8,128)(2,1)S(1)}, u32[]{:S(2)}, u32[]{:S(2)}) collective-permute-start(bf16[128,512]{1,0:T(8,128)(2,1)S(1)} %fusion.20), channel_id=1, source_target_pairs={{0,30},{2,0},{4,2},{6,4},{8,6},{10,8},{12,10},{14,12},{16,14},{18,... | collective-permute-start | bytes 393224 | tf_op jit(solution)/shard_map/ppermute | solution.py:12
  156.5 8.1 %collective-permute-start.30 = (bf16[128,512]{1,0:T(8,128)(2,1)S(1)}, bf16[128,512]{1,0:T(8,128)(2,1)S(1)}, u32[]{:S(2)}, u32[]{:S(2)}) collective-permute-start(bf16[128,512]{1,0:T(8,128)(2,1)S(1)} %fusion.49), channel_id=1, source_target_pairs={{0,2},{2,4},{4,6},{6,8},{8,10},{10,12},{12,14},{14,16},{16,18},{18... | collective-permute-start | bytes 393224 | tf_op jit(solution)/shard_map/ppermute | solution.py:12
  158.7 8.1 %collective-permute-start.24 = (bf16[128,512]{1,0:T(8,128)(2,1)S(1)}, bf16[128,512]{1,0:T(8,128)(2,1)S(1)}, u32[]{:S(2)}, u32[]{:S(2)}) collective-permute-start(bf16[128,512]{1,0:T(8,128)(2,1)S(1)} %fusion.24), channel_id=1, source_target_pairs={{0,30},{2,0},{4,2},{6,4},{8,6},{10,8},{12,10},{14,12},{16,14},{18,... | collective-permute-start | bytes 393224 | tf_op jit(solution)/shard_map/ppermute | solution.py:12
  164.8 8.1 %collective-permute-start.31 = (bf16[128,512]{1,0:T(8,128)(2,1)S(1)}, bf16[128,512]{1,0:T(8,128)(2,1)S(1)}, u32[]{:S(2)}, u32[]{:S(2)}) collective-permute-start(bf16[128,512]{1,0:T(8,128)(2,1)S(1)} %add_convert_fusion), channel_id=1, source_target_pairs={{0,2},{2,4},{4,6},{6,8},{8,10},{10,12},{12,14},{14,16},{16,18},{18... | collective-permute-start | bytes 393224 | tf_op jit(solution)/shard_map/ppermute | solution.py:12
  167.0 7.9 %collective-permute-start.32 = (bf16[128,512]{1,0:T(8,128)(2,1)S(1)}, bf16[128,512]{1,0:T(8,128)(2,1)S(1)}, u32[]{:S(2)}, u32[]{:S(2)}) collective-permute-start(bf16[128,512]{1,0:T(8,128)(2,1)S(1)} %convert_add_fusion), channel_id=1, source_target_pairs={{0,30},{2,0},{4,2},{6,4},{8,6},{10,8},{12,10},{14,12},{16,14},{18,... | collective-permute-start | bytes 393224 | tf_op jit(solution)/shard_map/ppermute | solution.py:12
  175.2 6.2 %collective-permute-start.33 = (bf16[128,256]{1,0:T(8,128)(2,1)S(1)}, bf16[128,256]{1,0:T(8,128)(2,1)S(1)}, u32[]{:S(2)}, u32[]{:S(2)}) collective-permute-start(bf16[128,256]{1,0:T(8,128)(2,1)S(1)} %select_convert_fusion), channel_id=1, source_target_pairs={{0,1},{1,0},{2,3},{3,2},{4,5},{5,4},{6,7},{7,6},{8,9},{9,8},{10,11... | collective-permute-start | bytes 196616 | tf_op jit(solution)/shard_map/ppermute | solution.py:12
